TPU v7x, 256 devices: a whole 4x4x8 slice. The times are simulated.
256 devices in a mesh: req: 32 (over z, x_hi, core), mlp: 8 (over x_lo, y).
Axes of the slice: x: 4 (x_hi: 2, x_lo: 2; x = x_hi * 2 + x_lo), y: 4, z: 8, core: 2. Of those that a mesh axis runs over, the one named last changes fastest.
Arguments:
- residual_in: bfloat16 [1024, 2560], P('req'), may hold values from -6 to 6
- queries: bfloat16 [1024, 2560], P('req', 'mlp')
- fresh_rotated_keys: bfloat16 [1024, 640], P('req', 'mlp'), may hold values from -6 to 6
- fresh_value_rows: bfloat16 [1024, 640], P('req', 'mlp'), may hold values from -6 to 6
- shared_prefix_keys: bfloat16 [32, 16384, 640], P(None, 'req', 'mlp'), may hold values from -6 to 6
- shared_prefix_values: bfloat16 [32, 16384, 640], P(None, 'req', 'mlp'), may hold values from -6 to 6
- sample_tail_keys: bfloat16 [32, 16, 128, 640], P('req', None, None, 'mlp'), may hold values from -6 to 6
- sample_tail_values: bfloat16 [32, 16, 128, 640], P('req', None, None, 'mlp'), may hold values from -6 to 6
- prompt_prefix_length: int32 [32], replicated, may hold values from 1 to 16384, as said below
- sample_tail_length: int32 [32, 16], P('req'), may hold values from 0 to 128, as said below
- out_weight: bfloat16 [2560, 2560], P('mlp'), may hold values from -0.125 to 0.125
- gate_weight: bfloat16 [2560, 4096], P(None, 'mlp'), may hold values from -0.125 to 0.125
- up_weight: bfloat16 [2560, 4096], P(None, 'mlp'), may hold values from -0.125 to 0.125
- down_weight: bfloat16 [4096, 2560], P('mlp'), may hold values from -0.09375 to 0.09375
- mlp_gain: float32 [2560], replicated, may hold values from 0.1 to 1.9
- final_gain: float32 [2560], replicated, may hold values from 0.1 to 1.9
- score_weight: float32 [2560], replicated, may hold values from -0.125 to 0.125
Outputs:
- layer_out: bfloat16 [1024, 2560], P('req', 'mlp')
- score: float32 [1024], P('req')
Inputs may be any that keep to these rules, and one draw needn't show every extreme that they name: `prompt_prefix_length`: one prompt in every draw has the full prefix length 16384. `sample_tail_length`: one sample in every draw has the full tail length 128.
All inputs are finite; a program needn't handle non-finite values.
Results may differ from a plain program's by a relative error of at most 0.02.
Values may be sent and summed in bfloat16 or wider, within the bound.
No kernel may reach another device: no remote copies, remote signals or barrier semaphores. Data moves between devices by JAX's collectives and lax.ppermute only.
A program may use at most 128 MiB of HBM per device.

v0:
```python
import jax
import jax.numpy as jnp
from jax import lax
from jax.sharding import PartitionSpec as P

D = 2560
QUERY_HEADS = 32
KEY_VALUE_HEADS = 8
HEAD_SIZE = 80
SAMPLE_COUNT = 16
DECODE_TOKENS = 2
TAIL_LENGTH = 128


def rms_scale(total_sq, width):
    return lax.rsqrt(total_sq / width + 1e-05)


def on_device(
    residual_in,
    queries,
    fresh_rotated_keys,
    fresh_value_rows,
    shared_prefix_keys,
    shared_prefix_values,
    sample_tail_keys,
    sample_tail_values,
    prompt_prefix_length,
    sample_tail_length,
    out_weight,
    gate_weight,
    up_weight,
    down_weight,
    mlp_gain,
    final_gain,
    score_weight,
):
    query_groups = QUERY_HEADS // KEY_VALUE_HEADS
    inv_root = HEAD_SIZE ** (-0.5)
    kv_local = fresh_rotated_keys.shape[1] // HEAD_SIZE
    prompts = shared_prefix_keys.shape[0]
    piece_len = shared_prefix_keys.shape[1]
    req_index = lax.axis_index("req")
    low = jnp.float32(-1e30)
    gathered = lax.all_gather(queries, "req", axis=0, tiled=True)
    query_all = gathered.reshape(
        prompts, SAMPLE_COUNT, DECODE_TOKENS, kv_local, query_groups, HEAD_SIZE
    )
    prefix_key_block = shared_prefix_keys.reshape(prompts, piece_len, kv_local, HEAD_SIZE)
    prefix_value_block = shared_prefix_values.reshape(prompts, piece_len, kv_local, HEAD_SIZE)
    score_pre = (
        jnp.einsum(
            "psjkgh,plkh->pksjgl", query_all, prefix_key_block, preferred_element_type=jnp.float32
        )
        * inv_root
    )
    key_place = req_index * piece_len + jnp.arange(piece_len)
    valid = (key_place[None, :] < prompt_prefix_length[:, None])[:, None, None, None, None, :]
    piece_top = jnp.max(jnp.where(valid, score_pre, low), -1)
    piece_w = jnp.where(valid, jnp.exp(score_pre - piece_top[..., None]), 0.0)
    piece_sum = jnp.sum(piece_w, -1)
    piece_out = jnp.einsum(
        "pksjgl,plkh->pksjgh",
        piece_w.astype(jnp.bfloat16),
        prefix_value_block,
        preferred_element_type=jnp.float32,
    )
    source_out, source_top, source_sum = (
        lax.all_to_all(piece_out, "req", split_axis=0, concat_axis=0, tiled=True),
        lax.all_to_all(piece_top, "req", split_axis=0, concat_axis=0, tiled=True),
        lax.all_to_all(piece_sum, "req", split_axis=0, concat_axis=0, tiled=True),
    )
    query_own = queries.reshape(SAMPLE_COUNT, DECODE_TOKENS, kv_local, query_groups, HEAD_SIZE)
    tail_key_block = sample_tail_keys.reshape(SAMPLE_COUNT, TAIL_LENGTH, kv_local, HEAD_SIZE)
    tail_value_block = sample_tail_values.reshape(SAMPLE_COUNT, TAIL_LENGTH, kv_local, HEAD_SIZE)
    fresh_k = fresh_rotated_keys.reshape(SAMPLE_COUNT, DECODE_TOKENS, kv_local, HEAD_SIZE)
    fresh_v = fresh_value_rows.reshape(SAMPLE_COUNT, DECODE_TOKENS, kv_local, HEAD_SIZE)
    score_tail = (
        jnp.einsum(
            "sjkgh,stkh->ksjgt", query_own, tail_key_block, preferred_element_type=jnp.float32
        )
        * inv_root
    )
    score_new = (
        jnp.einsum("sjkgh,sikh->ksjgi", query_own, fresh_k, preferred_element_type=jnp.float32)
        * inv_root
    )
    mask_tail = (jnp.arange(TAIL_LENGTH)[None, :] < sample_tail_length[0][:, None])[
        None, :, None, None, :
    ]
    causal = (jnp.arange(DECODE_TOKENS)[None, :] <= jnp.arange(DECODE_TOKENS)[:, None])[
        None, None, :, None, :
    ]
    local_top = jnp.maximum(
        jnp.max(jnp.where(mask_tail, score_tail, low), -1),
        jnp.max(jnp.where(causal, score_new, low), -1),
    )
    w_tail = jnp.where(mask_tail, jnp.exp(score_tail - local_top[..., None]), 0.0)
    w_new = jnp.where(causal, jnp.exp(score_new - local_top[..., None]), 0.0)
    local_sum = jnp.sum(w_tail, -1) + jnp.sum(w_new, -1)
    local_out = jnp.einsum(
        "ksjgt,stkh->ksjgh",
        w_tail.astype(jnp.bfloat16),
        tail_value_block,
        preferred_element_type=jnp.float32,
    )
    local_out = local_out + jnp.einsum(
        "ksjgi,sikh->ksjgh", w_new.astype(jnp.bfloat16), fresh_v, preferred_element_type=jnp.float32
    )
    overall = jnp.maximum(jnp.max(source_top, 0), local_top)
    source_w = jnp.exp(source_top - overall[None])
    local_w = jnp.exp(local_top - overall)
    numer = jnp.sum(source_w[..., None] * source_out, 0) + local_w[..., None] * local_out
    denom = jnp.sum(source_w * source_sum, 0) + local_w * local_sum
    attention_layer = (numer / denom[..., None]).astype(jnp.bfloat16)
    attention_layer = jnp.transpose(attention_layer, (1, 2, 0, 3, 4)).reshape(
        SAMPLE_COUNT * DECODE_TOKENS, kv_local * query_groups * HEAD_SIZE
    )
    projected = jnp.dot(attention_layer, out_weight, preferred_element_type=jnp.float32)
    mlp_count = lax.axis_size("mlp")
    mlp_index = lax.axis_index("mlp")
    share = D // mlp_count
    mid = residual_in.astype(jnp.float32) + lax.psum(projected.astype(jnp.bfloat16), "mlp").astype(
        jnp.float32
    )
    normed = (mid * rms_scale(jnp.sum(mid * mid, -1, keepdims=True), D) * mlp_gain).astype(
        jnp.bfloat16
    )
    gate = jnp.dot(normed, gate_weight, preferred_element_type=jnp.float32)
    upper = jnp.dot(normed, up_weight, preferred_element_type=jnp.float32)
    hidden = (jax.nn.silu(gate) * upper).astype(jnp.bfloat16)
    stream = mid + lax.psum(
        jnp.dot(hidden, down_weight, preferred_element_type=jnp.float32).astype(jnp.bfloat16), "mlp"
    ).astype(jnp.float32)
    score = jnp.sum(
        stream
        * rms_scale(jnp.sum(stream * stream, -1, keepdims=True), D)
        * final_gain
        * score_weight,
        -1,
    )
    layer_out = lax.dynamic_slice_in_dim(stream, mlp_index * share, share, 1).astype(jnp.bfloat16)
    return (layer_out, score)


def solution(mesh):
    placed = (
        P("req", None),
        P("req", "mlp"),
        P("req", "mlp"),
        P("req", "mlp"),
        P(None, "req", "mlp"),
        P(None, "req", "mlp"),
        P("req", None, None, "mlp"),
        P("req", None, None, "mlp"),
        P(),
        P("req", None),
        P("mlp", None),
        P(None, "mlp"),
        P(None, "mlp"),
        P("mlp", None),
        P(),
        P(),
        P(),
    )
    return jax.shard_map(
        on_device,
        mesh=mesh,
        in_specs=placed,
        out_specs=(P("req", "mlp"), P("req")),
        check_vma=False,
    )
```

profile of v0, /device:TPU:6, one launch (start us, length us, event | category | flops | bytes accessed | tf_op | source)
XLA Modules:
  0.0 322.3 jit_solution(5369909995095081894)
XLA Ops:
  7.2 43.4 %all_gather.3 = bf16[1024,320]{1,0:T(8,128)(2,1)S(1)} all-gather(bf16[32,320]{1,0:T(8,128)(2,1)} %param.18), channel_id=1, replica_groups=mesh['req'=32,'mlp'=8] {'req'}, dimensions={0}, use_global_device_ids=true | all-gather | bytes 675840 | tf_op jit(solution)/shard_map/all_gather | solution.py:45
  50.6 1.6 reshape.254
  52.3 0.1 broadcast_compare_fusion
  52.4 2.8 select_reduce_fusion
  55.2 2.3 fusion
  57.4 0.9 copy-done.1
  58.4 0.7 reshape.268
  59.1 8.4 %all-to-all-start.2 = ((f32[32,1,128]{2,1,0:T(1,128)}), f32[32,1,128]{2,1,0:T(1,128)S(1)}, u32[]{:S(2)}, u32[]{:S(2)}) async-start(f32[32,1,128]{2,1,0:T(1,128)} %reshape.268), calls=%async_computation.2 | async-start | bytes 32768 | tf_op jit(solution)/shard_map/all_to_all | solution.py:71
  67.6 0.7 reshape.266
  68.3 6.4 %all-to-all-done.2 = f32[32,1,128]{2,1,0:T(1,128)S(1)} async-done(((f32[32,1,128]{2,1,0:T(1,128)}), f32[32,1,128]{2,1,0:T(1,128)S(1)}, u32[]{:S(2)}, u32[]{:S(2)}) %all-to-all-start.2) | async-done | bytes 16416 | tf_op jit(solution)/shard_map/all_to_all | solution.py:71
  74.7 6.3 %all-to-all-start = ((f32[32,1,128]{2,1,0:T(1,128)}), f32[32,1,128]{2,1,0:T(1,128)S(1)}, u32[]{:S(2)}, u32[]{:S(2)}) async-start(f32[32,1,128]{2,1,0:T(1,128)} %reshape.266), calls=%async_computation | async-start | bytes 32768 | tf_op jit(solution)/shard_map/all_to_all | solution.py:70
  81.0 7.2 %fusion.11 = f32[32,1,16,2,4,80]{5,2,4,3,1,0:T(8,128)} fusion(bf16[32,512,80]{1,2,0:T(8,128)(2,1)} %param.22, f32[32,16,2,4,512]{4,1,3,2,0:T(8,128)} %copy-done.1, f32[32,16,2,4]{1,3,2,0:T(4,128)S(1)} %get-tuple-element.8, pred[32,512]{1,0:T(8,128)(4,1)S(1)} %broadcast_compare_fusion), kind=kOutput, calls=%fused_computation.15 | convolution fusion | flops 343932928 | bytes 12353536 | tf_op jit(solution)/shard_map/pksjgl,plkh->pksjgh/dot_general | solution.py:62
  88.3 10.1 %all-to-all-start.1 = ((f32[32,1,16,2,4,80]{5,2,4,3,1,0:T(8,128)}), f32[32,1,16,2,4,80]{5,2,4,3,1,0:T(8,128)}, u32[]{:S(2)}, u32[]{:S(2)}) async-start(f32[32,1,16,2,4,80]{5,2,4,3,1,0:T(8,128)} %fusion.11), calls=%async_computation.1 | async-start | bytes 4194304 | tf_op jit(solution)/shard_map/all_to_all | solution.py:69
  98.4 0.1 reshape.255
  98.5 0.4 select_reduce_fusion.2
  99.0 0.1 copy.35
  99.1 0.1 iota_compare_fusion
  99.2 0.3 select_reduce_fusion.1
  99.4 0.1 copy.34
  99.5 0.5 broadcast.104
  100.1 0.7 reduce.15
  100.7 0.1 reshape.267
  100.9 0.1 bitcast_reduce_fusion.2
  100.9 0.1 copy.39
  101.0 0.1 fusion.39
  101.2 0.1 copy.44
  101.3 0.2 fusion.31
  101.5 0.1 copy.43
  101.6 0.7 reduce.16
  102.3 0.1 reshape.269
  102.4 0.1 bitcast_reduce_fusion.1
  102.5 0.1 copy.45
  102.6 0.1 copy.38
  102.8 0.3 fusion.22
  103.1 45.6 %all-to-all-done.1 = f32[32,1,16,2,4,80]{5,2,4,3,1,0:T(8,128)} async-done(((f32[32,1,16,2,4,80]{5,2,4,3,1,0:T(8,128)}), f32[32,1,16,2,4,80]{5,2,4,3,1,0:T(8,128)}, u32[]{:S(2)}, u32[]{:S(2)}) %all-to-all-start.1) | async-done | bytes 1310752 | tf_op jit(solution)/shard_map/all_to_all | solution.py:69
  148.7 1.9 bitcast_reduce_fusion
  150.6 0.3 fusion.19
  150.9 0.1 reshape_transpose.3
  151.0 2.5 convolution_convert_fusion.1
  153.5 0.0 all-reduce.5.cloned.1.call-start
  153.6 74.1 %all-reduce.3.cloned.1.call-done = bf16[32,2560]{1,0:T(8,128)(2,1)} async-done(((bf16[32,2560]{1,0:T(8,128)(2,1)}), bf16[32,2560]{1,0:T(8,128)(2,1)}) %all-reduce.3.cloned.1.call-update) | async-done | bytes 163856 | tf_op jit(solution)/shard_map/psum | solution.py:123
  227.7 1.1 multiply_reduce_fusion.2
  228.9 2.4 fusion.45
  231.3 4.3 %convolution_convert_fusion = bf16[32,2560]{1,0:T(8,128)(2,1)} fusion(bf16[512,2560]{1,0:T(8,128)(2,1)} %param.30, bf16[2560,512]{1,0:T(8,128)(2,1)} %param.29, f32[32,512]{1,0:T(8,128)S(1)} %fusion.45, bf16[32,2560]{1,0:T(8,128)(2,1)S(1)} %copy-done.3, bf16[32,2560]{1,0:T(8,128)(2,1)S(1)} %copy-done.2, f32[2560]{0:T(1024)S(1)} %copy-done.6, ...), kind=kOutput, calls=%fused_computation.9 | convolution fusion | flops 168443904 | bytes 5810304 | tf_op jit(solution)/shard_map/dot_general | solution.py:133
  235.7 77.2 %all-reduce.5.cloned.1.call-done = bf16[32,2560]{1,0:T(8,128)(2,1)} async-done(((bf16[32,2560]{1,0:T(8,128)(2,1)}), bf16[32,2560]{1,0:T(8,128)(2,1)}) %all-reduce.5.cloned.1.call-update) | async-done | bytes 163856 | tf_op jit(solution)/shard_map/psum | solution.py:132
  312.9 1.1 multiply_reduce_fusion.1
  314.0 0.7 dynamic-slice_convert_fusion
  314.7 0.7 multiply_reduce_fusion
  (40 shorter events, 0.3 us)
Async XLA Ops:
  7.2 45.2 %copy-start = (bf16[32,512,80]{1,2,0:T(8,128)(2,1)S(1)}, bf16[32,512,80]{1,2,0:T(8,128)(2,1)}, u32[]{:S(2)}) copy-start(bf16[32,512,80]{1,2,0:T(8,128)(2,1)} %param.21) | copy-start | bytes 7864324
  7.2 45.1 %copy-start.9 = (s32[32]{0:T(128)S(1)}, s32[32]{0:T(128)}, u32[]{:S(2)}) copy-start(s32[32]{0:T(128)} %param.25) | copy-start | bytes 388
  55.2 3.2 copy-start.1
  59.1 15.6 %all-to-all-start.2 = ((f32[32,1,128]{2,1,0:T(1,128)}), f32[32,1,128]{2,1,0:T(1,128)S(1)}, u32[]{:S(2)}, u32[]{:S(2)}) async-start(f32[32,1,128]{2,1,0:T(1,128)} %reshape.268), calls=%async_computation.2 | async-start | bytes 32768 | tf_op jit(solution)/shard_map/all_to_all | solution.py:71
  74.7 13.6 %all-to-all-start = ((f32[32,1,128]{2,1,0:T(1,128)}), f32[32,1,128]{2,1,0:T(1,128)S(1)}, u32[]{:S(2)}, u32[]{:S(2)}) async-start(f32[32,1,128]{2,1,0:T(1,128)} %reshape.266), calls=%async_computation | async-start | bytes 32768 | tf_op jit(solution)/shard_map/all_to_all | solution.py:70
  88.3 10.2 %copy-start.5 = (bf16[32,320]{1,0:T(8,128)(2,1)S(1)}, bf16[32,320]{1,0:T(8,128)(2,1)}, u32[]{:S(2)}) copy-start(bf16[32,320]{1,0:T(8,128)(2,1)} %param.18) | copy-start | bytes 61444
  88.3 10.3 %copy-start.12 = (bf16[32,80]{1,0:T(8,128)(2,1)S(1)}, bf16[32,80]{1,0:T(8,128)(2,1)}, u32[]{:S(2)}) copy-start(bf16[32,80]{1,0:T(8,128)(2,1)} %param.19) | copy-start | bytes 15364
  88.3 10.8 %copy-start.10 = (s32[1,16]{1,0:T(1,128)S(1)}, s32[1,16]{1,0:T(1,128)}, u32[]{:S(2)}) copy-start(s32[1,16]{1,0:T(1,128)} %param.26) | copy-start | bytes 196
  88.3 10.9 %copy-start.4 = (bf16[1,16,128,80]{2,3,1,0:T(8,128)(2,1)S(1)}, bf16[1,16,128,80]{2,3,1,0:T(8,128)(2,1)}, u32[]{:S(2)}) copy-start(bf16[1,16,128,80]{2,3,1,0:T(8,128)(2,1)} %param.23) | copy-start | bytes 983044
  88.3 14.5 %copy-start.11 = (bf16[1,16,128,80]{2,3,1,0:T(8,128)(2,1)S(1)}, bf16[1,16,128,80]{2,3,1,0:T(8,128)(2,1)}, u32[]{:S(2)}) copy-start(bf16[1,16,128,80]{2,3,1,0:T(8,128)(2,1)} %param.24) | copy-start | bytes 983044
  88.3 60.4 %all-to-all-start.1 = ((f32[32,1,16,2,4,80]{5,2,4,3,1,0:T(8,128)}), f32[32,1,16,2,4,80]{5,2,4,3,1,0:T(8,128)}, u32[]{:S(2)}, u32[]{:S(2)}) async-start(f32[32,1,16,2,4,80]{5,2,4,3,1,0:T(8,128)} %fusion.11), calls=%async_computation.1 | async-start | bytes 4194304 | tf_op jit(solution)/shard_map/all_to_all | solution.py:69
  98.4 129.3 %all-reduce.3.cloned.1.call-start = ((), (), s32[]{:S(2)}) async-start(), calls=%async_computation.3 | async-start | bytes 327680 | tf_op jit(solution)/shard_map/psum | solution.py:123
  99.0 51.7 %copy-start.13 = (bf16[32,80]{1,0:T(8,128)(2,1)S(1)}, bf16[32,80]{1,0:T(8,128)(2,1)}, u32[]{:S(2)}) copy-start(bf16[32,80]{1,0:T(8,128)(2,1)} %param.20) | copy-start | bytes 15364
  150.6 77.1 %copy-start.2 = (bf16[32,2560]{1,0:T(8,128)(2,1)S(1)}, bf16[32,2560]{1,0:T(8,128)(2,1)}, u32[]{:S(2)}) copy-start(bf16[32,2560]{1,0:T(8,128)(2,1)} %param.17) | copy-start | bytes 491524
  150.6 78.2 %copy-start.6 = (f32[2560]{0:T(1024)S(1)}, f32[2560]{0:T(1024)}, u32[]{:S(2)}) copy-start(f32[2560]{0:T(1024)} %param.31) | copy-start | bytes 30724
  153.5 159.4 %all-reduce.5.cloned.1.call-start = ((), (), s32[]{:S(2)}) async-start(), calls=%async_computation.4 | async-start | bytes 327680 | tf_op jit(solution)/shard_map/psum | solution.py:132
  227.7 3.6 %copy-start.3 = (bf16[32,2560]{1,0:T(8,128)(2,1)S(1)}, bf16[32,2560]{1,0:T(8,128)(2,1)}, u32[]{:S(2)}) copy-start(bf16[32,2560]{1,0:T(8,128)(2,1)} %all-reduce.3.cloned.1.call-done) | copy-start | bytes 491524
  231.3 83.4 %copy-start.7 = (f32[2560]{0:T(1024)S(1)}, f32[2560]{0:T(1024)}, u32[]{:S(2)}) copy-start(f32[2560]{0:T(1024)} %param.33) | copy-start | bytes 30724
  231.3 83.4 %copy-start.8 = (f32[2560]{0:T(1024)S(1)}, f32[2560]{0:T(1024)}, u32[]{:S(2)}) copy-start(f32[2560]{0:T(1024)} %param.32) | copy-start | bytes 30724
Sparse Core Ops, SparseCore 0:
  153.7 73.9 all-reduce.2
  235.8 77.0 all-reduce.4
where the time goes:
time: 323 us; the launch traced here: 322 us
  waiting for transfers between devices  203 us (63%)
  blocking collectives  43.4 us (13%)
  starting transfers between devices  24.9 us (8%)
  matrix products  20.6 us (6%)
  between operations  14.4 us (4%)
  other arithmetic  9.26 us (3%)
  local copies, waits for them, and re-layouts  6.46 us (2%)
    psum x1, waiting for transfers between devices, on_device(): lax.psum(jnp.dot(hidden, down_weight, preferred_element_type=jnp.float32)...  77.2 us
    psum x1, waiting for transfers between devices, on_device(): lax.psum(projected.astype(jnp.bfloat16), 'mlp').astype(jnp.float32)  74.1 us
    all_to_all x1, waiting for transfers between devices, on_device(): lax.all_to_all(piece_out, 'req', split_axis=0, concat_axis=0, tiled=True)  45.6 us
    all_gather x1, blocking collectives, on_device(): gathered = lax.all_gather(queries, 'req', axis=0, tiled=True)  43.4 us
    all_to_all x1, starting transfers between devices, on_device(): lax.all_to_all(piece_out, 'req', split_axis=0, concat_axis=0, tiled=True)  10.1 us
    all_to_all x1, starting transfers between devices, on_device(): lax.all_to_all(piece_sum, 'req', split_axis=0, concat_axis=0, tiled=True)  8.41 us
    dot_general x1, matrix products, on_device(): jnp.einsum('pksjgl,plkh->pksjgh', piece_w.astype(jnp.bfloat16), prefix_va...  7.23 us
  transfers between devices with their start and end apart: 5, of which 4 were waited for; matrix products, arithmetic and copies ran while one was open for 4% of the time, Pallas kernels for 0%

commit v1 on v0

--- a/solution.py
+++ b/solution.py
@@ -14,6 +14,59 @@
 
 def rms_scale(total_sq, width):
     return lax.rsqrt(total_sq / width + 1e-05)
+
+
+def exchange(x, axis, n, bit):
+    return lax.ppermute(x, axis, perm=[(i, i ^ (1 << bit)) for i in range(n)])
+
+
+def gather_rows(x, axis, n, bits):
+    me = lax.axis_index(axis)
+    buf = x[None]
+    taken = []
+    for b in bits:
+        other = exchange(buf, axis, n, b)
+        high = ((me >> b) & 1) == 1
+        buf = jnp.stack([jnp.where(high, other, buf), jnp.where(high, buf, other)])
+        taken.insert(0, b)
+    nb = len(bits)
+    order = sorted(range(nb), key=lambda i: -taken[i])
+    buf = jnp.transpose(buf, order + list(range(nb, buf.ndim)))
+    return buf.reshape((n * x.shape[0],) + x.shape[1:])
+
+
+def merge_partials(a, b):
+    ma = a[..., HEAD_SIZE:HEAD_SIZE + 1, :]
+    mb = b[..., HEAD_SIZE:HEAD_SIZE + 1, :]
+    top = jnp.maximum(ma, mb)
+    wa = jnp.exp(ma - top)
+    wb = jnp.exp(mb - top)
+    outs = a[..., :HEAD_SIZE, :] * wa + b[..., :HEAD_SIZE, :] * wb
+    sums = a[..., HEAD_SIZE + 1:, :] * wa + b[..., HEAD_SIZE + 1:, :] * wb
+    return jnp.concatenate([outs, top, sums], axis=-2)
+
+
+def reduce_partials(packed, axis, n, bits):
+    me = lax.axis_index(axis)
+    nb = len(bits)
+    cur = packed.reshape((2,) * nb + packed.shape[1:])
+    left = list(range(nb - 1, -1, -1))
+    for b in bits:
+        ax = left.index(b)
+        own = (me >> b) & 1
+        keep = lax.dynamic_index_in_dim(cur, own, ax, keepdims=False)
+        send = lax.dynamic_index_in_dim(cur, 1 - own, ax, keepdims=False)
+        cur = merge_partials(keep, exchange(send, axis, n, b))
+        left.remove(b)
+    return cur
+
+
+def allreduce_bf16(x, axis, n, bits):
+    cur = x.astype(jnp.bfloat16)
+    for b in bits:
+        other = exchange(cur, axis, n, b)
+        cur = (cur.astype(jnp.float32) + other.astype(jnp.float32)).astype(jnp.bfloat16)
+    return cur
 
 
 def on_device(
@@ -40,9 +93,19 @@
     kv_local = fresh_rotated_keys.shape[1] // HEAD_SIZE
     prompts = shared_prefix_keys.shape[0]
     piece_len = shared_prefix_keys.shape[1]
+    req_count = lax.axis_size("req")
+    req_bits = req_count.bit_length() - 1
+    mlp_count = lax.axis_size("mlp")
+    mlp_bits = mlp_count.bit_length() - 1
     req_index = lax.axis_index("req")
     low = jnp.float32(-1e30)
-    gathered = lax.all_gather(queries, "req", axis=0, tiled=True)
+    rows = kv_local * SAMPLE_COUNT * DECODE_TOKENS * query_groups
+
+    gather_order = [req_bits - 1] + ([1] if req_bits > 1 else []) + list(range(req_bits - 2, 1, -1)) + [0]
+    gather_order = [b for i, b in enumerate(gather_order) if b not in gather_order[:i]]
+    reduce_order = gather_order[::-1]
+
+    gathered = gather_rows(queries, "req", req_count, gather_order)
     query_all = gathered.reshape(
         prompts, SAMPLE_COUNT, DECODE_TOKENS, kv_local, query_groups, HEAD_SIZE
     )
@@ -60,16 +123,21 @@
     piece_w = jnp.where(valid, jnp.exp(score_pre - piece_top[..., None]), 0.0)
     piece_sum = jnp.sum(piece_w, -1)
     piece_out = jnp.einsum(
-        "pksjgl,plkh->pksjgh",
+        "pksjgl,plkh->phksjg",
         piece_w.astype(jnp.bfloat16),
         prefix_value_block,
         preferred_element_type=jnp.float32,
     )
-    source_out, source_top, source_sum = (
-        lax.all_to_all(piece_out, "req", split_axis=0, concat_axis=0, tiled=True),
-        lax.all_to_all(piece_top, "req", split_axis=0, concat_axis=0, tiled=True),
-        lax.all_to_all(piece_sum, "req", split_axis=0, concat_axis=0, tiled=True),
-    )
+    packed = jnp.concatenate(
+        [
+            piece_out.reshape(prompts, HEAD_SIZE, rows),
+            piece_top.reshape(prompts, 1, rows),
+            piece_sum.reshape(prompts, 1, rows),
+        ],
+        axis=1,
+    )
+    own_part = reduce_partials(packed, "req", req_count, reduce_order)
+
     query_own = queries.reshape(SAMPLE_COUNT, DECODE_TOKENS, kv_local, query_groups, HEAD_SIZE)
     tail_key_block = sample_tail_keys.reshape(SAMPLE_COUNT, TAIL_LENGTH, kv_local, HEAD_SIZE)
     tail_value_block = sample_tail_values.reshape(SAMPLE_COUNT, TAIL_LENGTH, kv_local, HEAD_SIZE)
@@ -107,30 +175,34 @@
     local_out = local_out + jnp.einsum(
         "ksjgi,sikh->ksjgh", w_new.astype(jnp.bfloat16), fresh_v, preferred_element_type=jnp.float32
     )
-    overall = jnp.maximum(jnp.max(source_top, 0), local_top)
-    source_w = jnp.exp(source_top - overall[None])
+    lead = (kv_local, SAMPLE_COUNT, DECODE_TOKENS, query_groups)
+    source_out = jnp.transpose(own_part[:HEAD_SIZE].reshape((HEAD_SIZE,) + lead), (1, 2, 3, 4, 0))
+    source_top = own_part[HEAD_SIZE].reshape(lead)
+    source_sum = own_part[HEAD_SIZE + 1].reshape(lead)
+    overall = jnp.maximum(source_top, local_top)
+    source_w = jnp.exp(source_top - overall)
     local_w = jnp.exp(local_top - overall)
-    numer = jnp.sum(source_w[..., None] * source_out, 0) + local_w[..., None] * local_out
-    denom = jnp.sum(source_w * source_sum, 0) + local_w * local_sum
+    numer = source_w[..., None] * source_out + local_w[..., None] * local_out
+    denom = source_w * source_sum + local_w * local_sum
     attention_layer = (numer / denom[..., None]).astype(jnp.bfloat16)
     attention_layer = jnp.transpose(attention_layer, (1, 2, 0, 3, 4)).reshape(
         SAMPLE_COUNT * DECODE_TOKENS, kv_local * query_groups * HEAD_SIZE
     )
     projected = jnp.dot(attention_layer, out_weight, preferred_element_type=jnp.float32)
-    mlp_count = lax.axis_size("mlp")
     mlp_index = lax.axis_index("mlp")
     share = D // mlp_count
-    mid = residual_in.astype(jnp.float32) + lax.psum(projected.astype(jnp.bfloat16), "mlp").astype(
-        jnp.float32
-    )
+    mlp_order = list(range(mlp_bits - 1, -1, -1))
+    mid = residual_in.astype(jnp.float32) + allreduce_bf16(
+        projected, "mlp", mlp_count, mlp_order
+    ).astype(jnp.float32)
     normed = (mid * rms_scale(jnp.sum(mid * mid, -1, keepdims=True), D) * mlp_gain).astype(
         jnp.bfloat16
     )
     gate = jnp.dot(normed, gate_weight, preferred_element_type=jnp.float32)
     upper = jnp.dot(normed, up_weight, preferred_element_type=jnp.float32)
     hidden = (jax.nn.silu(gate) * upper).astype(jnp.bfloat16)
-    stream = mid + lax.psum(
-        jnp.dot(hidden, down_weight, preferred_element_type=jnp.float32).astype(jnp.bfloat16), "mlp"
+    stream = mid + allreduce_bf16(
+        jnp.dot(hidden, down_weight, preferred_element_type=jnp.float32), "mlp", mlp_count, mlp_order
     ).astype(jnp.float32)
     score = jnp.sum(
         stream

time: 323 us -> 154 us (0.48)
  waiting for transfers between devices: 203 us -> 66.7 us
  blocking collectives: 43.4 us -> 0 us
  between operations: 14.4 us -> 1.14 us
  local copies, waits for them, and re-layouts: 6.46 us -> 18.9 us
  other arithmetic: 9.26 us -> 16.7 us
  starting transfers between devices: 24.9 us -> 32 us
    psum x2 -> x0, waiting for transfers between devices: 151 us -> none  [the longest x1 77.2 us: on_device(): lax.psum(jnp.dot(hidden, down_weight, preferred_element_type=jnp.float32)...]
    ppermute x0 -> x16, waiting for transfers between devices: none -> 66.7 us  [exchange(): return lax.ppermute(x, axis, perm=[(i, i ^ 1 << bit) for i in range(n)])]
    all_to_all x3 -> x0, waiting for transfers between devices: 52 us -> none  [the longest x1 45.6 us: on_device(): lax.all_to_all(piece_out, 'req', split_axis=0, concat_axis=0, tiled=True)]
    all_gather x1 -> x0, blocking collectives: 43.4 us -> none  [on_device(): gathered = lax.all_gather(queries, 'req', axis=0, tiled=True)]
    ppermute x0 -> x16, starting transfers between devices: none -> 32 us  [exchange(): return lax.ppermute(x, axis, perm=[(i, i ^ 1 << bit) for i in range(n)])]
    all_to_all x3 -> x0, starting transfers between devices: 24.8 us -> none  [the longest x1 10.1 us: on_device(): lax.all_to_all(piece_out, 'req', split_axis=0, concat_axis=0, tiled=True)]
    dynamic_slice x0 -> x7, local copies, waits for them, and re-layouts: none -> 5.52 us  [the longest x4 3.23 us: reduce_partials(): keep = lax.dynamic_index_in_dim(cur, own, ax, keepdims=False)]
    concatenate x0 -> x2, local copies, waits for them, and re-layouts: none -> 5.16 us  [on_device(): jnp.concatenate([piece_out.reshape(prompts, HEAD_SIZE, rows), piece_top.r...]
  transfers between devices with their start and end apart: 5 -> 16, of which waited for: 4 -> 16; matrix products, arithmetic and copies ran while one was open for 4% -> 3% of each run, Pallas kernels for 0% -> 0%
where the time goes in v1:
time: 154 us; the launch traced here: 153 us
  waiting for transfers between devices  66.7 us (43%)
  starting transfers between devices  32 us (21%)
  local copies, waits for them, and re-layouts  18.9 us (12%)
  matrix products  17.8 us (12%)
  other arithmetic  16.7 us (11%)
    ppermute x16, waiting for transfers between devices, exchange(): return lax.ppermute(x, axis, perm=[(i, i ^ 1 << bit) for i in range(n)])  66.7 us
    ppermute x16, starting transfers between devices, exchange(): return lax.ppermute(x, axis, perm=[(i, i ^ 1 << bit) for i in range(n)])  32 us
    dot_general x1, matrix products, on_device(): jnp.einsum('psjkgh,plkh->pksjgl', query_all, prefix_key_block, preferred_...  5.96 us
    reduce_sum x1, other arithmetic, on_device(): piece_sum = jnp.sum(piece_w, -1)  5.41 us
    concatenate x2, local copies, waits for them, and re-layouts, on_device(): jnp.concatenate([piece_out.reshape(prompts, HEAD_SIZE, rows), piece_top.r...  5.16 us
    concatenate x1, other arithmetic, on_device(): jnp.concatenate([piece_out.reshape(prompts, HEAD_SIZE, rows), piece_top.r...  4 us
    dot_general x1, matrix products, on_device(): jnp.dot(hidden, down_weight, preferred_element_type=jnp.float32)  3.63 us
    dot_general x1, matrix products, on_device(): jnp.einsum('pksjgl,plkh->phksjg', piece_w.astype(jnp.bfloat16), prefix_va...  3.39 us
  transfers between devices with their start and end apart: 16, of which 16 were waited for; matrix products, arithmetic and copies ran while one was open for 3% of the time, Pallas kernels for 0%

profile of v1, /device:TPU:6, one launch (start us, length us, event | category | flops | bytes accessed | tf_op | source)
XLA Modules:
  0.0 153.3 jit_solution(3927057226163243649)
XLA Ops:
  0.7 7.3 %collective-permute-start = (bf16[1,32,320]{2,1,0:T(8,128)(2,1)}, bf16[1,32,320]{2,1,0:T(8,128)(2,1)S(1)}, u32[]{:S(2)}, u32[]{:S(2)}) collective-permute-start(bf16[1,32,320]{2,1,0:T(8,128)(2,1)} %bitcast.205), channel_id=1, source_target_pairs={{0,128},{8,136},{16,144},{24,152},{32,160},{40,168},{48,176},{56,1... | collective-permute-start | bytes 61448 | tf_op jit(solution)/shard_map/ppermute | solution.py:20
  7.9 2.0 %collective-permute-done = bf16[1,32,320]{2,1,0:T(8,128)(2,1)S(1)} collective-permute-done((bf16[1,32,320]{2,1,0:T(8,128)(2,1)}, bf16[1,32,320]{2,1,0:T(8,128)(2,1)S(1)}, u32[]{:S(2)}, u32[]{:S(2)}) %collective-permute-start) | collective-permute-done | bytes 20512 | tf_op jit(solution)/shard_map/ppermute | solution.py:20
  10.0 0.7 select_bitcast_fusion.5
  10.7 1.5 collective-permute-start.1
  12.2 4.2 %collective-permute-done.1 = bf16[2,1,32,320]{3,2,0,1:T(8,128)(2,1)S(1)} collective-permute-done((bf16[2,1,32,320]{3,2,0,1:T(8,128)(2,1)S(1)}, bf16[2,1,32,320]{3,2,0,1:T(8,128)(2,1)S(1)}, u32[]{:S(2)}, u32[]{:S(2)}) %collective-permute-start.1) | collective-permute-done | bytes 40992 | tf_op jit(solution)/shard_map/ppermute | solution.py:20
  16.5 2.1 %collective-permute-start.2 = (bf16[2,2,1,32,320]{4,3,1,0,2:T(8,128)(2,1)S(1)}, bf16[2,2,1,32,320]{4,3,1,0,2:T(8,128)(2,1)S(1)}, u32[]{:S(2)}, u32[]{:S(2)}) collective-permute-start(bf16[2,2,1,32,320]{4,3,1,0,2:T(8,128)(2,1)S(1)} %fusion.40), channel_id=1, source_target_pairs={{0,64},{8,72},{16,80},{24,88},{32,96},{40,104},{48,112},{56,120},{... | collective-permute-start | bytes 245768 | tf_op jit(solution)/shard_map/ppermute | solution.py:20
  18.6 4.6 %collective-permute-done.2 = bf16[2,2,1,32,320]{4,3,1,0,2:T(8,128)(2,1)S(1)} collective-permute-done((bf16[2,2,1,32,320]{4,3,1,0,2:T(8,128)(2,1)S(1)}, bf16[2,2,1,32,320]{4,3,1,0,2:T(8,128)(2,1)S(1)}, u32[]{:S(2)}, u32[]{:S(2)}) %collective-permute-start.2) | collective-permute-done | bytes 81952 | tf_op jit(solution)/shard_map/ppermute | solution.py:20
  23.5 5.6 %collective-permute-done.3 = bf16[2,2,2,1,32,320]{5,4,2,1,0,3:T(8,128)(2,1)S(1)} collective-permute-done((bf16[2,2,2,1,32,320]{5,4,2,1,0,3:T(8,128)(2,1)S(1)}, bf16[2,2,2,1,32,320]{5,4,2,1,0,3:T(8,128)(2,1)S(1)}, u32[]{:S(2)}, u32[]{:S(2)}) %collective-permute-start.3) | collective-permute-done | bytes 163872 | tf_op jit(solution)/shard_map/ppermute | solution.py:20
  29.7 1.6 %collective-permute-done.4 = bf16[2,2,2,2,1,32,320]{6,5,3,2,1,0,4:T(8,128)(2,1)S(1)} collective-permute-done((bf16[2,2,2,2,1,32,320]{6,5,3,2,1,0,4:T(8,128)(2,1)S(1)}, bf16[2,2,2,2,1,32,320]{6,5,3,2,1,0,4:T(8,128)(2,1)S(1)}, u32[]{:S(2)}, u32[]{:S(2)}) %collective-permute-start.4) | collective-permute-done | bytes 327712 | tf_op jit(solution)/shard_map/ppermute | solution.py:20
  31.8 1.7 %reshape.279 = bf16[32,16,2,4,80]{4,3,2,1,0:T(4,128)(2,1)} reshape(bf16[2,2,2,2,2,1,32,320]{7,6,4,3,2,1,0,5:T(8,128)(2,1)S(1)} %copy.156) | data formatting | bytes 1310720 | tf_op jit(solution)/shard_map/reshape.1
  33.5 6.0 %select_reduce_fusion = (f32[32,16,2,4]{1,3,2,0:T(4,128)S(1)}, f32[32,16,2,4,512]{4,1,3,2,0:T(8,128)}) fusion(pred[32,512]{1,0:T(8,128)(4,1)S(1)} %broadcast_compare_fusion, bf16[32,512,80]{1,2,0:T(8,128)(2,1)S(1)} %copy-done, bf16[32,16,2,4,80]{4,3,2,1,0:T(4,128)(2,1)} %reshape.279), kind=kOutput, calls=%fused_computation.1 | convolution fusion | flops 341831680 | bytes 11698176 | tf_op jit(solution)/shard_map/psjkgh,plkh->pksjgl/dot_general | solution.py:115
  39.9 5.4 %fusion = f32[32,16,2,4]{1,3,2,0:T(4,128)S(1)} fusion(f32[32,16,2,4,512]{4,1,3,2,0:T(8,128)} %get-tuple-element.43, f32[32,16,2,4]{1,3,2,0:T(4,128)S(1)} %get-tuple-element.42, pred[32,512]{1,0:T(8,128)(4,1)S(1)} %broadcast_compare_fusion), kind=kLoop, calls=%fused_computation.2 | loop fusion | flops 8384512 | bytes 8437760 | tf_op jit(solution)/shard_map/reduce_sum | solution.py:124
  45.7 3.4 %fusion.11 = f32[32,80,16,2,4]{1,2,4,3,0:T(8,128)S(1)} fusion(bf16[32,512,80]{1,2,0:T(8,128)(2,1)} %param.22, f32[32,16,2,4,512]{4,1,3,2,0:T(8,128)S(1)} %copy-done.1, f32[32,16,2,4]{1,3,2,0:T(4,128)S(1)} %get-tuple-element.42, pred[32,512]{1,0:T(8,128)(4,1)S(1)} %broadcast_compare_fusion), kind=kOutput, calls=%fused_computation.15 | convolution fusion | flops 343932928 | bytes 12353536 | tf_op jit(solution)/shard_map/pksjgl,plkh->phksjg/dot_general | solution.py:125
  49.1 2.1 %copy.158 = f32[32,80,16,2,4]{1,4,3,2,0:T(4,128)} copy(f32[32,80,16,2,4]{1,2,4,3,0:T(8,128)S(1)} %fusion.11) | data formatting | bytes 2621440 | tf_op jit(solution)/shard_map/pksjgl,plkh->phksjg/dot_general | solution.py:125
  51.3 1.3 copy.160
  52.5 3.0 %concatenate.31 = f32[2,2,2,2,2,1,128]{5,6,4,3,2,1,0:T(8,128)} reshape(f32[32,16,2,4]{3,2,1,0:T(2,128)} %copy.160) | data formatting | bytes 32768 | tf_op jit(solution)/shard_map/concatenate | solution.py:131
  55.5 2.2 %concatenate.30 = f32[2,2,2,2,2,1,128]{5,6,4,3,2,1,0:T(8,128)} reshape(f32[32,16,2,4]{3,2,1,0:T(2,128)S(1)} %copy.159) | data formatting | bytes 32768 | tf_op jit(solution)/shard_map/concatenate | solution.py:131
  57.7 4.0 %pad_maximum_fusion = f32[2,2,2,2,2,82,128]{5,6,4,3,2,1,0:T(8,128)S(1)} fusion(f32[2,2,2,2,2,1,128]{5,6,4,3,2,1,0:T(8,128)} %concatenate.31, f32[2,2,2,2,2,1,128]{5,6,4,3,2,1,0:T(8,128)} %concatenate.30, f32[2,2,2,2,2,80,128]{5,6,4,3,2,1,0:T(8,128)} %bitcast.196), kind=kLoop, calls=%fused_computation.14 | loop fusion | flops 671744 | bytes 2686976 | tf_op jit(solution)/shard_map/concatenate | solution.py:131
  61.7 1.5 constant_dynamic-slice_fusion.7
  63.2 2.2 %copy.164 = f32[2,2,2,2,1,82,128]{6,3,5,2,1,0,4:T(2,128)} copy(f32[2,2,2,2,1,82,128]{5,6,4,3,2,1,0:T(8,128)} %get-tuple-element.19) | data formatting | bytes 1343488 | tf_op jit(solution)/shard_map/jit(dynamic_index_in_dim)/dynamic_slice | solution.py:58
  66.1 1.6 %copy.163 = f32[2,2,2,2,1,82,128]{6,3,5,2,1,0,4:T(2,128)S(1)} copy(f32[2,2,2,2,1,82,128]{5,6,4,3,2,1,0:T(8,128)} %get-tuple-element.18) | data formatting | bytes 1343488 | tf_op jit(solution)/shard_map/jit(dynamic_index_in_dim)/dynamic_slice | solution.py:57
  67.9 0.7 fusion.78
  68.6 0.7 fusion.79
  69.3 1.5 fusion.23
  71.1 0.8 dynamic-slice_bitcast_fusion.1
  72.0 1.3 select_reduce_fusion.1
  73.3 8.7 %collective-permute-done.6 = f32[2,2,2,82,128]{4,2,3,1,0:T(2,128)S(1)} collective-permute-done((f32[2,2,2,82,128]{4,2,3,1,0:T(2,128)}, f32[2,2,2,82,128]{4,2,3,1,0:T(2,128)S(1)}, u32[]{:S(2)}, u32[]{:S(2)}) %collective-permute-start.6) | collective-permute-done | bytes 335904 | tf_op jit(solution)/shard_map/ppermute | solution.py:20
  82.5 1.8 %collective-permute-start.7 = (f32[2,2,82,128]{3,1,2,0:T(2,128)S(1)}, f32[2,2,82,128]{3,1,2,0:T(2,128)S(1)}, u32[]{:S(2)}, u32[]{:S(2)}) collective-permute-start(f32[2,2,82,128]{3,1,2,0:T(2,128)S(1)} %get-tuple-element.27), channel_id=1, source_target_pairs={{0,64},{8,72},{16,80},{24,88},{32,96},{40,104},{48,112},{56,120},{... | collective-permute-start | bytes 503816 | tf_op jit(solution)/shard_map/ppermute | solution.py:20
  84.9 7.7 %collective-permute-done.7 = f32[2,2,82,128]{3,1,2,0:T(2,128)S(1)} collective-permute-done((f32[2,2,82,128]{3,1,2,0:T(2,128)S(1)}, f32[2,2,82,128]{3,1,2,0:T(2,128)S(1)}, u32[]{:S(2)}, u32[]{:S(2)}) %collective-permute-start.7) | collective-permute-done | bytes 167968 | tf_op jit(solution)/shard_map/ppermute | solution.py:20
  93.0 1.5 collective-permute-start.8
  94.7 4.4 %collective-permute-done.8 = f32[2,82,128]{2,0,1:T(2,128)S(1)} collective-permute-done((f32[2,82,128]{2,0,1:T(2,128)S(1)}, f32[2,82,128]{2,0,1:T(2,128)S(1)}, u32[]{:S(2)}, u32[]{:S(2)}) %collective-permute-start.8) | collective-permute-done | bytes 84000 | tf_op jit(solution)/shard_map/ppermute | solution.py:20
  99.3 6.0 %collective-permute-start.9 = (f32[82,128]{1,0:T(8,128)S(1)}, f32[82,128]{1,0:T(8,128)S(1)}, u32[]{:S(2)}, u32[]{:S(2)}) collective-permute-start(f32[82,128]{1,0:T(8,128)S(1)} %bitcast.212), channel_id=1, source_target_pairs={{0,128},{8,136},{16,144},{24,152},{32,160},{40,168},{48,176},{56,1... | collective-permute-start | bytes 125960 | tf_op jit(solution)/shard_map/ppermute | solution.py:20
  105.3 2.0 %collective-permute-done.9 = f32[82,128]{1,0:T(8,128)S(1)} collective-permute-done((f32[82,128]{1,0:T(8,128)S(1)}, f32[82,128]{1,0:T(8,128)S(1)}, u32[]{:S(2)}, u32[]{:S(2)}) %collective-permute-start.9) | collective-permute-done | bytes 42016 | tf_op jit(solution)/shard_map/ppermute | solution.py:20
  108.2 1.9 %convolution_convert_fusion.1 = bf16[32,2560]{1,0:T(8,128)(2,1)S(1)} fusion(bf16[32,320]{1,0:T(8,128)(2,1)S(1)} %reshape_transpose.3, bf16[320,2560]{1,0:T(8,128)(2,1)} %param.27), kind=kOutput, calls=%fused_computation.10 | convolution fusion | flops 52510720 | bytes 1822720 | tf_op jit(solution)/shard_map/dot_general | solution.py:191
  110.2 0.9 collective-permute-start.10
  111.1 4.5 %collective-permute-done.10 = bf16[32,2560]{1,0:T(8,128)(2,1)S(1)} collective-permute-done((bf16[32,2560]{1,0:T(8,128)(2,1)S(1)}, bf16[32,2560]{1,0:T(8,128)(2,1)S(1)}, u32[]{:S(2)}, u32[]{:S(2)}) %collective-permute-start.10) | collective-permute-done | bytes 163872 | tf_op jit(solution)/shard_map/ppermute | solution.py:20
  115.6 3.3 %collective-permute-start.11 = (bf16[32,2560]{1,0:T(8,128)(2,1)S(1)}, bf16[32,2560]{1,0:T(8,128)(2,1)S(1)}, u32[]{:S(2)}, u32[]{:S(2)}) collective-permute-start(bf16[32,2560]{1,0:T(8,128)(2,1)S(1)} %add_convert_fusion.5), channel_id=1, source_target_pairs={{0,2},{1,3},{2,0},{3,1},{4,6},{5,7},{6,4},{7,5},{8,10},{9,11},{10,... | collective-permute-start | bytes 491528 | tf_op jit(solution)/shard_map/ppermute | solution.py:20
  118.9 4.6 %collective-permute-done.11 = bf16[32,2560]{1,0:T(8,128)(2,1)S(1)} collective-permute-done((bf16[32,2560]{1,0:T(8,128)(2,1)S(1)}, bf16[32,2560]{1,0:T(8,128)(2,1)S(1)}, u32[]{:S(2)}, u32[]{:S(2)}) %collective-permute-start.11) | collective-permute-done | bytes 163872 | tf_op jit(solution)/shard_map/ppermute | solution.py:20
  123.5 1.3 collective-permute-start.12
  124.8 4.1 %collective-permute-done.12 = bf16[32,2560]{1,0:T(8,128)(2,1)S(1)} collective-permute-done((bf16[32,2560]{1,0:T(8,128)(2,1)S(1)}, bf16[32,2560]{1,0:T(8,128)(2,1)S(1)}, u32[]{:S(2)}, u32[]{:S(2)}) %collective-permute-start.12) | collective-permute-done | bytes 163872 | tf_op jit(solution)/shard_map/ppermute | solution.py:20
  129.8 3.6 %convolution_convert_fusion = bf16[32,2560]{1,0:T(8,128)(2,1)S(1)} fusion(bf16[512,2560]{1,0:T(8,128)(2,1)} %param.30, bf16[32,2560]{1,0:T(8,128)(2,1)S(1)} %multiply_convert_fusion, bf16[2560,512]{1,0:T(8,128)(2,1)} %param.29, f32[32,512]{1,0:T(8,128)S(1)} %fusion.83), kind=kOutput, calls=%fused_computation.9 | convolution fusion | flops 167952384 | bytes 5636096 | tf_op jit(solution)/shard_map/dot_general | solution.py:205
  133.4 0.9 collective-permute-start.13
  134.3 4.5 %collective-permute-done.13 = bf16[32,2560]{1,0:T(8,128)(2,1)S(1)} collective-permute-done((bf16[32,2560]{1,0:T(8,128)(2,1)S(1)}, bf16[32,2560]{1,0:T(8,128)(2,1)S(1)}, u32[]{:S(2)}, u32[]{:S(2)}) %collective-permute-start.13) | collective-permute-done | bytes 163872 | tf_op jit(solution)/shard_map/ppermute | solution.py:20
  138.8 4.1 %collective-permute-start.14 = (bf16[32,2560]{1,0:T(8,128)(2,1)S(1)}, bf16[32,2560]{1,0:T(8,128)(2,1)S(1)}, u32[]{:S(2)}, u32[]{:S(2)}) collective-permute-start(bf16[32,2560]{1,0:T(8,128)(2,1)S(1)} %add_convert_fusion.2), channel_id=1, source_target_pairs={{0,2},{1,3},{2,0},{3,1},{4,6},{5,7},{6,4},{7,5},{8,10},{9,11},{10,... | collective-permute-start | bytes 491528 | tf_op jit(solution)/shard_map/ppermute | solution.py:20
  142.9 3.3 %collective-permute-done.14 = bf16[32,2560]{1,0:T(8,128)(2,1)S(1)} collective-permute-done((bf16[32,2560]{1,0:T(8,128)(2,1)S(1)}, bf16[32,2560]{1,0:T(8,128)(2,1)S(1)}, u32[]{:S(2)}, u32[]{:S(2)}) %collective-permute-start.14) | collective-permute-done | bytes 163872 | tf_op jit(solution)/shard_map/ppermute | solution.py:20
  146.3 0.8 collective-permute-start.15
  147.1 4.6 %collective-permute-done.15 = bf16[32,2560]{1,0:T(8,128)(2,1)S(1)} collective-permute-done((bf16[32,2560]{1,0:T(8,128)(2,1)S(1)}, bf16[32,2560]{1,0:T(8,128)(2,1)S(1)}, u32[]{:S(2)}, u32[]{:S(2)}) %collective-permute-start.15) | collective-permute-done | bytes 163872 | tf_op jit(solution)/shard_map/ppermute | solution.py:20
  152.6 0.7 multiply_reduce_fusion
  (96 shorter events, 7.9 us)
Async XLA Ops:
  0.6 32.8 %copy-start = (bf16[32,512,80]{1,2,0:T(8,128)(2,1)S(1)}, bf16[32,512,80]{1,2,0:T(8,128)(2,1)}, u32[]{:S(2)}) copy-start(bf16[32,512,80]{1,2,0:T(8,128)(2,1)} %param.21) | copy-start | bytes 7864324
  0.6 28.9 %copy-start.8 = (s32[32]{0:T(128)S(1)}, s32[32]{0:T(128)}, u32[]{:S(2)}) copy-start(s32[32]{0:T(128)} %param.25) | copy-start | bytes 388
  0.7 9.3 %collective-permute-start = (bf16[1,32,320]{2,1,0:T(8,128)(2,1)}, bf16[1,32,320]{2,1,0:T(8,128)(2,1)S(1)}, u32[]{:S(2)}, u32[]{:S(2)}) collective-permute-start(bf16[1,32,320]{2,1,0:T(8,128)(2,1)} %bitcast.205), channel_id=1, source_target_pairs={{0,128},{8,136},{16,144},{24,152},{32,160},{40,168},{48,176},{56,1... | collective-permute-start | bytes 61448 | tf_op jit(solution)/shard_map/ppermute | solution.py:20
  10.7 5.7 %collective-permute-start.1 = (bf16[2,1,32,320]{3,2,0,1:T(8,128)(2,1)S(1)}, bf16[2,1,32,320]{3,2,0,1:T(8,128)(2,1)S(1)}, u32[]{:S(2)}, u32[]{:S(2)}) collective-permute-start(bf16[2,1,32,320]{3,2,0,1:T(8,128)(2,1)S(1)} %fusion.50), channel_id=1, source_target_pairs={{0,16},{8,24},{16,0},{24,8},{32,48},{40,56},{48,32},{56,40},{64,80... | collective-permute-start | bytes 122888 | tf_op jit(solution)/shard_map/ppermute | solution.py:20
  16.5 6.8 %collective-permute-start.2 = (bf16[2,2,1,32,320]{4,3,1,0,2:T(8,128)(2,1)S(1)}, bf16[2,2,1,32,320]{4,3,1,0,2:T(8,128)(2,1)S(1)}, u32[]{:S(2)}, u32[]{:S(2)}) collective-permute-start(bf16[2,2,1,32,320]{4,3,1,0,2:T(8,128)(2,1)S(1)} %fusion.40), channel_id=1, source_target_pairs={{0,64},{8,72},{16,80},{24,88},{32,96},{40,104},{48,112},{56,120},{... | collective-permute-start | bytes 245768 | tf_op jit(solution)/shard_map/ppermute | solution.py:20
  23.3 5.8 %collective-permute-start.3 = (bf16[2,2,2,1,32,320]{5,4,2,1,0,3:T(8,128)(2,1)S(1)}, bf16[2,2,2,1,32,320]{5,4,2,1,0,3:T(8,128)(2,1)S(1)}, u32[]{:S(2)}, u32[]{:S(2)}) collective-permute-start(bf16[2,2,2,1,32,320]{5,4,2,1,0,3:T(8,128)(2,1)S(1)} %fusion.32), channel_id=1, source_target_pairs={{0,32},{8,40},{16,48},{24,56},{32,0},{40,8},{48,16},{56,24},{64,96... | collective-permute-start | bytes 491528 | tf_op jit(solution)/shard_map/ppermute | solution.py:20
  29.3 2.0 %collective-permute-start.4 = (bf16[2,2,2,2,1,32,320]{6,5,3,2,1,0,4:T(8,128)(2,1)S(1)}, bf16[2,2,2,2,1,32,320]{6,5,3,2,1,0,4:T(8,128)(2,1)S(1)}, u32[]{:S(2)}, u32[]{:S(2)}) collective-permute-start(bf16[2,2,2,2,1,32,320]{6,5,3,2,1,0,4:T(8,128)(2,1)S(1)} %fusion.29), channel_id=1, source_target_pairs={{0,8},{8,0},{16,24},{24,16},{32,40},{40,32},{48,56},{56,48},{64,72... | collective-permute-start | bytes 983048 | tf_op jit(solution)/shard_map/ppermute | solution.py:20
  39.9 5.8 %copy-start.1 = (f32[32,16,2,4,512]{4,1,3,2,0:T(8,128)S(1)}, f32[32,16,2,4,512]{4,1,3,2,0:T(8,128)}, u32[]{:S(2)}) copy-start(f32[32,16,2,4,512]{4,1,3,2,0:T(8,128)} %get-tuple-element.43) | copy-start | bytes 25165828
  61.7 3.8 %copy-start.4 = (bf16[32,320]{1,0:T(8,128)(2,1)S(1)}, bf16[32,320]{1,0:T(8,128)(2,1)}, u32[]{:S(2)}) copy-start(bf16[32,320]{1,0:T(8,128)(2,1)} %param.18) | copy-start | bytes 61444
  61.7 3.9 %copy-start.11 = (bf16[32,80]{1,0:T(8,128)(2,1)S(1)}, bf16[32,80]{1,0:T(8,128)(2,1)}, u32[]{:S(2)}) copy-start(bf16[32,80]{1,0:T(8,128)(2,1)} %param.19) | copy-start | bytes 15364
  65.4 2.5 %collective-permute-start.5 = (f32[2,2,2,2,82,128]{5,3,4,2,1,0:T(2,128)}, f32[2,2,2,2,82,128]{5,3,4,2,1,0:T(2,128)}, u32[]{:S(2)}, u32[]{:S(2)}) collective-permute-start(f32[2,2,2,2,82,128]{5,3,4,2,1,0:T(2,128)} %bitcast.35), channel_id=1, source_target_pairs={{0,8},{8,0},{16,24},{24,16},{32,40},{40,32},{48,56},{56,48},{64,72... | collective-permute-start | bytes 2015240 | tf_op jit(solution)/shard_map/ppermute | solution.py:20
  67.6 4.3 %copy-start.9 = (s32[1,16]{1,0:T(1,128)S(1)}, s32[1,16]{1,0:T(1,128)}, u32[]{:S(2)}) copy-start(s32[1,16]{1,0:T(1,128)} %param.26) | copy-start | bytes 196
  71.9 10.2 %collective-permute-start.6 = (f32[2,2,2,82,128]{4,2,3,1,0:T(2,128)}, f32[2,2,2,82,128]{4,2,3,1,0:T(2,128)S(1)}, u32[]{:S(2)}, u32[]{:S(2)}) collective-permute-start(f32[2,2,2,82,128]{4,2,3,1,0:T(2,128)} %get-tuple-element.23), channel_id=1, source_target_pairs={{0,32},{8,40},{16,48},{24,56},{32,0},{40,8},{48,16},{56,24},{64,96... | collective-permute-start | bytes 1007624 | tf_op jit(solution)/shard_map/ppermute | solution.py:20
  72.0 12.4 %copy-start.10 = (bf16[1,16,128,80]{2,3,1,0:T(8,128)(2,1)S(1)}, bf16[1,16,128,80]{2,3,1,0:T(8,128)(2,1)}, u32[]{:S(2)}) copy-start(bf16[1,16,128,80]{2,3,1,0:T(8,128)(2,1)} %param.24) | copy-start | bytes 983044
  82.3 25.5 %copy-start.12 = (bf16[32,80]{1,0:T(8,128)(2,1)S(1)}, bf16[32,80]{1,0:T(8,128)(2,1)}, u32[]{:S(2)}) copy-start(bf16[32,80]{1,0:T(8,128)(2,1)} %param.20) | copy-start | bytes 15364
  82.5 10.1 %collective-permute-start.7 = (f32[2,2,82,128]{3,1,2,0:T(2,128)S(1)}, f32[2,2,82,128]{3,1,2,0:T(2,128)S(1)}, u32[]{:S(2)}, u32[]{:S(2)}) collective-permute-start(f32[2,2,82,128]{3,1,2,0:T(2,128)S(1)} %get-tuple-element.27), channel_id=1, source_target_pairs={{0,64},{8,72},{16,80},{24,88},{32,96},{40,104},{48,112},{56,120},{... | collective-permute-start | bytes 503816 | tf_op jit(solution)/shard_map/ppermute | solution.py:20
  93.0 6.1 %collective-permute-start.8 = (f32[2,82,128]{2,0,1:T(2,128)S(1)}, f32[2,82,128]{2,0,1:T(2,128)S(1)}, u32[]{:S(2)}, u32[]{:S(2)}) collective-permute-start(f32[2,82,128]{2,0,1:T(2,128)S(1)} %bitcast.206), channel_id=1, source_target_pairs={{0,16},{8,24},{16,0},{24,8},{32,48},{40,56},{48,32},{56,40},{64,80... | collective-permute-start | bytes 251912 | tf_op jit(solution)/shard_map/ppermute | solution.py:20
  99.3 8.1 %collective-permute-start.9 = (f32[82,128]{1,0:T(8,128)S(1)}, f32[82,128]{1,0:T(8,128)S(1)}, u32[]{:S(2)}, u32[]{:S(2)}) collective-permute-start(f32[82,128]{1,0:T(8,128)S(1)} %bitcast.212), channel_id=1, source_target_pairs={{0,128},{8,136},{16,144},{24,152},{32,160},{40,168},{48,176},{56,1... | collective-permute-start | bytes 125960 | tf_op jit(solution)/shard_map/ppermute | solution.py:20
  107.8 21.1 %copy-start.3 = (bf16[32,2560]{1,0:T(8,128)(2,1)S(1)}, bf16[32,2560]{1,0:T(8,128)(2,1)}, u32[]{:S(2)}) copy-start(bf16[32,2560]{1,0:T(8,128)(2,1)} %param.17) | copy-start | bytes 491524
  107.8 21.3 %copy-start.7 = (f32[2560]{0:T(1024)S(1)}, f32[2560]{0:T(1024)}, u32[]{:S(2)}) copy-start(f32[2560]{0:T(1024)} %param.31) | copy-start | bytes 30724
  108.2 21.0 %copy-start.2 = (bf16[2560,512]{1,0:T(8,128)(2,1)S(1)}, bf16[2560,512]{1,0:T(8,128)(2,1)}, u32[]{:S(2)}) copy-start(bf16[2560,512]{1,0:T(8,128)(2,1)} %param.28) | copy-start | bytes 7864324
  110.2 5.4 %collective-permute-start.10 = (bf16[32,2560]{1,0:T(8,128)(2,1)S(1)}, bf16[32,2560]{1,0:T(8,128)(2,1)S(1)}, u32[]{:S(2)}, u32[]{:S(2)}) collective-permute-start(bf16[32,2560]{1,0:T(8,128)(2,1)S(1)} %convolution_convert_fusion.1), channel_id=1, source_target_pairs={{0,4},{1,5},{2,6},{3,7},{4,0},{5,1},{6,2},{7,3},{8,12},{9,13},{10,... | collective-permute-start | bytes 491528 | tf_op jit(solution)/shard_map/ppermute | solution.py:20
  115.6 7.8 %collective-permute-start.11 = (bf16[32,2560]{1,0:T(8,128)(2,1)S(1)}, bf16[32,2560]{1,0:T(8,128)(2,1)S(1)}, u32[]{:S(2)}, u32[]{:S(2)}) collective-permute-start(bf16[32,2560]{1,0:T(8,128)(2,1)S(1)} %add_convert_fusion.5), channel_id=1, source_target_pairs={{0,2},{1,3},{2,0},{3,1},{4,6},{5,7},{6,4},{7,5},{8,10},{9,11},{10,... | collective-permute-start | bytes 491528 | tf_op jit(solution)/shard_map/ppermute | solution.py:20
  123.5 5.4 %collective-permute-start.12 = (bf16[32,2560]{1,0:T(8,128)(2,1)S(1)}, bf16[32,2560]{1,0:T(8,128)(2,1)S(1)}, u32[]{:S(2)}, u32[]{:S(2)}) collective-permute-start(bf16[32,2560]{1,0:T(8,128)(2,1)S(1)} %add_convert_fusion.4), channel_id=1, source_target_pairs={{0,1},{1,0},{2,3},{3,2},{4,5},{5,4},{6,7},{7,6},{8,9},{9,8},{10,11... | collective-permute-start | bytes 491528 | tf_op jit(solution)/shard_map/ppermute | solution.py:20
  129.7 22.9 %copy-start.5 = (f32[2560]{0:T(1024)S(1)}, f32[2560]{0:T(1024)}, u32[]{:S(2)}) copy-start(f32[2560]{0:T(1024)} %param.33) | copy-start | bytes 30724
  129.7 22.9 %copy-start.6 = (f32[2560]{0:T(1024)S(1)}, f32[2560]{0:T(1024)}, u32[]{:S(2)}) copy-start(f32[2560]{0:T(1024)} %param.32) | copy-start | bytes 30724
  133.4 5.4 %collective-permute-start.13 = (bf16[32,2560]{1,0:T(8,128)(2,1)S(1)}, bf16[32,2560]{1,0:T(8,128)(2,1)S(1)}, u32[]{:S(2)}, u32[]{:S(2)}) collective-permute-start(bf16[32,2560]{1,0:T(8,128)(2,1)S(1)} %convolution_convert_fusion), channel_id=1, source_target_pairs={{0,4},{1,5},{2,6},{3,7},{4,0},{5,1},{6,2},{7,3},{8,12},{9,13},{10,... | collective-permute-start | bytes 491528 | tf_op jit(solution)/shard_map/ppermute | solution.py:20
  138.8 7.4 %collective-permute-start.14 = (bf16[32,2560]{1,0:T(8,128)(2,1)S(1)}, bf16[32,2560]{1,0:T(8,128)(2,1)S(1)}, u32[]{:S(2)}, u32[]{:S(2)}) collective-permute-start(bf16[32,2560]{1,0:T(8,128)(2,1)S(1)} %add_convert_fusion.2), channel_id=1, source_target_pairs={{0,2},{1,3},{2,0},{3,1},{4,6},{5,7},{6,4},{7,5},{8,10},{9,11},{10,... | collective-permute-start | bytes 491528 | tf_op jit(solution)/shard_map/ppermute | solution.py:20
  146.3 5.4 %collective-permute-start.15 = (bf16[32,2560]{1,0:T(8,128)(2,1)S(1)}, bf16[32,2560]{1,0:T(8,128)(2,1)S(1)}, u32[]{:S(2)}, u32[]{:S(2)}) collective-permute-start(bf16[32,2560]{1,0:T(8,128)(2,1)S(1)} %add_convert_fusion.1), channel_id=1, source_target_pairs={{0,1},{1,0},{2,3},{3,2},{4,5},{5,4},{6,7},{7,6},{8,9},{9,8},{10,11... | collective-permute-start | bytes 491528 | tf_op jit(solution)/shard_map/ppermute | solution.py:20

commit v2 on v0

--- a/solution.py
+++ b/solution.py
@@ -14,6 +14,48 @@
 
 def rms_scale(total_sq, width):
     return lax.rsqrt(total_sq / width + 1e-05)
+
+
+def shifted(x, axis, n, s):
+    return lax.ppermute(x, axis, perm=[(i, (i + s) % n) for i in range(n)])
+
+
+def roll_lead(x, shift, n):
+    both = jnp.concatenate([x, x], axis=0)
+    return lax.dynamic_slice_in_dim(both, (n - shift) % n, n, 0)
+
+
+def gather_all(x, axis, n):
+    me = lax.axis_index(axis)
+    got = [x] + [shifted(x, axis, n, (n - s) % n) for s in range(1, n)]
+    return roll_lead(jnp.stack(got), me, n)
+
+
+def scatter_all(x, axis, n):
+    me = lax.axis_index(axis)
+    mine = roll_lead(x, (n - me) % n, n)
+    got = [mine[0]] + [shifted(mine[s], axis, n, s) for s in range(1, n)]
+    return roll_lead(jnp.stack(got)[::-1], (me + 1) % n, n)
+
+
+def sum_all(x, axis, n):
+    part = x.astype(jnp.bfloat16)
+    got = [part] + [shifted(part, axis, n, s) for s in range(1, n)]
+    me = lax.axis_index(axis)
+    ordered = roll_lead(jnp.stack(got)[::-1], (me + 1) % n, n)
+    total = ordered[0].astype(jnp.float32)
+    for i in range(1, n):
+        total = total + ordered[i].astype(jnp.float32)
+    return total
+
+
+def merge_sources(parts):
+    tops = parts[:, HEAD_SIZE, :]
+    top = jnp.max(tops, 0)
+    w = jnp.exp(tops - top[None])
+    outs = jnp.sum(parts[:, :HEAD_SIZE, :] * w[:, None, :], 0)
+    sums = jnp.sum(parts[:, HEAD_SIZE + 1, :] * w, 0)
+    return outs, top, sums
 
 
 def on_device(
@@ -40,9 +82,13 @@
     kv_local = fresh_rotated_keys.shape[1] // HEAD_SIZE
     prompts = shared_prefix_keys.shape[0]
     piece_len = shared_prefix_keys.shape[1]
+    req_count = lax.axis_size("req")
+    mlp_count = lax.axis_size("mlp")
     req_index = lax.axis_index("req")
     low = jnp.float32(-1e30)
-    gathered = lax.all_gather(queries, "req", axis=0, tiled=True)
+    rows = kv_local * SAMPLE_COUNT * DECODE_TOKENS * query_groups
+
+    gathered = gather_all(queries, "req", req_count)
     query_all = gathered.reshape(
         prompts, SAMPLE_COUNT, DECODE_TOKENS, kv_local, query_groups, HEAD_SIZE
     )
@@ -60,16 +106,21 @@
     piece_w = jnp.where(valid, jnp.exp(score_pre - piece_top[..., None]), 0.0)
     piece_sum = jnp.sum(piece_w, -1)
     piece_out = jnp.einsum(
-        "pksjgl,plkh->pksjgh",
+        "pksjgl,plkh->phksjg",
         piece_w.astype(jnp.bfloat16),
         prefix_value_block,
         preferred_element_type=jnp.float32,
     )
-    source_out, source_top, source_sum = (
-        lax.all_to_all(piece_out, "req", split_axis=0, concat_axis=0, tiled=True),
-        lax.all_to_all(piece_top, "req", split_axis=0, concat_axis=0, tiled=True),
-        lax.all_to_all(piece_sum, "req", split_axis=0, concat_axis=0, tiled=True),
-    )
+    packed = jnp.concatenate(
+        [
+            piece_out.reshape(prompts, HEAD_SIZE, rows),
+            piece_top.reshape(prompts, 1, rows),
+            piece_sum.reshape(prompts, 1, rows),
+        ],
+        axis=1,
+    )
+    source_out, source_top, source_sum = merge_sources(scatter_all(packed, "req", req_count))
+
     query_own = queries.reshape(SAMPLE_COUNT, DECODE_TOKENS, kv_local, query_groups, HEAD_SIZE)
     tail_key_block = sample_tail_keys.reshape(SAMPLE_COUNT, TAIL_LENGTH, kv_local, HEAD_SIZE)
     tail_value_block = sample_tail_values.reshape(SAMPLE_COUNT, TAIL_LENGTH, kv_local, HEAD_SIZE)
@@ -107,31 +158,32 @@
     local_out = local_out + jnp.einsum(
         "ksjgi,sikh->ksjgh", w_new.astype(jnp.bfloat16), fresh_v, preferred_element_type=jnp.float32
     )
-    overall = jnp.maximum(jnp.max(source_top, 0), local_top)
-    source_w = jnp.exp(source_top - overall[None])
+    lead = (kv_local, SAMPLE_COUNT, DECODE_TOKENS, query_groups)
+    source_out = jnp.transpose(source_out.reshape((HEAD_SIZE,) + lead), (1, 2, 3, 4, 0))
+    source_top = source_top.reshape(lead)
+    source_sum = source_sum.reshape(lead)
+    overall = jnp.maximum(source_top, local_top)
+    source_w = jnp.exp(source_top - overall)
     local_w = jnp.exp(local_top - overall)
-    numer = jnp.sum(source_w[..., None] * source_out, 0) + local_w[..., None] * local_out
-    denom = jnp.sum(source_w * source_sum, 0) + local_w * local_sum
+    numer = source_w[..., None] * source_out + local_w[..., None] * local_out
+    denom = source_w * source_sum + local_w * local_sum
     attention_layer = (numer / denom[..., None]).astype(jnp.bfloat16)
     attention_layer = jnp.transpose(attention_layer, (1, 2, 0, 3, 4)).reshape(
         SAMPLE_COUNT * DECODE_TOKENS, kv_local * query_groups * HEAD_SIZE
     )
     projected = jnp.dot(attention_layer, out_weight, preferred_element_type=jnp.float32)
-    mlp_count = lax.axis_size("mlp")
     mlp_index = lax.axis_index("mlp")
     share = D // mlp_count
-    mid = residual_in.astype(jnp.float32) + lax.psum(projected.astype(jnp.bfloat16), "mlp").astype(
-        jnp.float32
-    )
+    mid = residual_in.astype(jnp.float32) + sum_all(projected, "mlp", mlp_count)
     normed = (mid * rms_scale(jnp.sum(mid * mid, -1, keepdims=True), D) * mlp_gain).astype(
         jnp.bfloat16
     )
     gate = jnp.dot(normed, gate_weight, preferred_element_type=jnp.float32)
     upper = jnp.dot(normed, up_weight, preferred_element_type=jnp.float32)
     hidden = (jax.nn.silu(gate) * upper).astype(jnp.bfloat16)
-    stream = mid + lax.psum(
-        jnp.dot(hidden, down_weight, preferred_element_type=jnp.float32).astype(jnp.bfloat16), "mlp"
-    ).astype(jnp.float32)
+    stream = mid + sum_all(
+        jnp.dot(hidden, down_weight, preferred_element_type=jnp.float32), "mlp", mlp_count
+    )
     score = jnp.sum(
         stream
         * rms_scale(jnp.sum(stream * stream, -1, keepdims=True), D)

time: 323 us -> 618 us (1.91); the launches traced: 322 us -> 605 us
  starting transfers between devices: 24.9 us -> 200 us
  local copies, waits for them, and re-layouts: 6.46 us -> 94 us
  waiting for transfers between devices: 203 us -> 260 us
  blocking collectives: 43.4 us -> 0 us
  other arithmetic: 9.26 us -> 26.7 us
  between operations: 14.4 us -> 1.36 us
    ppermute x0 -> x76, waiting for transfers between devices: none -> 260 us  [shifted(): return lax.ppermute(x, axis, perm=[(i, (i + s) % n) for i in range(n)])]
    ppermute x0 -> x76, starting transfers between devices: none -> 200 us  [shifted(): return lax.ppermute(x, axis, perm=[(i, (i + s) % n) for i in range(n)])]
    psum x2 -> x0, waiting for transfers between devices: 151 us -> none  [the longest x1 77.2 us: on_device(): lax.psum(jnp.dot(hidden, down_weight, preferred_element_type=jnp.float32)...]
    unnamed x34 -> x132, local copies, waits for them, and re-layouts: 2.78 us -> 68.1 us
    all_to_all x3 -> x0, waiting for transfers between devices: 52 us -> none  [the longest x1 45.6 us: on_device(): lax.all_to_all(piece_out, 'req', split_axis=0, concat_axis=0, tiled=True)]
    all_gather x1 -> x0, blocking collectives: 43.4 us -> none  [on_device(): gathered = lax.all_gather(queries, 'req', axis=0, tiled=True)]
    all_to_all x3 -> x0, starting transfers between devices: 24.8 us -> none  [the longest x1 10.1 us: on_device(): lax.all_to_all(piece_out, 'req', split_axis=0, concat_axis=0, tiled=True)]
    concatenate x0 -> x4, other arithmetic: none -> 12.1 us  [roll_lead(): both = jnp.concatenate([x, x], axis=0)]
  transfers between devices with their start and end apart: 5 -> 76, of which waited for: 4 -> 53; matrix products, arithmetic and copies ran while one was open for 4% -> 9% of each run, Pallas kernels for 0% -> 0%
where the time goes in v2:
time: 618 us; the launch traced here: 605 us
  waiting for transfers between devices  260 us (42%)
  starting transfers between devices  200 us (32%)
  local copies, waits for them, and re-layouts  94 us (15%)
  other arithmetic  26.7 us (4%)
  matrix products  23 us (4%)
    ppermute x76, waiting for transfers between devices, shifted(): return lax.ppermute(x, axis, perm=[(i, (i + s) % n) for i in range(n)])  260 us
    ppermute x76, starting transfers between devices, shifted(): return lax.ppermute(x, axis, perm=[(i, (i + s) % n) for i in range(n)])  200 us
    unnamed x132, local copies, waits for them, and re-layouts  68.1 us
  transfers between devices with their start and end apart: 76, of which 53 were waited for; matrix products, arithmetic and copies ran while one was open for 9% of the time, Pallas kernels for 0%

profile of v2, /device:TPU:6, one launch (start us, length us, event | category | flops | bytes accessed | tf_op | source)
XLA Modules:
  0.0 605.4 jit_solution(7759235375308477978)
XLA Ops:
  9.9 9.1 %collective-permute-start = (bf16[32,320]{1,0:T(8,128)(2,1)}, bf16[32,320]{1,0:T(8,128)(2,1)S(1)}, u32[]{:S(2)}, u32[]{:S(2)}) collective-permute-start(bf16[32,320]{1,0:T(8,128)(2,1)} %param.18), channel_id=1, source_target_pairs={{0,248},{8,0},{16,8},{24,16},{32,24},{40,32},{48,40},{56,48},{64,5... | collective-permute-start | bytes 61448 | tf_op jit(solution)/shard_map/ppermute | solution.py:20
  26.8 11.9 %collective-permute-start.1 = (bf16[32,320]{1,0:T(8,128)(2,1)S(1)}, bf16[32,320]{1,0:T(8,128)(2,1)S(1)}, u32[]{:S(2)}, u32[]{:S(2)}) collective-permute-start(bf16[32,320]{1,0:T(8,128)(2,1)S(1)} %copy-done.5), channel_id=1, source_target_pairs={{0,240},{8,248},{16,0},{24,8},{32,16},{40,24},{48,32},{56,40},{64,... | collective-permute-start | bytes 61448 | tf_op jit(solution)/shard_map/ppermute | solution.py:20
  56.7 5.5 collective-permute-start.5
  71.8 4.6 collective-permute-start.7
  91.0 7.1 %collective-permute-start.10 = (bf16[32,320]{1,0:T(8,128)(2,1)S(1)}, bf16[32,320]{1,0:T(8,128)(2,1)S(1)}, u32[]{:S(2)}, u32[]{:S(2)}) collective-permute-start(bf16[32,320]{1,0:T(8,128)(2,1)S(1)} %copy-done.5), channel_id=1, source_target_pairs={{0,168},{8,176},{16,184},{24,192},{32,200},{40,208},{48,216},{56,2... | collective-permute-start | bytes 61448 | tf_op jit(solution)/shard_map/ppermute | solution.py:20
  99.7 7.8 %collective-permute-start.11 = (bf16[32,320]{1,0:T(8,128)(2,1)S(1)}, bf16[32,320]{1,0:T(8,128)(2,1)S(1)}, u32[]{:S(2)}, u32[]{:S(2)}) collective-permute-start(bf16[32,320]{1,0:T(8,128)(2,1)S(1)} %copy-done.5), channel_id=1, source_target_pairs={{0,160},{8,168},{16,176},{24,184},{32,192},{40,200},{48,208},{56,2... | collective-permute-start | bytes 61448 | tf_op jit(solution)/shard_map/ppermute | solution.py:20
  118.2 9.5 %collective-permute-done.13 = bf16[32,320]{1,0:T(8,128)(2,1)S(1)} collective-permute-done((bf16[32,320]{1,0:T(8,128)(2,1)S(1)}, bf16[32,320]{1,0:T(8,128)(2,1)S(1)}, u32[]{:S(2)}, u32[]{:S(2)}) %collective-permute-start.13) | collective-permute-done | bytes 20512 | tf_op jit(solution)/shard_map/ppermute | solution.py:20
  128.9 8.4 %collective-permute-done.14 = bf16[32,320]{1,0:T(8,128)(2,1)S(1)} collective-permute-done((bf16[32,320]{1,0:T(8,128)(2,1)S(1)}, bf16[32,320]{1,0:T(8,128)(2,1)S(1)}, u32[]{:S(2)}, u32[]{:S(2)}) %collective-permute-start.14) | collective-permute-done | bytes 20512 | tf_op jit(solution)/shard_map/ppermute | solution.py:20
  137.9 7.1 %collective-permute-done.15 = bf16[32,320]{1,0:T(8,128)(2,1)S(1)} collective-permute-done((bf16[32,320]{1,0:T(8,128)(2,1)S(1)}, bf16[32,320]{1,0:T(8,128)(2,1)S(1)}, u32[]{:S(2)}, u32[]{:S(2)}) %collective-permute-start.15) | collective-permute-done | bytes 20512 | tf_op jit(solution)/shard_map/ppermute | solution.py:20
  145.7 6.6 %collective-permute-done.16 = bf16[32,320]{1,0:T(8,128)(2,1)S(1)} collective-permute-done((bf16[32,320]{1,0:T(8,128)(2,1)S(1)}, bf16[32,320]{1,0:T(8,128)(2,1)S(1)}, u32[]{:S(2)}, u32[]{:S(2)}) %collective-permute-start.16) | collective-permute-done | bytes 20512 | tf_op jit(solution)/shard_map/ppermute | solution.py:20
  152.8 9.0 %collective-permute-done.17 = bf16[32,320]{1,0:T(8,128)(2,1)S(1)} collective-permute-done((bf16[32,320]{1,0:T(8,128)(2,1)S(1)}, bf16[32,320]{1,0:T(8,128)(2,1)S(1)}, u32[]{:S(2)}, u32[]{:S(2)}) %collective-permute-start.17) | collective-permute-done | bytes 20512 | tf_op jit(solution)/shard_map/ppermute | solution.py:20
  162.5 8.4 %collective-permute-done.18 = bf16[32,320]{1,0:T(8,128)(2,1)S(1)} collective-permute-done((bf16[32,320]{1,0:T(8,128)(2,1)S(1)}, bf16[32,320]{1,0:T(8,128)(2,1)S(1)}, u32[]{:S(2)}, u32[]{:S(2)}) %collective-permute-start.18) | collective-permute-done | bytes 20512 | tf_op jit(solution)/shard_map/ppermute | solution.py:20
  178.3 5.8 collective-permute-done.20
  184.7 7.7 %collective-permute-done.21 = bf16[32,320]{1,0:T(8,128)(2,1)S(1)} collective-permute-done((bf16[32,320]{1,0:T(8,128)(2,1)S(1)}, bf16[32,320]{1,0:T(8,128)(2,1)S(1)}, u32[]{:S(2)}, u32[]{:S(2)}) %collective-permute-start.21) | collective-permute-done | bytes 20512 | tf_op jit(solution)/shard_map/ppermute | solution.py:20
  193.1 7.2 %collective-permute-done.22 = bf16[32,320]{1,0:T(8,128)(2,1)S(1)} collective-permute-done((bf16[32,320]{1,0:T(8,128)(2,1)S(1)}, bf16[32,320]{1,0:T(8,128)(2,1)S(1)}, u32[]{:S(2)}, u32[]{:S(2)}) %collective-permute-start.22) | collective-permute-done | bytes 20512 | tf_op jit(solution)/shard_map/ppermute | solution.py:20
  201.3 4.9 collective-permute-done.23
  206.8 4.8 collective-permute-done.24
  213.0 6.0 collective-permute-done.25
  246.7 6.0 select_reduce_fusion
  252.9 5.5 fusion
  258.7 4.9 fusion.18
  272.3 6.0 fusion.14
  282.0 14.7 %collective-permute-start.60 = (f32[82,128]{0,1:T(8,128)S(1)}, f32[82,128]{0,1:T(8,128)S(1)}, u32[]{:S(2)}, u32[]{:S(2)}) collective-permute-start(f32[82,128]{0,1:T(8,128)S(1)} %bitcast.389), channel_id=1, source_target_pairs={{0,240},{8,248},{16,0},{24,8},{32,16},{40,24},{48,32},{56,40},{64,... | collective-permute-start | bytes 125960 | tf_op jit(solution)/shard_map/ppermute | solution.py:20
  308.8 4.7 collective-permute-start.32
  316.1 4.6 collective-permute-done.33
  321.3 4.9 collective-permute-done.34
  326.8 6.7 %collective-permute-done.35 = f32[82,128]{0,1:T(8,128)S(1)} collective-permute-done((f32[82,128]{0,1:T(8,128)S(1)}, f32[82,128]{0,1:T(8,128)S(1)}, u32[]{:S(2)}, u32[]{:S(2)}) %collective-permute-start.35) | collective-permute-done | bytes 42016 | tf_op jit(solution)/shard_map/ppermute | solution.py:20
  336.5 4.8 collective-permute-done.36
  342.0 5.6 collective-permute-done.37
  354.0 14.1 %collective-permute-start.61 = (f32[82,128]{0,1:T(8,128)S(1)}, f32[82,128]{0,1:T(8,128)S(1)}, u32[]{:S(2)}, u32[]{:S(2)}) collective-permute-start(f32[82,128]{0,1:T(8,128)S(1)} %bitcast.365), channel_id=1, source_target_pairs={{0,248},{8,0},{16,8},{24,16},{32,24},{40,32},{48,40},{56,48},{64,5... | collective-permute-start | bytes 125960 | tf_op jit(solution)/shard_map/ppermute | solution.py:20
  368.7 4.6 collective-permute-start.41
  379.5 8.9 %collective-permute-done.42 = f32[82,128]{0,1:T(8,128)S(1)} collective-permute-done((f32[82,128]{0,1:T(8,128)S(1)}, f32[82,128]{0,1:T(8,128)S(1)}, u32[]{:S(2)}, u32[]{:S(2)}) %collective-permute-start.42) | collective-permute-done | bytes 42016 | tf_op jit(solution)/shard_map/ppermute | solution.py:20
  389.0 9.0 %collective-permute-done.43 = f32[82,128]{0,1:T(8,128)S(1)} collective-permute-done((f32[82,128]{0,1:T(8,128)S(1)}, f32[82,128]{0,1:T(8,128)S(1)}, u32[]{:S(2)}, u32[]{:S(2)}) %collective-permute-start.43) | collective-permute-done | bytes 42016 | tf_op jit(solution)/shard_map/ppermute | solution.py:20
  398.0 4.9 collective-permute-start.44
  411.1 4.9 collective-permute-done.45
  419.5 6.0 collective-permute-done.46
  426.5 9.5 %collective-permute-done.47 = f32[82,128]{0,1:T(8,128)S(1)} collective-permute-done((f32[82,128]{0,1:T(8,128)S(1)}, f32[82,128]{0,1:T(8,128)S(1)}, u32[]{:S(2)}, u32[]{:S(2)}) %collective-permute-start.47) | collective-permute-done | bytes 42016 | tf_op jit(solution)/shard_map/ppermute | solution.py:20
  439.0 7.6 %collective-permute-done.48 = f32[82,128]{0,1:T(8,128)S(1)} collective-permute-done((f32[82,128]{0,1:T(8,128)S(1)}, f32[82,128]{0,1:T(8,128)S(1)}, u32[]{:S(2)}, u32[]{:S(2)}) %collective-permute-start.48) | collective-permute-done | bytes 42016 | tf_op jit(solution)/shard_map/ppermute | solution.py:20
  447.2 5.3 collective-permute-done.49
  458.6 6.1 collective-permute-start.51
  467.1 6.3 %collective-permute-start.52 = (f32[82,128]{0,1:T(8,128)S(1)}, f32[82,128]{0,1:T(8,128)S(1)}, u32[]{:S(2)}, u32[]{:S(2)}) collective-permute-start(f32[82,128]{0,1:T(8,128)S(1)} %bitcast.372), channel_id=1, source_target_pairs={{0,176},{8,184},{16,192},{24,200},{32,208},{40,216},{48,224},{56,2... | collective-permute-start | bytes 125960 | tf_op jit(solution)/shard_map/ppermute | solution.py:20
  476.1 6.4 %collective-permute-start.53 = (f32[82,128]{0,1:T(8,128)S(1)}, f32[82,128]{0,1:T(8,128)S(1)}, u32[]{:S(2)}, u32[]{:S(2)}) collective-permute-start(f32[82,128]{0,1:T(8,128)S(1)} %bitcast.371), channel_id=1, source_target_pairs={{0,184},{8,192},{16,200},{24,208},{32,216},{40,224},{48,232},{56,2... | collective-permute-start | bytes 125960 | tf_op jit(solution)/shard_map/ppermute | solution.py:20
  485.7 4.9 collective-permute-start.54
  495.3 6.2 %collective-permute-done.55 = f32[82,128]{0,1:T(8,128)S(1)} collective-permute-done((f32[82,128]{0,1:T(8,128)S(1)}, f32[82,128]{0,1:T(8,128)S(1)}, u32[]{:S(2)}, u32[]{:S(2)}) %collective-permute-start.55) | collective-permute-done | bytes 42016 | tf_op jit(solution)/shard_map/ppermute | solution.py:20
  503.9 5.4 collective-permute-done.56
  524.0 5.2 slice_reduce_fusion.1
  543.7 12.8 %collective-permute-done.63 = bf16[32,2560]{1,0:T(8,128)(2,1)S(1)} collective-permute-done((bf16[32,2560]{1,0:T(8,128)(2,1)S(1)}, bf16[32,2560]{1,0:T(8,128)(2,1)S(1)}, u32[]{:S(2)}, u32[]{:S(2)}) %collective-permute-start.63) | collective-permute-done | bytes 163872 | tf_op jit(solution)/shard_map/ppermute | solution.py:20
  584.7 8.2 %collective-permute-done.70 = bf16[32,2560]{1,0:T(8,128)(2,1)S(1)} collective-permute-done((bf16[32,2560]{1,0:T(8,128)(2,1)S(1)}, bf16[32,2560]{1,0:T(8,128)(2,1)S(1)}, u32[]{:S(2)}, u32[]{:S(2)}) %collective-permute-start.70) | collective-permute-done | bytes 163872 | tf_op jit(solution)/shard_map/ppermute | solution.py:20
  (288 shorter events, 268.0 us)
Async XLA Ops:
  0.7 220.9 %collective-permute-start.29 = (bf16[32,320]{1,0:T(8,128)(2,1)}, bf16[32,320]{1,0:T(8,128)(2,1)S(1)}, u32[]{:S(2)}, u32[]{:S(2)}) collective-permute-start(bf16[32,320]{1,0:T(8,128)(2,1)} %param.18), channel_id=1, source_target_pairs={{0,16},{8,24},{16,32},{24,40},{32,48},{40,56},{48,64},{56,72},{64,... | collective-permute-start | bytes 61448 | tf_op jit(solution)/shard_map/ppermute | solution.py:20
  3.5 217.4 %collective-permute-start.28 = (bf16[32,320]{1,0:T(8,128)(2,1)}, bf16[32,320]{1,0:T(8,128)(2,1)S(1)}, u32[]{:S(2)}, u32[]{:S(2)}) collective-permute-start(bf16[32,320]{1,0:T(8,128)(2,1)} %param.18), channel_id=1, source_target_pairs={{0,24},{8,32},{16,40},{24,48},{32,56},{40,64},{48,72},{56,80},{64,... | collective-permute-start | bytes 61448 | tf_op jit(solution)/shard_map/ppermute | solution.py:20
  4.8 215.5 %collective-permute-start.27 = (bf16[32,320]{1,0:T(8,128)(2,1)}, bf16[32,320]{1,0:T(8,128)(2,1)S(1)}, u32[]{:S(2)}, u32[]{:S(2)}) collective-permute-start(bf16[32,320]{1,0:T(8,128)(2,1)} %param.18), channel_id=1, source_target_pairs={{0,32},{8,40},{16,48},{24,56},{32,64},{40,72},{48,80},{56,88},{64,... | collective-permute-start | bytes 61448 | tf_op jit(solution)/shard_map/ppermute | solution.py:20
  6.7 213.0 %collective-permute-start.26 = (bf16[32,320]{1,0:T(8,128)(2,1)}, bf16[32,320]{1,0:T(8,128)(2,1)S(1)}, u32[]{:S(2)}, u32[]{:S(2)}) collective-permute-start(bf16[32,320]{1,0:T(8,128)(2,1)} %param.18), channel_id=1, source_target_pairs={{0,40},{8,48},{16,56},{24,64},{32,72},{40,80},{48,88},{56,96},{64,... | collective-permute-start | bytes 61448 | tf_op jit(solution)/shard_map/ppermute | solution.py:20
  9.9 16.9 %collective-permute-start = (bf16[32,320]{1,0:T(8,128)(2,1)}, bf16[32,320]{1,0:T(8,128)(2,1)S(1)}, u32[]{:S(2)}, u32[]{:S(2)}) collective-permute-start(bf16[32,320]{1,0:T(8,128)(2,1)} %param.18), channel_id=1, source_target_pairs={{0,248},{8,0},{16,8},{24,16},{32,24},{40,32},{48,40},{56,48},{64,5... | collective-permute-start | bytes 61448 | tf_op jit(solution)/shard_map/ppermute | solution.py:20
  26.8 16.2 %collective-permute-start.1 = (bf16[32,320]{1,0:T(8,128)(2,1)S(1)}, bf16[32,320]{1,0:T(8,128)(2,1)S(1)}, u32[]{:S(2)}, u32[]{:S(2)}) collective-permute-start(bf16[32,320]{1,0:T(8,128)(2,1)S(1)} %copy-done.5), channel_id=1, source_target_pairs={{0,240},{8,248},{16,0},{24,8},{32,16},{40,24},{48,32},{56,40},{64,... | collective-permute-start | bytes 61448 | tf_op jit(solution)/shard_map/ppermute | solution.py:20
  63.8 7.9 %collective-permute-start.6 = (bf16[32,320]{1,0:T(8,128)(2,1)S(1)}, bf16[32,320]{1,0:T(8,128)(2,1)S(1)}, u32[]{:S(2)}, u32[]{:S(2)}) collective-permute-start(bf16[32,320]{1,0:T(8,128)(2,1)S(1)} %copy-done.5), channel_id=1, source_target_pairs={{0,200},{8,208},{16,216},{24,224},{32,232},{40,240},{48,248},{56,0... | collective-permute-start | bytes 61448 | tf_op jit(solution)/shard_map/ppermute | solution.py:20
  83.0 8.0 %collective-permute-start.9 = (bf16[32,320]{1,0:T(8,128)(2,1)S(1)}, bf16[32,320]{1,0:T(8,128)(2,1)S(1)}, u32[]{:S(2)}, u32[]{:S(2)}) collective-permute-start(bf16[32,320]{1,0:T(8,128)(2,1)S(1)} %copy-done.5), channel_id=1, source_target_pairs={{0,176},{8,184},{16,192},{24,200},{32,208},{40,216},{48,224},{56,2... | collective-permute-start | bytes 61448 | tf_op jit(solution)/shard_map/ppermute | solution.py:20
  91.0 8.7 %collective-permute-start.10 = (bf16[32,320]{1,0:T(8,128)(2,1)S(1)}, bf16[32,320]{1,0:T(8,128)(2,1)S(1)}, u32[]{:S(2)}, u32[]{:S(2)}) collective-permute-start(bf16[32,320]{1,0:T(8,128)(2,1)S(1)} %copy-done.5), channel_id=1, source_target_pairs={{0,168},{8,176},{16,184},{24,192},{32,200},{40,208},{48,216},{56,2... | collective-permute-start | bytes 61448 | tf_op jit(solution)/shard_map/ppermute | solution.py:20
  99.7 12.8 %collective-permute-start.11 = (bf16[32,320]{1,0:T(8,128)(2,1)S(1)}, bf16[32,320]{1,0:T(8,128)(2,1)S(1)}, u32[]{:S(2)}, u32[]{:S(2)}) collective-permute-start(bf16[32,320]{1,0:T(8,128)(2,1)S(1)} %copy-done.5), channel_id=1, source_target_pairs={{0,160},{8,168},{16,176},{24,184},{32,192},{40,200},{48,208},{56,2... | collective-permute-start | bytes 61448 | tf_op jit(solution)/shard_map/ppermute | solution.py:20
  117.6 10.2 %collective-permute-start.13 = (bf16[32,320]{1,0:T(8,128)(2,1)S(1)}, bf16[32,320]{1,0:T(8,128)(2,1)S(1)}, u32[]{:S(2)}, u32[]{:S(2)}) collective-permute-start(bf16[32,320]{1,0:T(8,128)(2,1)S(1)} %copy-done.5), channel_id=1, source_target_pairs={{0,144},{8,152},{16,160},{24,168},{32,176},{40,184},{48,192},{56,2... | collective-permute-start | bytes 61448 | tf_op jit(solution)/shard_map/ppermute | solution.py:20
  127.7 9.6 %collective-permute-start.14 = (bf16[32,320]{1,0:T(8,128)(2,1)S(1)}, bf16[32,320]{1,0:T(8,128)(2,1)S(1)}, u32[]{:S(2)}, u32[]{:S(2)}) collective-permute-start(bf16[32,320]{1,0:T(8,128)(2,1)S(1)} %copy-done.5), channel_id=1, source_target_pairs={{0,136},{8,144},{16,152},{24,160},{32,168},{40,176},{48,184},{56,1... | collective-permute-start | bytes 61448 | tf_op jit(solution)/shard_map/ppermute | solution.py:20
  152.2 9.6 %collective-permute-start.17 = (bf16[32,320]{1,0:T(8,128)(2,1)S(1)}, bf16[32,320]{1,0:T(8,128)(2,1)S(1)}, u32[]{:S(2)}, u32[]{:S(2)}) collective-permute-start(bf16[32,320]{1,0:T(8,128)(2,1)S(1)} %copy-done.5), channel_id=1, source_target_pairs={{0,112},{8,120},{16,128},{24,136},{32,144},{40,152},{48,160},{56,1... | collective-permute-start | bytes 61448 | tf_op jit(solution)/shard_map/ppermute | solution.py:20
  161.8 9.0 %collective-permute-start.18 = (bf16[32,320]{1,0:T(8,128)(2,1)S(1)}, bf16[32,320]{1,0:T(8,128)(2,1)S(1)}, u32[]{:S(2)}, u32[]{:S(2)}) collective-permute-start(bf16[32,320]{1,0:T(8,128)(2,1)S(1)} %copy-done.5), channel_id=1, source_target_pairs={{0,104},{8,112},{16,120},{24,128},{32,136},{40,144},{48,152},{56,1... | collective-permute-start | bytes 61448 | tf_op jit(solution)/shard_map/ppermute | solution.py:20
  184.1 8.3 %collective-permute-start.21 = (bf16[32,320]{1,0:T(8,128)(2,1)S(1)}, bf16[32,320]{1,0:T(8,128)(2,1)S(1)}, u32[]{:S(2)}, u32[]{:S(2)}) collective-permute-start(bf16[32,320]{1,0:T(8,128)(2,1)S(1)} %copy-done.5), channel_id=1, source_target_pairs={{0,80},{8,88},{16,96},{24,104},{32,112},{40,120},{48,128},{56,136}... | collective-permute-start | bytes 61448 | tf_op jit(solution)/shard_map/ppermute | solution.py:20
  192.5 7.8 %collective-permute-start.22 = (bf16[32,320]{1,0:T(8,128)(2,1)S(1)}, bf16[32,320]{1,0:T(8,128)(2,1)S(1)}, u32[]{:S(2)}, u32[]{:S(2)}) collective-permute-start(bf16[32,320]{1,0:T(8,128)(2,1)S(1)} %copy-done.5), channel_id=1, source_target_pairs={{0,72},{8,80},{16,88},{24,96},{32,104},{40,112},{48,120},{56,128},... | collective-permute-start | bytes 61448 | tf_op jit(solution)/shard_map/ppermute | solution.py:20
  280.1 88.7 %collective-permute-start.40 = (f32[82,128]{0,1:T(8,128)S(1)}, f32[82,128]{0,1:T(8,128)S(1)}, u32[]{:S(2)}, u32[]{:S(2)}) collective-permute-start(f32[82,128]{0,1:T(8,128)S(1)} %bitcast.391), channel_id=1, source_target_pairs={{0,80},{8,88},{16,96},{24,104},{32,112},{40,120},{48,128},{56,136}... | collective-permute-start | bytes 125960 | tf_op jit(solution)/shard_map/ppermute | solution.py:20
  282.0 232.9 %collective-permute-start.60 = (f32[82,128]{0,1:T(8,128)S(1)}, f32[82,128]{0,1:T(8,128)S(1)}, u32[]{:S(2)}, u32[]{:S(2)}) collective-permute-start(f32[82,128]{0,1:T(8,128)S(1)} %bitcast.389), channel_id=1, source_target_pairs={{0,240},{8,248},{16,0},{24,8},{32,16},{40,24},{48,32},{56,40},{64,... | collective-permute-start | bytes 125960 | tf_op jit(solution)/shard_map/ppermute | solution.py:20
  296.8 57.2 %collective-permute-start.39 = (f32[82,128]{0,1:T(8,128)S(1)}, f32[82,128]{0,1:T(8,128)S(1)}, u32[]{:S(2)}, u32[]{:S(2)}) collective-permute-start(f32[82,128]{0,1:T(8,128)S(1)} %bitcast.392), channel_id=1, source_target_pairs={{0,72},{8,80},{16,88},{24,96},{32,104},{40,112},{48,120},{56,128},... | collective-permute-start | bytes 125960 | tf_op jit(solution)/shard_map/ppermute | solution.py:20
  299.3 50.3 %collective-permute-start.38 = (f32[82,128]{0,1:T(8,128)S(1)}, f32[82,128]{0,1:T(8,128)S(1)}, u32[]{:S(2)}, u32[]{:S(2)}) collective-permute-start(f32[82,128]{0,1:T(8,128)S(1)} %bitcast.393), channel_id=1, source_target_pairs={{0,64},{8,72},{16,80},{24,88},{32,96},{40,104},{48,112},{56,120},{... | collective-permute-start | bytes 125960 | tf_op jit(solution)/shard_map/ppermute | solution.py:20
  333.5 7.9 %collective-permute-start.36 = (f32[82,128]{0,1:T(8,128)S(1)}, f32[82,128]{0,1:T(8,128)S(1)}, u32[]{:S(2)}, u32[]{:S(2)}) collective-permute-start(f32[82,128]{0,1:T(8,128)S(1)} %bitcast.395), channel_id=1, source_target_pairs={{0,48},{8,56},{16,64},{24,72},{32,80},{40,88},{48,96},{56,104},{64... | collective-permute-start | bytes 125960 | tf_op jit(solution)/shard_map/ppermute | solution.py:20
  347.6 166.7 %collective-permute-start.59 = (f32[82,128]{0,1:T(8,128)S(1)}, f32[82,128]{0,1:T(8,128)S(1)}, u32[]{:S(2)}, u32[]{:S(2)}) collective-permute-start(f32[82,128]{0,1:T(8,128)S(1)} %bitcast.390), channel_id=1, source_target_pairs={{0,232},{8,240},{16,248},{24,0},{32,8},{40,16},{48,24},{56,32},{64... | collective-permute-start | bytes 125960 | tf_op jit(solution)/shard_map/ppermute | solution.py:20
  349.6 164.1 %collective-permute-start.58 = (f32[82,128]{0,1:T(8,128)S(1)}, f32[82,128]{0,1:T(8,128)S(1)}, u32[]{:S(2)}, u32[]{:S(2)}) collective-permute-start(f32[82,128]{0,1:T(8,128)S(1)} %bitcast.366), channel_id=1, source_target_pairs={{0,224},{8,232},{16,240},{24,248},{32,0},{40,8},{48,16},{56,24},{6... | collective-permute-start | bytes 125960 | tf_op jit(solution)/shard_map/ppermute | solution.py:20
  354.0 161.6 %collective-permute-start.61 = (f32[82,128]{0,1:T(8,128)S(1)}, f32[82,128]{0,1:T(8,128)S(1)}, u32[]{:S(2)}, u32[]{:S(2)}) collective-permute-start(f32[82,128]{0,1:T(8,128)S(1)} %bitcast.365), channel_id=1, source_target_pairs={{0,248},{8,0},{16,8},{24,16},{32,24},{40,32},{48,40},{56,48},{64,5... | collective-permute-start | bytes 125960 | tf_op jit(solution)/shard_map/ppermute | solution.py:20
  368.7 7.8 %collective-permute-start.41 = (f32[82,128]{0,1:T(8,128)S(1)}, f32[82,128]{0,1:T(8,128)S(1)}, u32[]{:S(2)}, u32[]{:S(2)}) collective-permute-start(f32[82,128]{0,1:T(8,128)S(1)} %bitcast.383), channel_id=1, source_target_pairs={{0,88},{8,96},{16,104},{24,112},{32,120},{40,128},{48,136},{56,144... | collective-permute-start | bytes 125960 | tf_op jit(solution)/shard_map/ppermute | solution.py:20
  376.6 11.8 %collective-permute-start.42 = (f32[82,128]{0,1:T(8,128)S(1)}, f32[82,128]{0,1:T(8,128)S(1)}, u32[]{:S(2)}, u32[]{:S(2)}) collective-permute-start(f32[82,128]{0,1:T(8,128)S(1)} %bitcast.382), channel_id=1, source_target_pairs={{0,96},{8,104},{16,112},{24,120},{32,128},{40,136},{48,144},{56,15... | collective-permute-start | bytes 125960 | tf_op jit(solution)/shard_map/ppermute | solution.py:20
  388.4 9.6 %collective-permute-start.43 = (f32[82,128]{0,1:T(8,128)S(1)}, f32[82,128]{0,1:T(8,128)S(1)}, u32[]{:S(2)}, u32[]{:S(2)}) collective-permute-start(f32[82,128]{0,1:T(8,128)S(1)} %bitcast.381), channel_id=1, source_target_pairs={{0,104},{8,112},{16,120},{24,128},{32,136},{40,144},{48,152},{56,1... | collective-permute-start | bytes 125960 | tf_op jit(solution)/shard_map/ppermute | solution.py:20
  398.0 9.8 %collective-permute-start.44 = (f32[82,128]{0,1:T(8,128)S(1)}, f32[82,128]{0,1:T(8,128)S(1)}, u32[]{:S(2)}, u32[]{:S(2)}) collective-permute-start(f32[82,128]{0,1:T(8,128)S(1)} %bitcast.380), channel_id=1, source_target_pairs={{0,112},{8,120},{16,128},{24,136},{32,144},{40,152},{48,160},{56,1... | collective-permute-start | bytes 125960 | tf_op jit(solution)/shard_map/ppermute | solution.py:20
  407.8 8.2 %collective-permute-start.45 = (f32[82,128]{0,1:T(8,128)S(1)}, f32[82,128]{0,1:T(8,128)S(1)}, u32[]{:S(2)}, u32[]{:S(2)}) collective-permute-start(f32[82,128]{0,1:T(8,128)S(1)} %bitcast.379), channel_id=1, source_target_pairs={{0,120},{8,128},{16,136},{24,144},{32,152},{40,160},{48,168},{56,1... | collective-permute-start | bytes 125960 | tf_op jit(solution)/shard_map/ppermute | solution.py:20
  416.0 9.5 %collective-permute-start.46 = (f32[82,128]{0,1:T(8,128)S(1)}, f32[82,128]{0,1:T(8,128)S(1)}, u32[]{:S(2)}, u32[]{:S(2)}) collective-permute-start(f32[82,128]{0,1:T(8,128)S(1)} %bitcast.378), channel_id=1, source_target_pairs={{0,128},{8,136},{16,144},{24,152},{32,160},{40,168},{48,176},{56,1... | collective-permute-start | bytes 125960 | tf_op jit(solution)/shard_map/ppermute | solution.py:20
  425.4 10.5 %collective-permute-start.47 = (f32[82,128]{0,1:T(8,128)S(1)}, f32[82,128]{0,1:T(8,128)S(1)}, u32[]{:S(2)}, u32[]{:S(2)}) collective-permute-start(f32[82,128]{0,1:T(8,128)S(1)} %bitcast.377), channel_id=1, source_target_pairs={{0,136},{8,144},{16,152},{24,160},{32,168},{40,176},{48,184},{56,1... | collective-permute-start | bytes 125960 | tf_op jit(solution)/shard_map/ppermute | solution.py:20
  436.0 10.6 %collective-permute-start.48 = (f32[82,128]{0,1:T(8,128)S(1)}, f32[82,128]{0,1:T(8,128)S(1)}, u32[]{:S(2)}, u32[]{:S(2)}) collective-permute-start(f32[82,128]{0,1:T(8,128)S(1)} %bitcast.376), channel_id=1, source_target_pairs={{0,144},{8,152},{16,160},{24,168},{32,176},{40,184},{48,192},{56,2... | collective-permute-start | bytes 125960 | tf_op jit(solution)/shard_map/ppermute | solution.py:20
  458.6 8.5 %collective-permute-start.51 = (f32[82,128]{0,1:T(8,128)S(1)}, f32[82,128]{0,1:T(8,128)S(1)}, u32[]{:S(2)}, u32[]{:S(2)}) collective-permute-start(f32[82,128]{0,1:T(8,128)S(1)} %bitcast.373), channel_id=1, source_target_pairs={{0,168},{8,176},{16,184},{24,192},{32,200},{40,208},{48,216},{56,2... | collective-permute-start | bytes 125960 | tf_op jit(solution)/shard_map/ppermute | solution.py:20
  467.1 9.0 %collective-permute-start.52 = (f32[82,128]{0,1:T(8,128)S(1)}, f32[82,128]{0,1:T(8,128)S(1)}, u32[]{:S(2)}, u32[]{:S(2)}) collective-permute-start(f32[82,128]{0,1:T(8,128)S(1)} %bitcast.372), channel_id=1, source_target_pairs={{0,176},{8,184},{16,192},{24,200},{32,208},{40,216},{48,224},{56,2... | collective-permute-start | bytes 125960 | tf_op jit(solution)/shard_map/ppermute | solution.py:20
  476.1 9.5 %collective-permute-start.53 = (f32[82,128]{0,1:T(8,128)S(1)}, f32[82,128]{0,1:T(8,128)S(1)}, u32[]{:S(2)}, u32[]{:S(2)}) collective-permute-start(f32[82,128]{0,1:T(8,128)S(1)} %bitcast.371), channel_id=1, source_target_pairs={{0,184},{8,192},{16,200},{24,208},{32,216},{40,224},{48,232},{56,2... | collective-permute-start | bytes 125960 | tf_op jit(solution)/shard_map/ppermute | solution.py:20
  492.7 8.8 %collective-permute-start.55 = (f32[82,128]{0,1:T(8,128)S(1)}, f32[82,128]{0,1:T(8,128)S(1)}, u32[]{:S(2)}, u32[]{:S(2)}) collective-permute-start(f32[82,128]{0,1:T(8,128)S(1)} %bitcast.369), channel_id=1, source_target_pairs={{0,200},{8,208},{16,216},{24,224},{32,232},{40,240},{48,248},{56,0... | collective-permute-start | bytes 125960 | tf_op jit(solution)/shard_map/ppermute | solution.py:20
  533.0 9.0 %collective-permute-start.62 = (bf16[32,2560]{1,0:T(8,128)(2,1)S(1)}, bf16[32,2560]{1,0:T(8,128)(2,1)S(1)}, u32[]{:S(2)}, u32[]{:S(2)}) collective-permute-start(bf16[32,2560]{1,0:T(8,128)(2,1)S(1)} %get-tuple-element.51), channel_id=1, source_target_pairs={{0,1},{1,2},{2,3},{3,4},{4,5},{5,6},{6,7},{7,0},{8,9},{9,10},{10,1... | collective-permute-start | bytes 491528 | tf_op jit(solution)/shard_map/ppermute | solution.py:20
  534.5 24.9 %collective-permute-start.67 = (bf16[32,2560]{1,0:T(8,128)(2,1)S(1)}, bf16[32,2560]{1,0:T(8,128)(2,1)S(1)}, u32[]{:S(2)}, u32[]{:S(2)}) collective-permute-start(bf16[32,2560]{1,0:T(8,128)(2,1)S(1)} %get-tuple-element.51), channel_id=1, source_target_pairs={{0,6},{1,7},{2,0},{3,1},{4,2},{5,3},{6,4},{7,5},{8,14},{9,15},{10,... | collective-permute-start | bytes 491528 | tf_op jit(solution)/shard_map/ppermute | solution.py:20
  537.2 21.6 %collective-permute-start.66 = (bf16[32,2560]{1,0:T(8,128)(2,1)S(1)}, bf16[32,2560]{1,0:T(8,128)(2,1)S(1)}, u32[]{:S(2)}, u32[]{:S(2)}) collective-permute-start(bf16[32,2560]{1,0:T(8,128)(2,1)S(1)} %get-tuple-element.51), channel_id=1, source_target_pairs={{0,5},{1,6},{2,7},{3,0},{4,1},{5,2},{6,3},{7,4},{8,13},{9,14},{10,... | collective-permute-start | bytes 491528 | tf_op jit(solution)/shard_map/ppermute | solution.py:20
  539.7 18.3 %collective-permute-start.65 = (bf16[32,2560]{1,0:T(8,128)(2,1)S(1)}, bf16[32,2560]{1,0:T(8,128)(2,1)S(1)}, u32[]{:S(2)}, u32[]{:S(2)}) collective-permute-start(bf16[32,2560]{1,0:T(8,128)(2,1)S(1)} %get-tuple-element.51), channel_id=1, source_target_pairs={{0,4},{1,5},{2,6},{3,7},{4,0},{5,1},{6,2},{7,3},{8,12},{9,13},{10,... | collective-permute-start | bytes 491528 | tf_op jit(solution)/shard_map/ppermute | solution.py:20
  539.8 17.6 %collective-permute-start.64 = (bf16[32,2560]{1,0:T(8,128)(2,1)S(1)}, bf16[32,2560]{1,0:T(8,128)(2,1)S(1)}, u32[]{:S(2)}, u32[]{:S(2)}) collective-permute-start(bf16[32,2560]{1,0:T(8,128)(2,1)S(1)} %get-tuple-element.51), channel_id=1, source_target_pairs={{0,3},{1,4},{2,5},{3,6},{4,7},{5,0},{6,1},{7,2},{8,11},{9,12},{10,... | collective-permute-start | bytes 491528 | tf_op jit(solution)/shard_map/ppermute | solution.py:20
  542.0 14.5 %collective-permute-start.63 = (bf16[32,2560]{1,0:T(8,128)(2,1)S(1)}, bf16[32,2560]{1,0:T(8,128)(2,1)S(1)}, u32[]{:S(2)}, u32[]{:S(2)}) collective-permute-start(bf16[32,2560]{1,0:T(8,128)(2,1)S(1)} %get-tuple-element.51), channel_id=1, source_target_pairs={{0,2},{1,3},{2,4},{3,5},{4,6},{5,7},{6,0},{7,1},{8,10},{9,11},{10,... | collective-permute-start | bytes 491528 | tf_op jit(solution)/shard_map/ppermute | solution.py:20
  572.9 7.8 %collective-permute-start.69 = (bf16[32,2560]{1,0:T(8,128)(2,1)S(1)}, bf16[32,2560]{1,0:T(8,128)(2,1)S(1)}, u32[]{:S(2)}, u32[]{:S(2)}) collective-permute-start(bf16[32,2560]{1,0:T(8,128)(2,1)S(1)} %get-tuple-element.53), channel_id=1, source_target_pairs={{0,1},{1,2},{2,3},{3,4},{4,5},{5,6},{6,7},{7,0},{8,9},{9,10},{10,1... | collective-permute-start | bytes 491528 | tf_op jit(solution)/shard_map/ppermute | solution.py:20
  572.9 24.9 %collective-permute-start.74 = (bf16[32,2560]{1,0:T(8,128)(2,1)S(1)}, bf16[32,2560]{1,0:T(8,128)(2,1)S(1)}, u32[]{:S(2)}, u32[]{:S(2)}) collective-permute-start(bf16[32,2560]{1,0:T(8,128)(2,1)S(1)} %get-tuple-element.53), channel_id=1, source_target_pairs={{0,6},{1,7},{2,0},{3,1},{4,2},{5,3},{6,4},{7,5},{8,14},{9,15},{10,... | collective-permute-start | bytes 491528 | tf_op jit(solution)/shard_map/ppermute | solution.py:20
  576.8 20.4 %collective-permute-start.73 = (bf16[32,2560]{1,0:T(8,128)(2,1)S(1)}, bf16[32,2560]{1,0:T(8,128)(2,1)S(1)}, u32[]{:S(2)}, u32[]{:S(2)}) collective-permute-start(bf16[32,2560]{1,0:T(8,128)(2,1)S(1)} %get-tuple-element.53), channel_id=1, source_target_pairs={{0,5},{1,6},{2,7},{3,0},{4,1},{5,2},{6,3},{7,4},{8,13},{9,14},{10,... | collective-permute-start | bytes 491528 | tf_op jit(solution)/shard_map/ppermute | solution.py:20
  578.1 18.4 %collective-permute-start.72 = (bf16[32,2560]{1,0:T(8,128)(2,1)S(1)}, bf16[32,2560]{1,0:T(8,128)(2,1)S(1)}, u32[]{:S(2)}, u32[]{:S(2)}) collective-permute-start(bf16[32,2560]{1,0:T(8,128)(2,1)S(1)} %get-tuple-element.53), channel_id=1, source_target_pairs={{0,4},{1,5},{2,6},{3,7},{4,0},{5,1},{6,2},{7,3},{8,12},{9,13},{10,... | collective-permute-start | bytes 491528 | tf_op jit(solution)/shard_map/ppermute | solution.py:20
  579.4 16.4 %collective-permute-start.71 = (bf16[32,2560]{1,0:T(8,128)(2,1)S(1)}, bf16[32,2560]{1,0:T(8,128)(2,1)S(1)}, u32[]{:S(2)}, u32[]{:S(2)}) collective-permute-start(bf16[32,2560]{1,0:T(8,128)(2,1)S(1)} %get-tuple-element.53), channel_id=1, source_target_pairs={{0,3},{1,4},{2,5},{3,6},{4,7},{5,0},{6,1},{7,2},{8,11},{9,12},{10,... | collective-permute-start | bytes 491528 | tf_op jit(solution)/shard_map/ppermute | solution.py:20
  580.7 12.1 %collective-permute-start.70 = (bf16[32,2560]{1,0:T(8,128)(2,1)S(1)}, bf16[32,2560]{1,0:T(8,128)(2,1)S(1)}, u32[]{:S(2)}, u32[]{:S(2)}) collective-permute-start(bf16[32,2560]{1,0:T(8,128)(2,1)S(1)} %get-tuple-element.53), channel_id=1, source_target_pairs={{0,2},{1,3},{2,4},{3,5},{4,6},{5,7},{6,0},{7,1},{8,10},{9,11},{10,... | collective-permute-start | bytes 491528 | tf_op jit(solution)/shard_map/ppermute | solution.py:20
  (41 other events, 490.7 us)

commit v3 on v1

--- a/solution.py
+++ b/solution.py
@@ -1,6 +1,8 @@
 import jax
 import jax.numpy as jnp
 from jax import lax
+from jax.experimental import pallas as pl
+from jax.experimental.pallas import tpu as pltpu
 from jax.sharding import PartitionSpec as P
 
 D = 2560
@@ -11,6 +13,47 @@
 DECODE_TOKENS = 2
 TAIL_LENGTH = 128
 
+
+PACK = 88
+
+def prefix_kernel(count_ref, q_ref, k_ref, v_ref, out_ref):
+    p = pl.program_id(0)
+    q = q_ref[0]
+    k = k_ref[0]
+    v = v_ref[0]
+    s = lax.dot_general(k, q, (((1,), (1,)), ((), ())), preferred_element_type=jnp.float32)
+    s = s * (HEAD_SIZE ** -0.5)
+    place = lax.broadcasted_iota(jnp.int32, s.shape, 0)
+    valid = place < count_ref[p]
+    s = jnp.where(valid, s, jnp.float32(-1e30))
+    top = jnp.max(s, axis=0, keepdims=True)
+    w = jnp.where(valid, jnp.exp(s - top), 0.0)
+    total = jnp.sum(w, axis=0, keepdims=True)
+    o = lax.dot_general(v, w.astype(jnp.bfloat16), (((0,), (0,)), ((), ())), preferred_element_type=jnp.float32)
+    out_ref[0, 0:HEAD_SIZE, :] = o
+    out_ref[0, HEAD_SIZE:HEAD_SIZE + 1, :] = top
+    out_ref[0, HEAD_SIZE + 1:HEAD_SIZE + 2, :] = total
+    out_ref[0, HEAD_SIZE + 2:PACK, :] = jnp.zeros((PACK - HEAD_SIZE - 2, s.shape[1]), jnp.float32)
+
+def prefix_partials(count, q, k, v):
+    P_, rows, _ = q.shape
+    L = k.shape[1]
+    return pl.pallas_call(
+        prefix_kernel,
+        grid_spec=pltpu.PrefetchScalarGridSpec(
+            num_scalar_prefetch=1,
+            grid=(P_,),
+            in_specs=[
+                pl.BlockSpec((1, rows, HEAD_SIZE), lambda p, c: (p, 0, 0)),
+                pl.BlockSpec((1, L, HEAD_SIZE), lambda p, c: (p, 0, 0)),
+                pl.BlockSpec((1, L, HEAD_SIZE), lambda p, c: (p, 0, 0)),
+            ],
+            out_specs=pl.BlockSpec((1, PACK, rows), lambda p, c: (p, 0, 0)),
+        ),
+        out_shape=jax.ShapeDtypeStruct((P_, PACK, rows), jnp.float32),
+        cost_estimate=pl.CostEstimate(flops=4 * P_ * rows * L * HEAD_SIZE, transcendentals=P_ * rows * L,
+                                      bytes_accessed=2 * P_ * L * HEAD_SIZE * 2 + P_ * rows * HEAD_SIZE * 2 + P_ * PACK * rows * 4),
+    )(count, q, k, v)
 
 def rms_scale(total_sq, width):
     return lax.rsqrt(total_sq / width + 1e-05)
@@ -106,36 +149,11 @@
     reduce_order = gather_order[::-1]
 
     gathered = gather_rows(queries, "req", req_count, gather_order)
-    query_all = gathered.reshape(
-        prompts, SAMPLE_COUNT, DECODE_TOKENS, kv_local, query_groups, HEAD_SIZE
-    )
-    prefix_key_block = shared_prefix_keys.reshape(prompts, piece_len, kv_local, HEAD_SIZE)
-    prefix_value_block = shared_prefix_values.reshape(prompts, piece_len, kv_local, HEAD_SIZE)
-    score_pre = (
-        jnp.einsum(
-            "psjkgh,plkh->pksjgl", query_all, prefix_key_block, preferred_element_type=jnp.float32
-        )
-        * inv_root
-    )
-    key_place = req_index * piece_len + jnp.arange(piece_len)
-    valid = (key_place[None, :] < prompt_prefix_length[:, None])[:, None, None, None, None, :]
-    piece_top = jnp.max(jnp.where(valid, score_pre, low), -1)
-    piece_w = jnp.where(valid, jnp.exp(score_pre - piece_top[..., None]), 0.0)
-    piece_sum = jnp.sum(piece_w, -1)
-    piece_out = jnp.einsum(
-        "pksjgl,plkh->phksjg",
-        piece_w.astype(jnp.bfloat16),
-        prefix_value_block,
-        preferred_element_type=jnp.float32,
-    )
-    packed = jnp.concatenate(
-        [
-            piece_out.reshape(prompts, HEAD_SIZE, rows),
-            piece_top.reshape(prompts, 1, rows),
-            piece_sum.reshape(prompts, 1, rows),
-        ],
-        axis=1,
-    )
+    query_all = gathered.reshape(prompts, rows, HEAD_SIZE)
+    prefix_key_block = shared_prefix_keys.reshape(prompts, piece_len, HEAD_SIZE * kv_local)
+    prefix_value_block = shared_prefix_values.reshape(prompts, piece_len, HEAD_SIZE * kv_local)
+    count = jnp.clip(prompt_prefix_length - req_index * piece_len, 0, piece_len).astype(jnp.int32)
+    packed = prefix_partials(count, query_all, prefix_key_block, prefix_value_block)
     own_part = reduce_partials(packed, "req", req_count, reduce_order)
 
     query_own = queries.reshape(SAMPLE_COUNT, DECODE_TOKENS, kv_local, query_groups, HEAD_SIZE)

time: 154 us -> 162 us (1.052)
  Pallas kernels: 0 us -> 25.3 us
  matrix products: 17.8 us -> 6.66 us
  other arithmetic: 16.7 us -> 9.34 us
  waiting for transfers between devices: 66.7 us -> 69.6 us
  local copies, waits for them, and re-layouts: 18.9 us -> 17.2 us
    pallas_call x0 -> x1, Pallas kernels: none -> 25.3 us  [prefix_partials(): pl.pallas_call(prefix_kernel, grid_spec=pltpu.PrefetchScalarGridSpec(num_...]
    unnamed x27 -> x28, local copies, waits for them, and re-layouts: 0.49 us -> 11.2 us
    dot_general x2 -> x0, matrix products: 9.35 us -> none  [the longest x1 5.96 us: on_device(): jnp.einsum('psjkgh,plkh->pksjgl', query_all, prefix_key_block, preferred_...]
    reduce_sum x1 -> x0, other arithmetic: 5.41 us -> none  [on_device(): piece_sum = jnp.sum(piece_w, -1)]
    concatenate x2 -> x0, local copies, waits for them, and re-layouts: 5.16 us -> none  [on_device(): jnp.concatenate([piece_out.reshape(prompts, HEAD_SIZE, rows), piece_top.r...]
    concatenate x1 -> x0, other arithmetic: 4 us -> none  [on_device(): jnp.concatenate([piece_out.reshape(prompts, HEAD_SIZE, rows), piece_top.r...]
    ppermute x16, waiting for transfers between devices: 66.7 us -> 69.6 us  [exchange(): return lax.ppermute(x, axis, perm=[(i, i ^ 1 << bit) for i in range(n)])]
    dot_general x1 -> x0, local copies, waits for them, and re-layouts: 2.15 us -> none  [on_device(): jnp.einsum('pksjgl,plkh->phksjg', piece_w.astype(jnp.bfloat16), prefix_va...]
  transfers between devices with their start and end apart: 16 -> 16, of which waited for: 16 -> 15; matrix products, arithmetic and copies ran while one was open for 3% -> 8% of each run, Pallas kernels for 0% -> 0%
where the time goes in v3:
time: 162 us; the launch traced here: 161 us
  waiting for transfers between devices  69.6 us (43%)
  starting transfers between devices  31.8 us (20%)
  Pallas kernels  25.3 us (16%)
  local copies, waits for them, and re-layouts  17.2 us (11%)
  other arithmetic  9.34 us (6%)
  matrix products  6.66 us (4%)
    ppermute x16, waiting for transfers between devices, exchange(): return lax.ppermute(x, axis, perm=[(i, i ^ 1 << bit) for i in range(n)])  69.6 us
    ppermute x16, starting transfers between devices, exchange(): return lax.ppermute(x, axis, perm=[(i, i ^ 1 << bit) for i in range(n)])  31.8 us
    pallas_call x1, Pallas kernels, prefix_partials(): pl.pallas_call(prefix_kernel, grid_spec=pltpu.PrefetchScalarGridSpec(num_...  25.3 us
    unnamed x28, local copies, waits for them, and re-layouts  11.2 us
  transfers between devices with their start and end apart: 16, of which 15 were waited for; matrix products, arithmetic and copies ran while one was open for 8% of the time, Pallas kernels for 0%

profile of v3, /device:TPU:6, one launch (start us, length us, event | category | flops | bytes accessed | tf_op | source)
XLA Modules:
  0.0 161.0 jit_solution(13309467875654493687)
XLA Ops:
  0.6 7.3 %collective-permute-start = (bf16[1,32,320]{2,1,0:T(8,128)(2,1)}, bf16[1,32,320]{2,1,0:T(8,128)(2,1)S(1)}, u32[]{:S(2)}, u32[]{:S(2)}) collective-permute-start(bf16[1,32,320]{2,1,0:T(8,128)(2,1)} %bitcast.185), channel_id=1, source_target_pairs={{0,128},{8,136},{16,144},{24,152},{32,160},{40,168},{48,176},{56,1... | collective-permute-start | bytes 61448 | tf_op jit(solution)/shard_map/ppermute | solution.py:63
  7.9 2.0 %collective-permute-done = bf16[1,32,320]{2,1,0:T(8,128)(2,1)S(1)} collective-permute-done((bf16[1,32,320]{2,1,0:T(8,128)(2,1)}, bf16[1,32,320]{2,1,0:T(8,128)(2,1)S(1)}, u32[]{:S(2)}, u32[]{:S(2)}) %collective-permute-start) | collective-permute-done | bytes 20512 | tf_op jit(solution)/shard_map/ppermute | solution.py:63
  9.9 0.7 select_bitcast_fusion.5
  10.7 1.5 collective-permute-start.1
  12.2 4.2 %collective-permute-done.1 = bf16[2,1,32,320]{3,2,0,1:T(8,128)(2,1)S(1)} collective-permute-done((bf16[2,1,32,320]{3,2,0,1:T(8,128)(2,1)S(1)}, bf16[2,1,32,320]{3,2,0,1:T(8,128)(2,1)S(1)}, u32[]{:S(2)}, u32[]{:S(2)}) %collective-permute-start.1) | collective-permute-done | bytes 40992 | tf_op jit(solution)/shard_map/ppermute | solution.py:63
  16.5 2.1 %collective-permute-start.2 = (bf16[2,2,1,32,320]{4,3,1,0,2:T(8,128)(2,1)S(1)}, bf16[2,2,1,32,320]{4,3,1,0,2:T(8,128)(2,1)S(1)}, u32[]{:S(2)}, u32[]{:S(2)}) collective-permute-start(bf16[2,2,1,32,320]{4,3,1,0,2:T(8,128)(2,1)S(1)} %fusion.24), channel_id=1, source_target_pairs={{0,64},{8,72},{16,80},{24,88},{32,96},{40,104},{48,112},{56,120},{... | collective-permute-start | bytes 245768 | tf_op jit(solution)/shard_map/ppermute | solution.py:63
  18.6 4.6 %collective-permute-done.2 = bf16[2,2,1,32,320]{4,3,1,0,2:T(8,128)(2,1)S(1)} collective-permute-done((bf16[2,2,1,32,320]{4,3,1,0,2:T(8,128)(2,1)S(1)}, bf16[2,2,1,32,320]{4,3,1,0,2:T(8,128)(2,1)S(1)}, u32[]{:S(2)}, u32[]{:S(2)}) %collective-permute-start.2) | collective-permute-done | bytes 81952 | tf_op jit(solution)/shard_map/ppermute | solution.py:63
  23.4 5.6 %collective-permute-done.3 = bf16[2,2,2,1,32,320]{5,4,2,1,0,3:T(8,128)(2,1)S(1)} collective-permute-done((bf16[2,2,2,1,32,320]{5,4,2,1,0,3:T(8,128)(2,1)S(1)}, bf16[2,2,2,1,32,320]{5,4,2,1,0,3:T(8,128)(2,1)S(1)}, u32[]{:S(2)}, u32[]{:S(2)}) %collective-permute-start.3) | collective-permute-done | bytes 163872 | tf_op jit(solution)/shard_map/ppermute | solution.py:63
  29.2 0.8 fusion.12
  30.0 5.5 %copy.56.k_ref = bf16[32,512,80]{2,1,0:T(8,128)(2,1)} copy(bf16[32,512,80]{1,2,0:T(8,128)(2,1)} %param.21) | data formatting | bytes 5242880 | tf_op args[4]
  35.6 5.6 %copy.57.v_ref = bf16[32,512,80]{2,1,0:T(8,128)(2,1)} copy(bf16[32,512,80]{1,2,0:T(8,128)(2,1)} %param.22) | data formatting | bytes 5242880 | tf_op args[5]
  41.2 0.5 subtract_clamp_fusion.count_ref
  42.2 1.6 %reshape_reshape.3.q_ref = bf16[32,128,80]{2,1,0:T(8,128)(2,1)} reshape(bf16[2,2,2,2,2,1,32,320]{7,6,4,3,2,1,0,5:T(8,128)(2,1)S(1)} %copy.55) | data formatting | bytes 1310720 | tf_op jit(solution)/shard_map/reshape;reshape | solution.py:152
  43.8 25.3 %shard_map.176 = f32[32,88,128]{2,1,0:T(8,128)} custom-call(s32[32]{0:T(128)} %subtract_clamp_fusion.count_ref, bf16[32,128,80]{2,1,0:T(8,128)(2,1)} %reshape_reshape.3.q_ref, bf16[32,512,80]{2,1,0:T(8,128)(2,1)} %copy.56.k_ref, bf16[32,512,80]{2,1,0:T(8,128)(2,1)} %copy.57.v_ref), custom_call_target="tpu_custom_call" | custom-call | flops 671088640 | bytes 7340032 | tf_op jit(solution)/shard_map/pallas_call | solution.py:41
  69.0 1.4 constant_dynamic-slice_fusion.2
  70.5 0.9 copy.67
  71.4 0.5 collective-permute-start.5
  72.5 1.5 collective-permute-done.5
  74.1 0.9 subtract_exponential_fusion.1
  75.0 0.9 subtract_exponential_fusion
  75.8 1.2 fusion.6
  77.0 0.9 fusion.18
  78.5 10.3 %collective-permute-done.6 = f32[2,2,2,88,128]{4,3,2,1,0:T(8,128)S(1)} collective-permute-done((f32[2,2,2,88,128]{4,3,2,1,0:T(8,128)S(1)}, f32[2,2,2,88,128]{4,3,2,1,0:T(8,128)S(1)}, u32[]{:S(2)}, u32[]{:S(2)}) %collective-permute-start.6) | collective-permute-done | bytes 360480 | tf_op jit(solution)/shard_map/ppermute | solution.py:63
  89.0 1.8 %collective-permute-start.7 = (f32[2,2,88,128]{3,2,1,0:T(8,128)S(1)}, f32[2,2,88,128]{3,2,1,0:T(8,128)S(1)}, u32[]{:S(2)}, u32[]{:S(2)}) collective-permute-start(f32[2,2,88,128]{3,2,1,0:T(8,128)S(1)} %get-tuple-element.22), channel_id=1, source_target_pairs={{0,64},{8,72},{16,80},{24,88},{32,96},{40,104},{48,112},{56,120},{... | collective-permute-start | bytes 540680 | tf_op jit(solution)/shard_map/ppermute | solution.py:63
  91.2 8.7 %collective-permute-done.7 = f32[2,2,88,128]{3,2,1,0:T(8,128)S(1)} collective-permute-done((f32[2,2,88,128]{3,2,1,0:T(8,128)S(1)}, f32[2,2,88,128]{3,2,1,0:T(8,128)S(1)}, u32[]{:S(2)}, u32[]{:S(2)}) %collective-permute-start.7) | collective-permute-done | bytes 180256 | tf_op jit(solution)/shard_map/ppermute | solution.py:63
  100.0 1.5 collective-permute-start.8
  101.7 4.4 %collective-permute-done.8 = f32[2,88,128]{2,1,0:T(8,128)S(1)} collective-permute-done((f32[2,88,128]{2,1,0:T(8,128)S(1)}, f32[2,88,128]{2,1,0:T(8,128)S(1)}, u32[]{:S(2)}, u32[]{:S(2)}) %collective-permute-start.8) | collective-permute-done | bytes 90144 | tf_op jit(solution)/shard_map/ppermute | solution.py:63
  106.2 6.0 %collective-permute-start.9 = (f32[88,128]{1,0:T(8,128)S(1)}, f32[88,128]{1,0:T(8,128)S(1)}, u32[]{:S(2)}, u32[]{:S(2)}) collective-permute-start(f32[88,128]{1,0:T(8,128)S(1)} %dynamic-slice_bitcast_fusion.6), channel_id=1, source_target_pairs={{0,128},{8,136},{16,144},{24,152},{32,160},{40,168},{48,176},{56,1... | collective-permute-start | bytes 135176 | tf_op jit(solution)/shard_map/ppermute | solution.py:63
  112.3 1.9 %collective-permute-done.9 = f32[88,128]{1,0:T(8,128)S(1)} collective-permute-done((f32[88,128]{1,0:T(8,128)S(1)}, f32[88,128]{1,0:T(8,128)S(1)}, u32[]{:S(2)}, u32[]{:S(2)}) %collective-permute-start.9) | collective-permute-done | bytes 45088 | tf_op jit(solution)/shard_map/ppermute | solution.py:63
  114.3 0.5 broadcast.81
  114.8 0.7 fusion.51
  116.3 1.9 %convolution_convert_fusion.1 = bf16[32,2560]{1,0:T(8,128)(2,1)S(1)} fusion(bf16[32,320]{1,0:T(8,128)(2,1)S(1)} %reshape_transpose.3, bf16[320,2560]{1,0:T(8,128)(2,1)} %param.27), kind=kOutput, calls=%fused_computation.1 | convolution fusion | flops 52510720 | bytes 1822720 | tf_op jit(solution)/shard_map/dot_general | solution.py:209
  118.3 0.9 collective-permute-start.10
  119.2 4.5 %collective-permute-done.10 = bf16[32,2560]{1,0:T(8,128)(2,1)S(1)} collective-permute-done((bf16[32,2560]{1,0:T(8,128)(2,1)S(1)}, bf16[32,2560]{1,0:T(8,128)(2,1)S(1)}, u32[]{:S(2)}, u32[]{:S(2)}) %collective-permute-start.10) | collective-permute-done | bytes 163872 | tf_op jit(solution)/shard_map/ppermute | solution.py:63
  123.7 3.3 %collective-permute-start.11 = (bf16[32,2560]{1,0:T(8,128)(2,1)S(1)}, bf16[32,2560]{1,0:T(8,128)(2,1)S(1)}, u32[]{:S(2)}, u32[]{:S(2)}) collective-permute-start(bf16[32,2560]{1,0:T(8,128)(2,1)S(1)} %add_convert_fusion.5), channel_id=1, source_target_pairs={{0,2},{1,3},{2,0},{3,1},{4,6},{5,7},{6,4},{7,5},{8,10},{9,11},{10,... | collective-permute-start | bytes 491528 | tf_op jit(solution)/shard_map/ppermute | solution.py:63
  127.0 4.4 %collective-permute-done.11 = bf16[32,2560]{1,0:T(8,128)(2,1)S(1)} collective-permute-done((bf16[32,2560]{1,0:T(8,128)(2,1)S(1)}, bf16[32,2560]{1,0:T(8,128)(2,1)S(1)}, u32[]{:S(2)}, u32[]{:S(2)}) %collective-permute-start.11) | collective-permute-done | bytes 163872 | tf_op jit(solution)/shard_map/ppermute | solution.py:63
  131.4 1.2 collective-permute-start.12
  132.6 4.4 %collective-permute-done.12 = bf16[32,2560]{1,0:T(8,128)(2,1)S(1)} collective-permute-done((bf16[32,2560]{1,0:T(8,128)(2,1)S(1)}, bf16[32,2560]{1,0:T(8,128)(2,1)S(1)}, u32[]{:S(2)}, u32[]{:S(2)}) %collective-permute-start.12) | collective-permute-done | bytes 163872 | tf_op jit(solution)/shard_map/ppermute | solution.py:63
  137.3 0.5 fusion.52
  137.9 2.8 %convolution_convert_fusion = bf16[32,2560]{1,0:T(8,128)(2,1)S(1)} fusion(bf16[512,2560]{1,0:T(8,128)(2,1)S(1)} %copy-done, bf16[32,2560]{1,0:T(8,128)(2,1)S(1)} %multiply_convert_fusion, bf16[2560,512]{1,0:T(8,128)(2,1)} %param.29, f32[32,512]{1,0:T(8,128)S(1)} %fusion.52), kind=kOutput, calls=%fused_computation | convolution fusion | flops 167952384 | bytes 5636096 | tf_op jit(solution)/shard_map/dot_general | solution.py:223
  140.7 0.9 collective-permute-start.13
  141.7 4.5 %collective-permute-done.13 = bf16[32,2560]{1,0:T(8,128)(2,1)S(1)} collective-permute-done((bf16[32,2560]{1,0:T(8,128)(2,1)S(1)}, bf16[32,2560]{1,0:T(8,128)(2,1)S(1)}, u32[]{:S(2)}, u32[]{:S(2)}) %collective-permute-start.13) | collective-permute-done | bytes 163872 | tf_op jit(solution)/shard_map/ppermute | solution.py:63
  146.2 4.1 %collective-permute-start.14 = (bf16[32,2560]{1,0:T(8,128)(2,1)S(1)}, bf16[32,2560]{1,0:T(8,128)(2,1)S(1)}, u32[]{:S(2)}, u32[]{:S(2)}) collective-permute-start(bf16[32,2560]{1,0:T(8,128)(2,1)S(1)} %add_convert_fusion.2), channel_id=1, source_target_pairs={{0,2},{1,3},{2,0},{3,1},{4,6},{5,7},{6,4},{7,5},{8,10},{9,11},{10,... | collective-permute-start | bytes 491528 | tf_op jit(solution)/shard_map/ppermute | solution.py:63
  150.2 3.6 %collective-permute-done.14 = bf16[32,2560]{1,0:T(8,128)(2,1)S(1)} collective-permute-done((bf16[32,2560]{1,0:T(8,128)(2,1)S(1)}, bf16[32,2560]{1,0:T(8,128)(2,1)S(1)}, u32[]{:S(2)}, u32[]{:S(2)}) %collective-permute-start.14) | collective-permute-done | bytes 163872 | tf_op jit(solution)/shard_map/ppermute | solution.py:63
  153.9 0.5 collective-permute-start.15
  154.3 4.9 %collective-permute-done.15 = bf16[32,2560]{1,0:T(8,128)(2,1)S(1)} collective-permute-done((bf16[32,2560]{1,0:T(8,128)(2,1)S(1)}, bf16[32,2560]{1,0:T(8,128)(2,1)S(1)}, u32[]{:S(2)}, u32[]{:S(2)}) %collective-permute-start.15) | collective-permute-done | bytes 163872 | tf_op jit(solution)/shard_map/ppermute | solution.py:63
  159.5 0.7 dynamic-slice_convert_fusion
  160.2 0.7 multiply_reduce_fusion
  (92 shorter events, 4.6 us)
Async XLA Ops:
  0.6 137.2 %copy-start = (bf16[512,2560]{1,0:T(8,128)(2,1)S(1)}, bf16[512,2560]{1,0:T(8,128)(2,1)}, u32[]{:S(2)}) copy-start(bf16[512,2560]{1,0:T(8,128)(2,1)} %param.30) | copy-start | bytes 7864324
  0.6 9.3 %collective-permute-start = (bf16[1,32,320]{2,1,0:T(8,128)(2,1)}, bf16[1,32,320]{2,1,0:T(8,128)(2,1)S(1)}, u32[]{:S(2)}, u32[]{:S(2)}) collective-permute-start(bf16[1,32,320]{2,1,0:T(8,128)(2,1)} %bitcast.185), channel_id=1, source_target_pairs={{0,128},{8,136},{16,144},{24,152},{32,160},{40,168},{48,176},{56,1... | collective-permute-start | bytes 61448 | tf_op jit(solution)/shard_map/ppermute | solution.py:63
  10.7 5.7 %collective-permute-start.1 = (bf16[2,1,32,320]{3,2,0,1:T(8,128)(2,1)S(1)}, bf16[2,1,32,320]{3,2,0,1:T(8,128)(2,1)S(1)}, u32[]{:S(2)}, u32[]{:S(2)}) collective-permute-start(bf16[2,1,32,320]{3,2,0,1:T(8,128)(2,1)S(1)} %fusion.36), channel_id=1, source_target_pairs={{0,16},{8,24},{16,0},{24,8},{32,48},{40,56},{48,32},{56,40},{64,80... | collective-permute-start | bytes 122888 | tf_op jit(solution)/shard_map/ppermute | solution.py:63
  16.5 6.8 %collective-permute-start.2 = (bf16[2,2,1,32,320]{4,3,1,0,2:T(8,128)(2,1)S(1)}, bf16[2,2,1,32,320]{4,3,1,0,2:T(8,128)(2,1)S(1)}, u32[]{:S(2)}, u32[]{:S(2)}) collective-permute-start(bf16[2,2,1,32,320]{4,3,1,0,2:T(8,128)(2,1)S(1)} %fusion.24), channel_id=1, source_target_pairs={{0,64},{8,72},{16,80},{24,88},{32,96},{40,104},{48,112},{56,120},{... | collective-permute-start | bytes 245768 | tf_op jit(solution)/shard_map/ppermute | solution.py:63
  23.3 5.8 %collective-permute-start.3 = (bf16[2,2,2,1,32,320]{5,4,2,1,0,3:T(8,128)(2,1)S(1)}, bf16[2,2,2,1,32,320]{5,4,2,1,0,3:T(8,128)(2,1)S(1)}, u32[]{:S(2)}, u32[]{:S(2)}) collective-permute-start(bf16[2,2,2,1,32,320]{5,4,2,1,0,3:T(8,128)(2,1)S(1)} %fusion.15), channel_id=1, source_target_pairs={{0,32},{8,40},{16,48},{24,56},{32,0},{40,8},{48,16},{56,24},{64,96... | collective-permute-start | bytes 491528 | tf_op jit(solution)/shard_map/ppermute | solution.py:63
  30.0 11.6 %collective-permute-start.4 = (bf16[2,2,2,2,1,32,320]{6,5,3,2,1,0,4:T(8,128)(2,1)}, bf16[2,2,2,2,1,32,320]{6,5,3,2,1,0,4:T(8,128)(2,1)S(1)}, u32[]{:S(2)}, u32[]{:S(2)}) collective-permute-start(bf16[2,2,2,2,1,32,320]{6,5,3,2,1,0,4:T(8,128)(2,1)} %fusion.12), channel_id=1, source_target_pairs={{0,8},{8,0},{16,24},{24,16},{32,40},{40,32},{48,56},{56,48},{64,72... | collective-permute-start | bytes 983048 | tf_op jit(solution)/shard_map/ppermute | solution.py:63
  35.6 5.6 %copy-start.12 = (s32[32]{0:T(128)S(1)}, s32[32]{0:T(128)}, u32[]{:S(2)}) copy-start(s32[32]{0:T(128)} %param.25) | copy-start | bytes 388
  69.0 2.9 %copy-start.4 = (bf16[32,320]{1,0:T(8,128)(2,1)S(1)}, bf16[32,320]{1,0:T(8,128)(2,1)}, u32[]{:S(2)}) copy-start(bf16[32,320]{1,0:T(8,128)(2,1)} %param.18) | copy-start | bytes 61444
  69.0 3.0 %copy-start.10 = (bf16[32,80]{1,0:T(8,128)(2,1)S(1)}, bf16[32,80]{1,0:T(8,128)(2,1)}, u32[]{:S(2)}) copy-start(bf16[32,80]{1,0:T(8,128)(2,1)} %param.19) | copy-start | bytes 15364
  71.4 2.7 %collective-permute-start.5 = (f32[2,2,2,2,88,128]{5,4,3,1,0,2:T(8,128)}, f32[2,2,2,2,88,128]{5,4,3,1,0,2:T(8,128)}, u32[]{:S(2)}, u32[]{:S(2)}) collective-permute-start(f32[2,2,2,2,88,128]{5,4,3,1,0,2:T(8,128)} %bitcast.170), channel_id=1, source_target_pairs={{0,8},{8,0},{16,24},{24,16},{32,40},{40,32},{48,56},{56,48},{64,72... | collective-permute-start | bytes 2162696 | tf_op jit(solution)/shard_map/ppermute | solution.py:63
  72.5 5.6 %copy-start.8 = (s32[1,16]{1,0:T(1,128)S(1)}, s32[1,16]{1,0:T(1,128)}, u32[]{:S(2)}) copy-start(s32[1,16]{1,0:T(1,128)} %param.26) | copy-start | bytes 196
  72.5 5.7 %copy-start.3 = (bf16[1,16,128,80]{2,3,1,0:T(8,128)(2,1)S(1)}, bf16[1,16,128,80]{2,3,1,0:T(8,128)(2,1)}, u32[]{:S(2)}) copy-start(bf16[1,16,128,80]{2,3,1,0:T(8,128)(2,1)} %param.23) | copy-start | bytes 983044
  77.9 12.9 %copy-start.9 = (bf16[1,16,128,80]{2,3,1,0:T(8,128)(2,1)S(1)}, bf16[1,16,128,80]{2,3,1,0:T(8,128)(2,1)}, u32[]{:S(2)}) copy-start(bf16[1,16,128,80]{2,3,1,0:T(8,128)(2,1)} %param.24) | copy-start | bytes 983044
  78.0 10.8 %collective-permute-start.6 = (f32[2,2,2,88,128]{4,3,2,1,0:T(8,128)S(1)}, f32[2,2,2,88,128]{4,3,2,1,0:T(8,128)S(1)}, u32[]{:S(2)}, u32[]{:S(2)}) collective-permute-start(f32[2,2,2,88,128]{4,3,2,1,0:T(8,128)S(1)} %get-tuple-element.20), channel_id=1, source_target_pairs={{0,32},{8,40},{16,48},{24,56},{32,0},{40,8},{48,16},{56,24},{64,96... | collective-permute-start | bytes 1081352 | tf_op jit(solution)/shard_map/ppermute | solution.py:63
  88.9 27.0 %copy-start.11 = (bf16[32,80]{1,0:T(8,128)(2,1)S(1)}, bf16[32,80]{1,0:T(8,128)(2,1)}, u32[]{:S(2)}) copy-start(bf16[32,80]{1,0:T(8,128)(2,1)} %param.20) | copy-start | bytes 15364
  89.0 10.9 %collective-permute-start.7 = (f32[2,2,88,128]{3,2,1,0:T(8,128)S(1)}, f32[2,2,88,128]{3,2,1,0:T(8,128)S(1)}, u32[]{:S(2)}, u32[]{:S(2)}) collective-permute-start(f32[2,2,88,128]{3,2,1,0:T(8,128)S(1)} %get-tuple-element.22), channel_id=1, source_target_pairs={{0,64},{8,72},{16,80},{24,88},{32,96},{40,104},{48,112},{56,120},{... | collective-permute-start | bytes 540680 | tf_op jit(solution)/shard_map/ppermute | solution.py:63
  100.0 6.1 %collective-permute-start.8 = (f32[2,88,128]{2,1,0:T(8,128)S(1)}, f32[2,88,128]{2,1,0:T(8,128)S(1)}, u32[]{:S(2)}, u32[]{:S(2)}) collective-permute-start(f32[2,88,128]{2,1,0:T(8,128)S(1)} %get-tuple-element.24), channel_id=1, source_target_pairs={{0,16},{8,24},{16,0},{24,8},{32,48},{40,56},{48,32},{56,40},{64,80... | collective-permute-start | bytes 270344 | tf_op jit(solution)/shard_map/ppermute | solution.py:63
  106.2 8.1 %collective-permute-start.9 = (f32[88,128]{1,0:T(8,128)S(1)}, f32[88,128]{1,0:T(8,128)S(1)}, u32[]{:S(2)}, u32[]{:S(2)}) collective-permute-start(f32[88,128]{1,0:T(8,128)S(1)} %dynamic-slice_bitcast_fusion.6), channel_id=1, source_target_pairs={{0,128},{8,136},{16,144},{24,152},{32,160},{40,168},{48,176},{56,1... | collective-permute-start | bytes 135176 | tf_op jit(solution)/shard_map/ppermute | solution.py:63
  115.9 21.1 %copy-start.2 = (bf16[32,2560]{1,0:T(8,128)(2,1)S(1)}, bf16[32,2560]{1,0:T(8,128)(2,1)}, u32[]{:S(2)}) copy-start(bf16[32,2560]{1,0:T(8,128)(2,1)} %param.17) | copy-start | bytes 491524
  115.9 21.3 %copy-start.7 = (f32[2560]{0:T(1024)S(1)}, f32[2560]{0:T(1024)}, u32[]{:S(2)}) copy-start(f32[2560]{0:T(1024)} %param.31) | copy-start | bytes 30724
  116.3 21.0 %copy-start.1 = (bf16[2560,512]{1,0:T(8,128)(2,1)S(1)}, bf16[2560,512]{1,0:T(8,128)(2,1)}, u32[]{:S(2)}) copy-start(bf16[2560,512]{1,0:T(8,128)(2,1)} %param.28) | copy-start | bytes 7864324
  118.3 5.4 %collective-permute-start.10 = (bf16[32,2560]{1,0:T(8,128)(2,1)S(1)}, bf16[32,2560]{1,0:T(8,128)(2,1)S(1)}, u32[]{:S(2)}, u32[]{:S(2)}) collective-permute-start(bf16[32,2560]{1,0:T(8,128)(2,1)S(1)} %convolution_convert_fusion.1), channel_id=1, source_target_pairs={{0,4},{1,5},{2,6},{3,7},{4,0},{5,1},{6,2},{7,3},{8,12},{9,13},{10,... | collective-permute-start | bytes 491528 | tf_op jit(solution)/shard_map/ppermute | solution.py:63
  123.7 7.6 %collective-permute-start.11 = (bf16[32,2560]{1,0:T(8,128)(2,1)S(1)}, bf16[32,2560]{1,0:T(8,128)(2,1)S(1)}, u32[]{:S(2)}, u32[]{:S(2)}) collective-permute-start(bf16[32,2560]{1,0:T(8,128)(2,1)S(1)} %add_convert_fusion.5), channel_id=1, source_target_pairs={{0,2},{1,3},{2,0},{3,1},{4,6},{5,7},{6,4},{7,5},{8,10},{9,11},{10,... | collective-permute-start | bytes 491528 | tf_op jit(solution)/shard_map/ppermute | solution.py:63
  131.4 5.6 %collective-permute-start.12 = (bf16[32,2560]{1,0:T(8,128)(2,1)S(1)}, bf16[32,2560]{1,0:T(8,128)(2,1)S(1)}, u32[]{:S(2)}, u32[]{:S(2)}) collective-permute-start(bf16[32,2560]{1,0:T(8,128)(2,1)S(1)} %add_convert_fusion.4), channel_id=1, source_target_pairs={{0,1},{1,0},{2,3},{3,2},{4,5},{5,4},{6,7},{7,6},{8,9},{9,8},{10,11... | collective-permute-start | bytes 491528 | tf_op jit(solution)/shard_map/ppermute | solution.py:63
  137.9 22.3 %copy-start.5 = (f32[2560]{0:T(1024)S(1)}, f32[2560]{0:T(1024)}, u32[]{:S(2)}) copy-start(f32[2560]{0:T(1024)} %param.33) | copy-start | bytes 30724
  137.9 22.3 %copy-start.6 = (f32[2560]{0:T(1024)S(1)}, f32[2560]{0:T(1024)}, u32[]{:S(2)}) copy-start(f32[2560]{0:T(1024)} %param.32) | copy-start | bytes 30724
  140.7 5.4 %collective-permute-start.13 = (bf16[32,2560]{1,0:T(8,128)(2,1)S(1)}, bf16[32,2560]{1,0:T(8,128)(2,1)S(1)}, u32[]{:S(2)}, u32[]{:S(2)}) collective-permute-start(bf16[32,2560]{1,0:T(8,128)(2,1)S(1)} %convolution_convert_fusion), channel_id=1, source_target_pairs={{0,4},{1,5},{2,6},{3,7},{4,0},{5,1},{6,2},{7,3},{8,12},{9,13},{10,... | collective-permute-start | bytes 491528 | tf_op jit(solution)/shard_map/ppermute | solution.py:63
  146.2 7.7 %collective-permute-start.14 = (bf16[32,2560]{1,0:T(8,128)(2,1)S(1)}, bf16[32,2560]{1,0:T(8,128)(2,1)S(1)}, u32[]{:S(2)}, u32[]{:S(2)}) collective-permute-start(bf16[32,2560]{1,0:T(8,128)(2,1)S(1)} %add_convert_fusion.2), channel_id=1, source_target_pairs={{0,2},{1,3},{2,0},{3,1},{4,6},{5,7},{6,4},{7,5},{8,10},{9,11},{10,... | collective-permute-start | bytes 491528 | tf_op jit(solution)/shard_map/ppermute | solution.py:63
  153.9 5.4 %collective-permute-start.15 = (bf16[32,2560]{1,0:T(8,128)(2,1)S(1)}, bf16[32,2560]{1,0:T(8,128)(2,1)S(1)}, u32[]{:S(2)}, u32[]{:S(2)}) collective-permute-start(bf16[32,2560]{1,0:T(8,128)(2,1)S(1)} %add_convert_fusion.1), channel_id=1, source_target_pairs={{0,1},{1,0},{2,3},{3,2},{4,5},{5,4},{6,7},{7,6},{8,9},{9,8},{10,11... | collective-permute-start | bytes 491528 | tf_op jit(solution)/shard_map/ppermute | solution.py:63

commit v4 on v3

--- a/solution.py
+++ b/solution.py
@@ -15,45 +15,51 @@
 
 
 PACK = 88
-
-def prefix_kernel(count_ref, q_ref, k_ref, v_ref, out_ref):
-    p = pl.program_id(0)
-    q = q_ref[0]
-    k = k_ref[0]
-    v = v_ref[0]
-    s = lax.dot_general(k, q, (((1,), (1,)), ((), ())), preferred_element_type=jnp.float32)
-    s = s * (HEAD_SIZE ** -0.5)
-    place = lax.broadcasted_iota(jnp.int32, s.shape, 0)
-    valid = place < count_ref[p]
-    s = jnp.where(valid, s, jnp.float32(-1e30))
-    top = jnp.max(s, axis=0, keepdims=True)
-    w = jnp.where(valid, jnp.exp(s - top), 0.0)
-    total = jnp.sum(w, axis=0, keepdims=True)
-    o = lax.dot_general(v, w.astype(jnp.bfloat16), (((0,), (0,)), ((), ())), preferred_element_type=jnp.float32)
-    out_ref[0, 0:HEAD_SIZE, :] = o
-    out_ref[0, HEAD_SIZE:HEAD_SIZE + 1, :] = top
-    out_ref[0, HEAD_SIZE + 1:HEAD_SIZE + 2, :] = total
-    out_ref[0, HEAD_SIZE + 2:PACK, :] = jnp.zeros((PACK - HEAD_SIZE - 2, s.shape[1]), jnp.float32)
-
-def prefix_partials(count, q, k, v):
+BLOCK_PROMPTS = 4
+
+
+def prefix_kernel(count_ref, q_ref, kt_ref, vt_ref, out_ref):
+    step = pl.program_id(0)
+    for i in range(q_ref.shape[0]):
+        q = q_ref[i]
+        kt = kt_ref[i]
+        vt = vt_ref[i]
+        s = jnp.dot(q, kt, preferred_element_type=jnp.float32) * (HEAD_SIZE ** -0.5)
+        place = lax.broadcasted_iota(jnp.int32, s.shape, 1)
+        valid = place < count_ref[step * q_ref.shape[0] + i]
+        s = jnp.where(valid, s, jnp.float32(-1e30))
+        top = jnp.max(s, axis=1, keepdims=True)
+        w = jnp.where(valid, jnp.exp(s - top), 0.0)
+        total = jnp.sum(w, axis=1, keepdims=True)
+        o = lax.dot_general(vt, w.astype(jnp.bfloat16), (((1,), (1,)), ((), ())),
+                            preferred_element_type=jnp.float32)
+        lane = lax.broadcasted_iota(jnp.int32, (s.shape[0], 128), 1)
+        stats = jnp.where(lane == 0, top, jnp.where(lane == 1, total, 0.0))
+        out_ref[i, 0:HEAD_SIZE, :] = o
+        out_ref[i, HEAD_SIZE:PACK, :] = jnp.transpose(stats)[0:PACK - HEAD_SIZE, :]
+
+
+def prefix_partials(count, q, kt, vt):
     P_, rows, _ = q.shape
-    L = k.shape[1]
+    L = kt.shape[2]
+    bp = BLOCK_PROMPTS
     return pl.pallas_call(
         prefix_kernel,
         grid_spec=pltpu.PrefetchScalarGridSpec(
             num_scalar_prefetch=1,
-            grid=(P_,),
+            grid=(P_ // bp,),
             in_specs=[
-                pl.BlockSpec((1, rows, HEAD_SIZE), lambda p, c: (p, 0, 0)),
-                pl.BlockSpec((1, L, HEAD_SIZE), lambda p, c: (p, 0, 0)),
-                pl.BlockSpec((1, L, HEAD_SIZE), lambda p, c: (p, 0, 0)),
+                pl.BlockSpec((bp, rows, HEAD_SIZE), lambda p, c: (p, 0, 0)),
+                pl.BlockSpec((bp, HEAD_SIZE, L), lambda p, c: (p, 0, 0)),
+                pl.BlockSpec((bp, HEAD_SIZE, L), lambda p, c: (p, 0, 0)),
             ],
-            out_specs=pl.BlockSpec((1, PACK, rows), lambda p, c: (p, 0, 0)),
+            out_specs=pl.BlockSpec((bp, PACK, rows), lambda p, c: (p, 0, 0)),
         ),
         out_shape=jax.ShapeDtypeStruct((P_, PACK, rows), jnp.float32),
         cost_estimate=pl.CostEstimate(flops=4 * P_ * rows * L * HEAD_SIZE, transcendentals=P_ * rows * L,
                                       bytes_accessed=2 * P_ * L * HEAD_SIZE * 2 + P_ * rows * HEAD_SIZE * 2 + P_ * PACK * rows * 4),
-    )(count, q, k, v)
+    )(count, q, kt, vt)
+
 
 def rms_scale(total_sq, width):
     return lax.rsqrt(total_sq / width + 1e-05)
@@ -150,8 +156,8 @@
 
     gathered = gather_rows(queries, "req", req_count, gather_order)
     query_all = gathered.reshape(prompts, rows, HEAD_SIZE)
-    prefix_key_block = shared_prefix_keys.reshape(prompts, piece_len, HEAD_SIZE * kv_local)
-    prefix_value_block = shared_prefix_values.reshape(prompts, piece_len, HEAD_SIZE * kv_local)
+    prefix_key_block = jnp.swapaxes(shared_prefix_keys.reshape(prompts, piece_len, HEAD_SIZE * kv_local), 1, 2)
+    prefix_value_block = jnp.swapaxes(shared_prefix_values.reshape(prompts, piece_len, HEAD_SIZE * kv_local), 1, 2)
     count = jnp.clip(prompt_prefix_length - req_index * piece_len, 0, piece_len).astype(jnp.int32)
     packed = prefix_partials(count, query_all, prefix_key_block, prefix_value_block)
     own_part = reduce_partials(packed, "req", req_count, reduce_order)

time: 162 us -> 137 us (0.85)
  Pallas kernels: 25.3 us -> 10.8 us
  local copies, waits for them, and re-layouts: 17.2 us -> 6.1 us
    pallas_call x1, Pallas kernels: 25.3 us -> 10.8 us  [prefix_partials(): pl.pallas_call(prefix_kernel, grid_spec=pltpu.PrefetchScalarGridSpec(num_...]
    unnamed x28 -> x26, local copies, waits for them, and re-layouts: 11.2 us -> 0.08 us
  transfers between devices with their start and end apart: 16 -> 16, of which waited for: 15 -> 16; matrix products, arithmetic and copies ran while one was open for 8% -> 2% of each run, Pallas kernels for 0% -> 0%
where the time goes in v4:
time: 137 us; the launch traced here: 136 us
  waiting for transfers between devices  69.7 us (51%)
  starting transfers between devices  32.2 us (24%)
  Pallas kernels  10.8 us (8%)
  other arithmetic  9.33 us (7%)
  matrix products  6.66 us (5%)
  local copies, waits for them, and re-layouts  6.1 us (4%)
    ppermute x16, waiting for transfers between devices, exchange(): return lax.ppermute(x, axis, perm=[(i, i ^ 1 << bit) for i in range(n)])  69.7 us
    ppermute x16, starting transfers between devices, exchange(): return lax.ppermute(x, axis, perm=[(i, i ^ 1 << bit) for i in range(n)])  32.2 us
    pallas_call x1, Pallas kernels, prefix_partials(): pl.pallas_call(prefix_kernel, grid_spec=pltpu.PrefetchScalarGridSpec(num_...  10.8 us
    dot_general x1, matrix products, on_device(): jnp.dot(hidden, down_weight, preferred_element_type=jnp.float32)  2.83 us
  transfers between devices with their start and end apart: 16, of which 16 were waited for; matrix products, arithmetic and copies ran while one was open for 2% of the time, Pallas kernels for 0%

profile of v4, /device:TPU:6, one launch (start us, length us, event | category | flops | bytes accessed | tf_op | source)
XLA Modules:
  0.0 135.9 jit_solution(13231940543147896849)
XLA Ops:
  0.7 7.3 %collective-permute-start = (bf16[1,32,320]{2,1,0:T(8,128)(2,1)}, bf16[1,32,320]{2,1,0:T(8,128)(2,1)S(1)}, u32[]{:S(2)}, u32[]{:S(2)}) collective-permute-start(bf16[1,32,320]{2,1,0:T(8,128)(2,1)} %bitcast.189), channel_id=1, source_target_pairs={{0,128},{8,136},{16,144},{24,152},{32,160},{40,168},{48,176},{56,1... | collective-permute-start | bytes 61448 | tf_op jit(solution)/shard_map/ppermute | solution.py:69
  7.9 2.0 %collective-permute-done = bf16[1,32,320]{2,1,0:T(8,128)(2,1)S(1)} collective-permute-done((bf16[1,32,320]{2,1,0:T(8,128)(2,1)}, bf16[1,32,320]{2,1,0:T(8,128)(2,1)S(1)}, u32[]{:S(2)}, u32[]{:S(2)}) %collective-permute-start) | collective-permute-done | bytes 20512 | tf_op jit(solution)/shard_map/ppermute | solution.py:69
  10.0 0.7 select_bitcast_fusion.5
  10.7 1.5 %collective-permute-start.1 = (bf16[2,1,32,320]{3,2,0,1:T(8,128)(2,1)S(1)}, bf16[2,1,32,320]{3,2,0,1:T(8,128)(2,1)S(1)}, u32[]{:S(2)}, u32[]{:S(2)}) collective-permute-start(bf16[2,1,32,320]{3,2,0,1:T(8,128)(2,1)S(1)} %fusion.36), channel_id=1, source_target_pairs={{0,16},{8,24},{16,0},{24,8},{32,48},{40,56},{48,32},{56,40},{64,80... | collective-permute-start | bytes 122888 | tf_op jit(solution)/shard_map/ppermute | solution.py:69
  12.2 4.2 %collective-permute-done.1 = bf16[2,1,32,320]{3,2,0,1:T(8,128)(2,1)S(1)} collective-permute-done((bf16[2,1,32,320]{3,2,0,1:T(8,128)(2,1)S(1)}, bf16[2,1,32,320]{3,2,0,1:T(8,128)(2,1)S(1)}, u32[]{:S(2)}, u32[]{:S(2)}) %collective-permute-start.1) | collective-permute-done | bytes 40992 | tf_op jit(solution)/shard_map/ppermute | solution.py:69
  16.5 2.1 %collective-permute-start.2 = (bf16[2,2,1,32,320]{4,3,1,0,2:T(8,128)(2,1)S(1)}, bf16[2,2,1,32,320]{4,3,1,0,2:T(8,128)(2,1)S(1)}, u32[]{:S(2)}, u32[]{:S(2)}) collective-permute-start(bf16[2,2,1,32,320]{4,3,1,0,2:T(8,128)(2,1)S(1)} %fusion.24), channel_id=1, source_target_pairs={{0,64},{8,72},{16,80},{24,88},{32,96},{40,104},{48,112},{56,120},{... | collective-permute-start | bytes 245768 | tf_op jit(solution)/shard_map/ppermute | solution.py:69
  18.6 4.6 %collective-permute-done.2 = bf16[2,2,1,32,320]{4,3,1,0,2:T(8,128)(2,1)S(1)} collective-permute-done((bf16[2,2,1,32,320]{4,3,1,0,2:T(8,128)(2,1)S(1)}, bf16[2,2,1,32,320]{4,3,1,0,2:T(8,128)(2,1)S(1)}, u32[]{:S(2)}, u32[]{:S(2)}) %collective-permute-start.2) | collective-permute-done | bytes 81952 | tf_op jit(solution)/shard_map/ppermute | solution.py:69
  23.5 5.6 %collective-permute-done.3 = bf16[2,2,2,1,32,320]{5,4,2,1,0,3:T(8,128)(2,1)S(1)} collective-permute-done((bf16[2,2,2,1,32,320]{5,4,2,1,0,3:T(8,128)(2,1)S(1)}, bf16[2,2,2,1,32,320]{5,4,2,1,0,3:T(8,128)(2,1)S(1)}, u32[]{:S(2)}, u32[]{:S(2)}) %collective-permute-start.3) | collective-permute-done | bytes 163872 | tf_op jit(solution)/shard_map/ppermute | solution.py:69
  29.2 0.8 fusion.12
  30.0 0.5 subtract_clamp_fusion.count_ref
  30.6 1.4 %collective-permute-done.4 = bf16[2,2,2,2,1,32,320]{6,5,3,2,1,0,4:T(8,128)(2,1)S(1)} collective-permute-done((bf16[2,2,2,2,1,32,320]{6,5,3,2,1,0,4:T(8,128)(2,1)}, bf16[2,2,2,2,1,32,320]{6,5,3,2,1,0,4:T(8,128)(2,1)S(1)}, u32[]{:S(2)}, u32[]{:S(2)}) %collective-permute-start.4) | collective-permute-done | bytes 327712 | tf_op jit(solution)/shard_map/ppermute | solution.py:69
  32.4 1.6 %reshape_reshape.3.q_ref = bf16[32,128,80]{2,1,0:T(8,128)(2,1)} reshape(bf16[2,2,2,2,2,1,32,320]{7,6,4,3,2,1,0,5:T(8,128)(2,1)S(1)} %copy.53) | data formatting | bytes 1310720 | tf_op jit(solution)/shard_map/reshape;reshape | solution.py:158
  34.0 10.8 %shard_map.176 = f32[32,88,128]{2,1,0:T(8,128)} custom-call(s32[32]{0:T(128)} %subtract_clamp_fusion.count_ref, bf16[32,128,80]{2,1,0:T(8,128)(2,1)} %reshape_reshape.3.q_ref, bf16[32,80,512]{2,1,0:T(8,128)(2,1)} %bitcast.186, bf16[32,80,512]{2,1,0:T(8,128)(2,1)} %bitcast.187), custom_call_target="tpu_custom_call" | custom-call | flops 671088640 | bytes 7340032 | tf_op jit(solution)/shard_map/pallas_call | solution.py:46
  44.9 1.4 %constant_dynamic-slice_fusion.2 = (f32[2,2,2,2,1,88,128]{6,5,4,3,2,1,0:T(8,128)S(1)}, f32[2,2,2,2,1,88,128]{6,5,4,3,2,1,0:T(8,128)S(1)}) fusion(f32[2,2,2,2,2,88,128]{6,5,4,3,2,1,0:T(8,128)} %bitcast.182, s32[]{:T(128)S(6)} %select_n.133, s32[]{:T(128)S(6)} %select_n.134), kind=kLoop, calls=%fused_computation.125 | loop fusion | bytes 2883592 | tf_op jit(solution)/shard_map/jit(dynamic_index_in_dim)/dynamic_slice | solution.py:106
  46.3 0.9 copy.63
  47.5 0.4 select_reduce_fusion.1
  48.0 1.8 %collective-permute-done.5 = f32[2,2,2,2,88,128]{5,4,3,1,0,2:T(8,128)} collective-permute-done((f32[2,2,2,2,88,128]{5,4,3,1,0,2:T(8,128)}, f32[2,2,2,2,88,128]{5,4,3,1,0,2:T(8,128)}, u32[]{:S(2)}, u32[]{:S(2)}) %collective-permute-start.5) | collective-permute-done | bytes 720928 | tf_op jit(solution)/shard_map/ppermute | solution.py:69
  49.8 0.9 subtract_exponential_fusion.1
  50.7 0.9 subtract_exponential_fusion
  51.5 1.2 fusion.6
  52.7 0.9 fusion.18
  54.2 10.0 %collective-permute-done.6 = f32[2,2,2,88,128]{4,3,2,1,0:T(8,128)S(1)} collective-permute-done((f32[2,2,2,88,128]{4,3,2,1,0:T(8,128)S(1)}, f32[2,2,2,88,128]{4,3,2,1,0:T(8,128)S(1)}, u32[]{:S(2)}, u32[]{:S(2)}) %collective-permute-start.6) | collective-permute-done | bytes 360480 | tf_op jit(solution)/shard_map/ppermute | solution.py:69
  64.5 1.9 %collective-permute-start.7 = (f32[2,2,88,128]{3,2,1,0:T(8,128)S(1)}, f32[2,2,88,128]{3,2,1,0:T(8,128)S(1)}, u32[]{:S(2)}, u32[]{:S(2)}) collective-permute-start(f32[2,2,88,128]{3,2,1,0:T(8,128)S(1)} %get-tuple-element.22), channel_id=1, source_target_pairs={{0,64},{8,72},{16,80},{24,88},{32,96},{40,104},{48,112},{56,120},{... | collective-permute-start | bytes 540680 | tf_op jit(solution)/shard_map/ppermute | solution.py:69
  66.3 0.3 fusion.9
  66.7 8.4 %collective-permute-done.7 = f32[2,2,88,128]{3,2,1,0:T(8,128)S(1)} collective-permute-done((f32[2,2,88,128]{3,2,1,0:T(8,128)S(1)}, f32[2,2,88,128]{3,2,1,0:T(8,128)S(1)}, u32[]{:S(2)}, u32[]{:S(2)}) %collective-permute-start.7) | collective-permute-done | bytes 180256 | tf_op jit(solution)/shard_map/ppermute | solution.py:69
  75.2 1.5 %collective-permute-start.8 = (f32[2,88,128]{2,1,0:T(8,128)S(1)}, f32[2,88,128]{2,1,0:T(8,128)S(1)}, u32[]{:S(2)}, u32[]{:S(2)}) collective-permute-start(f32[2,88,128]{2,1,0:T(8,128)S(1)} %get-tuple-element.24), channel_id=1, source_target_pairs={{0,16},{8,24},{16,0},{24,8},{32,48},{40,56},{48,32},{56,40},{64,80... | collective-permute-start | bytes 270344 | tf_op jit(solution)/shard_map/ppermute | solution.py:69
  76.9 4.4 %collective-permute-done.8 = f32[2,88,128]{2,1,0:T(8,128)S(1)} collective-permute-done((f32[2,88,128]{2,1,0:T(8,128)S(1)}, f32[2,88,128]{2,1,0:T(8,128)S(1)}, u32[]{:S(2)}, u32[]{:S(2)}) %collective-permute-start.8) | collective-permute-done | bytes 90144 | tf_op jit(solution)/shard_map/ppermute | solution.py:69
  81.4 6.0 %collective-permute-start.9 = (f32[88,128]{1,0:T(8,128)S(1)}, f32[88,128]{1,0:T(8,128)S(1)}, u32[]{:S(2)}, u32[]{:S(2)}) collective-permute-start(f32[88,128]{1,0:T(8,128)S(1)} %dynamic-slice_bitcast_fusion.6), channel_id=1, source_target_pairs={{0,128},{8,136},{16,144},{24,152},{32,160},{40,168},{48,176},{56,1... | collective-permute-start | bytes 135176 | tf_op jit(solution)/shard_map/ppermute | solution.py:69
  87.6 1.9 %collective-permute-done.9 = f32[88,128]{1,0:T(8,128)S(1)} collective-permute-done((f32[88,128]{1,0:T(8,128)S(1)}, f32[88,128]{1,0:T(8,128)S(1)}, u32[]{:S(2)}, u32[]{:S(2)}) %collective-permute-start.9) | collective-permute-done | bytes 45088 | tf_op jit(solution)/shard_map/ppermute | solution.py:69
  89.5 0.5 broadcast.81
  90.0 0.7 fusion.51
  91.6 1.9 %convolution_convert_fusion.1 = bf16[32,2560]{1,0:T(8,128)(2,1)S(1)} fusion(bf16[32,320]{1,0:T(8,128)(2,1)S(1)} %reshape_transpose.3, bf16[320,2560]{1,0:T(8,128)(2,1)} %param.27), kind=kOutput, calls=%fused_computation.1 | convolution fusion | flops 52510720 | bytes 1822720 | tf_op jit(solution)/shard_map/dot_general | solution.py:215
  93.5 0.9 collective-permute-start.10
  94.4 4.5 %collective-permute-done.10 = bf16[32,2560]{1,0:T(8,128)(2,1)S(1)} collective-permute-done((bf16[32,2560]{1,0:T(8,128)(2,1)S(1)}, bf16[32,2560]{1,0:T(8,128)(2,1)S(1)}, u32[]{:S(2)}, u32[]{:S(2)}) %collective-permute-start.10) | collective-permute-done | bytes 163872 | tf_op jit(solution)/shard_map/ppermute | solution.py:69
  99.0 3.3 %collective-permute-start.11 = (bf16[32,2560]{1,0:T(8,128)(2,1)S(1)}, bf16[32,2560]{1,0:T(8,128)(2,1)S(1)}, u32[]{:S(2)}, u32[]{:S(2)}) collective-permute-start(bf16[32,2560]{1,0:T(8,128)(2,1)S(1)} %add_convert_fusion.5), channel_id=1, source_target_pairs={{0,2},{1,3},{2,0},{3,1},{4,6},{5,7},{6,4},{7,5},{8,10},{9,11},{10,... | collective-permute-start | bytes 491528 | tf_op jit(solution)/shard_map/ppermute | solution.py:69
  102.2 4.4 %collective-permute-done.11 = bf16[32,2560]{1,0:T(8,128)(2,1)S(1)} collective-permute-done((bf16[32,2560]{1,0:T(8,128)(2,1)S(1)}, bf16[32,2560]{1,0:T(8,128)(2,1)S(1)}, u32[]{:S(2)}, u32[]{:S(2)}) %collective-permute-start.11) | collective-permute-done | bytes 163872 | tf_op jit(solution)/shard_map/ppermute | solution.py:69
  106.7 1.5 %collective-permute-start.12 = (bf16[32,2560]{1,0:T(8,128)(2,1)S(1)}, bf16[32,2560]{1,0:T(8,128)(2,1)S(1)}, u32[]{:S(2)}, u32[]{:S(2)}) collective-permute-start(bf16[32,2560]{1,0:T(8,128)(2,1)S(1)} %add_convert_fusion.4), channel_id=1, source_target_pairs={{0,1},{1,0},{2,3},{3,2},{4,5},{5,4},{6,7},{7,6},{8,9},{9,8},{10,11... | collective-permute-start | bytes 491528 | tf_op jit(solution)/shard_map/ppermute | solution.py:69
  108.1 4.1 %collective-permute-done.12 = bf16[32,2560]{1,0:T(8,128)(2,1)S(1)} collective-permute-done((bf16[32,2560]{1,0:T(8,128)(2,1)S(1)}, bf16[32,2560]{1,0:T(8,128)(2,1)S(1)}, u32[]{:S(2)}, u32[]{:S(2)}) %collective-permute-start.12) | collective-permute-done | bytes 163872 | tf_op jit(solution)/shard_map/ppermute | solution.py:69
  112.6 0.5 fusion.52
  113.1 2.8 %convolution_convert_fusion = bf16[32,2560]{1,0:T(8,128)(2,1)S(1)} fusion(bf16[512,2560]{1,0:T(8,128)(2,1)S(1)} %copy-done, bf16[32,2560]{1,0:T(8,128)(2,1)S(1)} %multiply_convert_fusion, bf16[2560,512]{1,0:T(8,128)(2,1)} %param.29, f32[32,512]{1,0:T(8,128)S(1)} %fusion.52), kind=kOutput, calls=%fused_computation | convolution fusion | flops 167952384 | bytes 5636096 | tf_op jit(solution)/shard_map/dot_general | solution.py:229
  116.0 0.9 collective-permute-start.13
  116.9 4.5 %collective-permute-done.13 = bf16[32,2560]{1,0:T(8,128)(2,1)S(1)} collective-permute-done((bf16[32,2560]{1,0:T(8,128)(2,1)S(1)}, bf16[32,2560]{1,0:T(8,128)(2,1)S(1)}, u32[]{:S(2)}, u32[]{:S(2)}) %collective-permute-start.13) | collective-permute-done | bytes 163872 | tf_op jit(solution)/shard_map/ppermute | solution.py:69
  121.4 4.1 %collective-permute-start.14 = (bf16[32,2560]{1,0:T(8,128)(2,1)S(1)}, bf16[32,2560]{1,0:T(8,128)(2,1)S(1)}, u32[]{:S(2)}, u32[]{:S(2)}) collective-permute-start(bf16[32,2560]{1,0:T(8,128)(2,1)S(1)} %add_convert_fusion.2), channel_id=1, source_target_pairs={{0,2},{1,3},{2,0},{3,1},{4,6},{5,7},{6,4},{7,5},{8,10},{9,11},{10,... | collective-permute-start | bytes 491528 | tf_op jit(solution)/shard_map/ppermute | solution.py:69
  125.5 3.3 %collective-permute-done.14 = bf16[32,2560]{1,0:T(8,128)(2,1)S(1)} collective-permute-done((bf16[32,2560]{1,0:T(8,128)(2,1)S(1)}, bf16[32,2560]{1,0:T(8,128)(2,1)S(1)}, u32[]{:S(2)}, u32[]{:S(2)}) %collective-permute-start.14) | collective-permute-done | bytes 163872 | tf_op jit(solution)/shard_map/ppermute | solution.py:69
  128.8 1.0 collective-permute-start.15
  129.8 4.4 %collective-permute-done.15 = bf16[32,2560]{1,0:T(8,128)(2,1)S(1)} collective-permute-done((bf16[32,2560]{1,0:T(8,128)(2,1)S(1)}, bf16[32,2560]{1,0:T(8,128)(2,1)S(1)}, u32[]{:S(2)}, u32[]{:S(2)}) %collective-permute-start.15) | collective-permute-done | bytes 163872 | tf_op jit(solution)/shard_map/ppermute | solution.py:69
  134.5 0.7 dynamic-slice_convert_fusion
  135.2 0.7 multiply_reduce_fusion
  (90 shorter events, 3.9 us)
Async XLA Ops:
  0.6 112.5 %copy-start = (bf16[512,2560]{1,0:T(8,128)(2,1)S(1)}, bf16[512,2560]{1,0:T(8,128)(2,1)}, u32[]{:S(2)}) copy-start(bf16[512,2560]{1,0:T(8,128)(2,1)} %param.30) | copy-start | bytes 7864324
  0.6 29.4 %copy-start.12 = (s32[32]{0:T(128)S(1)}, s32[32]{0:T(128)}, u32[]{:S(2)}) copy-start(s32[32]{0:T(128)} %param.25) | copy-start | bytes 388
  0.7 9.3 %collective-permute-start = (bf16[1,32,320]{2,1,0:T(8,128)(2,1)}, bf16[1,32,320]{2,1,0:T(8,128)(2,1)S(1)}, u32[]{:S(2)}, u32[]{:S(2)}) collective-permute-start(bf16[1,32,320]{2,1,0:T(8,128)(2,1)} %bitcast.189), channel_id=1, source_target_pairs={{0,128},{8,136},{16,144},{24,152},{32,160},{40,168},{48,176},{56,1... | collective-permute-start | bytes 61448 | tf_op jit(solution)/shard_map/ppermute | solution.py:69
  10.7 5.7 %collective-permute-start.1 = (bf16[2,1,32,320]{3,2,0,1:T(8,128)(2,1)S(1)}, bf16[2,1,32,320]{3,2,0,1:T(8,128)(2,1)S(1)}, u32[]{:S(2)}, u32[]{:S(2)}) collective-permute-start(bf16[2,1,32,320]{3,2,0,1:T(8,128)(2,1)S(1)} %fusion.36), channel_id=1, source_target_pairs={{0,16},{8,24},{16,0},{24,8},{32,48},{40,56},{48,32},{56,40},{64,80... | collective-permute-start | bytes 122888 | tf_op jit(solution)/shard_map/ppermute | solution.py:69
  16.5 6.8 %collective-permute-start.2 = (bf16[2,2,1,32,320]{4,3,1,0,2:T(8,128)(2,1)S(1)}, bf16[2,2,1,32,320]{4,3,1,0,2:T(8,128)(2,1)S(1)}, u32[]{:S(2)}, u32[]{:S(2)}) collective-permute-start(bf16[2,2,1,32,320]{4,3,1,0,2:T(8,128)(2,1)S(1)} %fusion.24), channel_id=1, source_target_pairs={{0,64},{8,72},{16,80},{24,88},{32,96},{40,104},{48,112},{56,120},{... | collective-permute-start | bytes 245768 | tf_op jit(solution)/shard_map/ppermute | solution.py:69
  23.3 5.8 %collective-permute-start.3 = (bf16[2,2,2,1,32,320]{5,4,2,1,0,3:T(8,128)(2,1)S(1)}, bf16[2,2,2,1,32,320]{5,4,2,1,0,3:T(8,128)(2,1)S(1)}, u32[]{:S(2)}, u32[]{:S(2)}) collective-permute-start(bf16[2,2,2,1,32,320]{5,4,2,1,0,3:T(8,128)(2,1)S(1)} %fusion.15), channel_id=1, source_target_pairs={{0,32},{8,40},{16,48},{24,56},{32,0},{40,8},{48,16},{56,24},{64,96... | collective-permute-start | bytes 491528 | tf_op jit(solution)/shard_map/ppermute | solution.py:69
  30.0 1.9 %collective-permute-start.4 = (bf16[2,2,2,2,1,32,320]{6,5,3,2,1,0,4:T(8,128)(2,1)}, bf16[2,2,2,2,1,32,320]{6,5,3,2,1,0,4:T(8,128)(2,1)S(1)}, u32[]{:S(2)}, u32[]{:S(2)}) collective-permute-start(bf16[2,2,2,2,1,32,320]{6,5,3,2,1,0,4:T(8,128)(2,1)} %fusion.12), channel_id=1, source_target_pairs={{0,8},{8,0},{16,24},{24,16},{32,40},{40,32},{48,56},{56,48},{64,72... | collective-permute-start | bytes 983048 | tf_op jit(solution)/shard_map/ppermute | solution.py:69
  44.9 2.5 %copy-start.4 = (bf16[32,320]{1,0:T(8,128)(2,1)S(1)}, bf16[32,320]{1,0:T(8,128)(2,1)}, u32[]{:S(2)}) copy-start(bf16[32,320]{1,0:T(8,128)(2,1)} %param.18) | copy-start | bytes 61444
  44.9 2.6 %copy-start.10 = (bf16[32,80]{1,0:T(8,128)(2,1)S(1)}, bf16[32,80]{1,0:T(8,128)(2,1)}, u32[]{:S(2)}) copy-start(bf16[32,80]{1,0:T(8,128)(2,1)} %param.19) | copy-start | bytes 15364
  47.3 2.5 %collective-permute-start.5 = (f32[2,2,2,2,88,128]{5,4,3,1,0,2:T(8,128)}, f32[2,2,2,2,88,128]{5,4,3,1,0,2:T(8,128)}, u32[]{:S(2)}, u32[]{:S(2)}) collective-permute-start(f32[2,2,2,2,88,128]{5,4,3,1,0,2:T(8,128)} %bitcast.172), channel_id=1, source_target_pairs={{0,8},{8,0},{16,24},{24,16},{32,40},{40,32},{48,56},{56,48},{64,72... | collective-permute-start | bytes 2162696 | tf_op jit(solution)/shard_map/ppermute | solution.py:69
  48.0 5.8 %copy-start.8 = (s32[1,16]{1,0:T(1,128)S(1)}, s32[1,16]{1,0:T(1,128)}, u32[]{:S(2)}) copy-start(s32[1,16]{1,0:T(1,128)} %param.26) | copy-start | bytes 196
  48.0 5.9 %copy-start.3 = (bf16[1,16,128,80]{2,3,1,0:T(8,128)(2,1)S(1)}, bf16[1,16,128,80]{2,3,1,0:T(8,128)(2,1)}, u32[]{:S(2)}) copy-start(bf16[1,16,128,80]{2,3,1,0:T(8,128)(2,1)} %param.23) | copy-start | bytes 983044
  53.6 12.7 %copy-start.9 = (bf16[1,16,128,80]{2,3,1,0:T(8,128)(2,1)S(1)}, bf16[1,16,128,80]{2,3,1,0:T(8,128)(2,1)}, u32[]{:S(2)}) copy-start(bf16[1,16,128,80]{2,3,1,0:T(8,128)(2,1)} %param.24) | copy-start | bytes 983044
  53.7 10.5 %collective-permute-start.6 = (f32[2,2,2,88,128]{4,3,2,1,0:T(8,128)S(1)}, f32[2,2,2,88,128]{4,3,2,1,0:T(8,128)S(1)}, u32[]{:S(2)}, u32[]{:S(2)}) collective-permute-start(f32[2,2,2,88,128]{4,3,2,1,0:T(8,128)S(1)} %get-tuple-element.20), channel_id=1, source_target_pairs={{0,32},{8,40},{16,48},{24,56},{32,0},{40,8},{48,16},{56,24},{64,96... | collective-permute-start | bytes 1081352 | tf_op jit(solution)/shard_map/ppermute | solution.py:69
  64.3 26.8 %copy-start.11 = (bf16[32,80]{1,0:T(8,128)(2,1)S(1)}, bf16[32,80]{1,0:T(8,128)(2,1)}, u32[]{:S(2)}) copy-start(bf16[32,80]{1,0:T(8,128)(2,1)} %param.20) | copy-start | bytes 15364
  64.5 10.6 %collective-permute-start.7 = (f32[2,2,88,128]{3,2,1,0:T(8,128)S(1)}, f32[2,2,88,128]{3,2,1,0:T(8,128)S(1)}, u32[]{:S(2)}, u32[]{:S(2)}) collective-permute-start(f32[2,2,88,128]{3,2,1,0:T(8,128)S(1)} %get-tuple-element.22), channel_id=1, source_target_pairs={{0,64},{8,72},{16,80},{24,88},{32,96},{40,104},{48,112},{56,120},{... | collective-permute-start | bytes 540680 | tf_op jit(solution)/shard_map/ppermute | solution.py:69
  75.2 6.1 %collective-permute-start.8 = (f32[2,88,128]{2,1,0:T(8,128)S(1)}, f32[2,88,128]{2,1,0:T(8,128)S(1)}, u32[]{:S(2)}, u32[]{:S(2)}) collective-permute-start(f32[2,88,128]{2,1,0:T(8,128)S(1)} %get-tuple-element.24), channel_id=1, source_target_pairs={{0,16},{8,24},{16,0},{24,8},{32,48},{40,56},{48,32},{56,40},{64,80... | collective-permute-start | bytes 270344 | tf_op jit(solution)/shard_map/ppermute | solution.py:69
  81.4 8.1 %collective-permute-start.9 = (f32[88,128]{1,0:T(8,128)S(1)}, f32[88,128]{1,0:T(8,128)S(1)}, u32[]{:S(2)}, u32[]{:S(2)}) collective-permute-start(f32[88,128]{1,0:T(8,128)S(1)} %dynamic-slice_bitcast_fusion.6), channel_id=1, source_target_pairs={{0,128},{8,136},{16,144},{24,152},{32,160},{40,168},{48,176},{56,1... | collective-permute-start | bytes 135176 | tf_op jit(solution)/shard_map/ppermute | solution.py:69
  91.1 21.1 %copy-start.2 = (bf16[32,2560]{1,0:T(8,128)(2,1)S(1)}, bf16[32,2560]{1,0:T(8,128)(2,1)}, u32[]{:S(2)}) copy-start(bf16[32,2560]{1,0:T(8,128)(2,1)} %param.17) | copy-start | bytes 491524
  91.1 21.3 %copy-start.7 = (f32[2560]{0:T(1024)S(1)}, f32[2560]{0:T(1024)}, u32[]{:S(2)}) copy-start(f32[2560]{0:T(1024)} %param.31) | copy-start | bytes 30724
  91.6 21.0 %copy-start.1 = (bf16[2560,512]{1,0:T(8,128)(2,1)S(1)}, bf16[2560,512]{1,0:T(8,128)(2,1)}, u32[]{:S(2)}) copy-start(bf16[2560,512]{1,0:T(8,128)(2,1)} %param.28) | copy-start | bytes 7864324
  93.5 5.4 %collective-permute-start.10 = (bf16[32,2560]{1,0:T(8,128)(2,1)S(1)}, bf16[32,2560]{1,0:T(8,128)(2,1)S(1)}, u32[]{:S(2)}, u32[]{:S(2)}) collective-permute-start(bf16[32,2560]{1,0:T(8,128)(2,1)S(1)} %convolution_convert_fusion.1), channel_id=1, source_target_pairs={{0,4},{1,5},{2,6},{3,7},{4,0},{5,1},{6,2},{7,3},{8,12},{9,13},{10,... | collective-permute-start | bytes 491528 | tf_op jit(solution)/shard_map/ppermute | solution.py:69
  99.0 7.6 %collective-permute-start.11 = (bf16[32,2560]{1,0:T(8,128)(2,1)S(1)}, bf16[32,2560]{1,0:T(8,128)(2,1)S(1)}, u32[]{:S(2)}, u32[]{:S(2)}) collective-permute-start(bf16[32,2560]{1,0:T(8,128)(2,1)S(1)} %add_convert_fusion.5), channel_id=1, source_target_pairs={{0,2},{1,3},{2,0},{3,1},{4,6},{5,7},{6,4},{7,5},{8,10},{9,11},{10,... | collective-permute-start | bytes 491528 | tf_op jit(solution)/shard_map/ppermute | solution.py:69
  106.7 5.6 %collective-permute-start.12 = (bf16[32,2560]{1,0:T(8,128)(2,1)S(1)}, bf16[32,2560]{1,0:T(8,128)(2,1)S(1)}, u32[]{:S(2)}, u32[]{:S(2)}) collective-permute-start(bf16[32,2560]{1,0:T(8,128)(2,1)S(1)} %add_convert_fusion.4), channel_id=1, source_target_pairs={{0,1},{1,0},{2,3},{3,2},{4,5},{5,4},{6,7},{7,6},{8,9},{9,8},{10,11... | collective-permute-start | bytes 491528 | tf_op jit(solution)/shard_map/ppermute | solution.py:69
  113.1 22.1 %copy-start.5 = (f32[2560]{0:T(1024)S(1)}, f32[2560]{0:T(1024)}, u32[]{:S(2)}) copy-start(f32[2560]{0:T(1024)} %param.33) | copy-start | bytes 30724
  113.1 22.0 %copy-start.6 = (f32[2560]{0:T(1024)S(1)}, f32[2560]{0:T(1024)}, u32[]{:S(2)}) copy-start(f32[2560]{0:T(1024)} %param.32) | copy-start | bytes 30724
  116.0 5.4 %collective-permute-start.13 = (bf16[32,2560]{1,0:T(8,128)(2,1)S(1)}, bf16[32,2560]{1,0:T(8,128)(2,1)S(1)}, u32[]{:S(2)}, u32[]{:S(2)}) collective-permute-start(bf16[32,2560]{1,0:T(8,128)(2,1)S(1)} %convolution_convert_fusion), channel_id=1, source_target_pairs={{0,4},{1,5},{2,6},{3,7},{4,0},{5,1},{6,2},{7,3},{8,12},{9,13},{10,... | collective-permute-start | bytes 491528 | tf_op jit(solution)/shard_map/ppermute | solution.py:69
  121.4 7.4 %collective-permute-start.14 = (bf16[32,2560]{1,0:T(8,128)(2,1)S(1)}, bf16[32,2560]{1,0:T(8,128)(2,1)S(1)}, u32[]{:S(2)}, u32[]{:S(2)}) collective-permute-start(bf16[32,2560]{1,0:T(8,128)(2,1)S(1)} %add_convert_fusion.2), channel_id=1, source_target_pairs={{0,2},{1,3},{2,0},{3,1},{4,6},{5,7},{6,4},{7,5},{8,10},{9,11},{10,... | collective-permute-start | bytes 491528 | tf_op jit(solution)/shard_map/ppermute | solution.py:69
  128.8 5.4 %collective-permute-start.15 = (bf16[32,2560]{1,0:T(8,128)(2,1)S(1)}, bf16[32,2560]{1,0:T(8,128)(2,1)S(1)}, u32[]{:S(2)}, u32[]{:S(2)}) collective-permute-start(bf16[32,2560]{1,0:T(8,128)(2,1)S(1)} %add_convert_fusion.1), channel_id=1, source_target_pairs={{0,1},{1,0},{2,3},{3,2},{4,5},{5,4},{6,7},{7,6},{8,9},{9,8},{10,11... | collective-permute-start | bytes 491528 | tf_op jit(solution)/shard_map/ppermute | solution.py:69

commit v5 on v4

--- a/solution.py
+++ b/solution.py
@@ -95,17 +95,39 @@
     return jnp.concatenate([outs, top, sums], axis=-2)
 
 
+def encode_partials(x):
+    stats = x[..., HEAD_SIZE:HEAD_SIZE + 2, :]
+    hi = lax.reduce_precision(stats, exponent_bits=8, mantissa_bits=7)
+    rest = stats - hi
+    mid = lax.reduce_precision(rest, exponent_bits=8, mantissa_bits=7)
+    lo = rest - mid
+    pad = jnp.zeros(x.shape[:-2] + (PACK - HEAD_SIZE - 6, x.shape[-1]), jnp.float32)
+    return jnp.concatenate([x[..., :HEAD_SIZE, :], hi, mid, lo, pad], axis=-2).astype(jnp.bfloat16)
+
+
+def decode_partials(y):
+    y = y.astype(jnp.float32)
+    base = HEAD_SIZE
+    stats = (y[..., base:base + 2, :] + y[..., base + 2:base + 4, :]) + y[..., base + 4:base + 6, :]
+    pad = jnp.zeros(y.shape[:-2] + (PACK - HEAD_SIZE - 2, y.shape[-1]), jnp.float32)
+    return jnp.concatenate([y[..., :HEAD_SIZE, :], stats, pad], axis=-2)
+
+
 def reduce_partials(packed, axis, n, bits):
     me = lax.axis_index(axis)
     nb = len(bits)
     cur = packed.reshape((2,) * nb + packed.shape[1:])
     left = list(range(nb - 1, -1, -1))
-    for b in bits:
+    for i, b in enumerate(bits):
         ax = left.index(b)
         own = (me >> b) & 1
         keep = lax.dynamic_index_in_dim(cur, own, ax, keepdims=False)
         send = lax.dynamic_index_in_dim(cur, 1 - own, ax, keepdims=False)
-        cur = merge_partials(keep, exchange(send, axis, n, b))
+        if i == 0:
+            got = exchange(send, axis, n, b)
+        else:
+            got = decode_partials(exchange(encode_partials(send), axis, n, b))
+        cur = merge_partials(keep, got)
         left.remove(b)
     return cur
 

time: 137 us -> 129 us (0.942)
  waiting for transfers between devices: 69.7 us -> 57.8 us
  matrix products: 6.66 us -> 8.6 us
  starting transfers between devices: 32.2 us -> 33.7 us
    ppermute x16, waiting for transfers between devices: 69.7 us -> 57.8 us  [exchange(): return lax.ppermute(x, axis, perm=[(i, i ^ 1 << bit) for i in range(n)])]
    ppermute x16, starting transfers between devices: 32.2 us -> 33.7 us  [exchange(): return lax.ppermute(x, axis, perm=[(i, i ^ 1 << bit) for i in range(n)])]
  transfers between devices with their start and end apart: 16 -> 16, of which waited for: 16 -> 16; matrix products, arithmetic and copies ran while one was open for 2% -> 3% of each run, Pallas kernels for 0% -> 0%
where the time goes in v5:
time: 129 us; the launch traced here: 128 us
  waiting for transfers between devices  57.8 us (45%)
  starting transfers between devices  33.7 us (26%)
  Pallas kernels  10.8 us (8%)
  other arithmetic  9.47 us (7%)
  matrix products  8.6 us (7%)
  local copies, waits for them, and re-layouts  6.47 us (5%)
    ppermute x16, waiting for transfers between devices, exchange(): return lax.ppermute(x, axis, perm=[(i, i ^ 1 << bit) for i in range(n)])  57.8 us
    ppermute x16, starting transfers between devices, exchange(): return lax.ppermute(x, axis, perm=[(i, i ^ 1 << bit) for i in range(n)])  33.7 us
    pallas_call x1, Pallas kernels, prefix_partials(): pl.pallas_call(prefix_kernel, grid_spec=pltpu.PrefetchScalarGridSpec(num_...  10.8 us
    dot_general x1, matrix products, on_device(): jnp.dot(hidden, down_weight, preferred_element_type=jnp.float32)  2.83 us
  transfers between devices with their start and end apart: 16, of which 16 were waited for; matrix products, arithmetic and copies ran while one was open for 3% of the time, Pallas kernels for 0%

profile of v5, /device:TPU:6, one launch (start us, length us, event | category | flops | bytes accessed | tf_op | source)
XLA Modules:
  0.0 128.1 jit_solution(12193294292288673892)
XLA Ops:
  0.7 7.3 %collective-permute-start = (bf16[1,32,320]{2,1,0:T(8,128)(2,1)}, bf16[1,32,320]{2,1,0:T(8,128)(2,1)S(1)}, u32[]{:S(2)}, u32[]{:S(2)}) collective-permute-start(bf16[1,32,320]{2,1,0:T(8,128)(2,1)} %bitcast.197), channel_id=1, source_target_pairs={{0,128},{8,136},{16,144},{24,152},{32,160},{40,168},{48,176},{56,1... | collective-permute-start | bytes 61448 | tf_op jit(solution)/shard_map/ppermute | solution.py:69
  7.9 2.0 %collective-permute-done = bf16[1,32,320]{2,1,0:T(8,128)(2,1)S(1)} collective-permute-done((bf16[1,32,320]{2,1,0:T(8,128)(2,1)}, bf16[1,32,320]{2,1,0:T(8,128)(2,1)S(1)}, u32[]{:S(2)}, u32[]{:S(2)}) %collective-permute-start) | collective-permute-done | bytes 20512 | tf_op jit(solution)/shard_map/ppermute | solution.py:69
  10.0 0.7 select_bitcast_fusion.5
  10.7 1.5 %collective-permute-start.1 = (bf16[2,1,32,320]{3,2,0,1:T(8,128)(2,1)S(1)}, bf16[2,1,32,320]{3,2,0,1:T(8,128)(2,1)S(1)}, u32[]{:S(2)}, u32[]{:S(2)}) collective-permute-start(bf16[2,1,32,320]{3,2,0,1:T(8,128)(2,1)S(1)} %fusion.36), channel_id=1, source_target_pairs={{0,16},{8,24},{16,0},{24,8},{32,48},{40,56},{48,32},{56,40},{64,80... | collective-permute-start | bytes 122888 | tf_op jit(solution)/shard_map/ppermute | solution.py:69
  12.2 4.2 %collective-permute-done.1 = bf16[2,1,32,320]{3,2,0,1:T(8,128)(2,1)S(1)} collective-permute-done((bf16[2,1,32,320]{3,2,0,1:T(8,128)(2,1)S(1)}, bf16[2,1,32,320]{3,2,0,1:T(8,128)(2,1)S(1)}, u32[]{:S(2)}, u32[]{:S(2)}) %collective-permute-start.1) | collective-permute-done | bytes 40992 | tf_op jit(solution)/shard_map/ppermute | solution.py:69
  16.5 2.1 %collective-permute-start.2 = (bf16[2,2,1,32,320]{4,3,1,0,2:T(8,128)(2,1)S(1)}, bf16[2,2,1,32,320]{4,3,1,0,2:T(8,128)(2,1)S(1)}, u32[]{:S(2)}, u32[]{:S(2)}) collective-permute-start(bf16[2,2,1,32,320]{4,3,1,0,2:T(8,128)(2,1)S(1)} %fusion.24), channel_id=1, source_target_pairs={{0,64},{8,72},{16,80},{24,88},{32,96},{40,104},{48,112},{56,120},{... | collective-permute-start | bytes 245768 | tf_op jit(solution)/shard_map/ppermute | solution.py:69
  18.6 4.6 %collective-permute-done.2 = bf16[2,2,1,32,320]{4,3,1,0,2:T(8,128)(2,1)S(1)} collective-permute-done((bf16[2,2,1,32,320]{4,3,1,0,2:T(8,128)(2,1)S(1)}, bf16[2,2,1,32,320]{4,3,1,0,2:T(8,128)(2,1)S(1)}, u32[]{:S(2)}, u32[]{:S(2)}) %collective-permute-start.2) | collective-permute-done | bytes 81952 | tf_op jit(solution)/shard_map/ppermute | solution.py:69
  23.5 5.6 %collective-permute-done.3 = bf16[2,2,2,1,32,320]{5,4,2,1,0,3:T(8,128)(2,1)S(1)} collective-permute-done((bf16[2,2,2,1,32,320]{5,4,2,1,0,3:T(8,128)(2,1)S(1)}, bf16[2,2,2,1,32,320]{5,4,2,1,0,3:T(8,128)(2,1)S(1)}, u32[]{:S(2)}, u32[]{:S(2)}) %collective-permute-start.3) | collective-permute-done | bytes 163872 | tf_op jit(solution)/shard_map/ppermute | solution.py:69
  29.2 0.8 fusion.12
  30.0 0.5 subtract_clamp_fusion.count_ref
  30.5 1.4 %collective-permute-done.4 = bf16[2,2,2,2,1,32,320]{6,5,3,2,1,0,4:T(8,128)(2,1)S(1)} collective-permute-done((bf16[2,2,2,2,1,32,320]{6,5,3,2,1,0,4:T(8,128)(2,1)}, bf16[2,2,2,2,1,32,320]{6,5,3,2,1,0,4:T(8,128)(2,1)S(1)}, u32[]{:S(2)}, u32[]{:S(2)}) %collective-permute-start.4) | collective-permute-done | bytes 327712 | tf_op jit(solution)/shard_map/ppermute | solution.py:69
  32.4 1.6 %reshape_reshape.3.q_ref = bf16[32,128,80]{2,1,0:T(8,128)(2,1)} reshape(bf16[2,2,2,2,2,1,32,320]{7,6,4,3,2,1,0,5:T(8,128)(2,1)S(1)} %copy.53) | data formatting | bytes 1310720 | tf_op jit(solution)/shard_map/reshape;reshape | solution.py:180
  34.0 10.8 %shard_map.176 = f32[32,88,128]{2,1,0:T(8,128)} custom-call(s32[32]{0:T(128)} %subtract_clamp_fusion.count_ref, bf16[32,128,80]{2,1,0:T(8,128)(2,1)} %reshape_reshape.3.q_ref, bf16[32,80,512]{2,1,0:T(8,128)(2,1)} %bitcast.194, bf16[32,80,512]{2,1,0:T(8,128)(2,1)} %bitcast.195), custom_call_target="tpu_custom_call" | custom-call | flops 671088640 | bytes 7340032 | tf_op jit(solution)/shard_map/pallas_call | solution.py:46
  44.9 1.5 %constant_dynamic-slice_fusion.3 = (f32[2,2,2,2,1,88,128]{6,5,4,3,2,1,0:T(8,128)S(1)}, f32[2,2,2,2,1,88,128]{6,5,4,3,2,1,0:T(8,128)S(1)}) fusion(f32[2,2,2,2,2,88,128]{6,5,4,3,2,1,0:T(8,128)} %bitcast.190, s32[]{:T(128)S(6)} %select_n.133, s32[]{:T(128)S(6)} %select_n.134), kind=kLoop, calls=%fused_computation.140 | loop fusion | bytes 2883592 | tf_op jit(solution)/shard_map/jit(dynamic_index_in_dim)/dynamic_slice | solution.py:124
  46.3 0.9 copy.63
  47.6 1.3 select_reduce_fusion
  48.9 0.9 collective-permute-done.5
  49.8 0.9 subtract_exponential_fusion.1
  50.7 0.9 subtract_exponential_fusion
  51.5 1.2 fusion.6
  52.7 0.9 fusion.18
  54.5 6.1 %collective-permute-done.6 = bf16[2,2,2,88,128]{4,3,2,1,0:T(8,128)(2,1)S(1)} collective-permute-done((bf16[2,2,2,88,128]{4,3,2,1,0:T(8,128)(2,1)S(1)}, bf16[2,2,2,88,128]{4,3,2,1,0:T(8,128)(2,1)S(1)}, u32[]{:S(2)}, u32[]{:S(2)}) %collective-permute-start.6) | collective-permute-done | bytes 180256 | tf_op jit(solution)/shard_map/ppermute | solution.py:69
  61.0 1.9 %collective-permute-start.7 = (bf16[2,2,88,128]{3,2,1,0:T(8,128)(2,1)S(1)}, bf16[2,2,88,128]{3,2,1,0:T(8,128)(2,1)S(1)}, u32[]{:S(2)}, u32[]{:S(2)}) collective-permute-start(bf16[2,2,88,128]{3,2,1,0:T(8,128)(2,1)S(1)} %concatenate.44), channel_id=1, source_target_pairs={{0,64},{8,72},{16,80},{24,88},{32,96},{40,104},{48,112},{56,120},{... | collective-permute-start | bytes 270344 | tf_op jit(solution)/shard_map/ppermute | solution.py:69
  62.8 1.3 %fusion.9 = f32[16,2,4,80]{3,2,1,0:T(4,128)S(1)} fusion(bf16[1,16,128,80]{2,3,1,0:T(8,128)(2,1)} %param.24, f32[16,2,4,128]{3,2,1,0:T(4,128)S(1)} %get-tuple-element.42, f32[16,2,4]{2,1,0:T(2,128)S(1)} %max.65, pred[16,128]{1,0:T(8,128)(4,1)S(1)} %iota_compare_fusion), kind=kOutput, calls=%fused_computation.31 | convolution fusion | flops 2670592 | bytes 436736 | tf_op jit(solution)/shard_map/ksjgt,stkh->ksjgh/dot_general | solution.py:215
  64.1 3.6 %collective-permute-done.7 = bf16[2,2,88,128]{3,2,1,0:T(8,128)(2,1)S(1)} collective-permute-done((bf16[2,2,88,128]{3,2,1,0:T(8,128)(2,1)S(1)}, bf16[2,2,88,128]{3,2,1,0:T(8,128)(2,1)S(1)}, u32[]{:S(2)}, u32[]{:S(2)}) %collective-permute-start.7) | collective-permute-done | bytes 90144 | tf_op jit(solution)/shard_map/ppermute | solution.py:69
  68.0 1.5 %collective-permute-start.8 = (bf16[2,88,128]{2,1,0:T(8,128)(2,1)S(1)}, bf16[2,88,128]{2,1,0:T(8,128)(2,1)S(1)}, u32[]{:S(2)}, u32[]{:S(2)}) collective-permute-start(bf16[2,88,128]{2,1,0:T(8,128)(2,1)S(1)} %concatenate.47), channel_id=1, source_target_pairs={{0,16},{8,24},{16,0},{24,8},{32,48},{40,56},{48,32},{56,40},{64,80... | collective-permute-start | bytes 135176 | tf_op jit(solution)/shard_map/ppermute | solution.py:69
  69.7 3.9 %collective-permute-done.8 = bf16[2,88,128]{2,1,0:T(8,128)(2,1)S(1)} collective-permute-done((bf16[2,88,128]{2,1,0:T(8,128)(2,1)S(1)}, bf16[2,88,128]{2,1,0:T(8,128)(2,1)S(1)}, u32[]{:S(2)}, u32[]{:S(2)}) %collective-permute-start.8) | collective-permute-done | bytes 45088 | tf_op jit(solution)/shard_map/ppermute | solution.py:69
  73.8 6.0 %collective-permute-start.9 = (bf16[88,128]{1,0:T(8,128)(2,1)S(1)}, bf16[88,128]{1,0:T(8,128)(2,1)S(1)}, u32[]{:S(2)}, u32[]{:S(2)}) collective-permute-start(bf16[88,128]{1,0:T(8,128)(2,1)S(1)} %concatenate.50), channel_id=1, source_target_pairs={{0,128},{8,136},{16,144},{24,152},{32,160},{40,168},{48,176},{56,1... | collective-permute-start | bytes 67592 | tf_op jit(solution)/shard_map/ppermute | solution.py:69
  80.0 1.9 %collective-permute-done.9 = bf16[88,128]{1,0:T(8,128)(2,1)S(1)} collective-permute-done((bf16[88,128]{1,0:T(8,128)(2,1)S(1)}, bf16[88,128]{1,0:T(8,128)(2,1)S(1)}, u32[]{:S(2)}, u32[]{:S(2)}) %collective-permute-start.9) | collective-permute-done | bytes 22560 | tf_op jit(solution)/shard_map/ppermute | solution.py:69
  81.9 0.5 broadcast.97
  82.4 0.7 fusion.57
  84.0 1.9 %convolution_convert_fusion.1 = bf16[32,2560]{1,0:T(8,128)(2,1)S(1)} fusion(bf16[32,320]{1,0:T(8,128)(2,1)S(1)} %reshape_transpose.3, bf16[320,2560]{1,0:T(8,128)(2,1)} %param.27), kind=kOutput, calls=%fused_computation.1 | convolution fusion | flops 52510720 | bytes 1822720 | tf_op jit(solution)/shard_map/dot_general | solution.py:237
  85.9 0.9 collective-permute-start.10
  86.8 4.5 %collective-permute-done.10 = bf16[32,2560]{1,0:T(8,128)(2,1)S(1)} collective-permute-done((bf16[32,2560]{1,0:T(8,128)(2,1)S(1)}, bf16[32,2560]{1,0:T(8,128)(2,1)S(1)}, u32[]{:S(2)}, u32[]{:S(2)}) %collective-permute-start.10) | collective-permute-done | bytes 163872 | tf_op jit(solution)/shard_map/ppermute | solution.py:69
  91.4 3.3 %collective-permute-start.11 = (bf16[32,2560]{1,0:T(8,128)(2,1)S(1)}, bf16[32,2560]{1,0:T(8,128)(2,1)S(1)}, u32[]{:S(2)}, u32[]{:S(2)}) collective-permute-start(bf16[32,2560]{1,0:T(8,128)(2,1)S(1)} %add_convert_fusion.5), channel_id=1, source_target_pairs={{0,2},{1,3},{2,0},{3,1},{4,6},{5,7},{6,4},{7,5},{8,10},{9,11},{10,... | collective-permute-start | bytes 491528 | tf_op jit(solution)/shard_map/ppermute | solution.py:69
  94.7 4.2 %collective-permute-done.11 = bf16[32,2560]{1,0:T(8,128)(2,1)S(1)} collective-permute-done((bf16[32,2560]{1,0:T(8,128)(2,1)S(1)}, bf16[32,2560]{1,0:T(8,128)(2,1)S(1)}, u32[]{:S(2)}, u32[]{:S(2)}) %collective-permute-start.11) | collective-permute-done | bytes 163872 | tf_op jit(solution)/shard_map/ppermute | solution.py:69
  98.9 2.3 %collective-permute-start.12 = (bf16[32,2560]{1,0:T(8,128)(2,1)S(1)}, bf16[32,2560]{1,0:T(8,128)(2,1)S(1)}, u32[]{:S(2)}, u32[]{:S(2)}) collective-permute-start(bf16[32,2560]{1,0:T(8,128)(2,1)S(1)} %add_convert_fusion.4), channel_id=1, source_target_pairs={{0,1},{1,0},{2,3},{3,2},{4,5},{5,4},{6,7},{7,6},{8,9},{9,8},{10,11... | collective-permute-start | bytes 491528 | tf_op jit(solution)/shard_map/ppermute | solution.py:69
  101.2 3.3 %collective-permute-done.12 = bf16[32,2560]{1,0:T(8,128)(2,1)S(1)} collective-permute-done((bf16[32,2560]{1,0:T(8,128)(2,1)S(1)}, bf16[32,2560]{1,0:T(8,128)(2,1)S(1)}, u32[]{:S(2)}, u32[]{:S(2)}) %collective-permute-start.12) | collective-permute-done | bytes 163872 | tf_op jit(solution)/shard_map/ppermute | solution.py:69
  104.8 0.5 fusion.58
  105.4 2.8 %convolution_convert_fusion = bf16[32,2560]{1,0:T(8,128)(2,1)S(1)} fusion(bf16[512,2560]{1,0:T(8,128)(2,1)S(1)} %copy-done, bf16[32,2560]{1,0:T(8,128)(2,1)S(1)} %multiply_convert_fusion, bf16[2560,512]{1,0:T(8,128)(2,1)} %param.29, f32[32,512]{1,0:T(8,128)S(1)} %fusion.58), kind=kOutput, calls=%fused_computation | convolution fusion | flops 167952384 | bytes 5636096 | tf_op jit(solution)/shard_map/dot_general | solution.py:251
  108.2 0.9 collective-permute-start.13
  109.1 4.5 %collective-permute-done.13 = bf16[32,2560]{1,0:T(8,128)(2,1)S(1)} collective-permute-done((bf16[32,2560]{1,0:T(8,128)(2,1)S(1)}, bf16[32,2560]{1,0:T(8,128)(2,1)S(1)}, u32[]{:S(2)}, u32[]{:S(2)}) %collective-permute-start.13) | collective-permute-done | bytes 163872 | tf_op jit(solution)/shard_map/ppermute | solution.py:69
  113.7 4.0 %collective-permute-start.14 = (bf16[32,2560]{1,0:T(8,128)(2,1)S(1)}, bf16[32,2560]{1,0:T(8,128)(2,1)S(1)}, u32[]{:S(2)}, u32[]{:S(2)}) collective-permute-start(bf16[32,2560]{1,0:T(8,128)(2,1)S(1)} %add_convert_fusion.2), channel_id=1, source_target_pairs={{0,2},{1,3},{2,0},{3,1},{4,6},{5,7},{6,4},{7,5},{8,10},{9,11},{10,... | collective-permute-start | bytes 491528 | tf_op jit(solution)/shard_map/ppermute | solution.py:69
  117.7 3.3 %collective-permute-done.14 = bf16[32,2560]{1,0:T(8,128)(2,1)S(1)} collective-permute-done((bf16[32,2560]{1,0:T(8,128)(2,1)S(1)}, bf16[32,2560]{1,0:T(8,128)(2,1)S(1)}, u32[]{:S(2)}, u32[]{:S(2)}) %collective-permute-start.14) | collective-permute-done | bytes 163872 | tf_op jit(solution)/shard_map/ppermute | solution.py:69
  121.1 1.7 %collective-permute-start.15 = (bf16[32,2560]{1,0:T(8,128)(2,1)S(1)}, bf16[32,2560]{1,0:T(8,128)(2,1)S(1)}, u32[]{:S(2)}, u32[]{:S(2)}) collective-permute-start(bf16[32,2560]{1,0:T(8,128)(2,1)S(1)} %add_convert_fusion.1), channel_id=1, source_target_pairs={{0,1},{1,0},{2,3},{3,2},{4,5},{5,4},{6,7},{7,6},{8,9},{9,8},{10,11... | collective-permute-start | bytes 491528 | tf_op jit(solution)/shard_map/ppermute | solution.py:69
  122.7 3.7 %collective-permute-done.15 = bf16[32,2560]{1,0:T(8,128)(2,1)S(1)} collective-permute-done((bf16[32,2560]{1,0:T(8,128)(2,1)S(1)}, bf16[32,2560]{1,0:T(8,128)(2,1)S(1)}, u32[]{:S(2)}, u32[]{:S(2)}) %collective-permute-start.15) | collective-permute-done | bytes 163872 | tf_op jit(solution)/shard_map/ppermute | solution.py:69
  126.7 0.7 dynamic-slice_convert_fusion
  127.4 0.7 multiply_reduce_fusion
  (109 shorter events, 4.6 us)
Async XLA Ops:
  0.6 104.7 %copy-start = (bf16[512,2560]{1,0:T(8,128)(2,1)S(1)}, bf16[512,2560]{1,0:T(8,128)(2,1)}, u32[]{:S(2)}) copy-start(bf16[512,2560]{1,0:T(8,128)(2,1)} %param.30) | copy-start | bytes 7864324
  0.6 29.4 %copy-start.10 = (s32[32]{0:T(128)S(1)}, s32[32]{0:T(128)}, u32[]{:S(2)}) copy-start(s32[32]{0:T(128)} %param.25) | copy-start | bytes 388
  0.7 9.3 %collective-permute-start = (bf16[1,32,320]{2,1,0:T(8,128)(2,1)}, bf16[1,32,320]{2,1,0:T(8,128)(2,1)S(1)}, u32[]{:S(2)}, u32[]{:S(2)}) collective-permute-start(bf16[1,32,320]{2,1,0:T(8,128)(2,1)} %bitcast.197), channel_id=1, source_target_pairs={{0,128},{8,136},{16,144},{24,152},{32,160},{40,168},{48,176},{56,1... | collective-permute-start | bytes 61448 | tf_op jit(solution)/shard_map/ppermute | solution.py:69
  10.7 5.7 %collective-permute-start.1 = (bf16[2,1,32,320]{3,2,0,1:T(8,128)(2,1)S(1)}, bf16[2,1,32,320]{3,2,0,1:T(8,128)(2,1)S(1)}, u32[]{:S(2)}, u32[]{:S(2)}) collective-permute-start(bf16[2,1,32,320]{3,2,0,1:T(8,128)(2,1)S(1)} %fusion.36), channel_id=1, source_target_pairs={{0,16},{8,24},{16,0},{24,8},{32,48},{40,56},{48,32},{56,40},{64,80... | collective-permute-start | bytes 122888 | tf_op jit(solution)/shard_map/ppermute | solution.py:69
  16.5 6.8 %collective-permute-start.2 = (bf16[2,2,1,32,320]{4,3,1,0,2:T(8,128)(2,1)S(1)}, bf16[2,2,1,32,320]{4,3,1,0,2:T(8,128)(2,1)S(1)}, u32[]{:S(2)}, u32[]{:S(2)}) collective-permute-start(bf16[2,2,1,32,320]{4,3,1,0,2:T(8,128)(2,1)S(1)} %fusion.24), channel_id=1, source_target_pairs={{0,64},{8,72},{16,80},{24,88},{32,96},{40,104},{48,112},{56,120},{... | collective-permute-start | bytes 245768 | tf_op jit(solution)/shard_map/ppermute | solution.py:69
  23.3 5.8 %collective-permute-start.3 = (bf16[2,2,2,1,32,320]{5,4,2,1,0,3:T(8,128)(2,1)S(1)}, bf16[2,2,2,1,32,320]{5,4,2,1,0,3:T(8,128)(2,1)S(1)}, u32[]{:S(2)}, u32[]{:S(2)}) collective-permute-start(bf16[2,2,2,1,32,320]{5,4,2,1,0,3:T(8,128)(2,1)S(1)} %fusion.15), channel_id=1, source_target_pairs={{0,32},{8,40},{16,48},{24,56},{32,0},{40,8},{48,16},{56,24},{64,96... | collective-permute-start | bytes 491528 | tf_op jit(solution)/shard_map/ppermute | solution.py:69
  30.0 1.9 %collective-permute-start.4 = (bf16[2,2,2,2,1,32,320]{6,5,3,2,1,0,4:T(8,128)(2,1)}, bf16[2,2,2,2,1,32,320]{6,5,3,2,1,0,4:T(8,128)(2,1)S(1)}, u32[]{:S(2)}, u32[]{:S(2)}) collective-permute-start(bf16[2,2,2,2,1,32,320]{6,5,3,2,1,0,4:T(8,128)(2,1)} %fusion.12), channel_id=1, source_target_pairs={{0,8},{8,0},{16,24},{24,16},{32,40},{40,32},{48,56},{56,48},{64,72... | collective-permute-start | bytes 983048 | tf_op jit(solution)/shard_map/ppermute | solution.py:69
  44.9 2.5 %copy-start.3 = (bf16[32,320]{1,0:T(8,128)(2,1)S(1)}, bf16[32,320]{1,0:T(8,128)(2,1)}, u32[]{:S(2)}) copy-start(bf16[32,320]{1,0:T(8,128)(2,1)} %param.18) | copy-start | bytes 61444
  44.9 2.6 %copy-start.7 = (s32[1,16]{1,0:T(1,128)S(1)}, s32[1,16]{1,0:T(1,128)}, u32[]{:S(2)}) copy-start(s32[1,16]{1,0:T(1,128)} %param.26) | copy-start | bytes 196
  47.3 2.5 %collective-permute-start.5 = (f32[2,2,2,2,88,128]{5,4,3,1,0,2:T(8,128)}, f32[2,2,2,2,88,128]{5,4,3,1,0,2:T(8,128)}, u32[]{:S(2)}, u32[]{:S(2)}) collective-permute-start(f32[2,2,2,2,88,128]{5,4,3,1,0,2:T(8,128)} %bitcast.180), channel_id=1, source_target_pairs={{0,8},{8,0},{16,24},{24,16},{32,40},{40,32},{48,56},{56,48},{64,72... | collective-permute-start | bytes 2162696 | tf_op jit(solution)/shard_map/ppermute | solution.py:69
  51.5 2.5 %copy-start.8 = (bf16[32,80]{1,0:T(8,128)(2,1)S(1)}, bf16[32,80]{1,0:T(8,128)(2,1)}, u32[]{:S(2)}) copy-start(bf16[32,80]{1,0:T(8,128)(2,1)} %param.19) | copy-start | bytes 15364
  53.9 6.7 %collective-permute-start.6 = (bf16[2,2,2,88,128]{4,3,2,1,0:T(8,128)(2,1)S(1)}, bf16[2,2,2,88,128]{4,3,2,1,0:T(8,128)(2,1)S(1)}, u32[]{:S(2)}, u32[]{:S(2)}) collective-permute-start(bf16[2,2,2,88,128]{4,3,2,1,0:T(8,128)(2,1)S(1)} %concatenate.41), channel_id=1, source_target_pairs={{0,32},{8,40},{16,48},{24,56},{32,0},{40,8},{48,16},{56,24},{64,96... | collective-permute-start | bytes 540680 | tf_op jit(solution)/shard_map/ppermute | solution.py:69
  60.8 22.7 %copy-start.9 = (bf16[32,80]{1,0:T(8,128)(2,1)S(1)}, bf16[32,80]{1,0:T(8,128)(2,1)}, u32[]{:S(2)}) copy-start(bf16[32,80]{1,0:T(8,128)(2,1)} %param.20) | copy-start | bytes 15364
  61.0 6.7 %collective-permute-start.7 = (bf16[2,2,88,128]{3,2,1,0:T(8,128)(2,1)S(1)}, bf16[2,2,88,128]{3,2,1,0:T(8,128)(2,1)S(1)}, u32[]{:S(2)}, u32[]{:S(2)}) collective-permute-start(bf16[2,2,88,128]{3,2,1,0:T(8,128)(2,1)S(1)} %concatenate.44), channel_id=1, source_target_pairs={{0,64},{8,72},{16,80},{24,88},{32,96},{40,104},{48,112},{56,120},{... | collective-permute-start | bytes 270344 | tf_op jit(solution)/shard_map/ppermute | solution.py:69
  68.0 5.6 %collective-permute-start.8 = (bf16[2,88,128]{2,1,0:T(8,128)(2,1)S(1)}, bf16[2,88,128]{2,1,0:T(8,128)(2,1)S(1)}, u32[]{:S(2)}, u32[]{:S(2)}) collective-permute-start(bf16[2,88,128]{2,1,0:T(8,128)(2,1)S(1)} %concatenate.47), channel_id=1, source_target_pairs={{0,16},{8,24},{16,0},{24,8},{32,48},{40,56},{48,32},{56,40},{64,80... | collective-permute-start | bytes 135176 | tf_op jit(solution)/shard_map/ppermute | solution.py:69
  73.8 8.0 %collective-permute-start.9 = (bf16[88,128]{1,0:T(8,128)(2,1)S(1)}, bf16[88,128]{1,0:T(8,128)(2,1)S(1)}, u32[]{:S(2)}, u32[]{:S(2)}) collective-permute-start(bf16[88,128]{1,0:T(8,128)(2,1)S(1)} %concatenate.50), channel_id=1, source_target_pairs={{0,128},{8,136},{16,144},{24,152},{32,160},{40,168},{48,176},{56,1... | collective-permute-start | bytes 67592 | tf_op jit(solution)/shard_map/ppermute | solution.py:69
  83.5 21.0 %copy-start.2 = (bf16[32,2560]{1,0:T(8,128)(2,1)S(1)}, bf16[32,2560]{1,0:T(8,128)(2,1)}, u32[]{:S(2)}) copy-start(bf16[32,2560]{1,0:T(8,128)(2,1)} %param.17) | copy-start | bytes 491524
  83.5 21.2 %copy-start.6 = (f32[2560]{0:T(1024)S(1)}, f32[2560]{0:T(1024)}, u32[]{:S(2)}) copy-start(f32[2560]{0:T(1024)} %param.31) | copy-start | bytes 30724
  84.0 20.9 %copy-start.1 = (bf16[2560,512]{1,0:T(8,128)(2,1)S(1)}, bf16[2560,512]{1,0:T(8,128)(2,1)}, u32[]{:S(2)}) copy-start(bf16[2560,512]{1,0:T(8,128)(2,1)} %param.28) | copy-start | bytes 7864324
  85.9 5.4 %collective-permute-start.10 = (bf16[32,2560]{1,0:T(8,128)(2,1)S(1)}, bf16[32,2560]{1,0:T(8,128)(2,1)S(1)}, u32[]{:S(2)}, u32[]{:S(2)}) collective-permute-start(bf16[32,2560]{1,0:T(8,128)(2,1)S(1)} %convolution_convert_fusion.1), channel_id=1, source_target_pairs={{0,4},{1,5},{2,6},{3,7},{4,0},{5,1},{6,2},{7,3},{8,12},{9,13},{10,... | collective-permute-start | bytes 491528 | tf_op jit(solution)/shard_map/ppermute | solution.py:69
  91.4 7.5 %collective-permute-start.11 = (bf16[32,2560]{1,0:T(8,128)(2,1)S(1)}, bf16[32,2560]{1,0:T(8,128)(2,1)S(1)}, u32[]{:S(2)}, u32[]{:S(2)}) collective-permute-start(bf16[32,2560]{1,0:T(8,128)(2,1)S(1)} %add_convert_fusion.5), channel_id=1, source_target_pairs={{0,2},{1,3},{2,0},{3,1},{4,6},{5,7},{6,4},{7,5},{8,10},{9,11},{10,... | collective-permute-start | bytes 491528 | tf_op jit(solution)/shard_map/ppermute | solution.py:69
  98.9 5.6 %collective-permute-start.12 = (bf16[32,2560]{1,0:T(8,128)(2,1)S(1)}, bf16[32,2560]{1,0:T(8,128)(2,1)S(1)}, u32[]{:S(2)}, u32[]{:S(2)}) collective-permute-start(bf16[32,2560]{1,0:T(8,128)(2,1)S(1)} %add_convert_fusion.4), channel_id=1, source_target_pairs={{0,1},{1,0},{2,3},{3,2},{4,5},{5,4},{6,7},{7,6},{8,9},{9,8},{10,11... | collective-permute-start | bytes 491528 | tf_op jit(solution)/shard_map/ppermute | solution.py:69
  105.4 22.0 %copy-start.4 = (f32[2560]{0:T(1024)S(1)}, f32[2560]{0:T(1024)}, u32[]{:S(2)}) copy-start(f32[2560]{0:T(1024)} %param.33) | copy-start | bytes 30724
  105.4 22.0 %copy-start.5 = (f32[2560]{0:T(1024)S(1)}, f32[2560]{0:T(1024)}, u32[]{:S(2)}) copy-start(f32[2560]{0:T(1024)} %param.32) | copy-start | bytes 30724
  108.2 5.4 %collective-permute-start.13 = (bf16[32,2560]{1,0:T(8,128)(2,1)S(1)}, bf16[32,2560]{1,0:T(8,128)(2,1)S(1)}, u32[]{:S(2)}, u32[]{:S(2)}) collective-permute-start(bf16[32,2560]{1,0:T(8,128)(2,1)S(1)} %convolution_convert_fusion), channel_id=1, source_target_pairs={{0,4},{1,5},{2,6},{3,7},{4,0},{5,1},{6,2},{7,3},{8,12},{9,13},{10,... | collective-permute-start | bytes 491528 | tf_op jit(solution)/shard_map/ppermute | solution.py:69
  113.7 7.3 %collective-permute-start.14 = (bf16[32,2560]{1,0:T(8,128)(2,1)S(1)}, bf16[32,2560]{1,0:T(8,128)(2,1)S(1)}, u32[]{:S(2)}, u32[]{:S(2)}) collective-permute-start(bf16[32,2560]{1,0:T(8,128)(2,1)S(1)} %add_convert_fusion.2), channel_id=1, source_target_pairs={{0,2},{1,3},{2,0},{3,1},{4,6},{5,7},{6,4},{7,5},{8,10},{9,11},{10,... | collective-permute-start | bytes 491528 | tf_op jit(solution)/shard_map/ppermute | solution.py:69
  121.1 5.4 %collective-permute-start.15 = (bf16[32,2560]{1,0:T(8,128)(2,1)S(1)}, bf16[32,2560]{1,0:T(8,128)(2,1)S(1)}, u32[]{:S(2)}, u32[]{:S(2)}) collective-permute-start(bf16[32,2560]{1,0:T(8,128)(2,1)S(1)} %add_convert_fusion.1), channel_id=1, source_target_pairs={{0,1},{1,0},{2,3},{3,2},{4,5},{5,4},{6,7},{7,6},{8,9},{9,8},{10,11... | collective-permute-start | bytes 491528 | tf_op jit(solution)/shard_map/ppermute | solution.py:69

commit v6 on v5

--- a/solution.py
+++ b/solution.py
@@ -15,10 +15,10 @@
 
 
 PACK = 88
-BLOCK_PROMPTS = 4
-
-
-def prefix_kernel(count_ref, q_ref, kt_ref, vt_ref, out_ref):
+BLOCK_PROMPTS = 8
+
+
+def prefix_kernel(count_ref, half_ref, q_ref, kt_ref, vt_ref, out_ref):
     step = pl.program_id(0)
     for i in range(q_ref.shape[0]):
         q = q_ref[i]
@@ -26,7 +26,7 @@
         vt = vt_ref[i]
         s = jnp.dot(q, kt, preferred_element_type=jnp.float32) * (HEAD_SIZE ** -0.5)
         place = lax.broadcasted_iota(jnp.int32, s.shape, 1)
-        valid = place < count_ref[step * q_ref.shape[0] + i]
+        valid = place < count_ref[2 * (step * q_ref.shape[0] + i) + half_ref[0]]
         s = jnp.where(valid, s, jnp.float32(-1e30))
         top = jnp.max(s, axis=1, keepdims=True)
         w = jnp.where(valid, jnp.exp(s - top), 0.0)
@@ -39,26 +39,26 @@
         out_ref[i, HEAD_SIZE:PACK, :] = jnp.transpose(stats)[0:PACK - HEAD_SIZE, :]
 
 
-def prefix_partials(count, q, kt, vt):
-    P_, rows, _ = q.shape
-    L = kt.shape[2]
-    bp = BLOCK_PROMPTS
+def prefix_partials(count, half, q, kt, vt):
+    pairs, _, rows, _ = q.shape
+    L = kt.shape[3]
+    bp = min(BLOCK_PROMPTS, pairs)
     return pl.pallas_call(
         prefix_kernel,
         grid_spec=pltpu.PrefetchScalarGridSpec(
-            num_scalar_prefetch=1,
-            grid=(P_ // bp,),
+            num_scalar_prefetch=2,
+            grid=(pairs // bp,),
             in_specs=[
-                pl.BlockSpec((bp, rows, HEAD_SIZE), lambda p, c: (p, 0, 0)),
-                pl.BlockSpec((bp, HEAD_SIZE, L), lambda p, c: (p, 0, 0)),
-                pl.BlockSpec((bp, HEAD_SIZE, L), lambda p, c: (p, 0, 0)),
+                pl.BlockSpec((bp, None, rows, HEAD_SIZE), lambda p, c, h: (p, h[0], 0, 0)),
+                pl.BlockSpec((bp, None, HEAD_SIZE, L), lambda p, c, h: (p, h[0], 0, 0)),
+                pl.BlockSpec((bp, None, HEAD_SIZE, L), lambda p, c, h: (p, h[0], 0, 0)),
             ],
-            out_specs=pl.BlockSpec((bp, PACK, rows), lambda p, c: (p, 0, 0)),
+            out_specs=pl.BlockSpec((bp, PACK, rows), lambda p, c, h: (p, 0, 0)),
         ),
-        out_shape=jax.ShapeDtypeStruct((P_, PACK, rows), jnp.float32),
-        cost_estimate=pl.CostEstimate(flops=4 * P_ * rows * L * HEAD_SIZE, transcendentals=P_ * rows * L,
-                                      bytes_accessed=2 * P_ * L * HEAD_SIZE * 2 + P_ * rows * HEAD_SIZE * 2 + P_ * PACK * rows * 4),
-    )(count, q, kt, vt)
+        out_shape=jax.ShapeDtypeStruct((pairs, PACK, rows), jnp.float32),
+        cost_estimate=pl.CostEstimate(flops=4 * pairs * rows * L * HEAD_SIZE, transcendentals=pairs * rows * L,
+                                      bytes_accessed=2 * pairs * L * HEAD_SIZE * 2 + pairs * rows * HEAD_SIZE * 2 + pairs * PACK * rows * 4),
+    )(count, half, q, kt, vt)
 
 
 def rms_scale(total_sq, width):
@@ -113,20 +113,15 @@
     return jnp.concatenate([y[..., :HEAD_SIZE, :], stats, pad], axis=-2)
 
 
-def reduce_partials(packed, axis, n, bits):
+def reduce_partials(cur, axis, n, left, bits):
     me = lax.axis_index(axis)
-    nb = len(bits)
-    cur = packed.reshape((2,) * nb + packed.shape[1:])
-    left = list(range(nb - 1, -1, -1))
-    for i, b in enumerate(bits):
+    left = list(left)
+    for b in bits:
         ax = left.index(b)
         own = (me >> b) & 1
         keep = lax.dynamic_index_in_dim(cur, own, ax, keepdims=False)
         send = lax.dynamic_index_in_dim(cur, 1 - own, ax, keepdims=False)
-        if i == 0:
-            got = exchange(send, axis, n, b)
-        else:
-            got = decode_partials(exchange(encode_partials(send), axis, n, b))
+        got = decode_partials(exchange(encode_partials(send), axis, n, b))
         cur = merge_partials(keep, got)
         left.remove(b)
     return cur
@@ -177,12 +172,27 @@
     reduce_order = gather_order[::-1]
 
     gathered = gather_rows(queries, "req", req_count, gather_order)
-    query_all = gathered.reshape(prompts, rows, HEAD_SIZE)
-    prefix_key_block = jnp.swapaxes(shared_prefix_keys.reshape(prompts, piece_len, HEAD_SIZE * kv_local), 1, 2)
-    prefix_value_block = jnp.swapaxes(shared_prefix_values.reshape(prompts, piece_len, HEAD_SIZE * kv_local), 1, 2)
+    pairs = prompts // 2
+    query_all = gathered.reshape(pairs, 2, rows, HEAD_SIZE)
+    prefix_key_block = jnp.swapaxes(
+        shared_prefix_keys.reshape(pairs, 2, piece_len, HEAD_SIZE * kv_local), 2, 3
+    )
+    prefix_value_block = jnp.swapaxes(
+        shared_prefix_values.reshape(pairs, 2, piece_len, HEAD_SIZE * kv_local), 2, 3
+    )
     count = jnp.clip(prompt_prefix_length - req_index * piece_len, 0, piece_len).astype(jnp.int32)
-    packed = prefix_partials(count, query_all, prefix_key_block, prefix_value_block)
-    own_part = reduce_partials(packed, "req", req_count, reduce_order)
+    own_low = (req_index & 1).astype(jnp.int32)
+    send_half = prefix_partials(
+        count, (1 - own_low)[None], query_all, prefix_key_block, prefix_value_block
+    )
+    got = exchange(send_half, "req", req_count, 0)
+    keep_half = prefix_partials(count, own_low[None], query_all, prefix_key_block, prefix_value_block)
+    merged = merge_partials(keep_half, got)
+    nb = req_count.bit_length() - 1
+    merged = merged.reshape((2,) * (nb - 1) + merged.shape[1:])
+    own_part = reduce_partials(
+        merged, "req", req_count, list(range(nb - 1, 0, -1)), [b for b in reduce_order if b != 0]
+    )
 
     query_own = queries.reshape(SAMPLE_COUNT, DECODE_TOKENS, kv_local, query_groups, HEAD_SIZE)
     tail_key_block = sample_tail_keys.reshape(SAMPLE_COUNT, TAIL_LENGTH, kv_local, HEAD_SIZE)

time: 129 us -> 126 us (0.977)
  local copies, waits for them, and re-layouts: 6.47 us -> 4.08 us
  starting transfers between devices: 33.7 us -> 32.1 us
  waiting for transfers between devices: 57.8 us -> 59.1 us
    ppermute x16, starting transfers between devices: 33.7 us -> 32.1 us  [exchange(): return lax.ppermute(x, axis, perm=[(i, i ^ 1 << bit) for i in range(n)])]
    dynamic_slice x2 -> x1, local copies, waits for them, and re-layouts: 1.5 us -> 0.02 us  [reduce_partials(): keep = lax.dynamic_index_in_dim(cur, own, ax, keepdims=False)]
    ppermute x16, waiting for transfers between devices: 57.8 us -> 59.1 us  [exchange(): return lax.ppermute(x, axis, perm=[(i, i ^ 1 << bit) for i in range(n)])]
    pallas_call x1 -> x2, Pallas kernels: 10.8 us -> 11.2 us  [prefix_partials(): pl.pallas_call(prefix_kernel, grid_spec=pltpu.PrefetchScalarGridSpec(num_...]
  transfers between devices with their start and end apart: 16 -> 16, of which waited for: 16 -> 15; matrix products, arithmetic and copies ran while one was open for 3% -> 3% of each run, Pallas kernels for 0% -> 4%
where the time goes in v6:
time: 126 us; the launch traced here: 125 us
  waiting for transfers between devices  59.1 us (47%)
  starting transfers between devices  32.1 us (25%)
  Pallas kernels  11.2 us (9%)
  other arithmetic  8.63 us (7%)
  matrix products  8.6 us (7%)
  local copies, waits for them, and re-layouts  4.08 us (3%)
    ppermute x16, waiting for transfers between devices, exchange(): return lax.ppermute(x, axis, perm=[(i, i ^ 1 << bit) for i in range(n)])  59.1 us
    ppermute x16, starting transfers between devices, exchange(): return lax.ppermute(x, axis, perm=[(i, i ^ 1 << bit) for i in range(n)])  32.1 us
    pallas_call x2, Pallas kernels, prefix_partials(): pl.pallas_call(prefix_kernel, grid_spec=pltpu.PrefetchScalarGridSpec(num_...  11.2 us
    dot_general x1, matrix products, on_device(): jnp.dot(hidden, down_weight, preferred_element_type=jnp.float32)  2.83 us
  transfers between devices with their start and end apart: 16, of which 15 were waited for; matrix products, arithmetic and copies ran while one was open for 3% of the time, Pallas kernels for 4%

profile of v6, /device:TPU:6, one launch (start us, length us, event | category | flops | bytes accessed | tf_op | source)
XLA Modules:
  0.0 125.0 jit_solution(5456801327206658655)
XLA Ops:
  0.7 7.3 %collective-permute-start = (bf16[1,32,320]{2,1,0:T(8,128)(2,1)}, bf16[1,32,320]{2,1,0:T(8,128)(2,1)S(1)}, u32[]{:S(2)}, u32[]{:S(2)}) collective-permute-start(bf16[1,32,320]{2,1,0:T(8,128)(2,1)} %bitcast.203), channel_id=1, source_target_pairs={{0,128},{8,136},{16,144},{24,152},{32,160},{40,168},{48,176},{56,1... | collective-permute-start | bytes 61448 | tf_op jit(solution)/shard_map/ppermute | solution.py:69
  7.9 2.0 %collective-permute-done = bf16[1,32,320]{2,1,0:T(8,128)(2,1)S(1)} collective-permute-done((bf16[1,32,320]{2,1,0:T(8,128)(2,1)}, bf16[1,32,320]{2,1,0:T(8,128)(2,1)S(1)}, u32[]{:S(2)}, u32[]{:S(2)}) %collective-permute-start) | collective-permute-done | bytes 20512 | tf_op jit(solution)/shard_map/ppermute | solution.py:69
  10.0 0.7 select_bitcast_fusion.5
  10.7 1.5 %collective-permute-start.1 = (bf16[2,1,32,320]{3,2,0,1:T(8,128)(2,1)S(1)}, bf16[2,1,32,320]{3,2,0,1:T(8,128)(2,1)S(1)}, u32[]{:S(2)}, u32[]{:S(2)}) collective-permute-start(bf16[2,1,32,320]{3,2,0,1:T(8,128)(2,1)S(1)} %fusion.36), channel_id=1, source_target_pairs={{0,16},{8,24},{16,0},{24,8},{32,48},{40,56},{48,32},{56,40},{64,80... | collective-permute-start | bytes 122888 | tf_op jit(solution)/shard_map/ppermute | solution.py:69
  12.2 4.2 %collective-permute-done.1 = bf16[2,1,32,320]{3,2,0,1:T(8,128)(2,1)S(1)} collective-permute-done((bf16[2,1,32,320]{3,2,0,1:T(8,128)(2,1)S(1)}, bf16[2,1,32,320]{3,2,0,1:T(8,128)(2,1)S(1)}, u32[]{:S(2)}, u32[]{:S(2)}) %collective-permute-start.1) | collective-permute-done | bytes 40992 | tf_op jit(solution)/shard_map/ppermute | solution.py:69
  16.5 2.1 %collective-permute-start.2 = (bf16[2,2,1,32,320]{4,3,1,0,2:T(8,128)(2,1)S(1)}, bf16[2,2,1,32,320]{4,3,1,0,2:T(8,128)(2,1)S(1)}, u32[]{:S(2)}, u32[]{:S(2)}) collective-permute-start(bf16[2,2,1,32,320]{4,3,1,0,2:T(8,128)(2,1)S(1)} %fusion.24), channel_id=1, source_target_pairs={{0,64},{8,72},{16,80},{24,88},{32,96},{40,104},{48,112},{56,120},{... | collective-permute-start | bytes 245768 | tf_op jit(solution)/shard_map/ppermute | solution.py:69
  18.6 4.6 %collective-permute-done.2 = bf16[2,2,1,32,320]{4,3,1,0,2:T(8,128)(2,1)S(1)} collective-permute-done((bf16[2,2,1,32,320]{4,3,1,0,2:T(8,128)(2,1)S(1)}, bf16[2,2,1,32,320]{4,3,1,0,2:T(8,128)(2,1)S(1)}, u32[]{:S(2)}, u32[]{:S(2)}) %collective-permute-start.2) | collective-permute-done | bytes 81952 | tf_op jit(solution)/shard_map/ppermute | solution.py:69
  23.5 5.6 %collective-permute-done.3 = bf16[2,2,2,1,32,320]{5,4,2,1,0,3:T(8,128)(2,1)S(1)} collective-permute-done((bf16[2,2,2,1,32,320]{5,4,2,1,0,3:T(8,128)(2,1)S(1)}, bf16[2,2,2,1,32,320]{5,4,2,1,0,3:T(8,128)(2,1)S(1)}, u32[]{:S(2)}, u32[]{:S(2)}) %collective-permute-start.3) | collective-permute-done | bytes 163872 | tf_op jit(solution)/shard_map/ppermute | solution.py:69
  29.2 0.8 fusion.12
  30.0 0.5 subtract_clamp_fusion.count_ref
  30.6 1.4 %collective-permute-done.4 = bf16[2,2,2,2,1,32,320]{6,5,3,2,1,0,4:T(8,128)(2,1)S(1)} collective-permute-done((bf16[2,2,2,2,1,32,320]{6,5,3,2,1,0,4:T(8,128)(2,1)}, bf16[2,2,2,2,1,32,320]{6,5,3,2,1,0,4:T(8,128)(2,1)S(1)}, u32[]{:S(2)}, u32[]{:S(2)}) %collective-permute-start.4) | collective-permute-done | bytes 327712 | tf_op jit(solution)/shard_map/ppermute | solution.py:69
  32.5 1.6 %reshape_reshape.3.q_ref = bf16[16,2,128,80]{3,2,1,0:T(8,128)(2,1)} reshape(bf16[2,2,2,2,2,1,32,320]{7,6,4,3,2,1,0,5:T(8,128)(2,1)S(1)} %copy.55) | data formatting | bytes 1310720 | tf_op jit(solution)/shard_map/reshape;reshape | solution.py:176
  34.1 5.7 %shard_map.177 = f32[16,88,128]{2,1,0:T(8,128)} custom-call(s32[32]{0:T(128)} %subtract_clamp_fusion.count_ref, s32[1]{0:T(128)} %bitcast.33.half_ref, bf16[16,2,128,80]{3,2,1,0:T(8,128)(2,1)} %reshape_reshape.3.q_ref, bf16[16,2,80,512]{3,2,1,0:T(8,128)(2,1)} %bitcast.192, bf16[16,2,80,512]{3,2,1,0:T(8,128)(2,1)} %bitcast.194), custom_call_target="tpu_custom_call" | custom-call | flops 335544320 | bytes 3670016 | tf_op jit(solution)/shard_map/pallas_call | solution.py:46
  40.1 1.3 %select_reduce_fusion = (f32[16,2,4]{2,1,0:T(2,128)S(1)}, f32[16,2,4,128]{3,2,1,0:T(4,128)S(1)}) fusion(pred[16,128]{1,0:T(8,128)(4,1)S(1)} %iota_compare_fusion, bf16[16,2,4,80]{3,2,1,0:T(4,128)(2,1)S(1)} %reshape.227, bf16[1,16,128,80]{2,3,1,0:T(8,128)(2,1)} %param.23), kind=kOutput, calls=%fused_computation.77 | convolution fusion | flops 2670464 | bytes 416256 | tf_op jit(solution)/shard_map/sjkgh,stkh->ksjgt/dot_general | solution.py:203
  41.3 5.5 %shard_map.176 = f32[16,88,128]{2,1,0:T(8,128)} custom-call(s32[32]{0:T(128)} %subtract_clamp_fusion.count_ref, s32[1]{0:T(128)} %bitcast.half_ref, bf16[16,2,128,80]{3,2,1,0:T(8,128)(2,1)} %reshape_reshape.3.q_ref, bf16[16,2,80,512]{3,2,1,0:T(8,128)(2,1)} %bitcast.193, bf16[16,2,80,512]{3,2,1,0:T(8,128)(2,1)} %bitcast.195), custom_call_target="tpu_custom_call" | custom-call | flops 335544320 | bytes 3670016 | tf_op jit(solution)/shard_map/pallas_call | solution.py:46
  46.9 0.9 subtract_exponential_fusion.1
  47.8 1.2 fusion.6
  48.9 0.9 fusion.18
  50.3 0.4 select_reduce_fusion.1
  50.7 6.4 %collective-permute-done.6 = bf16[2,2,2,88,128]{4,3,2,1,0:T(8,128)(2,1)S(1)} collective-permute-done((bf16[2,2,2,88,128]{4,3,2,1,0:T(8,128)(2,1)S(1)}, bf16[2,2,2,88,128]{4,3,2,1,0:T(8,128)(2,1)S(1)}, u32[]{:S(2)}, u32[]{:S(2)}) %collective-permute-start.6) | collective-permute-done | bytes 180256 | tf_op jit(solution)/shard_map/ppermute | solution.py:69
  57.4 1.9 %collective-permute-start.7 = (bf16[2,2,88,128]{3,2,0,1:T(8,128)(2,1)S(1)}, bf16[2,2,88,128]{3,2,0,1:T(8,128)(2,1)S(1)}, u32[]{:S(2)}, u32[]{:S(2)}) collective-permute-start(bf16[2,2,88,128]{3,2,0,1:T(8,128)(2,1)S(1)} %concatenate.44), channel_id=1, source_target_pairs={{0,64},{8,72},{16,80},{24,88},{32,96},{40,104},{48,112},{56,120},{... | collective-permute-start | bytes 270344 | tf_op jit(solution)/shard_map/ppermute | solution.py:69
  59.3 1.3 %fusion.9 = f32[16,2,4,80]{3,2,1,0:T(4,128)S(1)} fusion(bf16[1,16,128,80]{2,3,1,0:T(8,128)(2,1)} %param.24, f32[16,2,4,128]{3,2,1,0:T(4,128)S(1)} %get-tuple-element.40, f32[16,2,4]{2,1,0:T(2,128)S(1)} %max.65, pred[16,128]{1,0:T(8,128)(4,1)S(1)} %iota_compare_fusion), kind=kOutput, calls=%fused_computation.29 | convolution fusion | flops 2670592 | bytes 436736 | tf_op jit(solution)/shard_map/ksjgt,stkh->ksjgh/dot_general | solution.py:225
  60.6 3.8 %collective-permute-done.7 = bf16[2,2,88,128]{3,2,0,1:T(8,128)(2,1)S(1)} collective-permute-done((bf16[2,2,88,128]{3,2,0,1:T(8,128)(2,1)S(1)}, bf16[2,2,88,128]{3,2,0,1:T(8,128)(2,1)S(1)}, u32[]{:S(2)}, u32[]{:S(2)}) %collective-permute-start.7) | collective-permute-done | bytes 90144 | tf_op jit(solution)/shard_map/ppermute | solution.py:69
  64.7 1.5 %collective-permute-start.8 = (bf16[2,88,128]{2,1,0:T(8,128)(2,1)S(1)}, bf16[2,88,128]{2,1,0:T(8,128)(2,1)S(1)}, u32[]{:S(2)}, u32[]{:S(2)}) collective-permute-start(bf16[2,88,128]{2,1,0:T(8,128)(2,1)S(1)} %concatenate.47), channel_id=1, source_target_pairs={{0,16},{8,24},{16,0},{24,8},{32,48},{40,56},{48,32},{56,40},{64,80... | collective-permute-start | bytes 135176 | tf_op jit(solution)/shard_map/ppermute | solution.py:69
  66.4 3.9 %collective-permute-done.8 = bf16[2,88,128]{2,1,0:T(8,128)(2,1)S(1)} collective-permute-done((bf16[2,88,128]{2,1,0:T(8,128)(2,1)S(1)}, bf16[2,88,128]{2,1,0:T(8,128)(2,1)S(1)}, u32[]{:S(2)}, u32[]{:S(2)}) %collective-permute-start.8) | collective-permute-done | bytes 45088 | tf_op jit(solution)/shard_map/ppermute | solution.py:69
  70.6 6.0 %collective-permute-start.9 = (bf16[88,128]{1,0:T(8,128)(2,1)S(1)}, bf16[88,128]{1,0:T(8,128)(2,1)S(1)}, u32[]{:S(2)}, u32[]{:S(2)}) collective-permute-start(bf16[88,128]{1,0:T(8,128)(2,1)S(1)} %concatenate.50), channel_id=1, source_target_pairs={{0,128},{8,136},{16,144},{24,152},{32,160},{40,168},{48,176},{56,1... | collective-permute-start | bytes 67592 | tf_op jit(solution)/shard_map/ppermute | solution.py:69
  76.7 1.7 %collective-permute-done.9 = bf16[88,128]{1,0:T(8,128)(2,1)S(1)} collective-permute-done((bf16[88,128]{1,0:T(8,128)(2,1)S(1)}, bf16[88,128]{1,0:T(8,128)(2,1)S(1)}, u32[]{:S(2)}, u32[]{:S(2)}) %collective-permute-start.9) | collective-permute-done | bytes 22560 | tf_op jit(solution)/shard_map/ppermute | solution.py:69
  78.4 0.5 broadcast.97
  78.9 0.7 fusion.57
  80.0 0.3 fusion.5
  80.5 2.0 %convolution_convert_fusion.1 = bf16[32,2560]{1,0:T(8,128)(2,1)S(1)} fusion(bf16[32,320]{1,0:T(8,128)(2,1)S(1)} %reshape_transpose.3, bf16[320,2560]{1,0:T(8,128)(2,1)} %param.27), kind=kOutput, calls=%fused_computation.1 | convolution fusion | flops 52510720 | bytes 1822720 | tf_op jit(solution)/shard_map/dot_general | solution.py:247
  82.4 1.1 collective-permute-start.10
  83.5 4.5 %collective-permute-done.10 = bf16[32,2560]{1,0:T(8,128)(2,1)S(1)} collective-permute-done((bf16[32,2560]{1,0:T(8,128)(2,1)S(1)}, bf16[32,2560]{1,0:T(8,128)(2,1)S(1)}, u32[]{:S(2)}, u32[]{:S(2)}) %collective-permute-start.10) | collective-permute-done | bytes 163872 | tf_op jit(solution)/shard_map/ppermute | solution.py:69
  88.0 3.3 %collective-permute-start.11 = (bf16[32,2560]{1,0:T(8,128)(2,1)S(1)}, bf16[32,2560]{1,0:T(8,128)(2,1)S(1)}, u32[]{:S(2)}, u32[]{:S(2)}) collective-permute-start(bf16[32,2560]{1,0:T(8,128)(2,1)S(1)} %add_convert_fusion.5), channel_id=1, source_target_pairs={{0,2},{1,3},{2,0},{3,1},{4,6},{5,7},{6,4},{7,5},{8,10},{9,11},{10,... | collective-permute-start | bytes 491528 | tf_op jit(solution)/shard_map/ppermute | solution.py:69
  91.3 4.5 %collective-permute-done.11 = bf16[32,2560]{1,0:T(8,128)(2,1)S(1)} collective-permute-done((bf16[32,2560]{1,0:T(8,128)(2,1)S(1)}, bf16[32,2560]{1,0:T(8,128)(2,1)S(1)}, u32[]{:S(2)}, u32[]{:S(2)}) %collective-permute-start.11) | collective-permute-done | bytes 163872 | tf_op jit(solution)/shard_map/ppermute | solution.py:69
  95.9 1.3 %collective-permute-start.12 = (bf16[32,2560]{1,0:T(8,128)(2,1)S(1)}, bf16[32,2560]{1,0:T(8,128)(2,1)S(1)}, u32[]{:S(2)}, u32[]{:S(2)}) collective-permute-start(bf16[32,2560]{1,0:T(8,128)(2,1)S(1)} %add_convert_fusion.4), channel_id=1, source_target_pairs={{0,1},{1,0},{2,3},{3,2},{4,5},{5,4},{6,7},{7,6},{8,9},{9,8},{10,11... | collective-permute-start | bytes 491528 | tf_op jit(solution)/shard_map/ppermute | solution.py:69
  97.2 4.1 %collective-permute-done.12 = bf16[32,2560]{1,0:T(8,128)(2,1)S(1)} collective-permute-done((bf16[32,2560]{1,0:T(8,128)(2,1)S(1)}, bf16[32,2560]{1,0:T(8,128)(2,1)S(1)}, u32[]{:S(2)}, u32[]{:S(2)}) %collective-permute-start.12) | collective-permute-done | bytes 163872 | tf_op jit(solution)/shard_map/ppermute | solution.py:69
  101.6 0.5 fusion.58
  102.2 2.8 %convolution_convert_fusion = bf16[32,2560]{1,0:T(8,128)(2,1)S(1)} fusion(bf16[512,2560]{1,0:T(8,128)(2,1)S(1)} %copy-done, bf16[32,2560]{1,0:T(8,128)(2,1)S(1)} %multiply_convert_fusion, bf16[2560,512]{1,0:T(8,128)(2,1)} %param.29, f32[32,512]{1,0:T(8,128)S(1)} %fusion.58), kind=kOutput, calls=%fused_computation | convolution fusion | flops 167952384 | bytes 5636096 | tf_op jit(solution)/shard_map/dot_general | solution.py:261
  105.0 0.9 collective-permute-start.13
  105.9 4.5 %collective-permute-done.13 = bf16[32,2560]{1,0:T(8,128)(2,1)S(1)} collective-permute-done((bf16[32,2560]{1,0:T(8,128)(2,1)S(1)}, bf16[32,2560]{1,0:T(8,128)(2,1)S(1)}, u32[]{:S(2)}, u32[]{:S(2)}) %collective-permute-start.13) | collective-permute-done | bytes 163872 | tf_op jit(solution)/shard_map/ppermute | solution.py:69
  110.5 4.1 %collective-permute-start.14 = (bf16[32,2560]{1,0:T(8,128)(2,1)S(1)}, bf16[32,2560]{1,0:T(8,128)(2,1)S(1)}, u32[]{:S(2)}, u32[]{:S(2)}) collective-permute-start(bf16[32,2560]{1,0:T(8,128)(2,1)S(1)} %add_convert_fusion.2), channel_id=1, source_target_pairs={{0,2},{1,3},{2,0},{3,1},{4,6},{5,7},{6,4},{7,5},{8,10},{9,11},{10,... | collective-permute-start | bytes 491528 | tf_op jit(solution)/shard_map/ppermute | solution.py:69
  114.5 3.3 %collective-permute-done.14 = bf16[32,2560]{1,0:T(8,128)(2,1)S(1)} collective-permute-done((bf16[32,2560]{1,0:T(8,128)(2,1)S(1)}, bf16[32,2560]{1,0:T(8,128)(2,1)S(1)}, u32[]{:S(2)}, u32[]{:S(2)}) %collective-permute-start.14) | collective-permute-done | bytes 163872 | tf_op jit(solution)/shard_map/ppermute | solution.py:69
  117.9 0.8 collective-permute-start.15
  118.7 4.6 %collective-permute-done.15 = bf16[32,2560]{1,0:T(8,128)(2,1)S(1)} collective-permute-done((bf16[32,2560]{1,0:T(8,128)(2,1)S(1)}, bf16[32,2560]{1,0:T(8,128)(2,1)S(1)}, u32[]{:S(2)}, u32[]{:S(2)}) %collective-permute-start.15) | collective-permute-done | bytes 163872 | tf_op jit(solution)/shard_map/ppermute | solution.py:69
  123.3 0.2 multiply_reduce_fusion.1
  123.5 0.7 dynamic-slice_convert_fusion
  124.2 0.7 multiply_reduce_fusion
  (109 shorter events, 3.6 us)
Async XLA Ops:
  0.6 101.5 %copy-start = (bf16[512,2560]{1,0:T(8,128)(2,1)S(1)}, bf16[512,2560]{1,0:T(8,128)(2,1)}, u32[]{:S(2)}) copy-start(bf16[512,2560]{1,0:T(8,128)(2,1)} %param.30) | copy-start | bytes 7864324
  0.6 29.4 %copy-start.10 = (s32[32]{0:T(128)S(1)}, s32[32]{0:T(128)}, u32[]{:S(2)}) copy-start(s32[32]{0:T(128)} %param.25) | copy-start | bytes 388
  0.7 9.3 %collective-permute-start = (bf16[1,32,320]{2,1,0:T(8,128)(2,1)}, bf16[1,32,320]{2,1,0:T(8,128)(2,1)S(1)}, u32[]{:S(2)}, u32[]{:S(2)}) collective-permute-start(bf16[1,32,320]{2,1,0:T(8,128)(2,1)} %bitcast.203), channel_id=1, source_target_pairs={{0,128},{8,136},{16,144},{24,152},{32,160},{40,168},{48,176},{56,1... | collective-permute-start | bytes 61448 | tf_op jit(solution)/shard_map/ppermute | solution.py:69
  10.7 5.7 %collective-permute-start.1 = (bf16[2,1,32,320]{3,2,0,1:T(8,128)(2,1)S(1)}, bf16[2,1,32,320]{3,2,0,1:T(8,128)(2,1)S(1)}, u32[]{:S(2)}, u32[]{:S(2)}) collective-permute-start(bf16[2,1,32,320]{3,2,0,1:T(8,128)(2,1)S(1)} %fusion.36), channel_id=1, source_target_pairs={{0,16},{8,24},{16,0},{24,8},{32,48},{40,56},{48,32},{56,40},{64,80... | collective-permute-start | bytes 122888 | tf_op jit(solution)/shard_map/ppermute | solution.py:69
  16.5 6.8 %collective-permute-start.2 = (bf16[2,2,1,32,320]{4,3,1,0,2:T(8,128)(2,1)S(1)}, bf16[2,2,1,32,320]{4,3,1,0,2:T(8,128)(2,1)S(1)}, u32[]{:S(2)}, u32[]{:S(2)}) collective-permute-start(bf16[2,2,1,32,320]{4,3,1,0,2:T(8,128)(2,1)S(1)} %fusion.24), channel_id=1, source_target_pairs={{0,64},{8,72},{16,80},{24,88},{32,96},{40,104},{48,112},{56,120},{... | collective-permute-start | bytes 245768 | tf_op jit(solution)/shard_map/ppermute | solution.py:69
  23.3 5.8 %collective-permute-start.3 = (bf16[2,2,2,1,32,320]{5,4,2,1,0,3:T(8,128)(2,1)S(1)}, bf16[2,2,2,1,32,320]{5,4,2,1,0,3:T(8,128)(2,1)S(1)}, u32[]{:S(2)}, u32[]{:S(2)}) collective-permute-start(bf16[2,2,2,1,32,320]{5,4,2,1,0,3:T(8,128)(2,1)S(1)} %fusion.15), channel_id=1, source_target_pairs={{0,32},{8,40},{16,48},{24,56},{32,0},{40,8},{48,16},{56,24},{64,96... | collective-permute-start | bytes 491528 | tf_op jit(solution)/shard_map/ppermute | solution.py:69
  30.0 1.9 %collective-permute-start.4 = (bf16[2,2,2,2,1,32,320]{6,5,3,2,1,0,4:T(8,128)(2,1)}, bf16[2,2,2,2,1,32,320]{6,5,3,2,1,0,4:T(8,128)(2,1)S(1)}, u32[]{:S(2)}, u32[]{:S(2)}) collective-permute-start(bf16[2,2,2,2,1,32,320]{6,5,3,2,1,0,4:T(8,128)(2,1)} %fusion.12), channel_id=1, source_target_pairs={{0,8},{8,0},{16,24},{24,16},{32,40},{40,32},{48,56},{56,48},{64,72... | collective-permute-start | bytes 983048 | tf_op jit(solution)/shard_map/ppermute | solution.py:69
  34.1 5.8 %copy-start.3 = (bf16[32,320]{1,0:T(8,128)(2,1)S(1)}, bf16[32,320]{1,0:T(8,128)(2,1)}, u32[]{:S(2)}) copy-start(bf16[32,320]{1,0:T(8,128)(2,1)} %param.18) | copy-start | bytes 61444
  34.1 5.9 %copy-start.7 = (s32[1,16]{1,0:T(1,128)S(1)}, s32[1,16]{1,0:T(1,128)}, u32[]{:S(2)}) copy-start(s32[1,16]{1,0:T(1,128)} %param.26) | copy-start | bytes 196
  39.7 7.1 %collective-permute-start.5 = (f32[16,88,128]{2,1,0:T(8,128)}, f32[16,88,128]{2,1,0:T(8,128)S(1)}, u32[]{:S(2)}, u32[]{:S(2)}) collective-permute-start(f32[16,88,128]{2,1,0:T(8,128)} %shard_map.177), channel_id=1, source_target_pairs={{0,8},{8,0},{16,24},{24,16},{32,40},{40,32},{48,56},{56,48},{64,72... | collective-permute-start | bytes 2162696 | tf_op jit(solution)/shard_map/ppermute | solution.py:69
  47.7 2.5 %copy-start.8 = (bf16[32,80]{1,0:T(8,128)(2,1)S(1)}, bf16[32,80]{1,0:T(8,128)(2,1)}, u32[]{:S(2)}) copy-start(bf16[32,80]{1,0:T(8,128)(2,1)} %param.19) | copy-start | bytes 15364
  50.1 6.9 %collective-permute-start.6 = (bf16[2,2,2,88,128]{4,3,2,1,0:T(8,128)(2,1)S(1)}, bf16[2,2,2,88,128]{4,3,2,1,0:T(8,128)(2,1)S(1)}, u32[]{:S(2)}, u32[]{:S(2)}) collective-permute-start(bf16[2,2,2,88,128]{4,3,2,1,0:T(8,128)(2,1)S(1)} %concatenate.41), channel_id=1, source_target_pairs={{0,32},{8,40},{16,48},{24,56},{32,0},{40,8},{48,16},{56,24},{64,96... | collective-permute-start | bytes 540680 | tf_op jit(solution)/shard_map/ppermute | solution.py:69
  57.3 22.7 %copy-start.9 = (bf16[32,80]{1,0:T(8,128)(2,1)S(1)}, bf16[32,80]{1,0:T(8,128)(2,1)}, u32[]{:S(2)}) copy-start(bf16[32,80]{1,0:T(8,128)(2,1)} %param.20) | copy-start | bytes 15364
  57.4 7.0 %collective-permute-start.7 = (bf16[2,2,88,128]{3,2,0,1:T(8,128)(2,1)S(1)}, bf16[2,2,88,128]{3,2,0,1:T(8,128)(2,1)S(1)}, u32[]{:S(2)}, u32[]{:S(2)}) collective-permute-start(bf16[2,2,88,128]{3,2,0,1:T(8,128)(2,1)S(1)} %concatenate.44), channel_id=1, source_target_pairs={{0,64},{8,72},{16,80},{24,88},{32,96},{40,104},{48,112},{56,120},{... | collective-permute-start | bytes 270344 | tf_op jit(solution)/shard_map/ppermute | solution.py:69
  64.7 5.6 %collective-permute-start.8 = (bf16[2,88,128]{2,1,0:T(8,128)(2,1)S(1)}, bf16[2,88,128]{2,1,0:T(8,128)(2,1)S(1)}, u32[]{:S(2)}, u32[]{:S(2)}) collective-permute-start(bf16[2,88,128]{2,1,0:T(8,128)(2,1)S(1)} %concatenate.47), channel_id=1, source_target_pairs={{0,16},{8,24},{16,0},{24,8},{32,48},{40,56},{48,32},{56,40},{64,80... | collective-permute-start | bytes 135176 | tf_op jit(solution)/shard_map/ppermute | solution.py:69
  70.6 7.8 %collective-permute-start.9 = (bf16[88,128]{1,0:T(8,128)(2,1)S(1)}, bf16[88,128]{1,0:T(8,128)(2,1)S(1)}, u32[]{:S(2)}, u32[]{:S(2)}) collective-permute-start(bf16[88,128]{1,0:T(8,128)(2,1)S(1)} %concatenate.50), channel_id=1, source_target_pairs={{0,128},{8,136},{16,144},{24,152},{32,160},{40,168},{48,176},{56,1... | collective-permute-start | bytes 67592 | tf_op jit(solution)/shard_map/ppermute | solution.py:69
  80.0 21.3 %copy-start.2 = (bf16[32,2560]{1,0:T(8,128)(2,1)S(1)}, bf16[32,2560]{1,0:T(8,128)(2,1)}, u32[]{:S(2)}) copy-start(bf16[32,2560]{1,0:T(8,128)(2,1)} %param.17) | copy-start | bytes 491524
  80.0 21.5 %copy-start.6 = (f32[2560]{0:T(1024)S(1)}, f32[2560]{0:T(1024)}, u32[]{:S(2)}) copy-start(f32[2560]{0:T(1024)} %param.31) | copy-start | bytes 30724
  80.4 21.2 %copy-start.1 = (bf16[2560,512]{1,0:T(8,128)(2,1)S(1)}, bf16[2560,512]{1,0:T(8,128)(2,1)}, u32[]{:S(2)}) copy-start(bf16[2560,512]{1,0:T(8,128)(2,1)} %param.28) | copy-start | bytes 7864324
  82.4 5.6 %collective-permute-start.10 = (bf16[32,2560]{1,0:T(8,128)(2,1)S(1)}, bf16[32,2560]{1,0:T(8,128)(2,1)S(1)}, u32[]{:S(2)}, u32[]{:S(2)}) collective-permute-start(bf16[32,2560]{1,0:T(8,128)(2,1)S(1)} %convolution_convert_fusion.1), channel_id=1, source_target_pairs={{0,4},{1,5},{2,6},{3,7},{4,0},{5,1},{6,2},{7,3},{8,12},{9,13},{10,... | collective-permute-start | bytes 491528 | tf_op jit(solution)/shard_map/ppermute | solution.py:69
  88.0 7.8 %collective-permute-start.11 = (bf16[32,2560]{1,0:T(8,128)(2,1)S(1)}, bf16[32,2560]{1,0:T(8,128)(2,1)S(1)}, u32[]{:S(2)}, u32[]{:S(2)}) collective-permute-start(bf16[32,2560]{1,0:T(8,128)(2,1)S(1)} %add_convert_fusion.5), channel_id=1, source_target_pairs={{0,2},{1,3},{2,0},{3,1},{4,6},{5,7},{6,4},{7,5},{8,10},{9,11},{10,... | collective-permute-start | bytes 491528 | tf_op jit(solution)/shard_map/ppermute | solution.py:69
  95.9 5.4 %collective-permute-start.12 = (bf16[32,2560]{1,0:T(8,128)(2,1)S(1)}, bf16[32,2560]{1,0:T(8,128)(2,1)S(1)}, u32[]{:S(2)}, u32[]{:S(2)}) collective-permute-start(bf16[32,2560]{1,0:T(8,128)(2,1)S(1)} %add_convert_fusion.4), channel_id=1, source_target_pairs={{0,1},{1,0},{2,3},{3,2},{4,5},{5,4},{6,7},{7,6},{8,9},{9,8},{10,11... | collective-permute-start | bytes 491528 | tf_op jit(solution)/shard_map/ppermute | solution.py:69
  102.2 22.1 %copy-start.4 = (f32[2560]{0:T(1024)S(1)}, f32[2560]{0:T(1024)}, u32[]{:S(2)}) copy-start(f32[2560]{0:T(1024)} %param.33) | copy-start | bytes 30724
  102.2 22.0 %copy-start.5 = (f32[2560]{0:T(1024)S(1)}, f32[2560]{0:T(1024)}, u32[]{:S(2)}) copy-start(f32[2560]{0:T(1024)} %param.32) | copy-start | bytes 30724
  105.0 5.4 %collective-permute-start.13 = (bf16[32,2560]{1,0:T(8,128)(2,1)S(1)}, bf16[32,2560]{1,0:T(8,128)(2,1)S(1)}, u32[]{:S(2)}, u32[]{:S(2)}) collective-permute-start(bf16[32,2560]{1,0:T(8,128)(2,1)S(1)} %convolution_convert_fusion), channel_id=1, source_target_pairs={{0,4},{1,5},{2,6},{3,7},{4,0},{5,1},{6,2},{7,3},{8,12},{9,13},{10,... | collective-permute-start | bytes 491528 | tf_op jit(solution)/shard_map/ppermute | solution.py:69
  110.5 7.4 %collective-permute-start.14 = (bf16[32,2560]{1,0:T(8,128)(2,1)S(1)}, bf16[32,2560]{1,0:T(8,128)(2,1)S(1)}, u32[]{:S(2)}, u32[]{:S(2)}) collective-permute-start(bf16[32,2560]{1,0:T(8,128)(2,1)S(1)} %add_convert_fusion.2), channel_id=1, source_target_pairs={{0,2},{1,3},{2,0},{3,1},{4,6},{5,7},{6,4},{7,5},{8,10},{9,11},{10,... | collective-permute-start | bytes 491528 | tf_op jit(solution)/shard_map/ppermute | solution.py:69
  117.9 5.4 %collective-permute-start.15 = (bf16[32,2560]{1,0:T(8,128)(2,1)S(1)}, bf16[32,2560]{1,0:T(8,128)(2,1)S(1)}, u32[]{:S(2)}, u32[]{:S(2)}) collective-permute-start(bf16[32,2560]{1,0:T(8,128)(2,1)S(1)} %add_convert_fusion.1), channel_id=1, source_target_pairs={{0,1},{1,0},{2,3},{3,2},{4,5},{5,4},{6,7},{7,6},{8,9},{9,8},{10,11... | collective-permute-start | bytes 491528 | tf_op jit(solution)/shard_map/ppermute | solution.py:69

commit v7 on v6

--- a/solution.py
+++ b/solution.py
@@ -127,10 +127,10 @@
     return cur
 
 
-def allreduce_bf16(x, axis, n, bits):
+def allreduce_bf16(x, axis, n, masks):
     cur = x.astype(jnp.bfloat16)
-    for b in bits:
-        other = exchange(cur, axis, n, b)
+    for m in masks:
+        other = lax.ppermute(cur, axis, perm=[(i, i ^ m) for i in range(n)])
         cur = (cur.astype(jnp.float32) + other.astype(jnp.float32)).astype(jnp.bfloat16)
     return cur
 
@@ -247,7 +247,7 @@
     projected = jnp.dot(attention_layer, out_weight, preferred_element_type=jnp.float32)
     mlp_index = lax.axis_index("mlp")
     share = D // mlp_count
-    mlp_order = list(range(mlp_bits - 1, -1, -1))
+    mlp_order = [4, 1, 3] if mlp_count == 8 else [1 << b for b in range(mlp_bits)]
     mid = residual_in.astype(jnp.float32) + allreduce_bf16(
         projected, "mlp", mlp_count, mlp_order
     ).astype(jnp.float32)

time: 126 us -> 123 us (0.976)
    ppermute x16 -> x10, waiting for transfers between devices: 59.1 us -> 33.7 us  [exchange(): return lax.ppermute(x, axis, perm=[(i, i ^ 1 << bit) for i in range(n)])]
    ppermute x0 -> x6, waiting for transfers between devices: none -> 24.7 us  [allreduce_bf16(): other = lax.ppermute(cur, axis, perm=[(i, i ^ m) for i in range(n)])]
    ppermute x16 -> x10, starting transfers between devices: 32.1 us -> 20.6 us  [exchange(): return lax.ppermute(x, axis, perm=[(i, i ^ 1 << bit) for i in range(n)])]
    ppermute x0 -> x6, starting transfers between devices: none -> 10.3 us  [allreduce_bf16(): other = lax.ppermute(cur, axis, perm=[(i, i ^ m) for i in range(n)])]
where the time goes in v7:
time: 123 us
  waiting for transfers between devices  58.3 us (47%)
  starting transfers between devices  30.9 us (25%)
  Pallas kernels  11.2 us (9%)
  other arithmetic  8.63 us (7%)
  matrix products  8.6 us (7%)
  local copies, waits for them, and re-layouts  4.08 us (3%)
    ppermute x10, waiting for transfers between devices, exchange(): return lax.ppermute(x, axis, perm=[(i, i ^ 1 << bit) for i in range(n)])  33.7 us
    ppermute x6, waiting for transfers between devices, allreduce_bf16(): other = lax.ppermute(cur, axis, perm=[(i, i ^ m) for i in range(n)])  24.7 us
    ppermute x10, starting transfers between devices, exchange(): return lax.ppermute(x, axis, perm=[(i, i ^ 1 << bit) for i in range(n)])  20.6 us
    pallas_call x2, Pallas kernels, prefix_partials(): pl.pallas_call(prefix_kernel, grid_spec=pltpu.PrefetchScalarGridSpec(num_...  11.2 us
    ppermute x6, starting transfers between devices, allreduce_bf16(): other = lax.ppermute(cur, axis, perm=[(i, i ^ m) for i in range(n)])  10.3 us
    dot_general x1, matrix products, on_device(): jnp.dot(hidden, down_weight, preferred_element_type=jnp.float32)  2.82 us
  transfers between devices with their start and end apart: 16, of which 15 were waited for; matrix products, arithmetic and copies ran while one was open for 3% of the time, Pallas kernels for 4%

profile of v7, /device:TPU:6, one launch (start us, length us, event | category | flops | bytes accessed | tf_op | source)
XLA Modules:
  0.0 123.0 jit_solution(6328170124454661961)
XLA Ops:
  0.7 7.3 %collective-permute-start = (bf16[1,32,320]{2,1,0:T(8,128)(2,1)}, bf16[1,32,320]{2,1,0:T(8,128)(2,1)S(1)}, u32[]{:S(2)}, u32[]{:S(2)}) collective-permute-start(bf16[1,32,320]{2,1,0:T(8,128)(2,1)} %bitcast.203), channel_id=1, source_target_pairs={{0,128},{8,136},{16,144},{24,152},{32,160},{40,168},{48,176},{56,1... | collective-permute-start | bytes 61448 | tf_op jit(solution)/shard_map/ppermute | solution.py:69
  7.9 2.0 %collective-permute-done = bf16[1,32,320]{2,1,0:T(8,128)(2,1)S(1)} collective-permute-done((bf16[1,32,320]{2,1,0:T(8,128)(2,1)}, bf16[1,32,320]{2,1,0:T(8,128)(2,1)S(1)}, u32[]{:S(2)}, u32[]{:S(2)}) %collective-permute-start) | collective-permute-done | bytes 20512 | tf_op jit(solution)/shard_map/ppermute | solution.py:69
  10.0 0.7 select_bitcast_fusion.5
  10.7 1.5 %collective-permute-start.1 = (bf16[2,1,32,320]{3,2,0,1:T(8,128)(2,1)S(1)}, bf16[2,1,32,320]{3,2,0,1:T(8,128)(2,1)S(1)}, u32[]{:S(2)}, u32[]{:S(2)}) collective-permute-start(bf16[2,1,32,320]{3,2,0,1:T(8,128)(2,1)S(1)} %fusion.36), channel_id=1, source_target_pairs={{0,16},{8,24},{16,0},{24,8},{32,48},{40,56},{48,32},{56,40},{64,80... | collective-permute-start | bytes 122888 | tf_op jit(solution)/shard_map/ppermute | solution.py:69
  12.2 4.2 %collective-permute-done.1 = bf16[2,1,32,320]{3,2,0,1:T(8,128)(2,1)S(1)} collective-permute-done((bf16[2,1,32,320]{3,2,0,1:T(8,128)(2,1)S(1)}, bf16[2,1,32,320]{3,2,0,1:T(8,128)(2,1)S(1)}, u32[]{:S(2)}, u32[]{:S(2)}) %collective-permute-start.1) | collective-permute-done | bytes 40992 | tf_op jit(solution)/shard_map/ppermute | solution.py:69
  16.5 2.1 %collective-permute-start.2 = (bf16[2,2,1,32,320]{4,3,1,0,2:T(8,128)(2,1)S(1)}, bf16[2,2,1,32,320]{4,3,1,0,2:T(8,128)(2,1)S(1)}, u32[]{:S(2)}, u32[]{:S(2)}) collective-permute-start(bf16[2,2,1,32,320]{4,3,1,0,2:T(8,128)(2,1)S(1)} %fusion.24), channel_id=1, source_target_pairs={{0,64},{8,72},{16,80},{24,88},{32,96},{40,104},{48,112},{56,120},{... | collective-permute-start | bytes 245768 | tf_op jit(solution)/shard_map/ppermute | solution.py:69
  18.6 4.6 %collective-permute-done.2 = bf16[2,2,1,32,320]{4,3,1,0,2:T(8,128)(2,1)S(1)} collective-permute-done((bf16[2,2,1,32,320]{4,3,1,0,2:T(8,128)(2,1)S(1)}, bf16[2,2,1,32,320]{4,3,1,0,2:T(8,128)(2,1)S(1)}, u32[]{:S(2)}, u32[]{:S(2)}) %collective-permute-start.2) | collective-permute-done | bytes 81952 | tf_op jit(solution)/shard_map/ppermute | solution.py:69
  23.5 5.6 %collective-permute-done.3 = bf16[2,2,2,1,32,320]{5,4,2,1,0,3:T(8,128)(2,1)S(1)} collective-permute-done((bf16[2,2,2,1,32,320]{5,4,2,1,0,3:T(8,128)(2,1)S(1)}, bf16[2,2,2,1,32,320]{5,4,2,1,0,3:T(8,128)(2,1)S(1)}, u32[]{:S(2)}, u32[]{:S(2)}) %collective-permute-start.3) | collective-permute-done | bytes 163872 | tf_op jit(solution)/shard_map/ppermute | solution.py:69
  29.2 0.8 fusion.12
  30.0 0.5 subtract_clamp_fusion.count_ref
  30.6 1.4 %collective-permute-done.4 = bf16[2,2,2,2,1,32,320]{6,5,3,2,1,0,4:T(8,128)(2,1)S(1)} collective-permute-done((bf16[2,2,2,2,1,32,320]{6,5,3,2,1,0,4:T(8,128)(2,1)}, bf16[2,2,2,2,1,32,320]{6,5,3,2,1,0,4:T(8,128)(2,1)S(1)}, u32[]{:S(2)}, u32[]{:S(2)}) %collective-permute-start.4) | collective-permute-done | bytes 327712 | tf_op jit(solution)/shard_map/ppermute | solution.py:69
  32.5 1.6 %reshape_reshape.3.q_ref = bf16[16,2,128,80]{3,2,1,0:T(8,128)(2,1)} reshape(bf16[2,2,2,2,2,1,32,320]{7,6,4,3,2,1,0,5:T(8,128)(2,1)S(1)} %copy.55) | data formatting | bytes 1310720 | tf_op jit(solution)/shard_map/reshape;reshape | solution.py:176
  34.1 5.7 %shard_map.177 = f32[16,88,128]{2,1,0:T(8,128)} custom-call(s32[32]{0:T(128)} %subtract_clamp_fusion.count_ref, s32[1]{0:T(128)} %bitcast.33.half_ref, bf16[16,2,128,80]{3,2,1,0:T(8,128)(2,1)} %reshape_reshape.3.q_ref, bf16[16,2,80,512]{3,2,1,0:T(8,128)(2,1)} %bitcast.192, bf16[16,2,80,512]{3,2,1,0:T(8,128)(2,1)} %bitcast.194), custom_call_target="tpu_custom_call" | custom-call | flops 335544320 | bytes 3670016 | tf_op jit(solution)/shard_map/pallas_call | solution.py:46
  40.1 1.3 %select_reduce_fusion = (f32[16,2,4]{2,1,0:T(2,128)S(1)}, f32[16,2,4,128]{3,2,1,0:T(4,128)S(1)}) fusion(pred[16,128]{1,0:T(8,128)(4,1)S(1)} %iota_compare_fusion, bf16[16,2,4,80]{3,2,1,0:T(4,128)(2,1)S(1)} %reshape.227, bf16[1,16,128,80]{2,3,1,0:T(8,128)(2,1)} %param.23), kind=kOutput, calls=%fused_computation.77 | convolution fusion | flops 2670464 | bytes 416256 | tf_op jit(solution)/shard_map/sjkgh,stkh->ksjgt/dot_general | solution.py:203
  41.3 5.5 %shard_map.176 = f32[16,88,128]{2,1,0:T(8,128)} custom-call(s32[32]{0:T(128)} %subtract_clamp_fusion.count_ref, s32[1]{0:T(128)} %bitcast.half_ref, bf16[16,2,128,80]{3,2,1,0:T(8,128)(2,1)} %reshape_reshape.3.q_ref, bf16[16,2,80,512]{3,2,1,0:T(8,128)(2,1)} %bitcast.193, bf16[16,2,80,512]{3,2,1,0:T(8,128)(2,1)} %bitcast.195), custom_call_target="tpu_custom_call" | custom-call | flops 335544320 | bytes 3670016 | tf_op jit(solution)/shard_map/pallas_call | solution.py:46
  46.9 0.9 subtract_exponential_fusion.1
  47.8 1.2 fusion.6
  48.9 0.9 fusion.18
  50.3 0.4 select_reduce_fusion.1
  50.7 6.4 %collective-permute-done.6 = bf16[2,2,2,88,128]{4,3,2,1,0:T(8,128)(2,1)S(1)} collective-permute-done((bf16[2,2,2,88,128]{4,3,2,1,0:T(8,128)(2,1)S(1)}, bf16[2,2,2,88,128]{4,3,2,1,0:T(8,128)(2,1)S(1)}, u32[]{:S(2)}, u32[]{:S(2)}) %collective-permute-start.6) | collective-permute-done | bytes 180256 | tf_op jit(solution)/shard_map/ppermute | solution.py:69
  57.4 1.9 %collective-permute-start.7 = (bf16[2,2,88,128]{3,2,0,1:T(8,128)(2,1)S(1)}, bf16[2,2,88,128]{3,2,0,1:T(8,128)(2,1)S(1)}, u32[]{:S(2)}, u32[]{:S(2)}) collective-permute-start(bf16[2,2,88,128]{3,2,0,1:T(8,128)(2,1)S(1)} %concatenate.44), channel_id=1, source_target_pairs={{0,64},{8,72},{16,80},{24,88},{32,96},{40,104},{48,112},{56,120},{... | collective-permute-start | bytes 270344 | tf_op jit(solution)/shard_map/ppermute | solution.py:69
  59.3 1.3 %fusion.9 = f32[16,2,4,80]{3,2,1,0:T(4,128)S(1)} fusion(bf16[1,16,128,80]{2,3,1,0:T(8,128)(2,1)} %param.24, f32[16,2,4,128]{3,2,1,0:T(4,128)S(1)} %get-tuple-element.40, f32[16,2,4]{2,1,0:T(2,128)S(1)} %max.65, pred[16,128]{1,0:T(8,128)(4,1)S(1)} %iota_compare_fusion), kind=kOutput, calls=%fused_computation.29 | convolution fusion | flops 2670592 | bytes 436736 | tf_op jit(solution)/shard_map/ksjgt,stkh->ksjgh/dot_general | solution.py:225
  60.6 3.8 %collective-permute-done.7 = bf16[2,2,88,128]{3,2,0,1:T(8,128)(2,1)S(1)} collective-permute-done((bf16[2,2,88,128]{3,2,0,1:T(8,128)(2,1)S(1)}, bf16[2,2,88,128]{3,2,0,1:T(8,128)(2,1)S(1)}, u32[]{:S(2)}, u32[]{:S(2)}) %collective-permute-start.7) | collective-permute-done | bytes 90144 | tf_op jit(solution)/shard_map/ppermute | solution.py:69
  64.7 1.5 %collective-permute-start.8 = (bf16[2,88,128]{2,1,0:T(8,128)(2,1)S(1)}, bf16[2,88,128]{2,1,0:T(8,128)(2,1)S(1)}, u32[]{:S(2)}, u32[]{:S(2)}) collective-permute-start(bf16[2,88,128]{2,1,0:T(8,128)(2,1)S(1)} %concatenate.47), channel_id=1, source_target_pairs={{0,16},{8,24},{16,0},{24,8},{32,48},{40,56},{48,32},{56,40},{64,80... | collective-permute-start | bytes 135176 | tf_op jit(solution)/shard_map/ppermute | solution.py:69
  66.4 3.9 %collective-permute-done.8 = bf16[2,88,128]{2,1,0:T(8,128)(2,1)S(1)} collective-permute-done((bf16[2,88,128]{2,1,0:T(8,128)(2,1)S(1)}, bf16[2,88,128]{2,1,0:T(8,128)(2,1)S(1)}, u32[]{:S(2)}, u32[]{:S(2)}) %collective-permute-start.8) | collective-permute-done | bytes 45088 | tf_op jit(solution)/shard_map/ppermute | solution.py:69
  70.6 6.0 %collective-permute-start.9 = (bf16[88,128]{1,0:T(8,128)(2,1)S(1)}, bf16[88,128]{1,0:T(8,128)(2,1)S(1)}, u32[]{:S(2)}, u32[]{:S(2)}) collective-permute-start(bf16[88,128]{1,0:T(8,128)(2,1)S(1)} %concatenate.50), channel_id=1, source_target_pairs={{0,128},{8,136},{16,144},{24,152},{32,160},{40,168},{48,176},{56,1... | collective-permute-start | bytes 67592 | tf_op jit(solution)/shard_map/ppermute | solution.py:69
  76.7 1.7 %collective-permute-done.9 = bf16[88,128]{1,0:T(8,128)(2,1)S(1)} collective-permute-done((bf16[88,128]{1,0:T(8,128)(2,1)S(1)}, bf16[88,128]{1,0:T(8,128)(2,1)S(1)}, u32[]{:S(2)}, u32[]{:S(2)}) %collective-permute-start.9) | collective-permute-done | bytes 22560 | tf_op jit(solution)/shard_map/ppermute | solution.py:69
  78.4 0.5 broadcast.97
  78.9 0.7 fusion.57
  80.0 0.3 fusion.5
  80.5 2.0 %convolution_convert_fusion.1 = bf16[32,2560]{1,0:T(8,128)(2,1)S(1)} fusion(bf16[32,320]{1,0:T(8,128)(2,1)S(1)} %reshape_transpose.3, bf16[320,2560]{1,0:T(8,128)(2,1)} %param.27), kind=kOutput, calls=%fused_computation.1 | convolution fusion | flops 52510720 | bytes 1822720 | tf_op jit(solution)/shard_map/dot_general | solution.py:247
  82.4 1.1 collective-permute-start.10
  83.5 4.5 %collective-permute-done.10 = bf16[32,2560]{1,0:T(8,128)(2,1)S(1)} collective-permute-done((bf16[32,2560]{1,0:T(8,128)(2,1)S(1)}, bf16[32,2560]{1,0:T(8,128)(2,1)S(1)}, u32[]{:S(2)}, u32[]{:S(2)}) %collective-permute-start.10) | collective-permute-done | bytes 163872 | tf_op jit(solution)/shard_map/ppermute | solution.py:133
  88.0 1.7 %collective-permute-start.11 = (bf16[32,2560]{1,0:T(8,128)(2,1)S(1)}, bf16[32,2560]{1,0:T(8,128)(2,1)S(1)}, u32[]{:S(2)}, u32[]{:S(2)}) collective-permute-start(bf16[32,2560]{1,0:T(8,128)(2,1)S(1)} %add_convert_fusion.5), channel_id=1, source_target_pairs={{0,1},{1,0},{2,3},{3,2},{4,5},{5,4},{6,7},{7,6},{8,9},{9,8},{10,11... | collective-permute-start | bytes 491528 | tf_op jit(solution)/shard_map/ppermute | solution.py:133
  89.7 3.7 %collective-permute-done.11 = bf16[32,2560]{1,0:T(8,128)(2,1)S(1)} collective-permute-done((bf16[32,2560]{1,0:T(8,128)(2,1)S(1)}, bf16[32,2560]{1,0:T(8,128)(2,1)S(1)}, u32[]{:S(2)}, u32[]{:S(2)}) %collective-permute-start.11) | collective-permute-done | bytes 163872 | tf_op jit(solution)/shard_map/ppermute | solution.py:133
  93.5 3.1 %collective-permute-start.12 = (bf16[32,2560]{1,0:T(8,128)(2,1)S(1)}, bf16[32,2560]{1,0:T(8,128)(2,1)S(1)}, u32[]{:S(2)}, u32[]{:S(2)}) collective-permute-start(bf16[32,2560]{1,0:T(8,128)(2,1)S(1)} %add_convert_fusion.4), channel_id=1, source_target_pairs={{0,3},{1,2},{2,1},{3,0},{4,7},{5,6},{6,5},{7,4},{8,11},{9,10},{10,... | collective-permute-start | bytes 491528 | tf_op jit(solution)/shard_map/ppermute | solution.py:133
  96.6 3.5 %collective-permute-done.12 = bf16[32,2560]{1,0:T(8,128)(2,1)S(1)} collective-permute-done((bf16[32,2560]{1,0:T(8,128)(2,1)S(1)}, bf16[32,2560]{1,0:T(8,128)(2,1)S(1)}, u32[]{:S(2)}, u32[]{:S(2)}) %collective-permute-start.12) | collective-permute-done | bytes 163872 | tf_op jit(solution)/shard_map/ppermute | solution.py:133
  100.4 0.5 fusion.58
  101.0 2.8 %convolution_convert_fusion = bf16[32,2560]{1,0:T(8,128)(2,1)S(1)} fusion(bf16[512,2560]{1,0:T(8,128)(2,1)S(1)} %copy-done, bf16[32,2560]{1,0:T(8,128)(2,1)S(1)} %multiply_convert_fusion, bf16[2560,512]{1,0:T(8,128)(2,1)} %param.29, f32[32,512]{1,0:T(8,128)S(1)} %fusion.58), kind=kOutput, calls=%fused_computation | convolution fusion | flops 167952384 | bytes 5636096 | tf_op jit(solution)/shard_map/dot_general | solution.py:261
  103.8 0.9 collective-permute-start.13
  104.7 4.5 %collective-permute-done.13 = bf16[32,2560]{1,0:T(8,128)(2,1)S(1)} collective-permute-done((bf16[32,2560]{1,0:T(8,128)(2,1)S(1)}, bf16[32,2560]{1,0:T(8,128)(2,1)S(1)}, u32[]{:S(2)}, u32[]{:S(2)}) %collective-permute-start.13) | collective-permute-done | bytes 163872 | tf_op jit(solution)/shard_map/ppermute | solution.py:133
  109.3 0.5 collective-permute-start.14
  109.7 5.0 %collective-permute-done.14 = bf16[32,2560]{1,0:T(8,128)(2,1)S(1)} collective-permute-done((bf16[32,2560]{1,0:T(8,128)(2,1)S(1)}, bf16[32,2560]{1,0:T(8,128)(2,1)S(1)}, u32[]{:S(2)}, u32[]{:S(2)}) %collective-permute-start.14) | collective-permute-done | bytes 163872 | tf_op jit(solution)/shard_map/ppermute | solution.py:133
  114.7 3.1 %collective-permute-start.15 = (bf16[32,2560]{1,0:T(8,128)(2,1)S(1)}, bf16[32,2560]{1,0:T(8,128)(2,1)S(1)}, u32[]{:S(2)}, u32[]{:S(2)}) collective-permute-start(bf16[32,2560]{1,0:T(8,128)(2,1)S(1)} %add_convert_fusion.1), channel_id=1, source_target_pairs={{0,3},{1,2},{2,1},{3,0},{4,7},{5,6},{6,5},{7,4},{8,11},{9,10},{10,... | collective-permute-start | bytes 491528 | tf_op jit(solution)/shard_map/ppermute | solution.py:133
  117.8 3.5 %collective-permute-done.15 = bf16[32,2560]{1,0:T(8,128)(2,1)S(1)} collective-permute-done((bf16[32,2560]{1,0:T(8,128)(2,1)S(1)}, bf16[32,2560]{1,0:T(8,128)(2,1)S(1)}, u32[]{:S(2)}, u32[]{:S(2)}) %collective-permute-start.15) | collective-permute-done | bytes 163872 | tf_op jit(solution)/shard_map/ppermute | solution.py:133
  121.3 0.2 multiply_reduce_fusion.1
  121.6 0.7 dynamic-slice_convert_fusion
  122.3 0.7 multiply_reduce_fusion
  (109 shorter events, 3.6 us)
Async XLA Ops:
  0.6 100.3 %copy-start = (bf16[512,2560]{1,0:T(8,128)(2,1)S(1)}, bf16[512,2560]{1,0:T(8,128)(2,1)}, u32[]{:S(2)}) copy-start(bf16[512,2560]{1,0:T(8,128)(2,1)} %param.30) | copy-start | bytes 7864324
  0.6 29.4 %copy-start.10 = (s32[32]{0:T(128)S(1)}, s32[32]{0:T(128)}, u32[]{:S(2)}) copy-start(s32[32]{0:T(128)} %param.25) | copy-start | bytes 388
  0.7 9.3 %collective-permute-start = (bf16[1,32,320]{2,1,0:T(8,128)(2,1)}, bf16[1,32,320]{2,1,0:T(8,128)(2,1)S(1)}, u32[]{:S(2)}, u32[]{:S(2)}) collective-permute-start(bf16[1,32,320]{2,1,0:T(8,128)(2,1)} %bitcast.203), channel_id=1, source_target_pairs={{0,128},{8,136},{16,144},{24,152},{32,160},{40,168},{48,176},{56,1... | collective-permute-start | bytes 61448 | tf_op jit(solution)/shard_map/ppermute | solution.py:69
  10.7 5.7 %collective-permute-start.1 = (bf16[2,1,32,320]{3,2,0,1:T(8,128)(2,1)S(1)}, bf16[2,1,32,320]{3,2,0,1:T(8,128)(2,1)S(1)}, u32[]{:S(2)}, u32[]{:S(2)}) collective-permute-start(bf16[2,1,32,320]{3,2,0,1:T(8,128)(2,1)S(1)} %fusion.36), channel_id=1, source_target_pairs={{0,16},{8,24},{16,0},{24,8},{32,48},{40,56},{48,32},{56,40},{64,80... | collective-permute-start | bytes 122888 | tf_op jit(solution)/shard_map/ppermute | solution.py:69
  16.5 6.8 %collective-permute-start.2 = (bf16[2,2,1,32,320]{4,3,1,0,2:T(8,128)(2,1)S(1)}, bf16[2,2,1,32,320]{4,3,1,0,2:T(8,128)(2,1)S(1)}, u32[]{:S(2)}, u32[]{:S(2)}) collective-permute-start(bf16[2,2,1,32,320]{4,3,1,0,2:T(8,128)(2,1)S(1)} %fusion.24), channel_id=1, source_target_pairs={{0,64},{8,72},{16,80},{24,88},{32,96},{40,104},{48,112},{56,120},{... | collective-permute-start | bytes 245768 | tf_op jit(solution)/shard_map/ppermute | solution.py:69
  23.3 5.8 %collective-permute-start.3 = (bf16[2,2,2,1,32,320]{5,4,2,1,0,3:T(8,128)(2,1)S(1)}, bf16[2,2,2,1,32,320]{5,4,2,1,0,3:T(8,128)(2,1)S(1)}, u32[]{:S(2)}, u32[]{:S(2)}) collective-permute-start(bf16[2,2,2,1,32,320]{5,4,2,1,0,3:T(8,128)(2,1)S(1)} %fusion.15), channel_id=1, source_target_pairs={{0,32},{8,40},{16,48},{24,56},{32,0},{40,8},{48,16},{56,24},{64,96... | collective-permute-start | bytes 491528 | tf_op jit(solution)/shard_map/ppermute | solution.py:69
  30.0 1.9 %collective-permute-start.4 = (bf16[2,2,2,2,1,32,320]{6,5,3,2,1,0,4:T(8,128)(2,1)}, bf16[2,2,2,2,1,32,320]{6,5,3,2,1,0,4:T(8,128)(2,1)S(1)}, u32[]{:S(2)}, u32[]{:S(2)}) collective-permute-start(bf16[2,2,2,2,1,32,320]{6,5,3,2,1,0,4:T(8,128)(2,1)} %fusion.12), channel_id=1, source_target_pairs={{0,8},{8,0},{16,24},{24,16},{32,40},{40,32},{48,56},{56,48},{64,72... | collective-permute-start | bytes 983048 | tf_op jit(solution)/shard_map/ppermute | solution.py:69
  34.1 5.8 %copy-start.3 = (bf16[32,320]{1,0:T(8,128)(2,1)S(1)}, bf16[32,320]{1,0:T(8,128)(2,1)}, u32[]{:S(2)}) copy-start(bf16[32,320]{1,0:T(8,128)(2,1)} %param.18) | copy-start | bytes 61444
  34.1 5.9 %copy-start.7 = (s32[1,16]{1,0:T(1,128)S(1)}, s32[1,16]{1,0:T(1,128)}, u32[]{:S(2)}) copy-start(s32[1,16]{1,0:T(1,128)} %param.26) | copy-start | bytes 196
  39.7 7.1 %collective-permute-start.5 = (f32[16,88,128]{2,1,0:T(8,128)}, f32[16,88,128]{2,1,0:T(8,128)S(1)}, u32[]{:S(2)}, u32[]{:S(2)}) collective-permute-start(f32[16,88,128]{2,1,0:T(8,128)} %shard_map.177), channel_id=1, source_target_pairs={{0,8},{8,0},{16,24},{24,16},{32,40},{40,32},{48,56},{56,48},{64,72... | collective-permute-start | bytes 2162696 | tf_op jit(solution)/shard_map/ppermute | solution.py:69
  47.7 2.5 %copy-start.8 = (bf16[32,80]{1,0:T(8,128)(2,1)S(1)}, bf16[32,80]{1,0:T(8,128)(2,1)}, u32[]{:S(2)}) copy-start(bf16[32,80]{1,0:T(8,128)(2,1)} %param.19) | copy-start | bytes 15364
  50.1 6.9 %collective-permute-start.6 = (bf16[2,2,2,88,128]{4,3,2,1,0:T(8,128)(2,1)S(1)}, bf16[2,2,2,88,128]{4,3,2,1,0:T(8,128)(2,1)S(1)}, u32[]{:S(2)}, u32[]{:S(2)}) collective-permute-start(bf16[2,2,2,88,128]{4,3,2,1,0:T(8,128)(2,1)S(1)} %concatenate.41), channel_id=1, source_target_pairs={{0,32},{8,40},{16,48},{24,56},{32,0},{40,8},{48,16},{56,24},{64,96... | collective-permute-start | bytes 540680 | tf_op jit(solution)/shard_map/ppermute | solution.py:69
  57.3 22.7 %copy-start.9 = (bf16[32,80]{1,0:T(8,128)(2,1)S(1)}, bf16[32,80]{1,0:T(8,128)(2,1)}, u32[]{:S(2)}) copy-start(bf16[32,80]{1,0:T(8,128)(2,1)} %param.20) | copy-start | bytes 15364
  57.4 7.0 %collective-permute-start.7 = (bf16[2,2,88,128]{3,2,0,1:T(8,128)(2,1)S(1)}, bf16[2,2,88,128]{3,2,0,1:T(8,128)(2,1)S(1)}, u32[]{:S(2)}, u32[]{:S(2)}) collective-permute-start(bf16[2,2,88,128]{3,2,0,1:T(8,128)(2,1)S(1)} %concatenate.44), channel_id=1, source_target_pairs={{0,64},{8,72},{16,80},{24,88},{32,96},{40,104},{48,112},{56,120},{... | collective-permute-start | bytes 270344 | tf_op jit(solution)/shard_map/ppermute | solution.py:69
  64.7 5.6 %collective-permute-start.8 = (bf16[2,88,128]{2,1,0:T(8,128)(2,1)S(1)}, bf16[2,88,128]{2,1,0:T(8,128)(2,1)S(1)}, u32[]{:S(2)}, u32[]{:S(2)}) collective-permute-start(bf16[2,88,128]{2,1,0:T(8,128)(2,1)S(1)} %concatenate.47), channel_id=1, source_target_pairs={{0,16},{8,24},{16,0},{24,8},{32,48},{40,56},{48,32},{56,40},{64,80... | collective-permute-start | bytes 135176 | tf_op jit(solution)/shard_map/ppermute | solution.py:69
  70.6 7.8 %collective-permute-start.9 = (bf16[88,128]{1,0:T(8,128)(2,1)S(1)}, bf16[88,128]{1,0:T(8,128)(2,1)S(1)}, u32[]{:S(2)}, u32[]{:S(2)}) collective-permute-start(bf16[88,128]{1,0:T(8,128)(2,1)S(1)} %concatenate.50), channel_id=1, source_target_pairs={{0,128},{8,136},{16,144},{24,152},{32,160},{40,168},{48,176},{56,1... | collective-permute-start | bytes 67592 | tf_op jit(solution)/shard_map/ppermute | solution.py:69
  80.0 20.1 %copy-start.2 = (bf16[32,2560]{1,0:T(8,128)(2,1)S(1)}, bf16[32,2560]{1,0:T(8,128)(2,1)}, u32[]{:S(2)}) copy-start(bf16[32,2560]{1,0:T(8,128)(2,1)} %param.17) | copy-start | bytes 491524
  80.0 20.3 %copy-start.6 = (f32[2560]{0:T(1024)S(1)}, f32[2560]{0:T(1024)}, u32[]{:S(2)}) copy-start(f32[2560]{0:T(1024)} %param.31) | copy-start | bytes 30724
  80.4 20.0 %copy-start.1 = (bf16[2560,512]{1,0:T(8,128)(2,1)S(1)}, bf16[2560,512]{1,0:T(8,128)(2,1)}, u32[]{:S(2)}) copy-start(bf16[2560,512]{1,0:T(8,128)(2,1)} %param.28) | copy-start | bytes 7864324
  82.4 5.6 %collective-permute-start.10 = (bf16[32,2560]{1,0:T(8,128)(2,1)S(1)}, bf16[32,2560]{1,0:T(8,128)(2,1)S(1)}, u32[]{:S(2)}, u32[]{:S(2)}) collective-permute-start(bf16[32,2560]{1,0:T(8,128)(2,1)S(1)} %convolution_convert_fusion.1), channel_id=1, source_target_pairs={{0,4},{1,5},{2,6},{3,7},{4,0},{5,1},{6,2},{7,3},{8,12},{9,13},{10,... | collective-permute-start | bytes 491528 | tf_op jit(solution)/shard_map/ppermute | solution.py:133
  88.0 5.4 %collective-permute-start.11 = (bf16[32,2560]{1,0:T(8,128)(2,1)S(1)}, bf16[32,2560]{1,0:T(8,128)(2,1)S(1)}, u32[]{:S(2)}, u32[]{:S(2)}) collective-permute-start(bf16[32,2560]{1,0:T(8,128)(2,1)S(1)} %add_convert_fusion.5), channel_id=1, source_target_pairs={{0,1},{1,0},{2,3},{3,2},{4,5},{5,4},{6,7},{7,6},{8,9},{9,8},{10,11... | collective-permute-start | bytes 491528 | tf_op jit(solution)/shard_map/ppermute | solution.py:133
  93.5 6.6 %collective-permute-start.12 = (bf16[32,2560]{1,0:T(8,128)(2,1)S(1)}, bf16[32,2560]{1,0:T(8,128)(2,1)S(1)}, u32[]{:S(2)}, u32[]{:S(2)}) collective-permute-start(bf16[32,2560]{1,0:T(8,128)(2,1)S(1)} %add_convert_fusion.4), channel_id=1, source_target_pairs={{0,3},{1,2},{2,1},{3,0},{4,7},{5,6},{6,5},{7,4},{8,11},{9,10},{10,... | collective-permute-start | bytes 491528 | tf_op jit(solution)/shard_map/ppermute | solution.py:133
  101.0 21.3 %copy-start.4 = (f32[2560]{0:T(1024)S(1)}, f32[2560]{0:T(1024)}, u32[]{:S(2)}) copy-start(f32[2560]{0:T(1024)} %param.33) | copy-start | bytes 30724
  101.0 21.3 %copy-start.5 = (f32[2560]{0:T(1024)S(1)}, f32[2560]{0:T(1024)}, u32[]{:S(2)}) copy-start(f32[2560]{0:T(1024)} %param.32) | copy-start | bytes 30724
  103.8 5.4 %collective-permute-start.13 = (bf16[32,2560]{1,0:T(8,128)(2,1)S(1)}, bf16[32,2560]{1,0:T(8,128)(2,1)S(1)}, u32[]{:S(2)}, u32[]{:S(2)}) collective-permute-start(bf16[32,2560]{1,0:T(8,128)(2,1)S(1)} %convolution_convert_fusion), channel_id=1, source_target_pairs={{0,4},{1,5},{2,6},{3,7},{4,0},{5,1},{6,2},{7,3},{8,12},{9,13},{10,... | collective-permute-start | bytes 491528 | tf_op jit(solution)/shard_map/ppermute | solution.py:133
  109.3 5.4 %collective-permute-start.14 = (bf16[32,2560]{1,0:T(8,128)(2,1)S(1)}, bf16[32,2560]{1,0:T(8,128)(2,1)S(1)}, u32[]{:S(2)}, u32[]{:S(2)}) collective-permute-start(bf16[32,2560]{1,0:T(8,128)(2,1)S(1)} %add_convert_fusion.2), channel_id=1, source_target_pairs={{0,1},{1,0},{2,3},{3,2},{4,5},{5,4},{6,7},{7,6},{8,9},{9,8},{10,11... | collective-permute-start | bytes 491528 | tf_op jit(solution)/shard_map/ppermute | solution.py:133
  114.7 6.6 %collective-permute-start.15 = (bf16[32,2560]{1,0:T(8,128)(2,1)S(1)}, bf16[32,2560]{1,0:T(8,128)(2,1)S(1)}, u32[]{:S(2)}, u32[]{:S(2)}) collective-permute-start(bf16[32,2560]{1,0:T(8,128)(2,1)S(1)} %add_convert_fusion.1), channel_id=1, source_target_pairs={{0,3},{1,2},{2,1},{3,0},{4,7},{5,6},{6,5},{7,4},{8,11},{9,10},{10,... | collective-permute-start | bytes 491528 | tf_op jit(solution)/shard_map/ppermute | solution.py:133

commit v8 on v7

--- a/solution.py
+++ b/solution.py
@@ -127,10 +127,14 @@
     return cur
 
 
-def allreduce_bf16(x, axis, n, masks):
+def allreduce_bf16(x, req_count, mlp_count, orders):
     cur = x.astype(jnp.bfloat16)
-    for m in masks:
-        other = lax.ppermute(cur, axis, perm=[(i, i ^ m) for i in range(n)])
+    for k in range(len(orders[0])):
+        perm = []
+        for r in range(req_count):
+            mask = orders[r % len(orders)][k]
+            perm += [(r * mlp_count + m, r * mlp_count + (m ^ mask)) for m in range(mlp_count)]
+        other = lax.ppermute(cur, ("req", "mlp"), perm=perm)
         cur = (cur.astype(jnp.float32) + other.astype(jnp.float32)).astype(jnp.bfloat16)
     return cur
 
@@ -247,9 +251,9 @@
     projected = jnp.dot(attention_layer, out_weight, preferred_element_type=jnp.float32)
     mlp_index = lax.axis_index("mlp")
     share = D // mlp_count
-    mlp_order = [4, 1, 3] if mlp_count == 8 else [1 << b for b in range(mlp_bits)]
+    mlp_orders = [[4, 1, 3], [1, 3, 4]] if mlp_count == 8 else [[1 << b for b in range(mlp_bits)]]
     mid = residual_in.astype(jnp.float32) + allreduce_bf16(
-        projected, "mlp", mlp_count, mlp_order
+        projected, req_count, mlp_count, mlp_orders
     ).astype(jnp.float32)
     normed = (mid * rms_scale(jnp.sum(mid * mid, -1, keepdims=True), D) * mlp_gain).astype(
         jnp.bfloat16
@@ -258,7 +262,7 @@
     upper = jnp.dot(normed, up_weight, preferred_element_type=jnp.float32)
     hidden = (jax.nn.silu(gate) * upper).astype(jnp.bfloat16)
     stream = mid + allreduce_bf16(
-        jnp.dot(hidden, down_weight, preferred_element_type=jnp.float32), "mlp", mlp_count, mlp_order
+        jnp.dot(hidden, down_weight, preferred_element_type=jnp.float32), req_count, mlp_count, mlp_orders
     ).astype(jnp.float32)
     score = jnp.sum(
         stream

time: 123 us -> 123 us (level)
  no operation moved by 1% of the time
where the time goes in v8:
time: 123 us
  waiting for transfers between devices  58.3 us (47%)
  starting transfers between devices  30.9 us (25%)
  Pallas kernels  11.2 us (9%)
  other arithmetic  8.63 us (7%)
  matrix products  8.6 us (7%)
  local copies, waits for them, and re-layouts  4.08 us (3%)
    ppermute x10, waiting for transfers between devices, exchange(): return lax.ppermute(x, axis, perm=[(i, i ^ 1 << bit) for i in range(n)])  33.7 us
    ppermute x6, waiting for transfers between devices, allreduce_bf16(): other = lax.ppermute(cur, ('req', 'mlp'), perm=perm)  24.7 us
    ppermute x10, starting transfers between devices, exchange(): return lax.ppermute(x, axis, perm=[(i, i ^ 1 << bit) for i in range(n)])  20.6 us
    pallas_call x2, Pallas kernels, prefix_partials(): pl.pallas_call(prefix_kernel, grid_spec=pltpu.PrefetchScalarGridSpec(num_...  11.2 us
    ppermute x6, starting transfers between devices, allreduce_bf16(): other = lax.ppermute(cur, ('req', 'mlp'), perm=perm)  10.3 us
    dot_general x1, matrix products, on_device(): jnp.dot(hidden, down_weight, preferred_element_type=jnp.float32)  2.82 us
  transfers between devices with their start and end apart: 16, of which 15 were waited for; matrix products, arithmetic and copies ran while one was open for 3% of the time, Pallas kernels for 4%

profile of v8, /device:TPU:6, one launch (start us, length us, event | category | flops | bytes accessed | tf_op | source)
XLA Modules:
  0.0 123.0 jit_solution(8128997783238738285)
XLA Ops:
  0.7 7.3 %collective-permute-start = (bf16[1,32,320]{2,1,0:T(8,128)(2,1)}, bf16[1,32,320]{2,1,0:T(8,128)(2,1)S(1)}, u32[]{:S(2)}, u32[]{:S(2)}) collective-permute-start(bf16[1,32,320]{2,1,0:T(8,128)(2,1)} %bitcast.203), channel_id=1, source_target_pairs={{0,128},{8,136},{16,144},{24,152},{32,160},{40,168},{48,176},{56,1... | collective-permute-start | bytes 61448 | tf_op jit(solution)/shard_map/ppermute | solution.py:69
  7.9 2.0 %collective-permute-done = bf16[1,32,320]{2,1,0:T(8,128)(2,1)S(1)} collective-permute-done((bf16[1,32,320]{2,1,0:T(8,128)(2,1)}, bf16[1,32,320]{2,1,0:T(8,128)(2,1)S(1)}, u32[]{:S(2)}, u32[]{:S(2)}) %collective-permute-start) | collective-permute-done | bytes 20512 | tf_op jit(solution)/shard_map/ppermute | solution.py:69
  10.0 0.7 select_bitcast_fusion.5
  10.7 1.5 %collective-permute-start.1 = (bf16[2,1,32,320]{3,2,0,1:T(8,128)(2,1)S(1)}, bf16[2,1,32,320]{3,2,0,1:T(8,128)(2,1)S(1)}, u32[]{:S(2)}, u32[]{:S(2)}) collective-permute-start(bf16[2,1,32,320]{3,2,0,1:T(8,128)(2,1)S(1)} %fusion.36), channel_id=1, source_target_pairs={{0,16},{8,24},{16,0},{24,8},{32,48},{40,56},{48,32},{56,40},{64,80... | collective-permute-start | bytes 122888 | tf_op jit(solution)/shard_map/ppermute | solution.py:69
  12.2 4.2 %collective-permute-done.1 = bf16[2,1,32,320]{3,2,0,1:T(8,128)(2,1)S(1)} collective-permute-done((bf16[2,1,32,320]{3,2,0,1:T(8,128)(2,1)S(1)}, bf16[2,1,32,320]{3,2,0,1:T(8,128)(2,1)S(1)}, u32[]{:S(2)}, u32[]{:S(2)}) %collective-permute-start.1) | collective-permute-done | bytes 40992 | tf_op jit(solution)/shard_map/ppermute | solution.py:69
  16.5 2.1 %collective-permute-start.2 = (bf16[2,2,1,32,320]{4,3,1,0,2:T(8,128)(2,1)S(1)}, bf16[2,2,1,32,320]{4,3,1,0,2:T(8,128)(2,1)S(1)}, u32[]{:S(2)}, u32[]{:S(2)}) collective-permute-start(bf16[2,2,1,32,320]{4,3,1,0,2:T(8,128)(2,1)S(1)} %fusion.24), channel_id=1, source_target_pairs={{0,64},{8,72},{16,80},{24,88},{32,96},{40,104},{48,112},{56,120},{... | collective-permute-start | bytes 245768 | tf_op jit(solution)/shard_map/ppermute | solution.py:69
  18.6 4.6 %collective-permute-done.2 = bf16[2,2,1,32,320]{4,3,1,0,2:T(8,128)(2,1)S(1)} collective-permute-done((bf16[2,2,1,32,320]{4,3,1,0,2:T(8,128)(2,1)S(1)}, bf16[2,2,1,32,320]{4,3,1,0,2:T(8,128)(2,1)S(1)}, u32[]{:S(2)}, u32[]{:S(2)}) %collective-permute-start.2) | collective-permute-done | bytes 81952 | tf_op jit(solution)/shard_map/ppermute | solution.py:69
  23.5 5.6 %collective-permute-done.3 = bf16[2,2,2,1,32,320]{5,4,2,1,0,3:T(8,128)(2,1)S(1)} collective-permute-done((bf16[2,2,2,1,32,320]{5,4,2,1,0,3:T(8,128)(2,1)S(1)}, bf16[2,2,2,1,32,320]{5,4,2,1,0,3:T(8,128)(2,1)S(1)}, u32[]{:S(2)}, u32[]{:S(2)}) %collective-permute-start.3) | collective-permute-done | bytes 163872 | tf_op jit(solution)/shard_map/ppermute | solution.py:69
  29.2 0.8 fusion.12
  30.0 0.5 subtract_clamp_fusion.count_ref
  30.6 1.4 %collective-permute-done.4 = bf16[2,2,2,2,1,32,320]{6,5,3,2,1,0,4:T(8,128)(2,1)S(1)} collective-permute-done((bf16[2,2,2,2,1,32,320]{6,5,3,2,1,0,4:T(8,128)(2,1)}, bf16[2,2,2,2,1,32,320]{6,5,3,2,1,0,4:T(8,128)(2,1)S(1)}, u32[]{:S(2)}, u32[]{:S(2)}) %collective-permute-start.4) | collective-permute-done | bytes 327712 | tf_op jit(solution)/shard_map/ppermute | solution.py:69
  32.5 1.6 %reshape_reshape.3.q_ref = bf16[16,2,128,80]{3,2,1,0:T(8,128)(2,1)} reshape(bf16[2,2,2,2,2,1,32,320]{7,6,4,3,2,1,0,5:T(8,128)(2,1)S(1)} %copy.55) | data formatting | bytes 1310720 | tf_op jit(solution)/shard_map/reshape;reshape | solution.py:180
  34.1 5.7 %shard_map.177 = f32[16,88,128]{2,1,0:T(8,128)} custom-call(s32[32]{0:T(128)} %subtract_clamp_fusion.count_ref, s32[1]{0:T(128)} %bitcast.33.half_ref, bf16[16,2,128,80]{3,2,1,0:T(8,128)(2,1)} %reshape_reshape.3.q_ref, bf16[16,2,80,512]{3,2,1,0:T(8,128)(2,1)} %bitcast.192, bf16[16,2,80,512]{3,2,1,0:T(8,128)(2,1)} %bitcast.194), custom_call_target="tpu_custom_call" | custom-call | flops 335544320 | bytes 3670016 | tf_op jit(solution)/shard_map/pallas_call | solution.py:46
  40.1 1.3 %select_reduce_fusion = (f32[16,2,4]{2,1,0:T(2,128)S(1)}, f32[16,2,4,128]{3,2,1,0:T(4,128)S(1)}) fusion(pred[16,128]{1,0:T(8,128)(4,1)S(1)} %iota_compare_fusion, bf16[16,2,4,80]{3,2,1,0:T(4,128)(2,1)S(1)} %reshape.227, bf16[1,16,128,80]{2,3,1,0:T(8,128)(2,1)} %param.23), kind=kOutput, calls=%fused_computation.77 | convolution fusion | flops 2670464 | bytes 416256 | tf_op jit(solution)/shard_map/sjkgh,stkh->ksjgt/dot_general | solution.py:207
  41.3 5.5 %shard_map.176 = f32[16,88,128]{2,1,0:T(8,128)} custom-call(s32[32]{0:T(128)} %subtract_clamp_fusion.count_ref, s32[1]{0:T(128)} %bitcast.half_ref, bf16[16,2,128,80]{3,2,1,0:T(8,128)(2,1)} %reshape_reshape.3.q_ref, bf16[16,2,80,512]{3,2,1,0:T(8,128)(2,1)} %bitcast.193, bf16[16,2,80,512]{3,2,1,0:T(8,128)(2,1)} %bitcast.195), custom_call_target="tpu_custom_call" | custom-call | flops 335544320 | bytes 3670016 | tf_op jit(solution)/shard_map/pallas_call | solution.py:46
  46.9 0.9 subtract_exponential_fusion.1
  47.8 1.2 fusion.6
  48.9 0.9 fusion.18
  50.3 0.4 select_reduce_fusion.1
  50.7 6.4 %collective-permute-done.6 = bf16[2,2,2,88,128]{4,3,2,1,0:T(8,128)(2,1)S(1)} collective-permute-done((bf16[2,2,2,88,128]{4,3,2,1,0:T(8,128)(2,1)S(1)}, bf16[2,2,2,88,128]{4,3,2,1,0:T(8,128)(2,1)S(1)}, u32[]{:S(2)}, u32[]{:S(2)}) %collective-permute-start.6) | collective-permute-done | bytes 180256 | tf_op jit(solution)/shard_map/ppermute | solution.py:69
  57.4 1.9 %collective-permute-start.7 = (bf16[2,2,88,128]{3,2,0,1:T(8,128)(2,1)S(1)}, bf16[2,2,88,128]{3,2,0,1:T(8,128)(2,1)S(1)}, u32[]{:S(2)}, u32[]{:S(2)}) collective-permute-start(bf16[2,2,88,128]{3,2,0,1:T(8,128)(2,1)S(1)} %concatenate.44), channel_id=1, source_target_pairs={{0,64},{8,72},{16,80},{24,88},{32,96},{40,104},{48,112},{56,120},{... | collective-permute-start | bytes 270344 | tf_op jit(solution)/shard_map/ppermute | solution.py:69
  59.3 1.3 %fusion.9 = f32[16,2,4,80]{3,2,1,0:T(4,128)S(1)} fusion(bf16[1,16,128,80]{2,3,1,0:T(8,128)(2,1)} %param.24, f32[16,2,4,128]{3,2,1,0:T(4,128)S(1)} %get-tuple-element.40, f32[16,2,4]{2,1,0:T(2,128)S(1)} %max.65, pred[16,128]{1,0:T(8,128)(4,1)S(1)} %iota_compare_fusion), kind=kOutput, calls=%fused_computation.29 | convolution fusion | flops 2670592 | bytes 436736 | tf_op jit(solution)/shard_map/ksjgt,stkh->ksjgh/dot_general | solution.py:229
  60.6 3.8 %collective-permute-done.7 = bf16[2,2,88,128]{3,2,0,1:T(8,128)(2,1)S(1)} collective-permute-done((bf16[2,2,88,128]{3,2,0,1:T(8,128)(2,1)S(1)}, bf16[2,2,88,128]{3,2,0,1:T(8,128)(2,1)S(1)}, u32[]{:S(2)}, u32[]{:S(2)}) %collective-permute-start.7) | collective-permute-done | bytes 90144 | tf_op jit(solution)/shard_map/ppermute | solution.py:69
  64.7 1.5 %collective-permute-start.8 = (bf16[2,88,128]{2,1,0:T(8,128)(2,1)S(1)}, bf16[2,88,128]{2,1,0:T(8,128)(2,1)S(1)}, u32[]{:S(2)}, u32[]{:S(2)}) collective-permute-start(bf16[2,88,128]{2,1,0:T(8,128)(2,1)S(1)} %concatenate.47), channel_id=1, source_target_pairs={{0,16},{8,24},{16,0},{24,8},{32,48},{40,56},{48,32},{56,40},{64,80... | collective-permute-start | bytes 135176 | tf_op jit(solution)/shard_map/ppermute | solution.py:69
  66.4 3.9 %collective-permute-done.8 = bf16[2,88,128]{2,1,0:T(8,128)(2,1)S(1)} collective-permute-done((bf16[2,88,128]{2,1,0:T(8,128)(2,1)S(1)}, bf16[2,88,128]{2,1,0:T(8,128)(2,1)S(1)}, u32[]{:S(2)}, u32[]{:S(2)}) %collective-permute-start.8) | collective-permute-done | bytes 45088 | tf_op jit(solution)/shard_map/ppermute | solution.py:69
  70.6 6.0 %collective-permute-start.9 = (bf16[88,128]{1,0:T(8,128)(2,1)S(1)}, bf16[88,128]{1,0:T(8,128)(2,1)S(1)}, u32[]{:S(2)}, u32[]{:S(2)}) collective-permute-start(bf16[88,128]{1,0:T(8,128)(2,1)S(1)} %concatenate.50), channel_id=1, source_target_pairs={{0,128},{8,136},{16,144},{24,152},{32,160},{40,168},{48,176},{56,1... | collective-permute-start | bytes 67592 | tf_op jit(solution)/shard_map/ppermute | solution.py:69
  76.7 1.7 %collective-permute-done.9 = bf16[88,128]{1,0:T(8,128)(2,1)S(1)} collective-permute-done((bf16[88,128]{1,0:T(8,128)(2,1)S(1)}, bf16[88,128]{1,0:T(8,128)(2,1)S(1)}, u32[]{:S(2)}, u32[]{:S(2)}) %collective-permute-start.9) | collective-permute-done | bytes 22560 | tf_op jit(solution)/shard_map/ppermute | solution.py:69
  78.4 0.5 broadcast.97
  78.9 0.7 fusion.57
  80.0 0.3 fusion.5
  80.5 2.0 %convolution_convert_fusion.1 = bf16[32,2560]{1,0:T(8,128)(2,1)S(1)} fusion(bf16[32,320]{1,0:T(8,128)(2,1)S(1)} %reshape_transpose.3, bf16[320,2560]{1,0:T(8,128)(2,1)} %param.27), kind=kOutput, calls=%fused_computation.1 | convolution fusion | flops 52510720 | bytes 1822720 | tf_op jit(solution)/shard_map/dot_general | solution.py:251
  82.4 1.1 collective-permute-start.10
  83.5 4.5 %collective-permute-done.10 = bf16[32,2560]{1,0:T(8,128)(2,1)S(1)} collective-permute-done((bf16[32,2560]{1,0:T(8,128)(2,1)S(1)}, bf16[32,2560]{1,0:T(8,128)(2,1)S(1)}, u32[]{:S(2)}, u32[]{:S(2)}) %collective-permute-start.10) | collective-permute-done | bytes 163872 | tf_op jit(solution)/shard_map/ppermute | solution.py:137
  88.0 1.7 %collective-permute-start.11 = (bf16[32,2560]{1,0:T(8,128)(2,1)S(1)}, bf16[32,2560]{1,0:T(8,128)(2,1)S(1)}, u32[]{:S(2)}, u32[]{:S(2)}) collective-permute-start(bf16[32,2560]{1,0:T(8,128)(2,1)S(1)} %add_convert_fusion.5), channel_id=1, source_target_pairs={{0,1},{1,0},{2,3},{3,2},{4,5},{5,4},{6,7},{7,6},{8,11},{9,10},{10,... | collective-permute-start | bytes 491528 | tf_op jit(solution)/shard_map/ppermute | solution.py:137
  89.7 3.7 %collective-permute-done.11 = bf16[32,2560]{1,0:T(8,128)(2,1)S(1)} collective-permute-done((bf16[32,2560]{1,0:T(8,128)(2,1)S(1)}, bf16[32,2560]{1,0:T(8,128)(2,1)S(1)}, u32[]{:S(2)}, u32[]{:S(2)}) %collective-permute-start.11) | collective-permute-done | bytes 163872 | tf_op jit(solution)/shard_map/ppermute | solution.py:137
  93.5 3.1 %collective-permute-start.12 = (bf16[32,2560]{1,0:T(8,128)(2,1)S(1)}, bf16[32,2560]{1,0:T(8,128)(2,1)S(1)}, u32[]{:S(2)}, u32[]{:S(2)}) collective-permute-start(bf16[32,2560]{1,0:T(8,128)(2,1)S(1)} %add_convert_fusion.4), channel_id=1, source_target_pairs={{0,3},{1,2},{2,1},{3,0},{4,7},{5,6},{6,5},{7,4},{8,12},{9,13},{10,... | collective-permute-start | bytes 491528 | tf_op jit(solution)/shard_map/ppermute | solution.py:137
  96.6 3.5 %collective-permute-done.12 = bf16[32,2560]{1,0:T(8,128)(2,1)S(1)} collective-permute-done((bf16[32,2560]{1,0:T(8,128)(2,1)S(1)}, bf16[32,2560]{1,0:T(8,128)(2,1)S(1)}, u32[]{:S(2)}, u32[]{:S(2)}) %collective-permute-start.12) | collective-permute-done | bytes 163872 | tf_op jit(solution)/shard_map/ppermute | solution.py:137
  100.4 0.5 fusion.58
  101.0 2.8 %convolution_convert_fusion = bf16[32,2560]{1,0:T(8,128)(2,1)S(1)} fusion(bf16[512,2560]{1,0:T(8,128)(2,1)S(1)} %copy-done, bf16[32,2560]{1,0:T(8,128)(2,1)S(1)} %multiply_convert_fusion, bf16[2560,512]{1,0:T(8,128)(2,1)} %param.29, f32[32,512]{1,0:T(8,128)S(1)} %fusion.58), kind=kOutput, calls=%fused_computation | convolution fusion | flops 167952384 | bytes 5636096 | tf_op jit(solution)/shard_map/dot_general | solution.py:265
  103.8 0.9 collective-permute-start.13
  104.7 4.5 %collective-permute-done.13 = bf16[32,2560]{1,0:T(8,128)(2,1)S(1)} collective-permute-done((bf16[32,2560]{1,0:T(8,128)(2,1)S(1)}, bf16[32,2560]{1,0:T(8,128)(2,1)S(1)}, u32[]{:S(2)}, u32[]{:S(2)}) %collective-permute-start.13) | collective-permute-done | bytes 163872 | tf_op jit(solution)/shard_map/ppermute | solution.py:137
  109.3 0.5 collective-permute-start.14
  109.7 5.0 %collective-permute-done.14 = bf16[32,2560]{1,0:T(8,128)(2,1)S(1)} collective-permute-done((bf16[32,2560]{1,0:T(8,128)(2,1)S(1)}, bf16[32,2560]{1,0:T(8,128)(2,1)S(1)}, u32[]{:S(2)}, u32[]{:S(2)}) %collective-permute-start.14) | collective-permute-done | bytes 163872 | tf_op jit(solution)/shard_map/ppermute | solution.py:137
  114.7 3.1 %collective-permute-start.15 = (bf16[32,2560]{1,0:T(8,128)(2,1)S(1)}, bf16[32,2560]{1,0:T(8,128)(2,1)S(1)}, u32[]{:S(2)}, u32[]{:S(2)}) collective-permute-start(bf16[32,2560]{1,0:T(8,128)(2,1)S(1)} %add_convert_fusion.1), channel_id=1, source_target_pairs={{0,3},{1,2},{2,1},{3,0},{4,7},{5,6},{6,5},{7,4},{8,12},{9,13},{10,... | collective-permute-start | bytes 491528 | tf_op jit(solution)/shard_map/ppermute | solution.py:137
  117.8 3.5 %collective-permute-done.15 = bf16[32,2560]{1,0:T(8,128)(2,1)S(1)} collective-permute-done((bf16[32,2560]{1,0:T(8,128)(2,1)S(1)}, bf16[32,2560]{1,0:T(8,128)(2,1)S(1)}, u32[]{:S(2)}, u32[]{:S(2)}) %collective-permute-start.15) | collective-permute-done | bytes 163872 | tf_op jit(solution)/shard_map/ppermute | solution.py:137
  121.3 0.2 multiply_reduce_fusion.1
  121.6 0.7 dynamic-slice_convert_fusion
  122.3 0.7 multiply_reduce_fusion
  (109 shorter events, 3.6 us)
Async XLA Ops:
  0.6 100.3 %copy-start = (bf16[512,2560]{1,0:T(8,128)(2,1)S(1)}, bf16[512,2560]{1,0:T(8,128)(2,1)}, u32[]{:S(2)}) copy-start(bf16[512,2560]{1,0:T(8,128)(2,1)} %param.30) | copy-start | bytes 7864324
  0.6 29.4 %copy-start.10 = (s32[32]{0:T(128)S(1)}, s32[32]{0:T(128)}, u32[]{:S(2)}) copy-start(s32[32]{0:T(128)} %param.25) | copy-start | bytes 388
  0.7 9.3 %collective-permute-start = (bf16[1,32,320]{2,1,0:T(8,128)(2,1)}, bf16[1,32,320]{2,1,0:T(8,128)(2,1)S(1)}, u32[]{:S(2)}, u32[]{:S(2)}) collective-permute-start(bf16[1,32,320]{2,1,0:T(8,128)(2,1)} %bitcast.203), channel_id=1, source_target_pairs={{0,128},{8,136},{16,144},{24,152},{32,160},{40,168},{48,176},{56,1... | collective-permute-start | bytes 61448 | tf_op jit(solution)/shard_map/ppermute | solution.py:69
  10.7 5.7 %collective-permute-start.1 = (bf16[2,1,32,320]{3,2,0,1:T(8,128)(2,1)S(1)}, bf16[2,1,32,320]{3,2,0,1:T(8,128)(2,1)S(1)}, u32[]{:S(2)}, u32[]{:S(2)}) collective-permute-start(bf16[2,1,32,320]{3,2,0,1:T(8,128)(2,1)S(1)} %fusion.36), channel_id=1, source_target_pairs={{0,16},{8,24},{16,0},{24,8},{32,48},{40,56},{48,32},{56,40},{64,80... | collective-permute-start | bytes 122888 | tf_op jit(solution)/shard_map/ppermute | solution.py:69
  16.5 6.8 %collective-permute-start.2 = (bf16[2,2,1,32,320]{4,3,1,0,2:T(8,128)(2,1)S(1)}, bf16[2,2,1,32,320]{4,3,1,0,2:T(8,128)(2,1)S(1)}, u32[]{:S(2)}, u32[]{:S(2)}) collective-permute-start(bf16[2,2,1,32,320]{4,3,1,0,2:T(8,128)(2,1)S(1)} %fusion.24), channel_id=1, source_target_pairs={{0,64},{8,72},{16,80},{24,88},{32,96},{40,104},{48,112},{56,120},{... | collective-permute-start | bytes 245768 | tf_op jit(solution)/shard_map/ppermute | solution.py:69
  23.3 5.8 %collective-permute-start.3 = (bf16[2,2,2,1,32,320]{5,4,2,1,0,3:T(8,128)(2,1)S(1)}, bf16[2,2,2,1,32,320]{5,4,2,1,0,3:T(8,128)(2,1)S(1)}, u32[]{:S(2)}, u32[]{:S(2)}) collective-permute-start(bf16[2,2,2,1,32,320]{5,4,2,1,0,3:T(8,128)(2,1)S(1)} %fusion.15), channel_id=1, source_target_pairs={{0,32},{8,40},{16,48},{24,56},{32,0},{40,8},{48,16},{56,24},{64,96... | collective-permute-start | bytes 491528 | tf_op jit(solution)/shard_map/ppermute | solution.py:69
  30.0 1.9 %collective-permute-start.4 = (bf16[2,2,2,2,1,32,320]{6,5,3,2,1,0,4:T(8,128)(2,1)}, bf16[2,2,2,2,1,32,320]{6,5,3,2,1,0,4:T(8,128)(2,1)S(1)}, u32[]{:S(2)}, u32[]{:S(2)}) collective-permute-start(bf16[2,2,2,2,1,32,320]{6,5,3,2,1,0,4:T(8,128)(2,1)} %fusion.12), channel_id=1, source_target_pairs={{0,8},{8,0},{16,24},{24,16},{32,40},{40,32},{48,56},{56,48},{64,72... | collective-permute-start | bytes 983048 | tf_op jit(solution)/shard_map/ppermute | solution.py:69
  34.1 5.8 %copy-start.3 = (bf16[32,320]{1,0:T(8,128)(2,1)S(1)}, bf16[32,320]{1,0:T(8,128)(2,1)}, u32[]{:S(2)}) copy-start(bf16[32,320]{1,0:T(8,128)(2,1)} %param.18) | copy-start | bytes 61444
  34.1 5.9 %copy-start.7 = (s32[1,16]{1,0:T(1,128)S(1)}, s32[1,16]{1,0:T(1,128)}, u32[]{:S(2)}) copy-start(s32[1,16]{1,0:T(1,128)} %param.26) | copy-start | bytes 196
  39.7 7.1 %collective-permute-start.5 = (f32[16,88,128]{2,1,0:T(8,128)}, f32[16,88,128]{2,1,0:T(8,128)S(1)}, u32[]{:S(2)}, u32[]{:S(2)}) collective-permute-start(f32[16,88,128]{2,1,0:T(8,128)} %shard_map.177), channel_id=1, source_target_pairs={{0,8},{8,0},{16,24},{24,16},{32,40},{40,32},{48,56},{56,48},{64,72... | collective-permute-start | bytes 2162696 | tf_op jit(solution)/shard_map/ppermute | solution.py:69
  47.7 2.5 %copy-start.8 = (bf16[32,80]{1,0:T(8,128)(2,1)S(1)}, bf16[32,80]{1,0:T(8,128)(2,1)}, u32[]{:S(2)}) copy-start(bf16[32,80]{1,0:T(8,128)(2,1)} %param.19) | copy-start | bytes 15364
  50.1 6.9 %collective-permute-start.6 = (bf16[2,2,2,88,128]{4,3,2,1,0:T(8,128)(2,1)S(1)}, bf16[2,2,2,88,128]{4,3,2,1,0:T(8,128)(2,1)S(1)}, u32[]{:S(2)}, u32[]{:S(2)}) collective-permute-start(bf16[2,2,2,88,128]{4,3,2,1,0:T(8,128)(2,1)S(1)} %concatenate.41), channel_id=1, source_target_pairs={{0,32},{8,40},{16,48},{24,56},{32,0},{40,8},{48,16},{56,24},{64,96... | collective-permute-start | bytes 540680 | tf_op jit(solution)/shard_map/ppermute | solution.py:69
  57.3 22.7 %copy-start.9 = (bf16[32,80]{1,0:T(8,128)(2,1)S(1)}, bf16[32,80]{1,0:T(8,128)(2,1)}, u32[]{:S(2)}) copy-start(bf16[32,80]{1,0:T(8,128)(2,1)} %param.20) | copy-start | bytes 15364
  57.4 7.0 %collective-permute-start.7 = (bf16[2,2,88,128]{3,2,0,1:T(8,128)(2,1)S(1)}, bf16[2,2,88,128]{3,2,0,1:T(8,128)(2,1)S(1)}, u32[]{:S(2)}, u32[]{:S(2)}) collective-permute-start(bf16[2,2,88,128]{3,2,0,1:T(8,128)(2,1)S(1)} %concatenate.44), channel_id=1, source_target_pairs={{0,64},{8,72},{16,80},{24,88},{32,96},{40,104},{48,112},{56,120},{... | collective-permute-start | bytes 270344 | tf_op jit(solution)/shard_map/ppermute | solution.py:69
  64.7 5.6 %collective-permute-start.8 = (bf16[2,88,128]{2,1,0:T(8,128)(2,1)S(1)}, bf16[2,88,128]{2,1,0:T(8,128)(2,1)S(1)}, u32[]{:S(2)}, u32[]{:S(2)}) collective-permute-start(bf16[2,88,128]{2,1,0:T(8,128)(2,1)S(1)} %concatenate.47), channel_id=1, source_target_pairs={{0,16},{8,24},{16,0},{24,8},{32,48},{40,56},{48,32},{56,40},{64,80... | collective-permute-start | bytes 135176 | tf_op jit(solution)/shard_map/ppermute | solution.py:69
  70.6 7.8 %collective-permute-start.9 = (bf16[88,128]{1,0:T(8,128)(2,1)S(1)}, bf16[88,128]{1,0:T(8,128)(2,1)S(1)}, u32[]{:S(2)}, u32[]{:S(2)}) collective-permute-start(bf16[88,128]{1,0:T(8,128)(2,1)S(1)} %concatenate.50), channel_id=1, source_target_pairs={{0,128},{8,136},{16,144},{24,152},{32,160},{40,168},{48,176},{56,1... | collective-permute-start | bytes 67592 | tf_op jit(solution)/shard_map/ppermute | solution.py:69
  80.0 20.1 %copy-start.2 = (bf16[32,2560]{1,0:T(8,128)(2,1)S(1)}, bf16[32,2560]{1,0:T(8,128)(2,1)}, u32[]{:S(2)}) copy-start(bf16[32,2560]{1,0:T(8,128)(2,1)} %param.17) | copy-start | bytes 491524
  80.0 20.3 %copy-start.6 = (f32[2560]{0:T(1024)S(1)}, f32[2560]{0:T(1024)}, u32[]{:S(2)}) copy-start(f32[2560]{0:T(1024)} %param.31) | copy-start | bytes 30724
  80.4 20.0 %copy-start.1 = (bf16[2560,512]{1,0:T(8,128)(2,1)S(1)}, bf16[2560,512]{1,0:T(8,128)(2,1)}, u32[]{:S(2)}) copy-start(bf16[2560,512]{1,0:T(8,128)(2,1)} %param.28) | copy-start | bytes 7864324
  82.4 5.6 %collective-permute-start.10 = (bf16[32,2560]{1,0:T(8,128)(2,1)S(1)}, bf16[32,2560]{1,0:T(8,128)(2,1)S(1)}, u32[]{:S(2)}, u32[]{:S(2)}) collective-permute-start(bf16[32,2560]{1,0:T(8,128)(2,1)S(1)} %convolution_convert_fusion.1), channel_id=1, source_target_pairs={{0,4},{1,5},{2,6},{3,7},{4,0},{5,1},{6,2},{7,3},{8,9},{9,8},{10,11... | collective-permute-start | bytes 491528 | tf_op jit(solution)/shard_map/ppermute | solution.py:137
  88.0 5.4 %collective-permute-start.11 = (bf16[32,2560]{1,0:T(8,128)(2,1)S(1)}, bf16[32,2560]{1,0:T(8,128)(2,1)S(1)}, u32[]{:S(2)}, u32[]{:S(2)}) collective-permute-start(bf16[32,2560]{1,0:T(8,128)(2,1)S(1)} %add_convert_fusion.5), channel_id=1, source_target_pairs={{0,1},{1,0},{2,3},{3,2},{4,5},{5,4},{6,7},{7,6},{8,11},{9,10},{10,... | collective-permute-start | bytes 491528 | tf_op jit(solution)/shard_map/ppermute | solution.py:137
  93.5 6.6 %collective-permute-start.12 = (bf16[32,2560]{1,0:T(8,128)(2,1)S(1)}, bf16[32,2560]{1,0:T(8,128)(2,1)S(1)}, u32[]{:S(2)}, u32[]{:S(2)}) collective-permute-start(bf16[32,2560]{1,0:T(8,128)(2,1)S(1)} %add_convert_fusion.4), channel_id=1, source_target_pairs={{0,3},{1,2},{2,1},{3,0},{4,7},{5,6},{6,5},{7,4},{8,12},{9,13},{10,... | collective-permute-start | bytes 491528 | tf_op jit(solution)/shard_map/ppermute | solution.py:137
  101.0 21.3 %copy-start.4 = (f32[2560]{0:T(1024)S(1)}, f32[2560]{0:T(1024)}, u32[]{:S(2)}) copy-start(f32[2560]{0:T(1024)} %param.33) | copy-start | bytes 30724
  101.0 21.3 %copy-start.5 = (f32[2560]{0:T(1024)S(1)}, f32[2560]{0:T(1024)}, u32[]{:S(2)}) copy-start(f32[2560]{0:T(1024)} %param.32) | copy-start | bytes 30724
  103.8 5.4 %collective-permute-start.13 = (bf16[32,2560]{1,0:T(8,128)(2,1)S(1)}, bf16[32,2560]{1,0:T(8,128)(2,1)S(1)}, u32[]{:S(2)}, u32[]{:S(2)}) collective-permute-start(bf16[32,2560]{1,0:T(8,128)(2,1)S(1)} %convolution_convert_fusion), channel_id=1, source_target_pairs={{0,4},{1,5},{2,6},{3,7},{4,0},{5,1},{6,2},{7,3},{8,9},{9,8},{10,11... | collective-permute-start | bytes 491528 | tf_op jit(solution)/shard_map/ppermute | solution.py:137
  109.3 5.4 %collective-permute-start.14 = (bf16[32,2560]{1,0:T(8,128)(2,1)S(1)}, bf16[32,2560]{1,0:T(8,128)(2,1)S(1)}, u32[]{:S(2)}, u32[]{:S(2)}) collective-permute-start(bf16[32,2560]{1,0:T(8,128)(2,1)S(1)} %add_convert_fusion.2), channel_id=1, source_target_pairs={{0,1},{1,0},{2,3},{3,2},{4,5},{5,4},{6,7},{7,6},{8,11},{9,10},{10,... | collective-permute-start | bytes 491528 | tf_op jit(solution)/shard_map/ppermute | solution.py:137
  114.7 6.6 %collective-permute-start.15 = (bf16[32,2560]{1,0:T(8,128)(2,1)S(1)}, bf16[32,2560]{1,0:T(8,128)(2,1)S(1)}, u32[]{:S(2)}, u32[]{:S(2)}) collective-permute-start(bf16[32,2560]{1,0:T(8,128)(2,1)S(1)} %add_convert_fusion.1), channel_id=1, source_target_pairs={{0,3},{1,2},{2,1},{3,0},{4,7},{5,6},{6,5},{7,4},{8,12},{9,13},{10,... | collective-permute-start | bytes 491528 | tf_op jit(solution)/shard_map/ppermute | solution.py:137

commit v9 on v8

--- a/solution.py
+++ b/solution.py
@@ -20,23 +20,45 @@
 
 def prefix_kernel(count_ref, half_ref, q_ref, kt_ref, vt_ref, out_ref):
     step = pl.program_id(0)
-    for i in range(q_ref.shape[0]):
+    rows = q_ref.shape[1]
+    length = kt_ref.shape[2]
+
+    def one(i, masked):
         q = q_ref[i]
         kt = kt_ref[i]
         vt = vt_ref[i]
         s = jnp.dot(q, kt, preferred_element_type=jnp.float32) * (HEAD_SIZE ** -0.5)
-        place = lax.broadcasted_iota(jnp.int32, s.shape, 1)
-        valid = place < count_ref[2 * (step * q_ref.shape[0] + i) + half_ref[0]]
-        s = jnp.where(valid, s, jnp.float32(-1e30))
+        if masked:
+            place = lax.broadcasted_iota(jnp.int32, s.shape, 1)
+            valid = place < count_ref[2 * (step * q_ref.shape[0] + i) + half_ref[0]]
+            s = jnp.where(valid, s, jnp.float32(-1e30))
         top = jnp.max(s, axis=1, keepdims=True)
-        w = jnp.where(valid, jnp.exp(s - top), 0.0)
+        w = jnp.exp(s - top)
+        if masked:
+            w = jnp.where(valid, w, 0.0)
         total = jnp.sum(w, axis=1, keepdims=True)
         o = lax.dot_general(vt, w.astype(jnp.bfloat16), (((1,), (1,)), ((), ())),
                             preferred_element_type=jnp.float32)
-        lane = lax.broadcasted_iota(jnp.int32, (s.shape[0], 128), 1)
+        lane = lax.broadcasted_iota(jnp.int32, (rows, 128), 1)
         stats = jnp.where(lane == 0, top, jnp.where(lane == 1, total, 0.0))
         out_ref[i, 0:HEAD_SIZE, :] = o
         out_ref[i, HEAD_SIZE:PACK, :] = jnp.transpose(stats)[0:PACK - HEAD_SIZE, :]
+
+    for i in range(q_ref.shape[0]):
+        count = count_ref[2 * (step * q_ref.shape[0] + i) + half_ref[0]]
+
+        @pl.when(count >= length)
+        def _():
+            one(i, False)
+
+        @pl.when(jnp.logical_and(count > 0, count < length))
+        def _():
+            one(i, True)
+
+        @pl.when(count <= 0)
+        def _():
+            row = lax.broadcasted_iota(jnp.int32, (PACK, rows), 0)
+            out_ref[i] = jnp.where(row == HEAD_SIZE, jnp.float32(-1e30), 0.0)
 
 
 def prefix_partials(count, half, q, kt, vt):

time: 123 us -> 131 us (1.065); the launches traced: 123 us -> 129 us
  Pallas kernels: 11.2 us -> 18.5 us
  starting transfers between devices: 30.9 us -> 24.7 us
  waiting for transfers between devices: 58.3 us -> 63.7 us
    pallas_call x2, Pallas kernels: 11.2 us -> 18.5 us  [prefix_partials(): pl.pallas_call(prefix_kernel, grid_spec=pltpu.PrefetchScalarGridSpec(num_...]
    ppermute x10, starting transfers between devices: 20.6 us -> 14.3 us  [exchange(): return lax.ppermute(x, axis, perm=[(i, i ^ 1 << bit) for i in range(n)])]
    ppermute x10, waiting for transfers between devices: 33.7 us -> 39.2 us  [exchange(): return lax.ppermute(x, axis, perm=[(i, i ^ 1 << bit) for i in range(n)])]
  transfers between devices with their start and end apart: 16 -> 16, of which waited for: 15 -> 15; matrix products, arithmetic and copies ran while one was open for 3% -> 3% of each run, Pallas kernels for 4% -> 7%
where the time goes in v9:
time: 131 us; the launch traced here: 129 us
  waiting for transfers between devices  63.7 us (49%)
  starting transfers between devices  24.7 us (19%)
  Pallas kernels  18.5 us (14%)
  other arithmetic  8.63 us (7%)
  matrix products  8.61 us (7%)
  local copies, waits for them, and re-layouts  4.08 us (3%)
    ppermute x10, waiting for transfers between devices, exchange(): return lax.ppermute(x, axis, perm=[(i, i ^ 1 << bit) for i in range(n)])  39.2 us
    ppermute x6, waiting for transfers between devices, allreduce_bf16(): other = lax.ppermute(cur, ('req', 'mlp'), perm=perm)  24.5 us
    pallas_call x2, Pallas kernels, prefix_partials(): pl.pallas_call(prefix_kernel, grid_spec=pltpu.PrefetchScalarGridSpec(num_...  18.5 us
    ppermute x10, starting transfers between devices, exchange(): return lax.ppermute(x, axis, perm=[(i, i ^ 1 << bit) for i in range(n)])  14.3 us
    ppermute x6, starting transfers between devices, allreduce_bf16(): other = lax.ppermute(cur, ('req', 'mlp'), perm=perm)  10.3 us
    dot_general x1, matrix products, on_device(): jnp.dot(hidden, down_weight, preferred_element_type=jnp.float32)  2.83 us
  transfers between devices with their start and end apart: 16, of which 15 were waited for; matrix products, arithmetic and copies ran while one was open for 3% of the time, Pallas kernels for 7%

profile of v9, /device:TPU:6, one launch (start us, length us, event | category | flops | bytes accessed | tf_op | source)
XLA Modules:
  0.0 129.4 jit_solution(2071680207068261750)
XLA Ops:
  0.7 7.3 %collective-permute-start = (bf16[1,32,320]{2,1,0:T(8,128)(2,1)}, bf16[1,32,320]{2,1,0:T(8,128)(2,1)S(1)}, u32[]{:S(2)}, u32[]{:S(2)}) collective-permute-start(bf16[1,32,320]{2,1,0:T(8,128)(2,1)} %bitcast.203), channel_id=1, source_target_pairs={{0,128},{8,136},{16,144},{24,152},{32,160},{40,168},{48,176},{56,1... | collective-permute-start | bytes 61448 | tf_op jit(solution)/shard_map/ppermute | solution.py:91
  7.9 2.0 %collective-permute-done = bf16[1,32,320]{2,1,0:T(8,128)(2,1)S(1)} collective-permute-done((bf16[1,32,320]{2,1,0:T(8,128)(2,1)}, bf16[1,32,320]{2,1,0:T(8,128)(2,1)S(1)}, u32[]{:S(2)}, u32[]{:S(2)}) %collective-permute-start) | collective-permute-done | bytes 20512 | tf_op jit(solution)/shard_map/ppermute | solution.py:91
  10.0 0.7 select_bitcast_fusion.5
  10.7 1.5 %collective-permute-start.1 = (bf16[2,1,32,320]{3,2,0,1:T(8,128)(2,1)S(1)}, bf16[2,1,32,320]{3,2,0,1:T(8,128)(2,1)S(1)}, u32[]{:S(2)}, u32[]{:S(2)}) collective-permute-start(bf16[2,1,32,320]{3,2,0,1:T(8,128)(2,1)S(1)} %fusion.36), channel_id=1, source_target_pairs={{0,16},{8,24},{16,0},{24,8},{32,48},{40,56},{48,32},{56,40},{64,80... | collective-permute-start | bytes 122888 | tf_op jit(solution)/shard_map/ppermute | solution.py:91
  12.2 4.2 %collective-permute-done.1 = bf16[2,1,32,320]{3,2,0,1:T(8,128)(2,1)S(1)} collective-permute-done((bf16[2,1,32,320]{3,2,0,1:T(8,128)(2,1)S(1)}, bf16[2,1,32,320]{3,2,0,1:T(8,128)(2,1)S(1)}, u32[]{:S(2)}, u32[]{:S(2)}) %collective-permute-start.1) | collective-permute-done | bytes 40992 | tf_op jit(solution)/shard_map/ppermute | solution.py:91
  16.5 2.1 %collective-permute-start.2 = (bf16[2,2,1,32,320]{4,3,1,0,2:T(8,128)(2,1)S(1)}, bf16[2,2,1,32,320]{4,3,1,0,2:T(8,128)(2,1)S(1)}, u32[]{:S(2)}, u32[]{:S(2)}) collective-permute-start(bf16[2,2,1,32,320]{4,3,1,0,2:T(8,128)(2,1)S(1)} %fusion.24), channel_id=1, source_target_pairs={{0,64},{8,72},{16,80},{24,88},{32,96},{40,104},{48,112},{56,120},{... | collective-permute-start | bytes 245768 | tf_op jit(solution)/shard_map/ppermute | solution.py:91
  18.6 4.6 %collective-permute-done.2 = bf16[2,2,1,32,320]{4,3,1,0,2:T(8,128)(2,1)S(1)} collective-permute-done((bf16[2,2,1,32,320]{4,3,1,0,2:T(8,128)(2,1)S(1)}, bf16[2,2,1,32,320]{4,3,1,0,2:T(8,128)(2,1)S(1)}, u32[]{:S(2)}, u32[]{:S(2)}) %collective-permute-start.2) | collective-permute-done | bytes 81952 | tf_op jit(solution)/shard_map/ppermute | solution.py:91
  23.5 5.6 %collective-permute-done.3 = bf16[2,2,2,1,32,320]{5,4,2,1,0,3:T(8,128)(2,1)S(1)} collective-permute-done((bf16[2,2,2,1,32,320]{5,4,2,1,0,3:T(8,128)(2,1)S(1)}, bf16[2,2,2,1,32,320]{5,4,2,1,0,3:T(8,128)(2,1)S(1)}, u32[]{:S(2)}, u32[]{:S(2)}) %collective-permute-start.3) | collective-permute-done | bytes 163872 | tf_op jit(solution)/shard_map/ppermute | solution.py:91
  29.2 0.8 fusion.12
  30.0 0.5 subtract_clamp_fusion.count_ref
  30.6 1.4 %collective-permute-done.4 = bf16[2,2,2,2,1,32,320]{6,5,3,2,1,0,4:T(8,128)(2,1)S(1)} collective-permute-done((bf16[2,2,2,2,1,32,320]{6,5,3,2,1,0,4:T(8,128)(2,1)}, bf16[2,2,2,2,1,32,320]{6,5,3,2,1,0,4:T(8,128)(2,1)S(1)}, u32[]{:S(2)}, u32[]{:S(2)}) %collective-permute-start.4) | collective-permute-done | bytes 327712 | tf_op jit(solution)/shard_map/ppermute | solution.py:91
  32.5 1.6 %reshape_reshape.3.q_ref = bf16[16,2,128,80]{3,2,1,0:T(8,128)(2,1)} reshape(bf16[2,2,2,2,2,1,32,320]{7,6,4,3,2,1,0,5:T(8,128)(2,1)S(1)} %copy.55) | data formatting | bytes 1310720 | tf_op jit(solution)/shard_map/reshape;reshape | solution.py:202
  34.1 9.1 %shard_map.177 = f32[16,88,128]{2,1,0:T(8,128)} custom-call(s32[32]{0:T(128)} %subtract_clamp_fusion.count_ref, s32[1]{0:T(128)} %bitcast.33.half_ref, bf16[16,2,128,80]{3,2,1,0:T(8,128)(2,1)} %reshape_reshape.3.q_ref, bf16[16,2,80,512]{3,2,1,0:T(8,128)(2,1)} %bitcast.192, bf16[16,2,80,512]{3,2,1,0:T(8,128)(2,1)} %bitcast.194), custom_call_target="tpu_custom_call" | custom-call | flops 335544320 | bytes 3670016 | tf_op jit(solution)/shard_map/pallas_call | solution.py:68
  43.5 1.3 select_reduce_fusion
  44.8 9.4 %shard_map.176 = f32[16,88,128]{2,1,0:T(8,128)} custom-call(s32[32]{0:T(128)} %subtract_clamp_fusion.count_ref, s32[1]{0:T(128)} %bitcast.half_ref, bf16[16,2,128,80]{3,2,1,0:T(8,128)(2,1)} %reshape_reshape.3.q_ref, bf16[16,2,80,512]{3,2,1,0:T(8,128)(2,1)} %bitcast.193, bf16[16,2,80,512]{3,2,1,0:T(8,128)(2,1)} %bitcast.195), custom_call_target="tpu_custom_call" | custom-call | flops 335544320 | bytes 3670016 | tf_op jit(solution)/shard_map/pallas_call | solution.py:68
  54.1 0.9 subtract_exponential_fusion.1
  55.0 1.2 fusion.6
  56.2 0.9 fusion.18
  57.5 0.4 select_reduce_fusion.1
  57.9 6.0 %collective-permute-done.6 = bf16[2,2,2,88,128]{4,3,2,1,0:T(8,128)(2,1)S(1)} collective-permute-done((bf16[2,2,2,88,128]{4,3,2,1,0:T(8,128)(2,1)S(1)}, bf16[2,2,2,88,128]{4,3,2,1,0:T(8,128)(2,1)S(1)}, u32[]{:S(2)}, u32[]{:S(2)}) %collective-permute-start.6) | collective-permute-done | bytes 180256 | tf_op jit(solution)/shard_map/ppermute | solution.py:91
  64.3 0.3 collective-permute-start.7
  64.6 1.3 %fusion.9 = f32[16,2,4,80]{3,2,1,0:T(4,128)S(1)} fusion(bf16[1,16,128,80]{2,3,1,0:T(8,128)(2,1)} %param.24, f32[16,2,4,128]{3,2,1,0:T(4,128)S(1)} %get-tuple-element.40, f32[16,2,4]{2,1,0:T(2,128)S(1)} %max.65, pred[16,128]{1,0:T(8,128)(4,1)S(1)} %iota_compare_fusion), kind=kOutput, calls=%fused_computation.29 | convolution fusion | flops 2670592 | bytes 436736 | tf_op jit(solution)/shard_map/ksjgt,stkh->ksjgh/dot_general | solution.py:251
  65.9 5.1 %collective-permute-done.7 = bf16[2,2,88,128]{3,2,0,1:T(8,128)(2,1)S(1)} collective-permute-done((bf16[2,2,88,128]{3,2,0,1:T(8,128)(2,1)S(1)}, bf16[2,2,88,128]{3,2,0,1:T(8,128)(2,1)S(1)}, u32[]{:S(2)}, u32[]{:S(2)}) %collective-permute-start.7) | collective-permute-done | bytes 90144 | tf_op jit(solution)/shard_map/ppermute | solution.py:91
  71.3 2.7 %collective-permute-start.8 = (bf16[2,88,128]{2,1,0:T(8,128)(2,1)S(1)}, bf16[2,88,128]{2,1,0:T(8,128)(2,1)S(1)}, u32[]{:S(2)}, u32[]{:S(2)}) collective-permute-start(bf16[2,88,128]{2,1,0:T(8,128)(2,1)S(1)} %concatenate.47), channel_id=1, source_target_pairs={{0,16},{8,24},{16,0},{24,8},{32,48},{40,56},{48,32},{56,40},{64,80... | collective-permute-start | bytes 135176 | tf_op jit(solution)/shard_map/ppermute | solution.py:91
  74.0 0.2 fusion.26
  74.2 2.7 %collective-permute-done.8 = bf16[2,88,128]{2,1,0:T(8,128)(2,1)S(1)} collective-permute-done((bf16[2,88,128]{2,1,0:T(8,128)(2,1)S(1)}, bf16[2,88,128]{2,1,0:T(8,128)(2,1)S(1)}, u32[]{:S(2)}, u32[]{:S(2)}) %collective-permute-start.8) | collective-permute-done | bytes 45088 | tf_op jit(solution)/shard_map/ppermute | solution.py:91
  77.4 7.5 %collective-permute-done.9 = bf16[88,128]{1,0:T(8,128)(2,1)S(1)} collective-permute-done((bf16[88,128]{1,0:T(8,128)(2,1)S(1)}, bf16[88,128]{1,0:T(8,128)(2,1)S(1)}, u32[]{:S(2)}, u32[]{:S(2)}) %collective-permute-start.9) | collective-permute-done | bytes 22560 | tf_op jit(solution)/shard_map/ppermute | solution.py:91
  85.0 0.5 broadcast.97
  85.5 0.7 fusion.57
  86.6 0.3 fusion.5
  87.0 2.0 %convolution_convert_fusion.1 = bf16[32,2560]{1,0:T(8,128)(2,1)S(1)} fusion(bf16[32,320]{1,0:T(8,128)(2,1)S(1)} %reshape_transpose.3, bf16[320,2560]{1,0:T(8,128)(2,1)} %param.27), kind=kOutput, calls=%fused_computation.1 | convolution fusion | flops 52510720 | bytes 1822720 | tf_op jit(solution)/shard_map/dot_general | solution.py:273
  89.0 0.9 collective-permute-start.10
  89.9 4.5 %collective-permute-done.10 = bf16[32,2560]{1,0:T(8,128)(2,1)S(1)} collective-permute-done((bf16[32,2560]{1,0:T(8,128)(2,1)S(1)}, bf16[32,2560]{1,0:T(8,128)(2,1)S(1)}, u32[]{:S(2)}, u32[]{:S(2)}) %collective-permute-start.10) | collective-permute-done | bytes 163872 | tf_op jit(solution)/shard_map/ppermute | solution.py:159
  94.4 1.7 %collective-permute-start.11 = (bf16[32,2560]{1,0:T(8,128)(2,1)S(1)}, bf16[32,2560]{1,0:T(8,128)(2,1)S(1)}, u32[]{:S(2)}, u32[]{:S(2)}) collective-permute-start(bf16[32,2560]{1,0:T(8,128)(2,1)S(1)} %add_convert_fusion.5), channel_id=1, source_target_pairs={{0,1},{1,0},{2,3},{3,2},{4,5},{5,4},{6,7},{7,6},{8,11},{9,10},{10,... | collective-permute-start | bytes 491528 | tf_op jit(solution)/shard_map/ppermute | solution.py:159
  96.1 3.7 %collective-permute-done.11 = bf16[32,2560]{1,0:T(8,128)(2,1)S(1)} collective-permute-done((bf16[32,2560]{1,0:T(8,128)(2,1)S(1)}, bf16[32,2560]{1,0:T(8,128)(2,1)S(1)}, u32[]{:S(2)}, u32[]{:S(2)}) %collective-permute-start.11) | collective-permute-done | bytes 163872 | tf_op jit(solution)/shard_map/ppermute | solution.py:159
  99.9 3.2 %collective-permute-start.12 = (bf16[32,2560]{1,0:T(8,128)(2,1)S(1)}, bf16[32,2560]{1,0:T(8,128)(2,1)S(1)}, u32[]{:S(2)}, u32[]{:S(2)}) collective-permute-start(bf16[32,2560]{1,0:T(8,128)(2,1)S(1)} %add_convert_fusion.4), channel_id=1, source_target_pairs={{0,3},{1,2},{2,1},{3,0},{4,7},{5,6},{6,5},{7,4},{8,12},{9,13},{10,... | collective-permute-start | bytes 491528 | tf_op jit(solution)/shard_map/ppermute | solution.py:159
  103.1 3.5 %collective-permute-done.12 = bf16[32,2560]{1,0:T(8,128)(2,1)S(1)} collective-permute-done((bf16[32,2560]{1,0:T(8,128)(2,1)S(1)}, bf16[32,2560]{1,0:T(8,128)(2,1)S(1)}, u32[]{:S(2)}, u32[]{:S(2)}) %collective-permute-start.12) | collective-permute-done | bytes 163872 | tf_op jit(solution)/shard_map/ppermute | solution.py:159
  106.8 0.5 fusion.58
  107.4 2.8 %convolution_convert_fusion = bf16[32,2560]{1,0:T(8,128)(2,1)S(1)} fusion(bf16[512,2560]{1,0:T(8,128)(2,1)S(1)} %copy-done, bf16[32,2560]{1,0:T(8,128)(2,1)S(1)} %multiply_convert_fusion, bf16[2560,512]{1,0:T(8,128)(2,1)} %param.29, f32[32,512]{1,0:T(8,128)S(1)} %fusion.58), kind=kOutput, calls=%fused_computation | convolution fusion | flops 167952384 | bytes 5636096 | tf_op jit(solution)/shard_map/dot_general | solution.py:287
  110.2 0.9 collective-permute-start.13
  111.1 4.5 %collective-permute-done.13 = bf16[32,2560]{1,0:T(8,128)(2,1)S(1)} collective-permute-done((bf16[32,2560]{1,0:T(8,128)(2,1)S(1)}, bf16[32,2560]{1,0:T(8,128)(2,1)S(1)}, u32[]{:S(2)}, u32[]{:S(2)}) %collective-permute-start.13) | collective-permute-done | bytes 163872 | tf_op jit(solution)/shard_map/ppermute | solution.py:159
  115.7 0.5 collective-permute-start.14
  116.2 4.9 %collective-permute-done.14 = bf16[32,2560]{1,0:T(8,128)(2,1)S(1)} collective-permute-done((bf16[32,2560]{1,0:T(8,128)(2,1)S(1)}, bf16[32,2560]{1,0:T(8,128)(2,1)S(1)}, u32[]{:S(2)}, u32[]{:S(2)}) %collective-permute-start.14) | collective-permute-done | bytes 163872 | tf_op jit(solution)/shard_map/ppermute | solution.py:159
  121.1 3.2 %collective-permute-start.15 = (bf16[32,2560]{1,0:T(8,128)(2,1)S(1)}, bf16[32,2560]{1,0:T(8,128)(2,1)S(1)}, u32[]{:S(2)}, u32[]{:S(2)}) collective-permute-start(bf16[32,2560]{1,0:T(8,128)(2,1)S(1)} %add_convert_fusion.1), channel_id=1, source_target_pairs={{0,3},{1,2},{2,1},{3,0},{4,7},{5,6},{6,5},{7,4},{8,12},{9,13},{10,... | collective-permute-start | bytes 491528 | tf_op jit(solution)/shard_map/ppermute | solution.py:159
  124.3 3.5 %collective-permute-done.15 = bf16[32,2560]{1,0:T(8,128)(2,1)S(1)} collective-permute-done((bf16[32,2560]{1,0:T(8,128)(2,1)S(1)}, bf16[32,2560]{1,0:T(8,128)(2,1)S(1)}, u32[]{:S(2)}, u32[]{:S(2)}) %collective-permute-start.15) | collective-permute-done | bytes 163872 | tf_op jit(solution)/shard_map/ppermute | solution.py:159
  127.7 0.2 multiply_reduce_fusion.1
  128.0 0.7 dynamic-slice_convert_fusion
  128.7 0.7 multiply_reduce_fusion
  (109 shorter events, 3.6 us)
Async XLA Ops:
  0.6 106.7 %copy-start = (bf16[512,2560]{1,0:T(8,128)(2,1)S(1)}, bf16[512,2560]{1,0:T(8,128)(2,1)}, u32[]{:S(2)}) copy-start(bf16[512,2560]{1,0:T(8,128)(2,1)} %param.30) | copy-start | bytes 7864324
  0.6 29.4 %copy-start.10 = (s32[32]{0:T(128)S(1)}, s32[32]{0:T(128)}, u32[]{:S(2)}) copy-start(s32[32]{0:T(128)} %param.25) | copy-start | bytes 388
  0.7 9.3 %collective-permute-start = (bf16[1,32,320]{2,1,0:T(8,128)(2,1)}, bf16[1,32,320]{2,1,0:T(8,128)(2,1)S(1)}, u32[]{:S(2)}, u32[]{:S(2)}) collective-permute-start(bf16[1,32,320]{2,1,0:T(8,128)(2,1)} %bitcast.203), channel_id=1, source_target_pairs={{0,128},{8,136},{16,144},{24,152},{32,160},{40,168},{48,176},{56,1... | collective-permute-start | bytes 61448 | tf_op jit(solution)/shard_map/ppermute | solution.py:91
  10.7 5.7 %collective-permute-start.1 = (bf16[2,1,32,320]{3,2,0,1:T(8,128)(2,1)S(1)}, bf16[2,1,32,320]{3,2,0,1:T(8,128)(2,1)S(1)}, u32[]{:S(2)}, u32[]{:S(2)}) collective-permute-start(bf16[2,1,32,320]{3,2,0,1:T(8,128)(2,1)S(1)} %fusion.36), channel_id=1, source_target_pairs={{0,16},{8,24},{16,0},{24,8},{32,48},{40,56},{48,32},{56,40},{64,80... | collective-permute-start | bytes 122888 | tf_op jit(solution)/shard_map/ppermute | solution.py:91
  16.5 6.8 %collective-permute-start.2 = (bf16[2,2,1,32,320]{4,3,1,0,2:T(8,128)(2,1)S(1)}, bf16[2,2,1,32,320]{4,3,1,0,2:T(8,128)(2,1)S(1)}, u32[]{:S(2)}, u32[]{:S(2)}) collective-permute-start(bf16[2,2,1,32,320]{4,3,1,0,2:T(8,128)(2,1)S(1)} %fusion.24), channel_id=1, source_target_pairs={{0,64},{8,72},{16,80},{24,88},{32,96},{40,104},{48,112},{56,120},{... | collective-permute-start | bytes 245768 | tf_op jit(solution)/shard_map/ppermute | solution.py:91
  23.3 5.8 %collective-permute-start.3 = (bf16[2,2,2,1,32,320]{5,4,2,1,0,3:T(8,128)(2,1)S(1)}, bf16[2,2,2,1,32,320]{5,4,2,1,0,3:T(8,128)(2,1)S(1)}, u32[]{:S(2)}, u32[]{:S(2)}) collective-permute-start(bf16[2,2,2,1,32,320]{5,4,2,1,0,3:T(8,128)(2,1)S(1)} %fusion.15), channel_id=1, source_target_pairs={{0,32},{8,40},{16,48},{24,56},{32,0},{40,8},{48,16},{56,24},{64,96... | collective-permute-start | bytes 491528 | tf_op jit(solution)/shard_map/ppermute | solution.py:91
  30.0 1.9 %collective-permute-start.4 = (bf16[2,2,2,2,1,32,320]{6,5,3,2,1,0,4:T(8,128)(2,1)}, bf16[2,2,2,2,1,32,320]{6,5,3,2,1,0,4:T(8,128)(2,1)S(1)}, u32[]{:S(2)}, u32[]{:S(2)}) collective-permute-start(bf16[2,2,2,2,1,32,320]{6,5,3,2,1,0,4:T(8,128)(2,1)} %fusion.12), channel_id=1, source_target_pairs={{0,8},{8,0},{16,24},{24,16},{32,40},{40,32},{48,56},{56,48},{64,72... | collective-permute-start | bytes 983048 | tf_op jit(solution)/shard_map/ppermute | solution.py:91
  34.1 9.2 %copy-start.3 = (bf16[32,320]{1,0:T(8,128)(2,1)S(1)}, bf16[32,320]{1,0:T(8,128)(2,1)}, u32[]{:S(2)}) copy-start(bf16[32,320]{1,0:T(8,128)(2,1)} %param.18) | copy-start | bytes 61444
  34.1 9.3 %copy-start.7 = (s32[1,16]{1,0:T(1,128)S(1)}, s32[1,16]{1,0:T(1,128)}, u32[]{:S(2)}) copy-start(s32[1,16]{1,0:T(1,128)} %param.26) | copy-start | bytes 196
  43.2 10.9 %collective-permute-start.5 = (f32[16,88,128]{2,1,0:T(8,128)}, f32[16,88,128]{2,1,0:T(8,128)S(1)}, u32[]{:S(2)}, u32[]{:S(2)}) collective-permute-start(f32[16,88,128]{2,1,0:T(8,128)} %shard_map.177), channel_id=1, source_target_pairs={{0,8},{8,0},{16,24},{24,16},{32,40},{40,32},{48,56},{56,48},{64,72... | collective-permute-start | bytes 2162696 | tf_op jit(solution)/shard_map/ppermute | solution.py:91
  55.0 2.5 %copy-start.8 = (bf16[32,80]{1,0:T(8,128)(2,1)S(1)}, bf16[32,80]{1,0:T(8,128)(2,1)}, u32[]{:S(2)}) copy-start(bf16[32,80]{1,0:T(8,128)(2,1)} %param.19) | copy-start | bytes 15364
  57.4 6.5 %collective-permute-start.6 = (bf16[2,2,2,88,128]{4,3,2,1,0:T(8,128)(2,1)S(1)}, bf16[2,2,2,88,128]{4,3,2,1,0:T(8,128)(2,1)S(1)}, u32[]{:S(2)}, u32[]{:S(2)}) collective-permute-start(bf16[2,2,2,88,128]{4,3,2,1,0:T(8,128)(2,1)S(1)} %concatenate.41), channel_id=1, source_target_pairs={{0,32},{8,40},{16,48},{24,56},{32,0},{40,8},{48,16},{56,24},{64,96... | collective-permute-start | bytes 540680 | tf_op jit(solution)/shard_map/ppermute | solution.py:91
  64.2 22.4 %copy-start.9 = (bf16[32,80]{1,0:T(8,128)(2,1)S(1)}, bf16[32,80]{1,0:T(8,128)(2,1)}, u32[]{:S(2)}) copy-start(bf16[32,80]{1,0:T(8,128)(2,1)} %param.20) | copy-start | bytes 15364
  64.3 6.7 %collective-permute-start.7 = (bf16[2,2,88,128]{3,2,0,1:T(8,128)(2,1)S(1)}, bf16[2,2,88,128]{3,2,0,1:T(8,128)(2,1)S(1)}, u32[]{:S(2)}, u32[]{:S(2)}) collective-permute-start(bf16[2,2,88,128]{3,2,0,1:T(8,128)(2,1)S(1)} %concatenate.44), channel_id=1, source_target_pairs={{0,64},{8,72},{16,80},{24,88},{32,96},{40,104},{48,112},{56,120},{... | collective-permute-start | bytes 270344 | tf_op jit(solution)/shard_map/ppermute | solution.py:91
  71.3 5.6 %collective-permute-start.8 = (bf16[2,88,128]{2,1,0:T(8,128)(2,1)S(1)}, bf16[2,88,128]{2,1,0:T(8,128)(2,1)S(1)}, u32[]{:S(2)}, u32[]{:S(2)}) collective-permute-start(bf16[2,88,128]{2,1,0:T(8,128)(2,1)S(1)} %concatenate.47), channel_id=1, source_target_pairs={{0,16},{8,24},{16,0},{24,8},{32,48},{40,56},{48,32},{56,40},{64,80... | collective-permute-start | bytes 135176 | tf_op jit(solution)/shard_map/ppermute | solution.py:91
  77.1 7.8 %collective-permute-start.9 = (bf16[88,128]{1,0:T(8,128)(2,1)S(1)}, bf16[88,128]{1,0:T(8,128)(2,1)S(1)}, u32[]{:S(2)}, u32[]{:S(2)}) collective-permute-start(bf16[88,128]{1,0:T(8,128)(2,1)S(1)} %concatenate.50), channel_id=1, source_target_pairs={{0,128},{8,136},{16,144},{24,152},{32,160},{40,168},{48,176},{56,1... | collective-permute-start | bytes 67592 | tf_op jit(solution)/shard_map/ppermute | solution.py:91
  86.6 19.9 %copy-start.2 = (bf16[32,2560]{1,0:T(8,128)(2,1)S(1)}, bf16[32,2560]{1,0:T(8,128)(2,1)}, u32[]{:S(2)}) copy-start(bf16[32,2560]{1,0:T(8,128)(2,1)} %param.17) | copy-start | bytes 491524
  86.6 20.1 %copy-start.6 = (f32[2560]{0:T(1024)S(1)}, f32[2560]{0:T(1024)}, u32[]{:S(2)}) copy-start(f32[2560]{0:T(1024)} %param.31) | copy-start | bytes 30724
  87.0 19.8 %copy-start.1 = (bf16[2560,512]{1,0:T(8,128)(2,1)S(1)}, bf16[2560,512]{1,0:T(8,128)(2,1)}, u32[]{:S(2)}) copy-start(bf16[2560,512]{1,0:T(8,128)(2,1)} %param.28) | copy-start | bytes 7864324
  89.0 5.4 %collective-permute-start.10 = (bf16[32,2560]{1,0:T(8,128)(2,1)S(1)}, bf16[32,2560]{1,0:T(8,128)(2,1)S(1)}, u32[]{:S(2)}, u32[]{:S(2)}) collective-permute-start(bf16[32,2560]{1,0:T(8,128)(2,1)S(1)} %convolution_convert_fusion.1), channel_id=1, source_target_pairs={{0,4},{1,5},{2,6},{3,7},{4,0},{5,1},{6,2},{7,3},{8,9},{9,8},{10,11... | collective-permute-start | bytes 491528 | tf_op jit(solution)/shard_map/ppermute | solution.py:159
  94.4 5.4 %collective-permute-start.11 = (bf16[32,2560]{1,0:T(8,128)(2,1)S(1)}, bf16[32,2560]{1,0:T(8,128)(2,1)S(1)}, u32[]{:S(2)}, u32[]{:S(2)}) collective-permute-start(bf16[32,2560]{1,0:T(8,128)(2,1)S(1)} %add_convert_fusion.5), channel_id=1, source_target_pairs={{0,1},{1,0},{2,3},{3,2},{4,5},{5,4},{6,7},{7,6},{8,11},{9,10},{10,... | collective-permute-start | bytes 491528 | tf_op jit(solution)/shard_map/ppermute | solution.py:159
  99.9 6.6 %collective-permute-start.12 = (bf16[32,2560]{1,0:T(8,128)(2,1)S(1)}, bf16[32,2560]{1,0:T(8,128)(2,1)S(1)}, u32[]{:S(2)}, u32[]{:S(2)}) collective-permute-start(bf16[32,2560]{1,0:T(8,128)(2,1)S(1)} %add_convert_fusion.4), channel_id=1, source_target_pairs={{0,3},{1,2},{2,1},{3,0},{4,7},{5,6},{6,5},{7,4},{8,12},{9,13},{10,... | collective-permute-start | bytes 491528 | tf_op jit(solution)/shard_map/ppermute | solution.py:159
  107.4 21.3 %copy-start.4 = (f32[2560]{0:T(1024)S(1)}, f32[2560]{0:T(1024)}, u32[]{:S(2)}) copy-start(f32[2560]{0:T(1024)} %param.33) | copy-start | bytes 30724
  107.4 21.3 %copy-start.5 = (f32[2560]{0:T(1024)S(1)}, f32[2560]{0:T(1024)}, u32[]{:S(2)}) copy-start(f32[2560]{0:T(1024)} %param.32) | copy-start | bytes 30724
  110.2 5.4 %collective-permute-start.13 = (bf16[32,2560]{1,0:T(8,128)(2,1)S(1)}, bf16[32,2560]{1,0:T(8,128)(2,1)S(1)}, u32[]{:S(2)}, u32[]{:S(2)}) collective-permute-start(bf16[32,2560]{1,0:T(8,128)(2,1)S(1)} %convolution_convert_fusion), channel_id=1, source_target_pairs={{0,4},{1,5},{2,6},{3,7},{4,0},{5,1},{6,2},{7,3},{8,9},{9,8},{10,11... | collective-permute-start | bytes 491528 | tf_op jit(solution)/shard_map/ppermute | solution.py:159
  115.7 5.4 %collective-permute-start.14 = (bf16[32,2560]{1,0:T(8,128)(2,1)S(1)}, bf16[32,2560]{1,0:T(8,128)(2,1)S(1)}, u32[]{:S(2)}, u32[]{:S(2)}) collective-permute-start(bf16[32,2560]{1,0:T(8,128)(2,1)S(1)} %add_convert_fusion.2), channel_id=1, source_target_pairs={{0,1},{1,0},{2,3},{3,2},{4,5},{5,4},{6,7},{7,6},{8,11},{9,10},{10,... | collective-permute-start | bytes 491528 | tf_op jit(solution)/shard_map/ppermute | solution.py:159
  121.1 6.6 %collective-permute-start.15 = (bf16[32,2560]{1,0:T(8,128)(2,1)S(1)}, bf16[32,2560]{1,0:T(8,128)(2,1)S(1)}, u32[]{:S(2)}, u32[]{:S(2)}) collective-permute-start(bf16[32,2560]{1,0:T(8,128)(2,1)S(1)} %add_convert_fusion.1), channel_id=1, source_target_pairs={{0,3},{1,2},{2,1},{3,0},{4,7},{5,6},{6,5},{7,4},{8,12},{9,13},{10,... | collective-permute-start | bytes 491528 | tf_op jit(solution)/shard_map/ppermute | solution.py:159

commit v10 on v8

--- a/solution.py
+++ b/solution.py
@@ -175,29 +175,6 @@
     gather_order = [b for i, b in enumerate(gather_order) if b not in gather_order[:i]]
     reduce_order = gather_order[::-1]
 
-    gathered = gather_rows(queries, "req", req_count, gather_order)
-    pairs = prompts // 2
-    query_all = gathered.reshape(pairs, 2, rows, HEAD_SIZE)
-    prefix_key_block = jnp.swapaxes(
-        shared_prefix_keys.reshape(pairs, 2, piece_len, HEAD_SIZE * kv_local), 2, 3
-    )
-    prefix_value_block = jnp.swapaxes(
-        shared_prefix_values.reshape(pairs, 2, piece_len, HEAD_SIZE * kv_local), 2, 3
-    )
-    count = jnp.clip(prompt_prefix_length - req_index * piece_len, 0, piece_len).astype(jnp.int32)
-    own_low = (req_index & 1).astype(jnp.int32)
-    send_half = prefix_partials(
-        count, (1 - own_low)[None], query_all, prefix_key_block, prefix_value_block
-    )
-    got = exchange(send_half, "req", req_count, 0)
-    keep_half = prefix_partials(count, own_low[None], query_all, prefix_key_block, prefix_value_block)
-    merged = merge_partials(keep_half, got)
-    nb = req_count.bit_length() - 1
-    merged = merged.reshape((2,) * (nb - 1) + merged.shape[1:])
-    own_part = reduce_partials(
-        merged, "req", req_count, list(range(nb - 1, 0, -1)), [b for b in reduce_order if b != 0]
-    )
-
     query_own = queries.reshape(SAMPLE_COUNT, DECODE_TOKENS, kv_local, query_groups, HEAD_SIZE)
     tail_key_block = sample_tail_keys.reshape(SAMPLE_COUNT, TAIL_LENGTH, kv_local, HEAD_SIZE)
     tail_value_block = sample_tail_values.reshape(SAMPLE_COUNT, TAIL_LENGTH, kv_local, HEAD_SIZE)
@@ -235,6 +212,32 @@
     local_out = local_out + jnp.einsum(
         "ksjgi,sikh->ksjgh", w_new.astype(jnp.bfloat16), fresh_v, preferred_element_type=jnp.float32
     )
+    gathered = gather_rows(queries, "req", req_count, gather_order)
+    gathered, local_out, local_top, local_sum = lax.optimization_barrier(
+        (gathered, local_out, local_top, local_sum)
+    )
+    pairs = prompts // 2
+    query_all = gathered.reshape(pairs, 2, rows, HEAD_SIZE)
+    prefix_key_block = jnp.swapaxes(
+        shared_prefix_keys.reshape(pairs, 2, piece_len, HEAD_SIZE * kv_local), 2, 3
+    )
+    prefix_value_block = jnp.swapaxes(
+        shared_prefix_values.reshape(pairs, 2, piece_len, HEAD_SIZE * kv_local), 2, 3
+    )
+    count = jnp.clip(prompt_prefix_length - req_index * piece_len, 0, piece_len).astype(jnp.int32)
+    own_low = (req_index & 1).astype(jnp.int32)
+    send_half = prefix_partials(
+        count, (1 - own_low)[None], query_all, prefix_key_block, prefix_value_block
+    )
+    got = exchange(send_half, "req", req_count, 0)
+    keep_half = prefix_partials(count, own_low[None], query_all, prefix_key_block, prefix_value_block)
+    merged = merge_partials(keep_half, got)
+    nb = req_count.bit_length() - 1
+    merged = merged.reshape((2,) * (nb - 1) + merged.shape[1:])
+    own_part = reduce_partials(
+        merged, "req", req_count, list(range(nb - 1, 0, -1)), [b for b in reduce_order if b != 0]
+    )
+
     lead = (kv_local, SAMPLE_COUNT, DECODE_TOKENS, query_groups)
     source_out = jnp.transpose(own_part[:HEAD_SIZE].reshape((HEAD_SIZE,) + lead), (1, 2, 3, 4, 0))
     source_top = own_part[HEAD_SIZE].reshape(lead)

time: 123 us -> 123 us (level)
  starting transfers between devices: 30.9 us -> 27.6 us
  local copies, waits for them, and re-layouts: 4.08 us -> 5.49 us
  waiting for transfers between devices: 58.3 us -> 59.6 us
    ppermute x10, starting transfers between devices: 20.6 us -> 17.3 us  [exchange(): return lax.ppermute(x, axis, perm=[(i, i ^ 1 << bit) for i in range(n)])]
    reshape x0 -> x1, local copies, waits for them, and re-layouts: none -> 1.62 us  [on_device(): query_all = gathered.reshape(pairs, 2, rows, HEAD_SIZE)]
  transfers between devices with their start and end apart: 16 -> 16, of which waited for: 15 -> 14; matrix products, arithmetic and copies ran while one was open for 3% -> 5% of each run, Pallas kernels for 4% -> 4%
where the time goes in v10:
time: 123 us
  waiting for transfers between devices  59.6 us (48%)
  starting transfers between devices  27.6 us (22%)
  Pallas kernels  11 us (9%)
  matrix products  8.95 us (7%)
  other arithmetic  8.73 us (7%)
  local copies, waits for them, and re-layouts  5.49 us (4%)
  between operations  1.26 us (1%)
    ppermute x10, waiting for transfers between devices, exchange(): return lax.ppermute(x, axis, perm=[(i, i ^ 1 << bit) for i in range(n)])  34.9 us
    ppermute x6, waiting for transfers between devices, allreduce_bf16(): other = lax.ppermute(cur, ('req', 'mlp'), perm=perm)  24.8 us
    ppermute x10, starting transfers between devices, exchange(): return lax.ppermute(x, axis, perm=[(i, i ^ 1 << bit) for i in range(n)])  17.3 us
    pallas_call x2, Pallas kernels, prefix_partials(): pl.pallas_call(prefix_kernel, grid_spec=pltpu.PrefetchScalarGridSpec(num_...  11 us
    ppermute x6, starting transfers between devices, allreduce_bf16(): other = lax.ppermute(cur, ('req', 'mlp'), perm=perm)  10.2 us
    dot_general x1, matrix products, on_device(): jnp.dot(hidden, down_weight, preferred_element_type=jnp.float32)  2.83 us
  transfers between devices with their start and end apart: 16, of which 14 were waited for; matrix products, arithmetic and copies ran while one was open for 5% of the time, Pallas kernels for 4%

profile of v10, /device:TPU:6, one launch (start us, length us, event | category | flops | bytes accessed | tf_op | source)
XLA Modules:
  0.0 122.7 jit_solution(15900318619933635371)
XLA Ops:
  0.7 7.3 %collective-permute-start = (bf16[1,32,320]{2,1,0:T(8,128)(2,1)}, bf16[1,32,320]{2,1,0:T(8,128)(2,1)S(1)}, u32[]{:S(2)}, u32[]{:S(2)}) collective-permute-start(bf16[1,32,320]{2,1,0:T(8,128)(2,1)} %bitcast.199), channel_id=1, source_target_pairs={{0,128},{8,136},{16,144},{24,152},{32,160},{40,168},{48,176},{56,1... | collective-permute-start | bytes 61448 | tf_op jit(solution)/shard_map/ppermute | solution.py:69
  7.9 0.9 reshape.182
  8.8 0.7 iota_compare_fusion
  9.5 1.3 %select_reduce_fusion = (f32[16,2,4]{2,1,0:T(2,128)S(1)}, f32[16,2,4,128]{3,2,1,0:T(4,128)S(1)}) fusion(pred[16,128]{1,0:T(8,128)(4,1)S(1)} %iota_compare_fusion, bf16[16,2,4,80]{3,2,1,0:T(4,128)(2,1)S(1)} %reshape.182, bf16[1,16,128,80]{2,3,1,0:T(8,128)(2,1)} %param.23), kind=kOutput, calls=%fused_computation.75 | convolution fusion | flops 2670464 | bytes 416256 | tf_op jit(solution)/shard_map/sjkgh,stkh->ksjgt/dot_general | solution.py:184
  10.8 1.1 select_reduce_fusion.1
  12.0 0.8 select_bitcast_fusion.5
  12.8 1.5 %collective-permute-start.1 = (bf16[2,1,32,320]{3,2,0,1:T(8,128)(2,1)S(1)}, bf16[2,1,32,320]{3,2,0,1:T(8,128)(2,1)S(1)}, u32[]{:S(2)}, u32[]{:S(2)}) collective-permute-start(bf16[2,1,32,320]{3,2,0,1:T(8,128)(2,1)S(1)} %fusion.34), channel_id=1, source_target_pairs={{0,16},{8,24},{16,0},{24,8},{32,48},{40,56},{48,32},{56,40},{64,80... | collective-permute-start | bytes 122888 | tf_op jit(solution)/shard_map/ppermute | solution.py:69
  14.6 3.9 %collective-permute-done.1 = bf16[2,1,32,320]{3,2,0,1:T(8,128)(2,1)S(1)} collective-permute-done((bf16[2,1,32,320]{3,2,0,1:T(8,128)(2,1)S(1)}, bf16[2,1,32,320]{3,2,0,1:T(8,128)(2,1)S(1)}, u32[]{:S(2)}, u32[]{:S(2)}) %collective-permute-start.1) | collective-permute-done | bytes 40992 | tf_op jit(solution)/shard_map/ppermute | solution.py:69
  18.5 1.6 %collective-permute-start.2 = (bf16[2,2,1,32,320]{4,3,1,0,2:T(8,128)(2,1)S(1)}, bf16[2,2,1,32,320]{4,3,1,0,2:T(8,128)(2,1)S(1)}, u32[]{:S(2)}, u32[]{:S(2)}) collective-permute-start(bf16[2,2,1,32,320]{4,3,1,0,2:T(8,128)(2,1)S(1)} %fusion.22), channel_id=1, source_target_pairs={{0,64},{8,72},{16,80},{24,88},{32,96},{40,104},{48,112},{56,120},{... | collective-permute-start | bytes 245768 | tf_op jit(solution)/shard_map/ppermute | solution.py:69
  20.3 4.9 %collective-permute-done.2 = bf16[2,2,1,32,320]{4,3,1,0,2:T(8,128)(2,1)S(1)} collective-permute-done((bf16[2,2,1,32,320]{4,3,1,0,2:T(8,128)(2,1)S(1)}, bf16[2,2,1,32,320]{4,3,1,0,2:T(8,128)(2,1)S(1)}, u32[]{:S(2)}, u32[]{:S(2)}) %collective-permute-start.2) | collective-permute-done | bytes 81952 | tf_op jit(solution)/shard_map/ppermute | solution.py:69
  25.4 0.3 fusion.5
  25.8 5.3 %collective-permute-done.3 = bf16[2,2,2,1,32,320]{5,4,2,1,0,3:T(8,128)(2,1)S(1)} collective-permute-done((bf16[2,2,2,1,32,320]{5,4,2,1,0,3:T(8,128)(2,1)S(1)}, bf16[2,2,2,1,32,320]{5,4,2,1,0,3:T(8,128)(2,1)S(1)}, u32[]{:S(2)}, u32[]{:S(2)}) %collective-permute-start.3) | collective-permute-done | bytes 163872 | tf_op jit(solution)/shard_map/ppermute | solution.py:69
  31.3 0.9 fusion
  32.2 0.5 subtract_clamp_fusion.count_ref
  32.8 0.3 collective-permute-done.4
  33.5 1.6 %reshape.187.q_ref = bf16[16,2,128,80]{3,2,1,0:T(8,128)(2,1)} reshape(bf16[1024,320]{1,0:T(8,128)(2,1)S(1)} %bitcast.191) | data formatting | bytes 1310720 | tf_op jit(solution)/shard_map/reshape | solution.py:220
  35.1 5.5 %shard_map.177 = f32[16,88,128]{2,1,0:T(8,128)} custom-call(s32[32]{0:T(128)} %subtract_clamp_fusion.count_ref, s32[1]{0:T(128)} %bitcast.50.half_ref, bf16[16,2,128,80]{3,2,1,0:T(8,128)(2,1)} %reshape.187.q_ref, bf16[16,2,80,512]{3,2,1,0:T(8,128)(2,1)} %bitcast.187, bf16[16,2,80,512]{3,2,1,0:T(8,128)(2,1)} %bitcast.189), custom_call_target="tpu_custom_call" | custom-call | flops 335544320 | bytes 3670016 | tf_op jit(solution)/shard_map/pallas_call | solution.py:46
  40.9 5.5 %shard_map.176 = f32[16,88,128]{2,1,0:T(8,128)} custom-call(s32[32]{0:T(128)} %subtract_clamp_fusion.count_ref, s32[1]{0:T(128)} %bitcast.half_ref, bf16[16,2,128,80]{3,2,1,0:T(8,128)(2,1)} %reshape.187.q_ref, bf16[16,2,80,512]{3,2,1,0:T(8,128)(2,1)} %bitcast.188, bf16[16,2,80,512]{3,2,1,0:T(8,128)(2,1)} %bitcast.190), custom_call_target="tpu_custom_call" | custom-call | flops 335544320 | bytes 3670016 | tf_op jit(solution)/shard_map/pallas_call | solution.py:46
  46.4 0.9 subtract_exponential_fusion.1
  47.3 1.2 fusion.2
  48.5 0.9 fusion.14
  49.8 6.7 %collective-permute-done.6 = bf16[2,2,2,88,128]{4,3,2,1,0:T(8,128)(2,1)S(1)} collective-permute-done((bf16[2,2,2,88,128]{4,3,2,1,0:T(8,128)(2,1)S(1)}, bf16[2,2,2,88,128]{4,3,2,1,0:T(8,128)(2,1)S(1)}, u32[]{:S(2)}, u32[]{:S(2)}) %collective-permute-start.6) | collective-permute-done | bytes 180256 | tf_op jit(solution)/shard_map/ppermute | solution.py:69
  56.9 0.8 collective-permute-start.7
  57.7 6.0 %collective-permute-done.7 = bf16[2,2,88,128]{3,2,0,1:T(8,128)(2,1)S(1)} collective-permute-done((bf16[2,2,88,128]{3,2,0,1:T(8,128)(2,1)S(1)}, bf16[2,2,88,128]{3,2,0,1:T(8,128)(2,1)S(1)}, u32[]{:S(2)}, u32[]{:S(2)}) %collective-permute-start.7) | collective-permute-done | bytes 90144 | tf_op jit(solution)/shard_map/ppermute | solution.py:69
  64.1 1.5 %collective-permute-start.8 = (bf16[2,88,128]{2,1,0:T(8,128)(2,1)S(1)}, bf16[2,88,128]{2,1,0:T(8,128)(2,1)S(1)}, u32[]{:S(2)}, u32[]{:S(2)}) collective-permute-start(bf16[2,88,128]{2,1,0:T(8,128)(2,1)S(1)} %concatenate.47), channel_id=1, source_target_pairs={{0,16},{8,24},{16,0},{24,8},{32,48},{40,56},{48,32},{56,40},{64,80... | collective-permute-start | bytes 135176 | tf_op jit(solution)/shard_map/ppermute | solution.py:69
  65.5 4.2 %collective-permute-done.8 = bf16[2,88,128]{2,1,0:T(8,128)(2,1)S(1)} collective-permute-done((bf16[2,88,128]{2,1,0:T(8,128)(2,1)S(1)}, bf16[2,88,128]{2,1,0:T(8,128)(2,1)S(1)}, u32[]{:S(2)}, u32[]{:S(2)}) %collective-permute-start.8) | collective-permute-done | bytes 45088 | tf_op jit(solution)/shard_map/ppermute | solution.py:69
  69.9 4.1 %collective-permute-start.9 = (bf16[88,128]{1,0:T(8,128)(2,1)S(1)}, bf16[88,128]{1,0:T(8,128)(2,1)S(1)}, u32[]{:S(2)}, u32[]{:S(2)}) collective-permute-start(bf16[88,128]{1,0:T(8,128)(2,1)S(1)} %concatenate.50), channel_id=1, source_target_pairs={{0,128},{8,136},{16,144},{24,152},{32,160},{40,168},{48,176},{56,1... | collective-permute-start | bytes 67592 | tf_op jit(solution)/shard_map/ppermute | solution.py:69
  74.0 3.7 %collective-permute-done.9 = bf16[88,128]{1,0:T(8,128)(2,1)S(1)} collective-permute-done((bf16[88,128]{1,0:T(8,128)(2,1)S(1)}, bf16[88,128]{1,0:T(8,128)(2,1)S(1)}, u32[]{:S(2)}, u32[]{:S(2)}) %collective-permute-start.9) | collective-permute-done | bytes 22560 | tf_op jit(solution)/shard_map/ppermute | solution.py:69
  77.7 0.5 broadcast.96
  78.2 0.7 fusion.55
  80.1 1.9 %convolution_convert_fusion.1 = bf16[32,2560]{1,0:T(8,128)(2,1)S(1)} fusion(bf16[32,320]{1,0:T(8,128)(2,1)S(1)} %reshape_transpose.3, bf16[320,2560]{1,0:T(8,128)(2,1)} %param.27), kind=kOutput, calls=%fused_computation.1 | convolution fusion | flops 52510720 | bytes 1822720 | tf_op jit(solution)/shard_map/dot_general | solution.py:254
  82.1 1.1 collective-permute-start.10
  83.1 4.5 %collective-permute-done.10 = bf16[32,2560]{1,0:T(8,128)(2,1)S(1)} collective-permute-done((bf16[32,2560]{1,0:T(8,128)(2,1)S(1)}, bf16[32,2560]{1,0:T(8,128)(2,1)S(1)}, u32[]{:S(2)}, u32[]{:S(2)}) %collective-permute-start.10) | collective-permute-done | bytes 163872 | tf_op jit(solution)/shard_map/ppermute | solution.py:137
  87.7 1.7 %collective-permute-start.11 = (bf16[32,2560]{1,0:T(8,128)(2,1)S(1)}, bf16[32,2560]{1,0:T(8,128)(2,1)S(1)}, u32[]{:S(2)}, u32[]{:S(2)}) collective-permute-start(bf16[32,2560]{1,0:T(8,128)(2,1)S(1)} %add_convert_fusion.5), channel_id=1, source_target_pairs={{0,1},{1,0},{2,3},{3,2},{4,5},{5,4},{6,7},{7,6},{8,11},{9,10},{10,... | collective-permute-start | bytes 491528 | tf_op jit(solution)/shard_map/ppermute | solution.py:137
  89.4 3.7 %collective-permute-done.11 = bf16[32,2560]{1,0:T(8,128)(2,1)S(1)} collective-permute-done((bf16[32,2560]{1,0:T(8,128)(2,1)S(1)}, bf16[32,2560]{1,0:T(8,128)(2,1)S(1)}, u32[]{:S(2)}, u32[]{:S(2)}) %collective-permute-start.11) | collective-permute-done | bytes 163872 | tf_op jit(solution)/shard_map/ppermute | solution.py:137
  93.2 3.1 %collective-permute-start.12 = (bf16[32,2560]{1,0:T(8,128)(2,1)S(1)}, bf16[32,2560]{1,0:T(8,128)(2,1)S(1)}, u32[]{:S(2)}, u32[]{:S(2)}) collective-permute-start(bf16[32,2560]{1,0:T(8,128)(2,1)S(1)} %add_convert_fusion.4), channel_id=1, source_target_pairs={{0,3},{1,2},{2,1},{3,0},{4,7},{5,6},{6,5},{7,4},{8,12},{9,13},{10,... | collective-permute-start | bytes 491528 | tf_op jit(solution)/shard_map/ppermute | solution.py:137
  96.2 3.5 %collective-permute-done.12 = bf16[32,2560]{1,0:T(8,128)(2,1)S(1)} collective-permute-done((bf16[32,2560]{1,0:T(8,128)(2,1)S(1)}, bf16[32,2560]{1,0:T(8,128)(2,1)S(1)}, u32[]{:S(2)}, u32[]{:S(2)}) %collective-permute-start.12) | collective-permute-done | bytes 163872 | tf_op jit(solution)/shard_map/ppermute | solution.py:137
  100.1 0.5 fusion.56
  100.7 2.8 %convolution_convert_fusion = bf16[32,2560]{1,0:T(8,128)(2,1)S(1)} fusion(bf16[512,2560]{1,0:T(8,128)(2,1)S(1)} %copy-done, bf16[32,2560]{1,0:T(8,128)(2,1)S(1)} %multiply_convert_fusion, bf16[2560,512]{1,0:T(8,128)(2,1)} %param.29, f32[32,512]{1,0:T(8,128)S(1)} %fusion.56), kind=kOutput, calls=%fused_computation | convolution fusion | flops 167952384 | bytes 5636096 | tf_op jit(solution)/shard_map/dot_general | solution.py:268
  103.5 0.9 collective-permute-start.13
  104.4 4.5 %collective-permute-done.13 = bf16[32,2560]{1,0:T(8,128)(2,1)S(1)} collective-permute-done((bf16[32,2560]{1,0:T(8,128)(2,1)S(1)}, bf16[32,2560]{1,0:T(8,128)(2,1)S(1)}, u32[]{:S(2)}, u32[]{:S(2)}) %collective-permute-start.13) | collective-permute-done | bytes 163872 | tf_op jit(solution)/shard_map/ppermute | solution.py:137
  108.9 0.4 collective-permute-start.14
  109.4 5.0 %collective-permute-done.14 = bf16[32,2560]{1,0:T(8,128)(2,1)S(1)} collective-permute-done((bf16[32,2560]{1,0:T(8,128)(2,1)S(1)}, bf16[32,2560]{1,0:T(8,128)(2,1)S(1)}, u32[]{:S(2)}, u32[]{:S(2)}) %collective-permute-start.14) | collective-permute-done | bytes 163872 | tf_op jit(solution)/shard_map/ppermute | solution.py:137
  114.4 3.1 %collective-permute-start.15 = (bf16[32,2560]{1,0:T(8,128)(2,1)S(1)}, bf16[32,2560]{1,0:T(8,128)(2,1)S(1)}, u32[]{:S(2)}, u32[]{:S(2)}) collective-permute-start(bf16[32,2560]{1,0:T(8,128)(2,1)S(1)} %add_convert_fusion.1), channel_id=1, source_target_pairs={{0,3},{1,2},{2,1},{3,0},{4,7},{5,6},{6,5},{7,4},{8,12},{9,13},{10,... | collective-permute-start | bytes 491528 | tf_op jit(solution)/shard_map/ppermute | solution.py:137
  117.5 3.5 %collective-permute-done.15 = bf16[32,2560]{1,0:T(8,128)(2,1)S(1)} collective-permute-done((bf16[32,2560]{1,0:T(8,128)(2,1)S(1)}, bf16[32,2560]{1,0:T(8,128)(2,1)S(1)}, u32[]{:S(2)}, u32[]{:S(2)}) %collective-permute-start.15) | collective-permute-done | bytes 163872 | tf_op jit(solution)/shard_map/ppermute | solution.py:137
  121.0 0.2 multiply_reduce_fusion.1
  121.2 0.7 dynamic-slice_convert_fusion
  121.9 0.7 multiply_reduce_fusion
  (116 shorter events, 4.6 us)
Async XLA Ops:
  0.6 100.0 %copy-start = (bf16[512,2560]{1,0:T(8,128)(2,1)S(1)}, bf16[512,2560]{1,0:T(8,128)(2,1)}, u32[]{:S(2)}) copy-start(bf16[512,2560]{1,0:T(8,128)(2,1)} %param.30) | copy-start | bytes 7864324
  0.6 24.8 %copy-start.7 = (bf16[1,16,128,80]{2,3,1,0:T(8,128)(2,1)S(1)}, bf16[1,16,128,80]{2,3,1,0:T(8,128)(2,1)}, u32[]{:S(2)}) copy-start(bf16[1,16,128,80]{2,3,1,0:T(8,128)(2,1)} %param.24) | copy-start | bytes 983044
  0.7 11.3 %collective-permute-start = (bf16[1,32,320]{2,1,0:T(8,128)(2,1)}, bf16[1,32,320]{2,1,0:T(8,128)(2,1)S(1)}, u32[]{:S(2)}, u32[]{:S(2)}) collective-permute-start(bf16[1,32,320]{2,1,0:T(8,128)(2,1)} %bitcast.199), channel_id=1, source_target_pairs={{0,128},{8,136},{16,144},{24,152},{32,160},{40,168},{48,176},{56,1... | collective-permute-start | bytes 61448 | tf_op jit(solution)/shard_map/ppermute | solution.py:69
  10.8 20.5 %copy-start.8 = (bf16[32,80]{1,0:T(8,128)(2,1)S(1)}, bf16[32,80]{1,0:T(8,128)(2,1)}, u32[]{:S(2)}) copy-start(bf16[32,80]{1,0:T(8,128)(2,1)} %param.20) | copy-start | bytes 15364
  11.9 20.3 %copy-start.9 = (s32[32]{0:T(128)S(1)}, s32[32]{0:T(128)}, u32[]{:S(2)}) copy-start(s32[32]{0:T(128)} %param.25) | copy-start | bytes 388
  12.8 5.7 %collective-permute-start.1 = (bf16[2,1,32,320]{3,2,0,1:T(8,128)(2,1)S(1)}, bf16[2,1,32,320]{3,2,0,1:T(8,128)(2,1)S(1)}, u32[]{:S(2)}, u32[]{:S(2)}) collective-permute-start(bf16[2,1,32,320]{3,2,0,1:T(8,128)(2,1)S(1)} %fusion.34), channel_id=1, source_target_pairs={{0,16},{8,24},{16,0},{24,8},{32,48},{40,56},{48,32},{56,40},{64,80... | collective-permute-start | bytes 122888 | tf_op jit(solution)/shard_map/ppermute | solution.py:69
  18.5 6.7 %collective-permute-start.2 = (bf16[2,2,1,32,320]{4,3,1,0,2:T(8,128)(2,1)S(1)}, bf16[2,2,1,32,320]{4,3,1,0,2:T(8,128)(2,1)S(1)}, u32[]{:S(2)}, u32[]{:S(2)}) collective-permute-start(bf16[2,2,1,32,320]{4,3,1,0,2:T(8,128)(2,1)S(1)} %fusion.22), channel_id=1, source_target_pairs={{0,64},{8,72},{16,80},{24,88},{32,96},{40,104},{48,112},{56,120},{... | collective-permute-start | bytes 245768 | tf_op jit(solution)/shard_map/ppermute | solution.py:69
  25.3 5.8 %collective-permute-start.3 = (bf16[2,2,2,1,32,320]{5,4,2,1,0,3:T(8,128)(2,1)S(1)}, bf16[2,2,2,1,32,320]{5,4,2,1,0,3:T(8,128)(2,1)S(1)}, u32[]{:S(2)}, u32[]{:S(2)}) collective-permute-start(bf16[2,2,2,1,32,320]{5,4,2,1,0,3:T(8,128)(2,1)S(1)} %fusion.11), channel_id=1, source_target_pairs={{0,32},{8,40},{16,48},{24,56},{32,0},{40,8},{48,16},{56,24},{64,96... | collective-permute-start | bytes 491528 | tf_op jit(solution)/shard_map/ppermute | solution.py:69
  31.2 1.8 %collective-permute-start.4 = (bf16[2,2,2,2,1,32,320]{6,5,3,2,1,0,4:T(8,128)(2,1)S(1)}, bf16[2,2,2,2,1,32,320]{6,5,3,2,1,0,4:T(8,128)(2,1)S(1)}, u32[]{:S(2)}, u32[]{:S(2)}) collective-permute-start(bf16[2,2,2,2,1,32,320]{6,5,3,2,1,0,4:T(8,128)(2,1)S(1)} %fusion.8), channel_id=1, source_target_pairs={{0,8},{8,0},{16,24},{24,16},{32,40},{40,32},{48,56},{56,48},{64,72... | collective-permute-start | bytes 983048 | tf_op jit(solution)/shard_map/ppermute | solution.py:69
  40.7 5.7 %collective-permute-start.5 = (f32[16,88,128]{2,1,0:T(8,128)}, f32[16,88,128]{2,1,0:T(8,128)S(1)}, u32[]{:S(2)}, u32[]{:S(2)}) collective-permute-start(f32[16,88,128]{2,1,0:T(8,128)} %shard_map.177), channel_id=1, source_target_pairs={{0,8},{8,0},{16,24},{24,16},{32,40},{40,32},{48,56},{56,48},{64,72... | collective-permute-start | bytes 2162696 | tf_op jit(solution)/shard_map/ppermute | solution.py:69
  49.7 6.8 %collective-permute-start.6 = (bf16[2,2,2,88,128]{4,3,2,1,0:T(8,128)(2,1)S(1)}, bf16[2,2,2,88,128]{4,3,2,1,0:T(8,128)(2,1)S(1)}, u32[]{:S(2)}, u32[]{:S(2)}) collective-permute-start(bf16[2,2,2,88,128]{4,3,2,1,0:T(8,128)(2,1)S(1)} %concatenate.41), channel_id=1, source_target_pairs={{0,32},{8,40},{16,48},{24,56},{32,0},{40,8},{48,16},{56,24},{64,96... | collective-permute-start | bytes 540680 | tf_op jit(solution)/shard_map/ppermute | solution.py:69
  56.7 23.2 %copy-start.3 = (f32[1,16,2,4,80]{4,3,2,1,0:T(4,128)S(1)}, f32[1,16,2,4,80]{4,3,2,1,0:T(4,128)}, u32[]{:S(2)}) copy-start(f32[1,16,2,4,80]{4,3,2,1,0:T(4,128)} %fusion) | copy-start | bytes 122884
  56.9 6.9 %collective-permute-start.7 = (bf16[2,2,88,128]{3,2,0,1:T(8,128)(2,1)S(1)}, bf16[2,2,88,128]{3,2,0,1:T(8,128)(2,1)S(1)}, u32[]{:S(2)}, u32[]{:S(2)}) collective-permute-start(bf16[2,2,88,128]{3,2,0,1:T(8,128)(2,1)S(1)} %concatenate.44), channel_id=1, source_target_pairs={{0,64},{8,72},{16,80},{24,88},{32,96},{40,104},{48,112},{56,120},{... | collective-permute-start | bytes 270344 | tf_op jit(solution)/shard_map/ppermute | solution.py:69
  63.9 35.9 %copy-start.2 = (bf16[32,2560]{1,0:T(8,128)(2,1)S(1)}, bf16[32,2560]{1,0:T(8,128)(2,1)}, u32[]{:S(2)}) copy-start(bf16[32,2560]{1,0:T(8,128)(2,1)} %param.17) | copy-start | bytes 491524
  63.9 36.0 %copy-start.6 = (f32[2560]{0:T(1024)S(1)}, f32[2560]{0:T(1024)}, u32[]{:S(2)}) copy-start(f32[2560]{0:T(1024)} %param.31) | copy-start | bytes 30724
  64.1 5.6 %collective-permute-start.8 = (bf16[2,88,128]{2,1,0:T(8,128)(2,1)S(1)}, bf16[2,88,128]{2,1,0:T(8,128)(2,1)S(1)}, u32[]{:S(2)}, u32[]{:S(2)}) collective-permute-start(bf16[2,88,128]{2,1,0:T(8,128)(2,1)S(1)} %concatenate.47), channel_id=1, source_target_pairs={{0,16},{8,24},{16,0},{24,8},{32,48},{40,56},{48,32},{56,40},{64,80... | collective-permute-start | bytes 135176 | tf_op jit(solution)/shard_map/ppermute | solution.py:69
  69.9 7.8 %collective-permute-start.9 = (bf16[88,128]{1,0:T(8,128)(2,1)S(1)}, bf16[88,128]{1,0:T(8,128)(2,1)S(1)}, u32[]{:S(2)}, u32[]{:S(2)}) collective-permute-start(bf16[88,128]{1,0:T(8,128)(2,1)S(1)} %concatenate.50), channel_id=1, source_target_pairs={{0,128},{8,136},{16,144},{24,152},{32,160},{40,168},{48,176},{56,1... | collective-permute-start | bytes 67592 | tf_op jit(solution)/shard_map/ppermute | solution.py:69
  80.1 20.0 %copy-start.1 = (bf16[2560,512]{1,0:T(8,128)(2,1)S(1)}, bf16[2560,512]{1,0:T(8,128)(2,1)}, u32[]{:S(2)}) copy-start(bf16[2560,512]{1,0:T(8,128)(2,1)} %param.28) | copy-start | bytes 7864324
  82.1 5.6 %collective-permute-start.10 = (bf16[32,2560]{1,0:T(8,128)(2,1)S(1)}, bf16[32,2560]{1,0:T(8,128)(2,1)S(1)}, u32[]{:S(2)}, u32[]{:S(2)}) collective-permute-start(bf16[32,2560]{1,0:T(8,128)(2,1)S(1)} %convolution_convert_fusion.1), channel_id=1, source_target_pairs={{0,4},{1,5},{2,6},{3,7},{4,0},{5,1},{6,2},{7,3},{8,9},{9,8},{10,11... | collective-permute-start | bytes 491528 | tf_op jit(solution)/shard_map/ppermute | solution.py:137
  87.7 5.4 %collective-permute-start.11 = (bf16[32,2560]{1,0:T(8,128)(2,1)S(1)}, bf16[32,2560]{1,0:T(8,128)(2,1)S(1)}, u32[]{:S(2)}, u32[]{:S(2)}) collective-permute-start(bf16[32,2560]{1,0:T(8,128)(2,1)S(1)} %add_convert_fusion.5), channel_id=1, source_target_pairs={{0,1},{1,0},{2,3},{3,2},{4,5},{5,4},{6,7},{7,6},{8,11},{9,10},{10,... | collective-permute-start | bytes 491528 | tf_op jit(solution)/shard_map/ppermute | solution.py:137
  93.2 6.6 %collective-permute-start.12 = (bf16[32,2560]{1,0:T(8,128)(2,1)S(1)}, bf16[32,2560]{1,0:T(8,128)(2,1)S(1)}, u32[]{:S(2)}, u32[]{:S(2)}) collective-permute-start(bf16[32,2560]{1,0:T(8,128)(2,1)S(1)} %add_convert_fusion.4), channel_id=1, source_target_pairs={{0,3},{1,2},{2,1},{3,0},{4,7},{5,6},{6,5},{7,4},{8,12},{9,13},{10,... | collective-permute-start | bytes 491528 | tf_op jit(solution)/shard_map/ppermute | solution.py:137
  100.6 21.3 %copy-start.4 = (f32[2560]{0:T(1024)S(1)}, f32[2560]{0:T(1024)}, u32[]{:S(2)}) copy-start(f32[2560]{0:T(1024)} %param.33) | copy-start | bytes 30724
  100.6 21.3 %copy-start.5 = (f32[2560]{0:T(1024)S(1)}, f32[2560]{0:T(1024)}, u32[]{:S(2)}) copy-start(f32[2560]{0:T(1024)} %param.32) | copy-start | bytes 30724
  103.5 5.4 %collective-permute-start.13 = (bf16[32,2560]{1,0:T(8,128)(2,1)S(1)}, bf16[32,2560]{1,0:T(8,128)(2,1)S(1)}, u32[]{:S(2)}, u32[]{:S(2)}) collective-permute-start(bf16[32,2560]{1,0:T(8,128)(2,1)S(1)} %convolution_convert_fusion), channel_id=1, source_target_pairs={{0,4},{1,5},{2,6},{3,7},{4,0},{5,1},{6,2},{7,3},{8,9},{9,8},{10,11... | collective-permute-start | bytes 491528 | tf_op jit(solution)/shard_map/ppermute | solution.py:137
  108.9 5.4 %collective-permute-start.14 = (bf16[32,2560]{1,0:T(8,128)(2,1)S(1)}, bf16[32,2560]{1,0:T(8,128)(2,1)S(1)}, u32[]{:S(2)}, u32[]{:S(2)}) collective-permute-start(bf16[32,2560]{1,0:T(8,128)(2,1)S(1)} %add_convert_fusion.2), channel_id=1, source_target_pairs={{0,1},{1,0},{2,3},{3,2},{4,5},{5,4},{6,7},{7,6},{8,11},{9,10},{10,... | collective-permute-start | bytes 491528 | tf_op jit(solution)/shard_map/ppermute | solution.py:137
  114.4 6.6 %collective-permute-start.15 = (bf16[32,2560]{1,0:T(8,128)(2,1)S(1)}, bf16[32,2560]{1,0:T(8,128)(2,1)S(1)}, u32[]{:S(2)}, u32[]{:S(2)}) collective-permute-start(bf16[32,2560]{1,0:T(8,128)(2,1)S(1)} %add_convert_fusion.1), channel_id=1, source_target_pairs={{0,3},{1,2},{2,1},{3,0},{4,7},{5,6},{6,5},{7,4},{8,12},{9,13},{10,... | collective-permute-start | bytes 491528 | tf_op jit(solution)/shard_map/ppermute | solution.py:137

commit v11 on v10

--- a/solution.py
+++ b/solution.py
@@ -69,7 +69,7 @@
     return lax.ppermute(x, axis, perm=[(i, i ^ (1 << bit)) for i in range(n)])
 
 
-def gather_rows(x, axis, n, bits):
+def gather_rows(x, axis, n, bits, tie, tie_after):
     me = lax.axis_index(axis)
     buf = x[None]
     taken = []
@@ -78,10 +78,12 @@
         high = ((me >> b) & 1) == 1
         buf = jnp.stack([jnp.where(high, other, buf), jnp.where(high, buf, other)])
         taken.insert(0, b)
+        if len(taken) == tie_after:
+            buf, tie = lax.optimization_barrier((buf, tie))
     nb = len(bits)
     order = sorted(range(nb), key=lambda i: -taken[i])
     buf = jnp.transpose(buf, order + list(range(nb, buf.ndim)))
-    return buf.reshape((n * x.shape[0],) + x.shape[1:])
+    return buf.reshape((n * x.shape[0],) + x.shape[1:]), tie
 
 
 def merge_partials(a, b):
@@ -175,7 +177,8 @@
     gather_order = [b for i, b in enumerate(gather_order) if b not in gather_order[:i]]
     reduce_order = gather_order[::-1]
 
-    query_own = queries.reshape(SAMPLE_COUNT, DECODE_TOKENS, kv_local, query_groups, HEAD_SIZE)
+    gathered, local_queries = gather_rows(queries, "req", req_count, gather_order, queries, 2)
+    query_own = local_queries.reshape(SAMPLE_COUNT, DECODE_TOKENS, kv_local, query_groups, HEAD_SIZE)
     tail_key_block = sample_tail_keys.reshape(SAMPLE_COUNT, TAIL_LENGTH, kv_local, HEAD_SIZE)
     tail_value_block = sample_tail_values.reshape(SAMPLE_COUNT, TAIL_LENGTH, kv_local, HEAD_SIZE)
     fresh_k = fresh_rotated_keys.reshape(SAMPLE_COUNT, DECODE_TOKENS, kv_local, HEAD_SIZE)
@@ -212,7 +215,6 @@
     local_out = local_out + jnp.einsum(
         "ksjgi,sikh->ksjgh", w_new.astype(jnp.bfloat16), fresh_v, preferred_element_type=jnp.float32
     )
-    gathered = gather_rows(queries, "req", req_count, gather_order)
     gathered, local_out, local_top, local_sum = lax.optimization_barrier(
         (gathered, local_out, local_top, local_sum)
     )

time: 123 us -> 122 us (level)
  waiting for transfers between devices: 59.6 us -> 51.3 us
  starting transfers between devices: 27.6 us -> 32.7 us
    ppermute x10, waiting for transfers between devices: 34.9 us -> 26.6 us  [exchange(): return lax.ppermute(x, axis, perm=[(i, i ^ 1 << bit) for i in range(n)])]
    ppermute x10, starting transfers between devices: 17.3 us -> 22.4 us  [exchange(): return lax.ppermute(x, axis, perm=[(i, i ^ 1 << bit) for i in range(n)])]
  transfers between devices with their start and end apart: 16 -> 16, of which waited for: 14 -> 14; matrix products, arithmetic and copies ran while one was open for 5% -> 7% of each run, Pallas kernels for 4% -> 5%
where the time goes in v11:
time: 122 us; the launch traced here: 121 us
  waiting for transfers between devices  51.3 us (42%)
  starting transfers between devices  32.7 us (27%)
  Pallas kernels  11 us (9%)
  matrix products  9.92 us (8%)
  other arithmetic  9.36 us (8%)
  local copies, waits for them, and re-layouts  5.44 us (4%)
    ppermute x10, waiting for transfers between devices, exchange(): return lax.ppermute(x, axis, perm=[(i, i ^ 1 << bit) for i in range(n)])  26.6 us
    ppermute x6, waiting for transfers between devices, allreduce_bf16(): other = lax.ppermute(cur, ('req', 'mlp'), perm=perm)  24.7 us
    ppermute x10, starting transfers between devices, exchange(): return lax.ppermute(x, axis, perm=[(i, i ^ 1 << bit) for i in range(n)])  22.4 us
    pallas_call x2, Pallas kernels, prefix_partials(): pl.pallas_call(prefix_kernel, grid_spec=pltpu.PrefetchScalarGridSpec(num_...  11 us
    ppermute x6, starting transfers between devices, allreduce_bf16(): other = lax.ppermute(cur, ('req', 'mlp'), perm=perm)  10.3 us
    dot_general x1, matrix products, on_device(): jnp.dot(hidden, down_weight, preferred_element_type=jnp.float32)  2.82 us
  transfers between devices with their start and end apart: 16, of which 14 were waited for; matrix products, arithmetic and copies ran while one was open for 7% of the time, Pallas kernels for 5%

profile of v11, /device:TPU:6, one launch (start us, length us, event | category | flops | bytes accessed | tf_op | source)
XLA Modules:
  0.0 121.0 jit_solution(4406920670710934266)
XLA Ops:
  0.6 7.3 %collective-permute-start = (bf16[1,32,320]{2,1,0:T(8,128)(2,1)}, bf16[1,32,320]{2,1,0:T(8,128)(2,1)S(1)}, u32[]{:S(2)}, u32[]{:S(2)}) collective-permute-start(bf16[1,32,320]{2,1,0:T(8,128)(2,1)} %bitcast.198), channel_id=1, source_target_pairs={{0,128},{8,136},{16,144},{24,152},{32,160},{40,168},{48,176},{56,1... | collective-permute-start | bytes 61448 | tf_op jit(solution)/shard_map/ppermute | solution.py:69
  7.9 0.7 iota_compare_fusion
  8.6 1.2 subtract_clamp_fusion.count_ref
  9.9 0.7 select_bitcast_fusion.5
  10.7 1.5 %collective-permute-start.1 = (bf16[2,1,32,320]{3,2,0,1:T(8,128)(2,1)S(1)}, bf16[2,1,32,320]{3,2,0,1:T(8,128)(2,1)S(1)}, u32[]{:S(2)}, u32[]{:S(2)}) collective-permute-start(bf16[2,1,32,320]{3,2,0,1:T(8,128)(2,1)S(1)} %fusion.33), channel_id=1, source_target_pairs={{0,16},{8,24},{16,0},{24,8},{32,48},{40,56},{48,32},{56,40},{64,80... | collective-permute-start | bytes 122888 | tf_op jit(solution)/shard_map/ppermute | solution.py:69
  12.2 4.2 %collective-permute-done.1 = bf16[2,1,32,320]{3,2,0,1:T(8,128)(2,1)S(1)} collective-permute-done((bf16[2,1,32,320]{3,2,0,1:T(8,128)(2,1)S(1)}, bf16[2,1,32,320]{3,2,0,1:T(8,128)(2,1)S(1)}, u32[]{:S(2)}, u32[]{:S(2)}) %collective-permute-start.1) | collective-permute-done | bytes 40992 | tf_op jit(solution)/shard_map/ppermute | solution.py:69
  16.5 2.1 %collective-permute-start.2 = (bf16[2,2,1,32,320]{4,3,1,0,2:T(8,128)(2,1)S(1)}, bf16[2,2,1,32,320]{4,3,1,0,2:T(8,128)(2,1)S(1)}, u32[]{:S(2)}, u32[]{:S(2)}) collective-permute-start(bf16[2,2,1,32,320]{4,3,1,0,2:T(8,128)(2,1)S(1)} %bitcast.191), channel_id=1, source_target_pairs={{0,64},{8,72},{16,80},{24,88},{32,96},{40,104},{48,112},{56,120},{... | collective-permute-start | bytes 245768 | tf_op jit(solution)/shard_map/ppermute | solution.py:69
  18.6 0.8 reshape.182
  19.4 1.3 %select_reduce_fusion = (f32[16,2,4]{2,1,0:T(2,128)S(1)}, f32[16,2,4,128]{3,2,1,0:T(4,128)S(1)}) fusion(pred[16,128]{1,0:T(8,128)(4,1)S(1)} %iota_compare_fusion, bf16[16,2,4,80]{3,2,1,0:T(4,128)(2,1)S(1)} %reshape.182, bf16[1,16,128,80]{2,3,1,0:T(8,128)(2,1)} %param.23), kind=kOutput, calls=%fused_computation.75 | convolution fusion | flops 2670464 | bytes 416256 | tf_op jit(solution)/shard_map/sjkgh,stkh->ksjgt/dot_general | solution.py:187
  20.7 1.1 select_reduce_fusion.1
  21.8 1.3 %collective-permute-done.2 = bf16[2,2,1,32,320]{4,3,1,0,2:T(8,128)(2,1)S(1)} collective-permute-done((bf16[2,2,1,32,320]{4,3,1,0,2:T(8,128)(2,1)S(1)}, bf16[2,2,1,32,320]{4,3,1,0,2:T(8,128)(2,1)S(1)}, u32[]{:S(2)}, u32[]{:S(2)}) %collective-permute-start.2) | collective-permute-done | bytes 81952 | tf_op jit(solution)/shard_map/ppermute | solution.py:69
  23.2 0.7 collective-permute-start.3
  24.5 4.5 %collective-permute-done.3 = bf16[2,2,2,1,32,320]{5,4,2,1,0,3:T(8,128)(2,1)S(1)} collective-permute-done((bf16[2,2,2,1,32,320]{5,4,2,1,0,3:T(8,128)(2,1)S(1)}, bf16[2,2,2,1,32,320]{5,4,2,1,0,3:T(8,128)(2,1)S(1)}, u32[]{:S(2)}, u32[]{:S(2)}) %collective-permute-start.3) | collective-permute-done | bytes 163872 | tf_op jit(solution)/shard_map/ppermute | solution.py:69
  29.3 1.3 %fusion.5 = f32[16,2,4,80]{3,2,1,0:T(4,128)S(1)} fusion(bf16[1,16,128,80]{2,3,1,0:T(8,128)(2,1)} %param.24, f32[16,2,4,128]{3,2,1,0:T(4,128)S(1)} %get-tuple-element.52, f32[16,2,4]{2,1,0:T(2,128)S(1)} %max.43, pred[16,128]{1,0:T(8,128)(4,1)S(1)} %iota_compare_fusion), kind=kOutput, calls=%fused_computation.25 | convolution fusion | flops 2670592 | bytes 436736 | tf_op jit(solution)/shard_map/ksjgt,stkh->ksjgh/dot_general | solution.py:209
  30.6 0.9 fusion
  32.0 1.6 %reshape.187.q_ref = bf16[16,2,128,80]{3,2,1,0:T(8,128)(2,1)} reshape(bf16[1024,320]{1,0:T(8,128)(2,1)S(1)} %bitcast.189) | data formatting | bytes 1310720 | tf_op jit(solution)/shard_map/reshape | solution.py:222
  33.6 5.5 %shard_map.177 = f32[16,88,128]{2,1,0:T(8,128)} custom-call(s32[32]{0:T(128)} %subtract_clamp_fusion.count_ref, s32[1]{0:T(128)} %bitcast.50.half_ref, bf16[16,2,128,80]{3,2,1,0:T(8,128)(2,1)} %reshape.187.q_ref, bf16[16,2,80,512]{3,2,1,0:T(8,128)(2,1)} %bitcast.185, bf16[16,2,80,512]{3,2,1,0:T(8,128)(2,1)} %bitcast.187), custom_call_target="tpu_custom_call" | custom-call | flops 335544320 | bytes 3670016 | tf_op jit(solution)/shard_map/pallas_call | solution.py:46
  39.1 0.5 collective-permute-start.5
  39.6 5.5 %shard_map.176 = f32[16,88,128]{2,1,0:T(8,128)} custom-call(s32[32]{0:T(128)} %subtract_clamp_fusion.count_ref, s32[1]{0:T(128)} %bitcast.half_ref, bf16[16,2,128,80]{3,2,1,0:T(8,128)(2,1)} %reshape.187.q_ref, bf16[16,2,80,512]{3,2,1,0:T(8,128)(2,1)} %bitcast.186, bf16[16,2,80,512]{3,2,1,0:T(8,128)(2,1)} %bitcast.188), custom_call_target="tpu_custom_call" | custom-call | flops 335544320 | bytes 3670016 | tf_op jit(solution)/shard_map/pallas_call | solution.py:46
  45.1 0.9 subtract_exponential_fusion.1
  46.0 1.2 fusion.2
  47.2 0.9 fusion.14
  48.4 0.7 collective-permute-start.6
  49.1 5.9 %collective-permute-done.6 = bf16[2,2,2,88,128]{4,3,2,1,0:T(8,128)(2,1)S(1)} collective-permute-done((bf16[2,2,2,88,128]{4,3,2,1,0:T(8,128)(2,1)S(1)}, bf16[2,2,2,88,128]{4,3,2,1,0:T(8,128)(2,1)S(1)}, u32[]{:S(2)}, u32[]{:S(2)}) %collective-permute-start.6) | collective-permute-done | bytes 180256 | tf_op jit(solution)/shard_map/ppermute | solution.py:69
  55.4 1.9 %collective-permute-start.7 = (bf16[2,2,88,128]{3,2,0,1:T(8,128)(2,1)S(1)}, bf16[2,2,88,128]{3,2,0,1:T(8,128)(2,1)S(1)}, u32[]{:S(2)}, u32[]{:S(2)}) collective-permute-start(bf16[2,2,88,128]{3,2,0,1:T(8,128)(2,1)S(1)} %concatenate.44), channel_id=1, source_target_pairs={{0,64},{8,72},{16,80},{24,88},{32,96},{40,104},{48,112},{56,120},{... | collective-permute-start | bytes 270344 | tf_op jit(solution)/shard_map/ppermute | solution.py:69
  57.3 4.7 %collective-permute-done.7 = bf16[2,2,88,128]{3,2,0,1:T(8,128)(2,1)S(1)} collective-permute-done((bf16[2,2,88,128]{3,2,0,1:T(8,128)(2,1)S(1)}, bf16[2,2,88,128]{3,2,0,1:T(8,128)(2,1)S(1)}, u32[]{:S(2)}, u32[]{:S(2)}) %collective-permute-start.7) | collective-permute-done | bytes 90144 | tf_op jit(solution)/shard_map/ppermute | solution.py:69
  62.2 1.5 %collective-permute-start.8 = (bf16[2,88,128]{2,1,0:T(8,128)(2,1)S(1)}, bf16[2,88,128]{2,1,0:T(8,128)(2,1)S(1)}, u32[]{:S(2)}, u32[]{:S(2)}) collective-permute-start(bf16[2,88,128]{2,1,0:T(8,128)(2,1)S(1)} %concatenate.47), channel_id=1, source_target_pairs={{0,16},{8,24},{16,0},{24,8},{32,48},{40,56},{48,32},{56,40},{64,80... | collective-permute-start | bytes 135176 | tf_op jit(solution)/shard_map/ppermute | solution.py:69
  63.7 4.1 %collective-permute-done.8 = bf16[2,88,128]{2,1,0:T(8,128)(2,1)S(1)} collective-permute-done((bf16[2,88,128]{2,1,0:T(8,128)(2,1)S(1)}, bf16[2,88,128]{2,1,0:T(8,128)(2,1)S(1)}, u32[]{:S(2)}, u32[]{:S(2)}) %collective-permute-start.8) | collective-permute-done | bytes 45088 | tf_op jit(solution)/shard_map/ppermute | solution.py:69
  68.1 6.1 %collective-permute-start.9 = (bf16[88,128]{1,0:T(8,128)(2,1)S(1)}, bf16[88,128]{1,0:T(8,128)(2,1)S(1)}, u32[]{:S(2)}, u32[]{:S(2)}) collective-permute-start(bf16[88,128]{1,0:T(8,128)(2,1)S(1)} %concatenate.50), channel_id=1, source_target_pairs={{0,128},{8,136},{16,144},{24,152},{32,160},{40,168},{48,176},{56,1... | collective-permute-start | bytes 67592 | tf_op jit(solution)/shard_map/ppermute | solution.py:69
  74.2 1.8 %collective-permute-done.9 = bf16[88,128]{1,0:T(8,128)(2,1)S(1)} collective-permute-done((bf16[88,128]{1,0:T(8,128)(2,1)S(1)}, bf16[88,128]{1,0:T(8,128)(2,1)S(1)}, u32[]{:S(2)}, u32[]{:S(2)}) %collective-permute-start.9) | collective-permute-done | bytes 22560 | tf_op jit(solution)/shard_map/ppermute | solution.py:69
  76.0 0.5 broadcast.96
  76.5 0.7 fusion.54
  78.4 1.9 %convolution_convert_fusion.1 = bf16[32,2560]{1,0:T(8,128)(2,1)S(1)} fusion(bf16[32,320]{1,0:T(8,128)(2,1)S(1)} %reshape_transpose.3, bf16[320,2560]{1,0:T(8,128)(2,1)} %param.27), kind=kOutput, calls=%fused_computation.1 | convolution fusion | flops 52510720 | bytes 1822720 | tf_op jit(solution)/shard_map/dot_general | solution.py:256
  80.4 1.1 collective-permute-start.10
  81.5 4.5 %collective-permute-done.10 = bf16[32,2560]{1,0:T(8,128)(2,1)S(1)} collective-permute-done((bf16[32,2560]{1,0:T(8,128)(2,1)S(1)}, bf16[32,2560]{1,0:T(8,128)(2,1)S(1)}, u32[]{:S(2)}, u32[]{:S(2)}) %collective-permute-start.10) | collective-permute-done | bytes 163872 | tf_op jit(solution)/shard_map/ppermute | solution.py:139
  86.0 1.7 %collective-permute-start.11 = (bf16[32,2560]{1,0:T(8,128)(2,1)S(1)}, bf16[32,2560]{1,0:T(8,128)(2,1)S(1)}, u32[]{:S(2)}, u32[]{:S(2)}) collective-permute-start(bf16[32,2560]{1,0:T(8,128)(2,1)S(1)} %add_convert_fusion.5), channel_id=1, source_target_pairs={{0,1},{1,0},{2,3},{3,2},{4,5},{5,4},{6,7},{7,6},{8,11},{9,10},{10,... | collective-permute-start | bytes 491528 | tf_op jit(solution)/shard_map/ppermute | solution.py:139
  87.7 3.7 %collective-permute-done.11 = bf16[32,2560]{1,0:T(8,128)(2,1)S(1)} collective-permute-done((bf16[32,2560]{1,0:T(8,128)(2,1)S(1)}, bf16[32,2560]{1,0:T(8,128)(2,1)S(1)}, u32[]{:S(2)}, u32[]{:S(2)}) %collective-permute-start.11) | collective-permute-done | bytes 163872 | tf_op jit(solution)/shard_map/ppermute | solution.py:139
  91.5 3.1 %collective-permute-start.12 = (bf16[32,2560]{1,0:T(8,128)(2,1)S(1)}, bf16[32,2560]{1,0:T(8,128)(2,1)S(1)}, u32[]{:S(2)}, u32[]{:S(2)}) collective-permute-start(bf16[32,2560]{1,0:T(8,128)(2,1)S(1)} %add_convert_fusion.4), channel_id=1, source_target_pairs={{0,3},{1,2},{2,1},{3,0},{4,7},{5,6},{6,5},{7,4},{8,12},{9,13},{10,... | collective-permute-start | bytes 491528 | tf_op jit(solution)/shard_map/ppermute | solution.py:139
  94.6 3.5 %collective-permute-done.12 = bf16[32,2560]{1,0:T(8,128)(2,1)S(1)} collective-permute-done((bf16[32,2560]{1,0:T(8,128)(2,1)S(1)}, bf16[32,2560]{1,0:T(8,128)(2,1)S(1)}, u32[]{:S(2)}, u32[]{:S(2)}) %collective-permute-start.12) | collective-permute-done | bytes 163872 | tf_op jit(solution)/shard_map/ppermute | solution.py:139
  98.4 0.5 fusion.55
  99.0 2.8 %convolution_convert_fusion = bf16[32,2560]{1,0:T(8,128)(2,1)S(1)} fusion(bf16[512,2560]{1,0:T(8,128)(2,1)S(1)} %copy-done, bf16[32,2560]{1,0:T(8,128)(2,1)S(1)} %multiply_convert_fusion, bf16[2560,512]{1,0:T(8,128)(2,1)} %param.29, f32[32,512]{1,0:T(8,128)S(1)} %fusion.55), kind=kOutput, calls=%fused_computation | convolution fusion | flops 167952384 | bytes 5636096 | tf_op jit(solution)/shard_map/dot_general | solution.py:270
  101.8 0.9 collective-permute-start.13
  102.7 4.5 %collective-permute-done.13 = bf16[32,2560]{1,0:T(8,128)(2,1)S(1)} collective-permute-done((bf16[32,2560]{1,0:T(8,128)(2,1)S(1)}, bf16[32,2560]{1,0:T(8,128)(2,1)S(1)}, u32[]{:S(2)}, u32[]{:S(2)}) %collective-permute-start.13) | collective-permute-done | bytes 163872 | tf_op jit(solution)/shard_map/ppermute | solution.py:139
  107.7 4.9 %collective-permute-done.14 = bf16[32,2560]{1,0:T(8,128)(2,1)S(1)} collective-permute-done((bf16[32,2560]{1,0:T(8,128)(2,1)S(1)}, bf16[32,2560]{1,0:T(8,128)(2,1)S(1)}, u32[]{:S(2)}, u32[]{:S(2)}) %collective-permute-start.14) | collective-permute-done | bytes 163872 | tf_op jit(solution)/shard_map/ppermute | solution.py:139
  112.7 3.1 %collective-permute-start.15 = (bf16[32,2560]{1,0:T(8,128)(2,1)S(1)}, bf16[32,2560]{1,0:T(8,128)(2,1)S(1)}, u32[]{:S(2)}, u32[]{:S(2)}) collective-permute-start(bf16[32,2560]{1,0:T(8,128)(2,1)S(1)} %add_convert_fusion.1), channel_id=1, source_target_pairs={{0,3},{1,2},{2,1},{3,0},{4,7},{5,6},{6,5},{7,4},{8,12},{9,13},{10,... | collective-permute-start | bytes 491528 | tf_op jit(solution)/shard_map/ppermute | solution.py:139
  115.8 3.5 %collective-permute-done.15 = bf16[32,2560]{1,0:T(8,128)(2,1)S(1)} collective-permute-done((bf16[32,2560]{1,0:T(8,128)(2,1)S(1)}, bf16[32,2560]{1,0:T(8,128)(2,1)S(1)}, u32[]{:S(2)}, u32[]{:S(2)}) %collective-permute-start.15) | collective-permute-done | bytes 163872 | tf_op jit(solution)/shard_map/ppermute | solution.py:139
  119.5 0.7 dynamic-slice_convert_fusion
  120.2 0.7 multiply_reduce_fusion
  (112 shorter events, 4.9 us)
Async XLA Ops:
  0.6 98.3 %copy-start = (bf16[512,2560]{1,0:T(8,128)(2,1)S(1)}, bf16[512,2560]{1,0:T(8,128)(2,1)}, u32[]{:S(2)}) copy-start(bf16[512,2560]{1,0:T(8,128)(2,1)} %param.30) | copy-start | bytes 7864324
  0.6 9.3 %collective-permute-start = (bf16[1,32,320]{2,1,0:T(8,128)(2,1)}, bf16[1,32,320]{2,1,0:T(8,128)(2,1)S(1)}, u32[]{:S(2)}, u32[]{:S(2)}) collective-permute-start(bf16[1,32,320]{2,1,0:T(8,128)(2,1)} %bitcast.198), channel_id=1, source_target_pairs={{0,128},{8,136},{16,144},{24,152},{32,160},{40,168},{48,176},{56,1... | collective-permute-start | bytes 61448 | tf_op jit(solution)/shard_map/ppermute | solution.py:69
  10.7 5.7 %collective-permute-start.1 = (bf16[2,1,32,320]{3,2,0,1:T(8,128)(2,1)S(1)}, bf16[2,1,32,320]{3,2,0,1:T(8,128)(2,1)S(1)}, u32[]{:S(2)}, u32[]{:S(2)}) collective-permute-start(bf16[2,1,32,320]{3,2,0,1:T(8,128)(2,1)S(1)} %fusion.33), channel_id=1, source_target_pairs={{0,16},{8,24},{16,0},{24,8},{32,48},{40,56},{48,32},{56,40},{64,80... | collective-permute-start | bytes 122888 | tf_op jit(solution)/shard_map/ppermute | solution.py:69
  16.4 14.2 %copy-start.7 = (bf16[32,80]{1,0:T(8,128)(2,1)S(1)}, bf16[32,80]{1,0:T(8,128)(2,1)}, u32[]{:S(2)}) copy-start(bf16[32,80]{1,0:T(8,128)(2,1)} %param.20) | copy-start | bytes 15364
  16.5 6.7 %collective-permute-start.2 = (bf16[2,2,1,32,320]{4,3,1,0,2:T(8,128)(2,1)S(1)}, bf16[2,2,1,32,320]{4,3,1,0,2:T(8,128)(2,1)S(1)}, u32[]{:S(2)}, u32[]{:S(2)}) collective-permute-start(bf16[2,2,1,32,320]{4,3,1,0,2:T(8,128)(2,1)S(1)} %bitcast.191), channel_id=1, source_target_pairs={{0,64},{8,72},{16,80},{24,88},{32,96},{40,104},{48,112},{56,120},{... | collective-permute-start | bytes 245768 | tf_op jit(solution)/shard_map/ppermute | solution.py:69
  23.2 5.8 %collective-permute-start.3 = (bf16[2,2,2,1,32,320]{5,4,2,1,0,3:T(8,128)(2,1)S(1)}, bf16[2,2,2,1,32,320]{5,4,2,1,0,3:T(8,128)(2,1)S(1)}, u32[]{:S(2)}, u32[]{:S(2)}) collective-permute-start(bf16[2,2,2,1,32,320]{5,4,2,1,0,3:T(8,128)(2,1)S(1)} %fusion.11), channel_id=1, source_target_pairs={{0,32},{8,40},{16,48},{24,56},{32,0},{40,8},{48,16},{56,24},{64,96... | collective-permute-start | bytes 491528 | tf_op jit(solution)/shard_map/ppermute | solution.py:69
  29.2 2.3 %collective-permute-start.4 = (bf16[2,2,2,2,1,32,320]{6,5,3,2,1,0,4:T(8,128)(2,1)S(1)}, bf16[2,2,2,2,1,32,320]{6,5,3,2,1,0,4:T(8,128)(2,1)S(1)}, u32[]{:S(2)}, u32[]{:S(2)}) collective-permute-start(bf16[2,2,2,2,1,32,320]{6,5,3,2,1,0,4:T(8,128)(2,1)S(1)} %fusion.8), channel_id=1, source_target_pairs={{0,8},{8,0},{16,24},{24,16},{32,40},{40,32},{48,56},{56,48},{64,72... | collective-permute-start | bytes 983048 | tf_op jit(solution)/shard_map/ppermute | solution.py:69
  39.1 6.0 %collective-permute-start.5 = (f32[16,88,128]{2,1,0:T(8,128)}, f32[16,88,128]{2,1,0:T(8,128)S(1)}, u32[]{:S(2)}, u32[]{:S(2)}) collective-permute-start(f32[16,88,128]{2,1,0:T(8,128)} %shard_map.177), channel_id=1, source_target_pairs={{0,8},{8,0},{16,24},{24,16},{32,40},{40,32},{48,56},{56,48},{64,72... | collective-permute-start | bytes 2162696 | tf_op jit(solution)/shard_map/ppermute | solution.py:69
  48.4 6.6 %collective-permute-start.6 = (bf16[2,2,2,88,128]{4,3,2,1,0:T(8,128)(2,1)S(1)}, bf16[2,2,2,88,128]{4,3,2,1,0:T(8,128)(2,1)S(1)}, u32[]{:S(2)}, u32[]{:S(2)}) collective-permute-start(bf16[2,2,2,88,128]{4,3,2,1,0:T(8,128)(2,1)S(1)} %concatenate.41), channel_id=1, source_target_pairs={{0,32},{8,40},{16,48},{24,56},{32,0},{40,8},{48,16},{56,24},{64,96... | collective-permute-start | bytes 540680 | tf_op jit(solution)/shard_map/ppermute | solution.py:69
  55.1 23.0 %copy-start.3 = (f32[1,16,2,4,80]{4,3,2,1,0:T(4,128)S(1)}, f32[1,16,2,4,80]{4,3,2,1,0:T(4,128)}, u32[]{:S(2)}) copy-start(f32[1,16,2,4,80]{4,3,2,1,0:T(4,128)} %fusion) | copy-start | bytes 122884
  55.4 6.6 %collective-permute-start.7 = (bf16[2,2,88,128]{3,2,0,1:T(8,128)(2,1)S(1)}, bf16[2,2,88,128]{3,2,0,1:T(8,128)(2,1)S(1)}, u32[]{:S(2)}, u32[]{:S(2)}) collective-permute-start(bf16[2,2,88,128]{3,2,0,1:T(8,128)(2,1)S(1)} %concatenate.44), channel_id=1, source_target_pairs={{0,64},{8,72},{16,80},{24,88},{32,96},{40,104},{48,112},{56,120},{... | collective-permute-start | bytes 270344 | tf_op jit(solution)/shard_map/ppermute | solution.py:69
  62.1 36.0 %copy-start.2 = (bf16[32,2560]{1,0:T(8,128)(2,1)S(1)}, bf16[32,2560]{1,0:T(8,128)(2,1)}, u32[]{:S(2)}) copy-start(bf16[32,2560]{1,0:T(8,128)(2,1)} %param.17) | copy-start | bytes 491524
  62.1 36.2 %copy-start.6 = (f32[2560]{0:T(1024)S(1)}, f32[2560]{0:T(1024)}, u32[]{:S(2)}) copy-start(f32[2560]{0:T(1024)} %param.31) | copy-start | bytes 30724
  62.2 5.6 %collective-permute-start.8 = (bf16[2,88,128]{2,1,0:T(8,128)(2,1)S(1)}, bf16[2,88,128]{2,1,0:T(8,128)(2,1)S(1)}, u32[]{:S(2)}, u32[]{:S(2)}) collective-permute-start(bf16[2,88,128]{2,1,0:T(8,128)(2,1)S(1)} %concatenate.47), channel_id=1, source_target_pairs={{0,16},{8,24},{16,0},{24,8},{32,48},{40,56},{48,32},{56,40},{64,80... | collective-permute-start | bytes 135176 | tf_op jit(solution)/shard_map/ppermute | solution.py:69
  68.1 7.9 %collective-permute-start.9 = (bf16[88,128]{1,0:T(8,128)(2,1)S(1)}, bf16[88,128]{1,0:T(8,128)(2,1)S(1)}, u32[]{:S(2)}, u32[]{:S(2)}) collective-permute-start(bf16[88,128]{1,0:T(8,128)(2,1)S(1)} %concatenate.50), channel_id=1, source_target_pairs={{0,128},{8,136},{16,144},{24,152},{32,160},{40,168},{48,176},{56,1... | collective-permute-start | bytes 67592 | tf_op jit(solution)/shard_map/ppermute | solution.py:69
  78.4 20.0 %copy-start.1 = (bf16[2560,512]{1,0:T(8,128)(2,1)S(1)}, bf16[2560,512]{1,0:T(8,128)(2,1)}, u32[]{:S(2)}) copy-start(bf16[2560,512]{1,0:T(8,128)(2,1)} %param.28) | copy-start | bytes 7864324
  80.4 5.6 %collective-permute-start.10 = (bf16[32,2560]{1,0:T(8,128)(2,1)S(1)}, bf16[32,2560]{1,0:T(8,128)(2,1)S(1)}, u32[]{:S(2)}, u32[]{:S(2)}) collective-permute-start(bf16[32,2560]{1,0:T(8,128)(2,1)S(1)} %convolution_convert_fusion.1), channel_id=1, source_target_pairs={{0,4},{1,5},{2,6},{3,7},{4,0},{5,1},{6,2},{7,3},{8,9},{9,8},{10,11... | collective-permute-start | bytes 491528 | tf_op jit(solution)/shard_map/ppermute | solution.py:139
  86.0 5.4 %collective-permute-start.11 = (bf16[32,2560]{1,0:T(8,128)(2,1)S(1)}, bf16[32,2560]{1,0:T(8,128)(2,1)S(1)}, u32[]{:S(2)}, u32[]{:S(2)}) collective-permute-start(bf16[32,2560]{1,0:T(8,128)(2,1)S(1)} %add_convert_fusion.5), channel_id=1, source_target_pairs={{0,1},{1,0},{2,3},{3,2},{4,5},{5,4},{6,7},{7,6},{8,11},{9,10},{10,... | collective-permute-start | bytes 491528 | tf_op jit(solution)/shard_map/ppermute | solution.py:139
  91.5 6.6 %collective-permute-start.12 = (bf16[32,2560]{1,0:T(8,128)(2,1)S(1)}, bf16[32,2560]{1,0:T(8,128)(2,1)S(1)}, u32[]{:S(2)}, u32[]{:S(2)}) collective-permute-start(bf16[32,2560]{1,0:T(8,128)(2,1)S(1)} %add_convert_fusion.4), channel_id=1, source_target_pairs={{0,3},{1,2},{2,1},{3,0},{4,7},{5,6},{6,5},{7,4},{8,12},{9,13},{10,... | collective-permute-start | bytes 491528 | tf_op jit(solution)/shard_map/ppermute | solution.py:139
  98.9 21.3 %copy-start.4 = (f32[2560]{0:T(1024)S(1)}, f32[2560]{0:T(1024)}, u32[]{:S(2)}) copy-start(f32[2560]{0:T(1024)} %param.33) | copy-start | bytes 30724
  99.0 21.3 %copy-start.5 = (f32[2560]{0:T(1024)S(1)}, f32[2560]{0:T(1024)}, u32[]{:S(2)}) copy-start(f32[2560]{0:T(1024)} %param.32) | copy-start | bytes 30724
  101.8 5.4 %collective-permute-start.13 = (bf16[32,2560]{1,0:T(8,128)(2,1)S(1)}, bf16[32,2560]{1,0:T(8,128)(2,1)S(1)}, u32[]{:S(2)}, u32[]{:S(2)}) collective-permute-start(bf16[32,2560]{1,0:T(8,128)(2,1)S(1)} %convolution_convert_fusion), channel_id=1, source_target_pairs={{0,4},{1,5},{2,6},{3,7},{4,0},{5,1},{6,2},{7,3},{8,9},{9,8},{10,11... | collective-permute-start | bytes 491528 | tf_op jit(solution)/shard_map/ppermute | solution.py:139
  107.2 5.4 %collective-permute-start.14 = (bf16[32,2560]{1,0:T(8,128)(2,1)S(1)}, bf16[32,2560]{1,0:T(8,128)(2,1)S(1)}, u32[]{:S(2)}, u32[]{:S(2)}) collective-permute-start(bf16[32,2560]{1,0:T(8,128)(2,1)S(1)} %add_convert_fusion.2), channel_id=1, source_target_pairs={{0,1},{1,0},{2,3},{3,2},{4,5},{5,4},{6,7},{7,6},{8,11},{9,10},{10,... | collective-permute-start | bytes 491528 | tf_op jit(solution)/shard_map/ppermute | solution.py:139
  112.7 6.6 %collective-permute-start.15 = (bf16[32,2560]{1,0:T(8,128)(2,1)S(1)}, bf16[32,2560]{1,0:T(8,128)(2,1)S(1)}, u32[]{:S(2)}, u32[]{:S(2)}) collective-permute-start(bf16[32,2560]{1,0:T(8,128)(2,1)S(1)} %add_convert_fusion.1), channel_id=1, source_target_pairs={{0,3},{1,2},{2,1},{3,0},{4,7},{5,6},{6,5},{7,4},{8,12},{9,13},{10,... | collective-permute-start | bytes 491528 | tf_op jit(solution)/shard_map/ppermute | solution.py:139

commit v12 on v11

--- a/solution.py
+++ b/solution.py
@@ -40,7 +40,7 @@
 
 
 def prefix_partials(count, half, q, kt, vt):
-    pairs, _, rows, _ = q.shape
+    pairs, rows, _ = q.shape
     L = kt.shape[3]
     bp = min(BLOCK_PROMPTS, pairs)
     return pl.pallas_call(
@@ -49,7 +49,7 @@
             num_scalar_prefetch=2,
             grid=(pairs // bp,),
             in_specs=[
-                pl.BlockSpec((bp, None, rows, HEAD_SIZE), lambda p, c, h: (p, h[0], 0, 0)),
+                pl.BlockSpec((bp, rows, HEAD_SIZE), lambda p, c, h: (p, 0, 0)),
                 pl.BlockSpec((bp, None, HEAD_SIZE, L), lambda p, c, h: (p, h[0], 0, 0)),
                 pl.BlockSpec((bp, None, HEAD_SIZE, L), lambda p, c, h: (p, h[0], 0, 0)),
             ],
@@ -84,6 +84,28 @@
     order = sorted(range(nb), key=lambda i: -taken[i])
     buf = jnp.transpose(buf, order + list(range(nb, buf.ndim)))
     return buf.reshape((n * x.shape[0],) + x.shape[1:]), tie
+
+
+def gather_halves(x, axis, n, bits, tie, tie_after):
+    me = lax.axis_index(axis)
+    buf = x[None]
+    taken = []
+    for b in bits[:-1]:
+        other = exchange(buf, axis, n, b)
+        high = ((me >> b) & 1) == 1
+        buf = jnp.stack([jnp.where(high, other, buf), jnp.where(high, buf, other)])
+        taken.insert(0, b)
+        if len(taken) == tie_after:
+            buf, tie = lax.optimization_barrier((buf, tie))
+    other = exchange(buf, axis, n, bits[-1])
+    nb = len(taken)
+    order = sorted(range(nb), key=lambda i: -taken[i])
+    shape = ((n // 2) * x.shape[0],) + x.shape[1:]
+
+    def arrange(y):
+        return jnp.transpose(y, order + list(range(nb, y.ndim))).reshape(shape)
+
+    return arrange(buf), arrange(other), tie
 
 
 def merge_partials(a, b):
@@ -177,7 +199,10 @@
     gather_order = [b for i, b in enumerate(gather_order) if b not in gather_order[:i]]
     reduce_order = gather_order[::-1]
 
-    gathered, local_queries = gather_rows(queries, "req", req_count, gather_order, queries, 2)
+    assert gather_order[-1] == 0
+    own_queries, other_queries, local_queries = gather_halves(
+        queries, "req", req_count, gather_order, queries, 2
+    )
     query_own = local_queries.reshape(SAMPLE_COUNT, DECODE_TOKENS, kv_local, query_groups, HEAD_SIZE)
     tail_key_block = sample_tail_keys.reshape(SAMPLE_COUNT, TAIL_LENGTH, kv_local, HEAD_SIZE)
     tail_value_block = sample_tail_values.reshape(SAMPLE_COUNT, TAIL_LENGTH, kv_local, HEAD_SIZE)
@@ -215,11 +240,12 @@
     local_out = local_out + jnp.einsum(
         "ksjgi,sikh->ksjgh", w_new.astype(jnp.bfloat16), fresh_v, preferred_element_type=jnp.float32
     )
-    gathered, local_out, local_top, local_sum = lax.optimization_barrier(
-        (gathered, local_out, local_top, local_sum)
+    own_queries, other_queries, local_out, local_top, local_sum = lax.optimization_barrier(
+        (own_queries, other_queries, local_out, local_top, local_sum)
     )
     pairs = prompts // 2
-    query_all = gathered.reshape(pairs, 2, rows, HEAD_SIZE)
+    query_keep = own_queries.reshape(pairs, rows, HEAD_SIZE)
+    query_send = other_queries.reshape(pairs, rows, HEAD_SIZE)
     prefix_key_block = jnp.swapaxes(
         shared_prefix_keys.reshape(pairs, 2, piece_len, HEAD_SIZE * kv_local), 2, 3
     )
@@ -229,10 +255,10 @@
     count = jnp.clip(prompt_prefix_length - req_index * piece_len, 0, piece_len).astype(jnp.int32)
     own_low = (req_index & 1).astype(jnp.int32)
     send_half = prefix_partials(
-        count, (1 - own_low)[None], query_all, prefix_key_block, prefix_value_block
+        count, (1 - own_low)[None], query_send, prefix_key_block, prefix_value_block
     )
     got = exchange(send_half, "req", req_count, 0)
-    keep_half = prefix_partials(count, own_low[None], query_all, prefix_key_block, prefix_value_block)
+    keep_half = prefix_partials(count, own_low[None], query_keep, prefix_key_block, prefix_value_block)
     merged = merge_partials(keep_half, got)
     nb = req_count.bit_length() - 1
     merged = merged.reshape((2,) * (nb - 1) + merged.shape[1:])

time: 122 us -> 124 us (1.016)
  waiting for transfers between devices: 51.3 us -> 53 us
    ppermute x10, waiting for transfers between devices: 26.6 us -> 28.4 us  [exchange(): return lax.ppermute(x, axis, perm=[(i, i ^ 1 << bit) for i in range(n)])]
where the time goes in v12:
time: 124 us; the launch traced here: 123 us
  waiting for transfers between devices  53 us (43%)
  starting transfers between devices  31.8 us (26%)
  Pallas kernels  11.1 us (9%)
  other arithmetic  10.1 us (8%)
  matrix products  9.92 us (8%)
  local copies, waits for them, and re-layouts  6.06 us (5%)
    ppermute x10, waiting for transfers between devices, exchange(): return lax.ppermute(x, axis, perm=[(i, i ^ 1 << bit) for i in range(n)])  28.4 us
    ppermute x6, waiting for transfers between devices, allreduce_bf16(): other = lax.ppermute(cur, ('req', 'mlp'), perm=perm)  24.7 us
    ppermute x10, starting transfers between devices, exchange(): return lax.ppermute(x, axis, perm=[(i, i ^ 1 << bit) for i in range(n)])  21.4 us
    pallas_call x2, Pallas kernels, prefix_partials(): pl.pallas_call(prefix_kernel, grid_spec=pltpu.PrefetchScalarGridSpec(num_...  11.1 us
    ppermute x6, starting transfers between devices, allreduce_bf16(): other = lax.ppermute(cur, ('req', 'mlp'), perm=perm)  10.4 us
    dot_general x1, matrix products, on_device(): jnp.dot(hidden, down_weight, preferred_element_type=jnp.float32)  2.82 us
  transfers between devices with their start and end apart: 16, of which 14 were waited for; matrix products, arithmetic and copies ran while one was open for 7% of the time, Pallas kernels for 5%

profile of v12, /device:TPU:6, one launch (start us, length us, event | category | flops | bytes accessed | tf_op | source)
XLA Modules:
  0.0 123.2 jit_solution(844391183448518186)
XLA Ops:
  0.6 7.3 %collective-permute-start = (bf16[1,32,320]{2,1,0:T(8,128)(2,1)}, bf16[1,32,320]{2,1,0:T(8,128)(2,1)S(1)}, u32[]{:S(2)}, u32[]{:S(2)}) collective-permute-start(bf16[1,32,320]{2,1,0:T(8,128)(2,1)} %bitcast.187), channel_id=1, source_target_pairs={{0,128},{8,136},{16,144},{24,152},{32,160},{40,168},{48,176},{56,1... | collective-permute-start | bytes 61448 | tf_op jit(solution)/shard_map/ppermute | solution.py:69
  7.9 0.7 iota_compare_fusion
  8.6 1.2 subtract_clamp_fusion.count_ref
  9.9 0.7 select_bitcast_fusion.4
  10.7 1.5 %collective-permute-start.1 = (bf16[2,1,32,320]{3,2,0,1:T(8,128)(2,1)S(1)}, bf16[2,1,32,320]{3,2,0,1:T(8,128)(2,1)S(1)}, u32[]{:S(2)}, u32[]{:S(2)}) collective-permute-start(bf16[2,1,32,320]{3,2,0,1:T(8,128)(2,1)S(1)} %fusion.31), channel_id=1, source_target_pairs={{0,16},{8,24},{16,0},{24,8},{32,48},{40,56},{48,32},{56,40},{64,80... | collective-permute-start | bytes 122888 | tf_op jit(solution)/shard_map/ppermute | solution.py:69
  12.2 4.2 %collective-permute-done.1 = bf16[2,1,32,320]{3,2,0,1:T(8,128)(2,1)S(1)} collective-permute-done((bf16[2,1,32,320]{3,2,0,1:T(8,128)(2,1)S(1)}, bf16[2,1,32,320]{3,2,0,1:T(8,128)(2,1)S(1)}, u32[]{:S(2)}, u32[]{:S(2)}) %collective-permute-start.1) | collective-permute-done | bytes 40992 | tf_op jit(solution)/shard_map/ppermute | solution.py:69
  16.5 0.8 reshape.189
  17.3 2.1 %collective-permute-start.2 = (bf16[2,2,1,32,320]{4,3,1,0,2:T(8,128)(2,1)S(1)}, bf16[2,2,1,32,320]{4,3,1,0,2:T(8,128)(2,1)S(1)}, u32[]{:S(2)}, u32[]{:S(2)}) collective-permute-start(bf16[2,2,1,32,320]{4,3,1,0,2:T(8,128)(2,1)S(1)} %bitcast.179), channel_id=1, source_target_pairs={{0,64},{8,72},{16,80},{24,88},{32,96},{40,104},{48,112},{56,120},{... | collective-permute-start | bytes 245768 | tf_op jit(solution)/shard_map/ppermute | solution.py:69
  19.4 1.3 %select_reduce_fusion = (f32[16,2,4]{2,1,0:T(2,128)S(1)}, f32[16,2,4,128]{3,2,1,0:T(4,128)S(1)}) fusion(pred[16,128]{1,0:T(8,128)(4,1)S(1)} %iota_compare_fusion, bf16[16,2,4,80]{3,2,1,0:T(4,128)(2,1)S(1)} %reshape.189, bf16[1,16,128,80]{2,3,1,0:T(8,128)(2,1)} %param.23), kind=kOutput, calls=%fused_computation.70 | convolution fusion | flops 2670464 | bytes 416256 | tf_op jit(solution)/shard_map/sjkgh,stkh->ksjgt/dot_general | solution.py:212
  20.7 1.1 select_reduce_fusion.1
  21.8 2.1 %collective-permute-done.2 = bf16[2,2,1,32,320]{4,3,1,0,2:T(8,128)(2,1)S(1)} collective-permute-done((bf16[2,2,1,32,320]{4,3,1,0,2:T(8,128)(2,1)S(1)}, bf16[2,2,1,32,320]{4,3,1,0,2:T(8,128)(2,1)S(1)}, u32[]{:S(2)}, u32[]{:S(2)}) %collective-permute-start.2) | collective-permute-done | bytes 81952 | tf_op jit(solution)/shard_map/ppermute | solution.py:69
  24.8 5.0 %collective-permute-done.3 = bf16[2,2,2,1,32,320]{5,4,2,1,0,3:T(8,128)(2,1)S(1)} collective-permute-done((bf16[2,2,2,1,32,320]{5,4,2,1,0,3:T(8,128)(2,1)S(1)}, bf16[2,2,2,1,32,320]{5,4,2,1,0,3:T(8,128)(2,1)S(1)}, u32[]{:S(2)}, u32[]{:S(2)}) %collective-permute-start.3) | collective-permute-done | bytes 163872 | tf_op jit(solution)/shard_map/ppermute | solution.py:69
  30.1 1.3 %fusion.4 = f32[16,2,4,80]{3,2,1,0:T(4,128)S(1)} fusion(bf16[1,16,128,80]{2,3,1,0:T(8,128)(2,1)} %param.24, f32[16,2,4,128]{3,2,1,0:T(4,128)S(1)} %get-tuple-element.56, f32[16,2,4]{2,1,0:T(2,128)S(1)} %max.43, pred[16,128]{1,0:T(8,128)(4,1)S(1)} %iota_compare_fusion), kind=kOutput, calls=%fused_computation.21 | convolution fusion | flops 2670592 | bytes 436736 | tf_op jit(solution)/shard_map/ksjgt,stkh->ksjgh/dot_general | solution.py:234
  31.4 0.9 fusion
  32.4 1.1 reshape.197.q_ref
  33.6 5.5 %shard_map.177 = f32[16,88,128]{2,1,0:T(8,128)} custom-call(s32[32]{0:T(128)} %subtract_clamp_fusion.count_ref, s32[1]{0:T(128)} %bitcast.46.half_ref, bf16[16,128,80]{2,1,0:T(8,128)(2,1)} %reshape.197.q_ref, bf16[16,2,80,512]{3,2,1,0:T(8,128)(2,1)} %bitcast.172, bf16[16,2,80,512]{3,2,1,0:T(8,128)(2,1)} %bitcast.174), custom_call_target="tpu_custom_call" | custom-call | flops 335544320 | bytes 3670016 | tf_op jit(solution)/shard_map/pallas_call | solution.py:46
  39.1 0.5 collective-permute-start.5
  39.6 1.1 reshape.194.q_ref
  40.7 5.6 %shard_map.176 = f32[16,88,128]{2,1,0:T(8,128)} custom-call(s32[32]{0:T(128)} %subtract_clamp_fusion.count_ref, s32[1]{0:T(128)} %bitcast.half_ref, bf16[16,128,80]{2,1,0:T(8,128)(2,1)} %reshape.194.q_ref, bf16[16,2,80,512]{3,2,1,0:T(8,128)(2,1)} %bitcast.173, bf16[16,2,80,512]{3,2,1,0:T(8,128)(2,1)} %bitcast.175), custom_call_target="tpu_custom_call" | custom-call | flops 335544320 | bytes 3670016 | tf_op jit(solution)/shard_map/pallas_call | solution.py:46
  46.3 0.9 subtract_exponential_fusion.1
  47.2 0.9 subtract_exponential_fusion
  48.0 1.4 %fusion.2 = f32[16,80,128]{2,1,0:T(8,128)S(1)} fusion(f32[16,88,128]{2,1,0:T(8,128)} %collective-permute-done.5, f32[16,88,128]{2,1,0:T(8,128)} %shard_map.176, f32[16,128]{1,0:T(8,128)S(1)} %bitcast.188, f32[16,128]{1,0:T(8,128)S(1)} %bitcast.190), kind=kLoop, calls=%fused_computation.10 | loop fusion | flops 491520 | bytes 1982464 | tf_op jit(solution)/shard_map/add | solution.py:117
  49.4 0.9 fusion.12
  50.9 6.3 %collective-permute-done.6 = bf16[2,2,2,88,128]{4,3,2,1,0:T(8,128)(2,1)S(1)} collective-permute-done((bf16[2,2,2,88,128]{4,3,2,1,0:T(8,128)(2,1)S(1)}, bf16[2,2,2,88,128]{4,3,2,1,0:T(8,128)(2,1)S(1)}, u32[]{:S(2)}, u32[]{:S(2)}) %collective-permute-start.6) | collective-permute-done | bytes 180256 | tf_op jit(solution)/shard_map/ppermute | solution.py:69
  57.6 1.9 %collective-permute-start.7 = (bf16[2,2,88,128]{3,2,0,1:T(8,128)(2,1)S(1)}, bf16[2,2,88,128]{3,2,0,1:T(8,128)(2,1)S(1)}, u32[]{:S(2)}, u32[]{:S(2)}) collective-permute-start(bf16[2,2,88,128]{3,2,0,1:T(8,128)(2,1)S(1)} %concatenate.44), channel_id=1, source_target_pairs={{0,64},{8,72},{16,80},{24,88},{32,96},{40,104},{48,112},{56,120},{... | collective-permute-start | bytes 270344 | tf_op jit(solution)/shard_map/ppermute | solution.py:69
  59.5 4.7 %collective-permute-done.7 = bf16[2,2,88,128]{3,2,0,1:T(8,128)(2,1)S(1)} collective-permute-done((bf16[2,2,88,128]{3,2,0,1:T(8,128)(2,1)S(1)}, bf16[2,2,88,128]{3,2,0,1:T(8,128)(2,1)S(1)}, u32[]{:S(2)}, u32[]{:S(2)}) %collective-permute-start.7) | collective-permute-done | bytes 90144 | tf_op jit(solution)/shard_map/ppermute | solution.py:69
  64.5 1.5 %collective-permute-start.8 = (bf16[2,88,128]{2,1,0:T(8,128)(2,1)S(1)}, bf16[2,88,128]{2,1,0:T(8,128)(2,1)S(1)}, u32[]{:S(2)}, u32[]{:S(2)}) collective-permute-start(bf16[2,88,128]{2,1,0:T(8,128)(2,1)S(1)} %concatenate.47), channel_id=1, source_target_pairs={{0,16},{8,24},{16,0},{24,8},{32,48},{40,56},{48,32},{56,40},{64,80... | collective-permute-start | bytes 135176 | tf_op jit(solution)/shard_map/ppermute | solution.py:69
  66.0 4.1 %collective-permute-done.8 = bf16[2,88,128]{2,1,0:T(8,128)(2,1)S(1)} collective-permute-done((bf16[2,88,128]{2,1,0:T(8,128)(2,1)S(1)}, bf16[2,88,128]{2,1,0:T(8,128)(2,1)S(1)}, u32[]{:S(2)}, u32[]{:S(2)}) %collective-permute-start.8) | collective-permute-done | bytes 45088 | tf_op jit(solution)/shard_map/ppermute | solution.py:69
  70.3 6.1 %collective-permute-start.9 = (bf16[88,128]{1,0:T(8,128)(2,1)S(1)}, bf16[88,128]{1,0:T(8,128)(2,1)S(1)}, u32[]{:S(2)}, u32[]{:S(2)}) collective-permute-start(bf16[88,128]{1,0:T(8,128)(2,1)S(1)} %concatenate.50), channel_id=1, source_target_pairs={{0,128},{8,136},{16,144},{24,152},{32,160},{40,168},{48,176},{56,1... | collective-permute-start | bytes 67592 | tf_op jit(solution)/shard_map/ppermute | solution.py:69
  76.4 1.8 %collective-permute-done.9 = bf16[88,128]{1,0:T(8,128)(2,1)S(1)} collective-permute-done((bf16[88,128]{1,0:T(8,128)(2,1)S(1)}, bf16[88,128]{1,0:T(8,128)(2,1)S(1)}, u32[]{:S(2)}, u32[]{:S(2)}) %collective-permute-start.9) | collective-permute-done | bytes 22560 | tf_op jit(solution)/shard_map/ppermute | solution.py:69
  78.2 0.5 broadcast.96
  78.7 0.7 fusion.53
  80.6 2.0 %convolution_convert_fusion.1 = bf16[32,2560]{1,0:T(8,128)(2,1)S(1)} fusion(bf16[32,320]{1,0:T(8,128)(2,1)S(1)} %reshape_transpose.3, bf16[320,2560]{1,0:T(8,128)(2,1)} %param.27), kind=kOutput, calls=%fused_computation.1 | convolution fusion | flops 52510720 | bytes 1822720 | tf_op jit(solution)/shard_map/dot_general | solution.py:282
  82.6 1.1 collective-permute-start.10
  83.7 4.5 %collective-permute-done.10 = bf16[32,2560]{1,0:T(8,128)(2,1)S(1)} collective-permute-done((bf16[32,2560]{1,0:T(8,128)(2,1)S(1)}, bf16[32,2560]{1,0:T(8,128)(2,1)S(1)}, u32[]{:S(2)}, u32[]{:S(2)}) %collective-permute-start.10) | collective-permute-done | bytes 163872 | tf_op jit(solution)/shard_map/ppermute | solution.py:161
  88.2 1.7 %collective-permute-start.11 = (bf16[32,2560]{1,0:T(8,128)(2,1)S(1)}, bf16[32,2560]{1,0:T(8,128)(2,1)S(1)}, u32[]{:S(2)}, u32[]{:S(2)}) collective-permute-start(bf16[32,2560]{1,0:T(8,128)(2,1)S(1)} %add_convert_fusion.5), channel_id=1, source_target_pairs={{0,1},{1,0},{2,3},{3,2},{4,5},{5,4},{6,7},{7,6},{8,11},{9,10},{10,... | collective-permute-start | bytes 491528 | tf_op jit(solution)/shard_map/ppermute | solution.py:161
  89.9 3.7 %collective-permute-done.11 = bf16[32,2560]{1,0:T(8,128)(2,1)S(1)} collective-permute-done((bf16[32,2560]{1,0:T(8,128)(2,1)S(1)}, bf16[32,2560]{1,0:T(8,128)(2,1)S(1)}, u32[]{:S(2)}, u32[]{:S(2)}) %collective-permute-start.11) | collective-permute-done | bytes 163872 | tf_op jit(solution)/shard_map/ppermute | solution.py:161
  93.7 3.1 %collective-permute-start.12 = (bf16[32,2560]{1,0:T(8,128)(2,1)S(1)}, bf16[32,2560]{1,0:T(8,128)(2,1)S(1)}, u32[]{:S(2)}, u32[]{:S(2)}) collective-permute-start(bf16[32,2560]{1,0:T(8,128)(2,1)S(1)} %add_convert_fusion.4), channel_id=1, source_target_pairs={{0,3},{1,2},{2,1},{3,0},{4,7},{5,6},{6,5},{7,4},{8,12},{9,13},{10,... | collective-permute-start | bytes 491528 | tf_op jit(solution)/shard_map/ppermute | solution.py:161
  96.8 3.5 %collective-permute-done.12 = bf16[32,2560]{1,0:T(8,128)(2,1)S(1)} collective-permute-done((bf16[32,2560]{1,0:T(8,128)(2,1)S(1)}, bf16[32,2560]{1,0:T(8,128)(2,1)S(1)}, u32[]{:S(2)}, u32[]{:S(2)}) %collective-permute-start.12) | collective-permute-done | bytes 163872 | tf_op jit(solution)/shard_map/ppermute | solution.py:161
  100.6 0.5 fusion.54
  101.2 2.8 %convolution_convert_fusion = bf16[32,2560]{1,0:T(8,128)(2,1)S(1)} fusion(bf16[512,2560]{1,0:T(8,128)(2,1)S(1)} %copy-done, bf16[32,2560]{1,0:T(8,128)(2,1)S(1)} %multiply_convert_fusion, bf16[2560,512]{1,0:T(8,128)(2,1)} %param.29, f32[32,512]{1,0:T(8,128)S(1)} %fusion.54), kind=kOutput, calls=%fused_computation | convolution fusion | flops 167952384 | bytes 5636096 | tf_op jit(solution)/shard_map/dot_general | solution.py:296
  104.0 0.9 collective-permute-start.13
  104.9 4.5 %collective-permute-done.13 = bf16[32,2560]{1,0:T(8,128)(2,1)S(1)} collective-permute-done((bf16[32,2560]{1,0:T(8,128)(2,1)S(1)}, bf16[32,2560]{1,0:T(8,128)(2,1)S(1)}, u32[]{:S(2)}, u32[]{:S(2)}) %collective-permute-start.13) | collective-permute-done | bytes 163872 | tf_op jit(solution)/shard_map/ppermute | solution.py:161
  109.9 5.0 %collective-permute-done.14 = bf16[32,2560]{1,0:T(8,128)(2,1)S(1)} collective-permute-done((bf16[32,2560]{1,0:T(8,128)(2,1)S(1)}, bf16[32,2560]{1,0:T(8,128)(2,1)S(1)}, u32[]{:S(2)}, u32[]{:S(2)}) %collective-permute-start.14) | collective-permute-done | bytes 163872 | tf_op jit(solution)/shard_map/ppermute | solution.py:161
  114.9 3.1 %collective-permute-start.15 = (bf16[32,2560]{1,0:T(8,128)(2,1)S(1)}, bf16[32,2560]{1,0:T(8,128)(2,1)S(1)}, u32[]{:S(2)}, u32[]{:S(2)}) collective-permute-start(bf16[32,2560]{1,0:T(8,128)(2,1)S(1)} %add_convert_fusion.1), channel_id=1, source_target_pairs={{0,3},{1,2},{2,1},{3,0},{4,7},{5,6},{6,5},{7,4},{8,12},{9,13},{10,... | collective-permute-start | bytes 491528 | tf_op jit(solution)/shard_map/ppermute | solution.py:161
  118.0 3.5 %collective-permute-done.15 = bf16[32,2560]{1,0:T(8,128)(2,1)S(1)} collective-permute-done((bf16[32,2560]{1,0:T(8,128)(2,1)S(1)}, bf16[32,2560]{1,0:T(8,128)(2,1)S(1)}, u32[]{:S(2)}, u32[]{:S(2)}) %collective-permute-start.15) | collective-permute-done | bytes 163872 | tf_op jit(solution)/shard_map/ppermute | solution.py:161
  121.7 0.7 dynamic-slice_convert_fusion
  122.5 0.7 multiply_reduce_fusion
  (111 shorter events, 4.9 us)
Async XLA Ops:
  0.6 100.5 %copy-start = (bf16[512,2560]{1,0:T(8,128)(2,1)S(1)}, bf16[512,2560]{1,0:T(8,128)(2,1)}, u32[]{:S(2)}) copy-start(bf16[512,2560]{1,0:T(8,128)(2,1)} %param.30) | copy-start | bytes 7864324
  0.6 9.3 %collective-permute-start = (bf16[1,32,320]{2,1,0:T(8,128)(2,1)}, bf16[1,32,320]{2,1,0:T(8,128)(2,1)S(1)}, u32[]{:S(2)}, u32[]{:S(2)}) collective-permute-start(bf16[1,32,320]{2,1,0:T(8,128)(2,1)} %bitcast.187), channel_id=1, source_target_pairs={{0,128},{8,136},{16,144},{24,152},{32,160},{40,168},{48,176},{56,1... | collective-permute-start | bytes 61448 | tf_op jit(solution)/shard_map/ppermute | solution.py:69
  10.7 5.7 %collective-permute-start.1 = (bf16[2,1,32,320]{3,2,0,1:T(8,128)(2,1)S(1)}, bf16[2,1,32,320]{3,2,0,1:T(8,128)(2,1)S(1)}, u32[]{:S(2)}, u32[]{:S(2)}) collective-permute-start(bf16[2,1,32,320]{3,2,0,1:T(8,128)(2,1)S(1)} %fusion.31), channel_id=1, source_target_pairs={{0,16},{8,24},{16,0},{24,8},{32,48},{40,56},{48,32},{56,40},{64,80... | collective-permute-start | bytes 122888 | tf_op jit(solution)/shard_map/ppermute | solution.py:69
  17.3 14.1 %copy-start.7 = (bf16[32,80]{1,0:T(8,128)(2,1)S(1)}, bf16[32,80]{1,0:T(8,128)(2,1)}, u32[]{:S(2)}) copy-start(bf16[32,80]{1,0:T(8,128)(2,1)} %param.20) | copy-start | bytes 15364
  17.3 6.7 %collective-permute-start.2 = (bf16[2,2,1,32,320]{4,3,1,0,2:T(8,128)(2,1)S(1)}, bf16[2,2,1,32,320]{4,3,1,0,2:T(8,128)(2,1)S(1)}, u32[]{:S(2)}, u32[]{:S(2)}) collective-permute-start(bf16[2,2,1,32,320]{4,3,1,0,2:T(8,128)(2,1)S(1)} %bitcast.179), channel_id=1, source_target_pairs={{0,64},{8,72},{16,80},{24,88},{32,96},{40,104},{48,112},{56,120},{... | collective-permute-start | bytes 245768 | tf_op jit(solution)/shard_map/ppermute | solution.py:69
  24.1 5.8 %collective-permute-start.3 = (bf16[2,2,2,1,32,320]{5,4,2,1,0,3:T(8,128)(2,1)S(1)}, bf16[2,2,2,1,32,320]{5,4,2,1,0,3:T(8,128)(2,1)S(1)}, u32[]{:S(2)}, u32[]{:S(2)}) collective-permute-start(bf16[2,2,2,1,32,320]{5,4,2,1,0,3:T(8,128)(2,1)S(1)} %fusion.9), channel_id=1, source_target_pairs={{0,32},{8,40},{16,48},{24,56},{32,0},{40,8},{48,16},{56,24},{64,96... | collective-permute-start | bytes 491528 | tf_op jit(solution)/shard_map/ppermute | solution.py:69
  30.0 2.4 %collective-permute-start.4 = (bf16[2,2,2,2,1,32,320]{6,5,3,2,1,4,0:T(8,128)(2,1)S(1)}, bf16[2,2,2,2,1,32,320]{6,5,3,2,1,4,0:T(8,128)(2,1)S(1)}, u32[]{:S(2)}, u32[]{:S(2)}) collective-permute-start(bf16[2,2,2,2,1,32,320]{6,5,3,2,1,4,0:T(8,128)(2,1)S(1)} %get-tuple-element.30), channel_id=1, source_target_pairs={{0,8},{8,0},{16,24},{24,16},{32,40},{40,32},{48,56},{56,48},{64,72... | collective-permute-start | bytes 983048 | tf_op jit(solution)/shard_map/ppermute | solution.py:69
  39.1 7.2 %collective-permute-start.5 = (f32[16,88,128]{2,1,0:T(8,128)}, f32[16,88,128]{2,1,0:T(8,128)}, u32[]{:S(2)}, u32[]{:S(2)}) collective-permute-start(f32[16,88,128]{2,1,0:T(8,128)} %shard_map.177), channel_id=1, source_target_pairs={{0,8},{8,0},{16,24},{24,16},{32,40},{40,32},{48,56},{56,48},{64,72... | collective-permute-start | bytes 2162696 | tf_op jit(solution)/shard_map/ppermute | solution.py:69
  50.7 6.6 %collective-permute-start.6 = (bf16[2,2,2,88,128]{4,3,2,1,0:T(8,128)(2,1)S(1)}, bf16[2,2,2,88,128]{4,3,2,1,0:T(8,128)(2,1)S(1)}, u32[]{:S(2)}, u32[]{:S(2)}) collective-permute-start(bf16[2,2,2,88,128]{4,3,2,1,0:T(8,128)(2,1)S(1)} %concatenate.41), channel_id=1, source_target_pairs={{0,32},{8,40},{16,48},{24,56},{32,0},{40,8},{48,16},{56,24},{64,96... | collective-permute-start | bytes 540680 | tf_op jit(solution)/shard_map/ppermute | solution.py:69
  57.4 23.0 %copy-start.3 = (f32[1,16,2,4,80]{4,3,2,1,0:T(4,128)S(1)}, f32[1,16,2,4,80]{4,3,2,1,0:T(4,128)}, u32[]{:S(2)}) copy-start(f32[1,16,2,4,80]{4,3,2,1,0:T(4,128)} %fusion) | copy-start | bytes 122884
  57.6 6.6 %collective-permute-start.7 = (bf16[2,2,88,128]{3,2,0,1:T(8,128)(2,1)S(1)}, bf16[2,2,88,128]{3,2,0,1:T(8,128)(2,1)S(1)}, u32[]{:S(2)}, u32[]{:S(2)}) collective-permute-start(bf16[2,2,88,128]{3,2,0,1:T(8,128)(2,1)S(1)} %concatenate.44), channel_id=1, source_target_pairs={{0,64},{8,72},{16,80},{24,88},{32,96},{40,104},{48,112},{56,120},{... | collective-permute-start | bytes 270344 | tf_op jit(solution)/shard_map/ppermute | solution.py:69
  64.3 36.0 %copy-start.2 = (bf16[32,2560]{1,0:T(8,128)(2,1)S(1)}, bf16[32,2560]{1,0:T(8,128)(2,1)}, u32[]{:S(2)}) copy-start(bf16[32,2560]{1,0:T(8,128)(2,1)} %param.17) | copy-start | bytes 491524
  64.4 36.1 %copy-start.6 = (f32[2560]{0:T(1024)S(1)}, f32[2560]{0:T(1024)}, u32[]{:S(2)}) copy-start(f32[2560]{0:T(1024)} %param.31) | copy-start | bytes 30724
  64.5 5.6 %collective-permute-start.8 = (bf16[2,88,128]{2,1,0:T(8,128)(2,1)S(1)}, bf16[2,88,128]{2,1,0:T(8,128)(2,1)S(1)}, u32[]{:S(2)}, u32[]{:S(2)}) collective-permute-start(bf16[2,88,128]{2,1,0:T(8,128)(2,1)S(1)} %concatenate.47), channel_id=1, source_target_pairs={{0,16},{8,24},{16,0},{24,8},{32,48},{40,56},{48,32},{56,40},{64,80... | collective-permute-start | bytes 135176 | tf_op jit(solution)/shard_map/ppermute | solution.py:69
  70.3 7.9 %collective-permute-start.9 = (bf16[88,128]{1,0:T(8,128)(2,1)S(1)}, bf16[88,128]{1,0:T(8,128)(2,1)S(1)}, u32[]{:S(2)}, u32[]{:S(2)}) collective-permute-start(bf16[88,128]{1,0:T(8,128)(2,1)S(1)} %concatenate.50), channel_id=1, source_target_pairs={{0,128},{8,136},{16,144},{24,152},{32,160},{40,168},{48,176},{56,1... | collective-permute-start | bytes 67592 | tf_op jit(solution)/shard_map/ppermute | solution.py:69
  80.6 20.0 %copy-start.1 = (bf16[2560,512]{1,0:T(8,128)(2,1)S(1)}, bf16[2560,512]{1,0:T(8,128)(2,1)}, u32[]{:S(2)}) copy-start(bf16[2560,512]{1,0:T(8,128)(2,1)} %param.28) | copy-start | bytes 7864324
  82.6 5.6 %collective-permute-start.10 = (bf16[32,2560]{1,0:T(8,128)(2,1)S(1)}, bf16[32,2560]{1,0:T(8,128)(2,1)S(1)}, u32[]{:S(2)}, u32[]{:S(2)}) collective-permute-start(bf16[32,2560]{1,0:T(8,128)(2,1)S(1)} %convolution_convert_fusion.1), channel_id=1, source_target_pairs={{0,4},{1,5},{2,6},{3,7},{4,0},{5,1},{6,2},{7,3},{8,9},{9,8},{10,11... | collective-permute-start | bytes 491528 | tf_op jit(solution)/shard_map/ppermute | solution.py:161
  88.2 5.4 %collective-permute-start.11 = (bf16[32,2560]{1,0:T(8,128)(2,1)S(1)}, bf16[32,2560]{1,0:T(8,128)(2,1)S(1)}, u32[]{:S(2)}, u32[]{:S(2)}) collective-permute-start(bf16[32,2560]{1,0:T(8,128)(2,1)S(1)} %add_convert_fusion.5), channel_id=1, source_target_pairs={{0,1},{1,0},{2,3},{3,2},{4,5},{5,4},{6,7},{7,6},{8,11},{9,10},{10,... | collective-permute-start | bytes 491528 | tf_op jit(solution)/shard_map/ppermute | solution.py:161
  93.7 6.6 %collective-permute-start.12 = (bf16[32,2560]{1,0:T(8,128)(2,1)S(1)}, bf16[32,2560]{1,0:T(8,128)(2,1)S(1)}, u32[]{:S(2)}, u32[]{:S(2)}) collective-permute-start(bf16[32,2560]{1,0:T(8,128)(2,1)S(1)} %add_convert_fusion.4), channel_id=1, source_target_pairs={{0,3},{1,2},{2,1},{3,0},{4,7},{5,6},{6,5},{7,4},{8,12},{9,13},{10,... | collective-permute-start | bytes 491528 | tf_op jit(solution)/shard_map/ppermute | solution.py:161
  101.1 21.3 %copy-start.4 = (f32[2560]{0:T(1024)S(1)}, f32[2560]{0:T(1024)}, u32[]{:S(2)}) copy-start(f32[2560]{0:T(1024)} %param.33) | copy-start | bytes 30724
  101.2 21.3 %copy-start.5 = (f32[2560]{0:T(1024)S(1)}, f32[2560]{0:T(1024)}, u32[]{:S(2)}) copy-start(f32[2560]{0:T(1024)} %param.32) | copy-start | bytes 30724
  104.0 5.4 %collective-permute-start.13 = (bf16[32,2560]{1,0:T(8,128)(2,1)S(1)}, bf16[32,2560]{1,0:T(8,128)(2,1)S(1)}, u32[]{:S(2)}, u32[]{:S(2)}) collective-permute-start(bf16[32,2560]{1,0:T(8,128)(2,1)S(1)} %convolution_convert_fusion), channel_id=1, source_target_pairs={{0,4},{1,5},{2,6},{3,7},{4,0},{5,1},{6,2},{7,3},{8,9},{9,8},{10,11... | collective-permute-start | bytes 491528 | tf_op jit(solution)/shard_map/ppermute | solution.py:161
  109.4 5.4 %collective-permute-start.14 = (bf16[32,2560]{1,0:T(8,128)(2,1)S(1)}, bf16[32,2560]{1,0:T(8,128)(2,1)S(1)}, u32[]{:S(2)}, u32[]{:S(2)}) collective-permute-start(bf16[32,2560]{1,0:T(8,128)(2,1)S(1)} %add_convert_fusion.2), channel_id=1, source_target_pairs={{0,1},{1,0},{2,3},{3,2},{4,5},{5,4},{6,7},{7,6},{8,11},{9,10},{10,... | collective-permute-start | bytes 491528 | tf_op jit(solution)/shard_map/ppermute | solution.py:161
  114.9 6.6 %collective-permute-start.15 = (bf16[32,2560]{1,0:T(8,128)(2,1)S(1)}, bf16[32,2560]{1,0:T(8,128)(2,1)S(1)}, u32[]{:S(2)}, u32[]{:S(2)}) collective-permute-start(bf16[32,2560]{1,0:T(8,128)(2,1)S(1)} %add_convert_fusion.1), channel_id=1, source_target_pairs={{0,3},{1,2},{2,1},{3,0},{4,7},{5,6},{6,5},{7,4},{8,12},{9,13},{10,... | collective-permute-start | bytes 491528 | tf_op jit(solution)/shard_map/ppermute | solution.py:161

commit v13 on v11

--- a/solution.py
+++ b/solution.py
@@ -15,7 +15,7 @@
 
 
 PACK = 88
-BLOCK_PROMPTS = 8
+BLOCK_PROMPTS = 16
 
 
 def prefix_kernel(count_ref, half_ref, q_ref, kt_ref, vt_ref, out_ref):

time: 122 us -> 122 us (level)
  no operation moved by 1% of the time
where the time goes in v13:
time: 122 us; the launch traced here: 121 us
  waiting for transfers between devices  51.5 us (42%)
  starting transfers between devices  32.5 us (27%)
  Pallas kernels  11.2 us (9%)
  matrix products  9.92 us (8%)
  other arithmetic  9.36 us (8%)
  local copies, waits for them, and re-layouts  5.44 us (4%)
    ppermute x10, waiting for transfers between devices, exchange(): return lax.ppermute(x, axis, perm=[(i, i ^ 1 << bit) for i in range(n)])  26.6 us
    ppermute x6, waiting for transfers between devices, allreduce_bf16(): other = lax.ppermute(cur, ('req', 'mlp'), perm=perm)  24.9 us
    ppermute x10, starting transfers between devices, exchange(): return lax.ppermute(x, axis, perm=[(i, i ^ 1 << bit) for i in range(n)])  22.6 us
    pallas_call x2, Pallas kernels, prefix_partials(): pl.pallas_call(prefix_kernel, grid_spec=pltpu.PrefetchScalarGridSpec(num_...  11.2 us
    ppermute x6, starting transfers between devices, allreduce_bf16(): other = lax.ppermute(cur, ('req', 'mlp'), perm=perm)  9.98 us
    dot_general x1, matrix products, on_device(): jnp.dot(hidden, down_weight, preferred_element_type=jnp.float32)  2.82 us
  transfers between devices with their start and end apart: 16, of which 14 were waited for; matrix products, arithmetic and copies ran while one was open for 7% of the time, Pallas kernels for 5%

profile of v13, /device:TPU:6, one launch (start us, length us, event | category | flops | bytes accessed | tf_op | source)
XLA Modules:
  0.0 121.2 jit_solution(11701373180827270680)
XLA Ops:
  0.6 7.3 %collective-permute-start = (bf16[1,32,320]{2,1,0:T(8,128)(2,1)}, bf16[1,32,320]{2,1,0:T(8,128)(2,1)S(1)}, u32[]{:S(2)}, u32[]{:S(2)}) collective-permute-start(bf16[1,32,320]{2,1,0:T(8,128)(2,1)} %bitcast.198), channel_id=1, source_target_pairs={{0,128},{8,136},{16,144},{24,152},{32,160},{40,168},{48,176},{56,1... | collective-permute-start | bytes 61448 | tf_op jit(solution)/shard_map/ppermute | solution.py:69
  7.9 0.7 iota_compare_fusion
  8.6 1.2 subtract_clamp_fusion.count_ref
  9.9 0.7 select_bitcast_fusion.5
  10.7 1.5 %collective-permute-start.1 = (bf16[2,1,32,320]{3,2,0,1:T(8,128)(2,1)S(1)}, bf16[2,1,32,320]{3,2,0,1:T(8,128)(2,1)S(1)}, u32[]{:S(2)}, u32[]{:S(2)}) collective-permute-start(bf16[2,1,32,320]{3,2,0,1:T(8,128)(2,1)S(1)} %fusion.33), channel_id=1, source_target_pairs={{0,16},{8,24},{16,0},{24,8},{32,48},{40,56},{48,32},{56,40},{64,80... | collective-permute-start | bytes 122888 | tf_op jit(solution)/shard_map/ppermute | solution.py:69
  12.2 4.2 %collective-permute-done.1 = bf16[2,1,32,320]{3,2,0,1:T(8,128)(2,1)S(1)} collective-permute-done((bf16[2,1,32,320]{3,2,0,1:T(8,128)(2,1)S(1)}, bf16[2,1,32,320]{3,2,0,1:T(8,128)(2,1)S(1)}, u32[]{:S(2)}, u32[]{:S(2)}) %collective-permute-start.1) | collective-permute-done | bytes 40992 | tf_op jit(solution)/shard_map/ppermute | solution.py:69
  16.5 2.1 %collective-permute-start.2 = (bf16[2,2,1,32,320]{4,3,1,0,2:T(8,128)(2,1)S(1)}, bf16[2,2,1,32,320]{4,3,1,0,2:T(8,128)(2,1)S(1)}, u32[]{:S(2)}, u32[]{:S(2)}) collective-permute-start(bf16[2,2,1,32,320]{4,3,1,0,2:T(8,128)(2,1)S(1)} %bitcast.191), channel_id=1, source_target_pairs={{0,64},{8,72},{16,80},{24,88},{32,96},{40,104},{48,112},{56,120},{... | collective-permute-start | bytes 245768 | tf_op jit(solution)/shard_map/ppermute | solution.py:69
  18.6 0.8 reshape.182
  19.4 1.3 %select_reduce_fusion = (f32[16,2,4]{2,1,0:T(2,128)S(1)}, f32[16,2,4,128]{3,2,1,0:T(4,128)S(1)}) fusion(pred[16,128]{1,0:T(8,128)(4,1)S(1)} %iota_compare_fusion, bf16[16,2,4,80]{3,2,1,0:T(4,128)(2,1)S(1)} %reshape.182, bf16[1,16,128,80]{2,3,1,0:T(8,128)(2,1)} %param.23), kind=kOutput, calls=%fused_computation.75 | convolution fusion | flops 2670464 | bytes 416256 | tf_op jit(solution)/shard_map/sjkgh,stkh->ksjgt/dot_general | solution.py:187
  20.7 1.1 select_reduce_fusion.1
  21.8 1.3 %collective-permute-done.2 = bf16[2,2,1,32,320]{4,3,1,0,2:T(8,128)(2,1)S(1)} collective-permute-done((bf16[2,2,1,32,320]{4,3,1,0,2:T(8,128)(2,1)S(1)}, bf16[2,2,1,32,320]{4,3,1,0,2:T(8,128)(2,1)S(1)}, u32[]{:S(2)}, u32[]{:S(2)}) %collective-permute-start.2) | collective-permute-done | bytes 81952 | tf_op jit(solution)/shard_map/ppermute | solution.py:69
  23.2 0.7 collective-permute-start.3
  24.5 4.5 %collective-permute-done.3 = bf16[2,2,2,1,32,320]{5,4,2,1,0,3:T(8,128)(2,1)S(1)} collective-permute-done((bf16[2,2,2,1,32,320]{5,4,2,1,0,3:T(8,128)(2,1)S(1)}, bf16[2,2,2,1,32,320]{5,4,2,1,0,3:T(8,128)(2,1)S(1)}, u32[]{:S(2)}, u32[]{:S(2)}) %collective-permute-start.3) | collective-permute-done | bytes 163872 | tf_op jit(solution)/shard_map/ppermute | solution.py:69
  29.3 1.3 %fusion.5 = f32[16,2,4,80]{3,2,1,0:T(4,128)S(1)} fusion(bf16[1,16,128,80]{2,3,1,0:T(8,128)(2,1)} %param.24, f32[16,2,4,128]{3,2,1,0:T(4,128)S(1)} %get-tuple-element.52, f32[16,2,4]{2,1,0:T(2,128)S(1)} %max.43, pred[16,128]{1,0:T(8,128)(4,1)S(1)} %iota_compare_fusion), kind=kOutput, calls=%fused_computation.25 | convolution fusion | flops 2670592 | bytes 436736 | tf_op jit(solution)/shard_map/ksjgt,stkh->ksjgh/dot_general | solution.py:209
  30.6 0.9 fusion
  32.0 1.6 %reshape.187.q_ref = bf16[16,2,128,80]{3,2,1,0:T(8,128)(2,1)} reshape(bf16[1024,320]{1,0:T(8,128)(2,1)S(1)} %bitcast.189) | data formatting | bytes 1310720 | tf_op jit(solution)/shard_map/reshape | solution.py:222
  33.6 5.6 %shard_map.177 = f32[16,88,128]{2,1,0:T(8,128)} custom-call(s32[32]{0:T(128)} %subtract_clamp_fusion.count_ref, s32[1]{0:T(128)} %bitcast.50.half_ref, bf16[16,2,128,80]{3,2,1,0:T(8,128)(2,1)} %reshape.187.q_ref, bf16[16,2,80,512]{3,2,1,0:T(8,128)(2,1)} %bitcast.185, bf16[16,2,80,512]{3,2,1,0:T(8,128)(2,1)} %bitcast.187), custom_call_target="tpu_custom_call" | custom-call | flops 335544320 | bytes 3670016 | tf_op jit(solution)/shard_map/pallas_call | solution.py:46
  39.2 0.5 collective-permute-start.5
  39.7 5.6 %shard_map.176 = f32[16,88,128]{2,1,0:T(8,128)} custom-call(s32[32]{0:T(128)} %subtract_clamp_fusion.count_ref, s32[1]{0:T(128)} %bitcast.half_ref, bf16[16,2,128,80]{3,2,1,0:T(8,128)(2,1)} %reshape.187.q_ref, bf16[16,2,80,512]{3,2,1,0:T(8,128)(2,1)} %bitcast.186, bf16[16,2,80,512]{3,2,1,0:T(8,128)(2,1)} %bitcast.188), custom_call_target="tpu_custom_call" | custom-call | flops 335544320 | bytes 3670016 | tf_op jit(solution)/shard_map/pallas_call | solution.py:46
  45.3 0.9 subtract_exponential_fusion.1
  46.2 1.2 fusion.2
  47.4 0.9 fusion.14
  48.6 0.7 collective-permute-start.6
  49.3 5.9 %collective-permute-done.6 = bf16[2,2,2,88,128]{4,3,2,1,0:T(8,128)(2,1)S(1)} collective-permute-done((bf16[2,2,2,88,128]{4,3,2,1,0:T(8,128)(2,1)S(1)}, bf16[2,2,2,88,128]{4,3,2,1,0:T(8,128)(2,1)S(1)}, u32[]{:S(2)}, u32[]{:S(2)}) %collective-permute-start.6) | collective-permute-done | bytes 180256 | tf_op jit(solution)/shard_map/ppermute | solution.py:69
  55.5 1.9 %collective-permute-start.7 = (bf16[2,2,88,128]{3,2,0,1:T(8,128)(2,1)S(1)}, bf16[2,2,88,128]{3,2,0,1:T(8,128)(2,1)S(1)}, u32[]{:S(2)}, u32[]{:S(2)}) collective-permute-start(bf16[2,2,88,128]{3,2,0,1:T(8,128)(2,1)S(1)} %concatenate.44), channel_id=1, source_target_pairs={{0,64},{8,72},{16,80},{24,88},{32,96},{40,104},{48,112},{56,120},{... | collective-permute-start | bytes 270344 | tf_op jit(solution)/shard_map/ppermute | solution.py:69
  57.5 4.7 %collective-permute-done.7 = bf16[2,2,88,128]{3,2,0,1:T(8,128)(2,1)S(1)} collective-permute-done((bf16[2,2,88,128]{3,2,0,1:T(8,128)(2,1)S(1)}, bf16[2,2,88,128]{3,2,0,1:T(8,128)(2,1)S(1)}, u32[]{:S(2)}, u32[]{:S(2)}) %collective-permute-start.7) | collective-permute-done | bytes 90144 | tf_op jit(solution)/shard_map/ppermute | solution.py:69
  62.4 1.7 %collective-permute-start.8 = (bf16[2,88,128]{2,1,0:T(8,128)(2,1)S(1)}, bf16[2,88,128]{2,1,0:T(8,128)(2,1)S(1)}, u32[]{:S(2)}, u32[]{:S(2)}) collective-permute-start(bf16[2,88,128]{2,1,0:T(8,128)(2,1)S(1)} %concatenate.47), channel_id=1, source_target_pairs={{0,16},{8,24},{16,0},{24,8},{32,48},{40,56},{48,32},{56,40},{64,80... | collective-permute-start | bytes 135176 | tf_op jit(solution)/shard_map/ppermute | solution.py:69
  64.1 4.1 %collective-permute-done.8 = bf16[2,88,128]{2,1,0:T(8,128)(2,1)S(1)} collective-permute-done((bf16[2,88,128]{2,1,0:T(8,128)(2,1)S(1)}, bf16[2,88,128]{2,1,0:T(8,128)(2,1)S(1)}, u32[]{:S(2)}, u32[]{:S(2)}) %collective-permute-start.8) | collective-permute-done | bytes 45088 | tf_op jit(solution)/shard_map/ppermute | solution.py:69
  68.5 6.1 %collective-permute-start.9 = (bf16[88,128]{1,0:T(8,128)(2,1)S(1)}, bf16[88,128]{1,0:T(8,128)(2,1)S(1)}, u32[]{:S(2)}, u32[]{:S(2)}) collective-permute-start(bf16[88,128]{1,0:T(8,128)(2,1)S(1)} %concatenate.50), channel_id=1, source_target_pairs={{0,128},{8,136},{16,144},{24,152},{32,160},{40,168},{48,176},{56,1... | collective-permute-start | bytes 67592 | tf_op jit(solution)/shard_map/ppermute | solution.py:69
  74.6 1.8 %collective-permute-done.9 = bf16[88,128]{1,0:T(8,128)(2,1)S(1)} collective-permute-done((bf16[88,128]{1,0:T(8,128)(2,1)S(1)}, bf16[88,128]{1,0:T(8,128)(2,1)S(1)}, u32[]{:S(2)}, u32[]{:S(2)}) %collective-permute-start.9) | collective-permute-done | bytes 22560 | tf_op jit(solution)/shard_map/ppermute | solution.py:69
  76.4 0.5 broadcast.96
  76.9 0.7 fusion.54
  78.8 1.9 %convolution_convert_fusion.1 = bf16[32,2560]{1,0:T(8,128)(2,1)S(1)} fusion(bf16[32,320]{1,0:T(8,128)(2,1)S(1)} %reshape_transpose.3, bf16[320,2560]{1,0:T(8,128)(2,1)} %param.27), kind=kOutput, calls=%fused_computation.1 | convolution fusion | flops 52510720 | bytes 1822720 | tf_op jit(solution)/shard_map/dot_general | solution.py:256
  80.8 0.9 collective-permute-start.10
  81.6 4.5 %collective-permute-done.10 = bf16[32,2560]{1,0:T(8,128)(2,1)S(1)} collective-permute-done((bf16[32,2560]{1,0:T(8,128)(2,1)S(1)}, bf16[32,2560]{1,0:T(8,128)(2,1)S(1)}, u32[]{:S(2)}, u32[]{:S(2)}) %collective-permute-start.10) | collective-permute-done | bytes 163872 | tf_op jit(solution)/shard_map/ppermute | solution.py:139
  86.2 1.7 %collective-permute-start.11 = (bf16[32,2560]{1,0:T(8,128)(2,1)S(1)}, bf16[32,2560]{1,0:T(8,128)(2,1)S(1)}, u32[]{:S(2)}, u32[]{:S(2)}) collective-permute-start(bf16[32,2560]{1,0:T(8,128)(2,1)S(1)} %add_convert_fusion.5), channel_id=1, source_target_pairs={{0,1},{1,0},{2,3},{3,2},{4,5},{5,4},{6,7},{7,6},{8,11},{9,10},{10,... | collective-permute-start | bytes 491528 | tf_op jit(solution)/shard_map/ppermute | solution.py:139
  87.9 3.7 %collective-permute-done.11 = bf16[32,2560]{1,0:T(8,128)(2,1)S(1)} collective-permute-done((bf16[32,2560]{1,0:T(8,128)(2,1)S(1)}, bf16[32,2560]{1,0:T(8,128)(2,1)S(1)}, u32[]{:S(2)}, u32[]{:S(2)}) %collective-permute-start.11) | collective-permute-done | bytes 163872 | tf_op jit(solution)/shard_map/ppermute | solution.py:139
  91.7 3.1 %collective-permute-start.12 = (bf16[32,2560]{1,0:T(8,128)(2,1)S(1)}, bf16[32,2560]{1,0:T(8,128)(2,1)S(1)}, u32[]{:S(2)}, u32[]{:S(2)}) collective-permute-start(bf16[32,2560]{1,0:T(8,128)(2,1)S(1)} %add_convert_fusion.4), channel_id=1, source_target_pairs={{0,3},{1,2},{2,1},{3,0},{4,7},{5,6},{6,5},{7,4},{8,12},{9,13},{10,... | collective-permute-start | bytes 491528 | tf_op jit(solution)/shard_map/ppermute | solution.py:139
  94.7 3.6 %collective-permute-done.12 = bf16[32,2560]{1,0:T(8,128)(2,1)S(1)} collective-permute-done((bf16[32,2560]{1,0:T(8,128)(2,1)S(1)}, bf16[32,2560]{1,0:T(8,128)(2,1)S(1)}, u32[]{:S(2)}, u32[]{:S(2)}) %collective-permute-start.12) | collective-permute-done | bytes 163872 | tf_op jit(solution)/shard_map/ppermute | solution.py:139
  98.6 0.5 fusion.55
  99.2 2.8 %convolution_convert_fusion = bf16[32,2560]{1,0:T(8,128)(2,1)S(1)} fusion(bf16[512,2560]{1,0:T(8,128)(2,1)S(1)} %copy-done, bf16[32,2560]{1,0:T(8,128)(2,1)S(1)} %multiply_convert_fusion, bf16[2560,512]{1,0:T(8,128)(2,1)} %param.29, f32[32,512]{1,0:T(8,128)S(1)} %fusion.55), kind=kOutput, calls=%fused_computation | convolution fusion | flops 167952384 | bytes 5636096 | tf_op jit(solution)/shard_map/dot_general | solution.py:270
  102.0 0.9 collective-permute-start.13
  102.9 4.5 %collective-permute-done.13 = bf16[32,2560]{1,0:T(8,128)(2,1)S(1)} collective-permute-done((bf16[32,2560]{1,0:T(8,128)(2,1)S(1)}, bf16[32,2560]{1,0:T(8,128)(2,1)S(1)}, u32[]{:S(2)}, u32[]{:S(2)}) %collective-permute-start.13) | collective-permute-done | bytes 163872 | tf_op jit(solution)/shard_map/ppermute | solution.py:139
  107.9 5.0 %collective-permute-done.14 = bf16[32,2560]{1,0:T(8,128)(2,1)S(1)} collective-permute-done((bf16[32,2560]{1,0:T(8,128)(2,1)S(1)}, bf16[32,2560]{1,0:T(8,128)(2,1)S(1)}, u32[]{:S(2)}, u32[]{:S(2)}) %collective-permute-start.14) | collective-permute-done | bytes 163872 | tf_op jit(solution)/shard_map/ppermute | solution.py:139
  112.9 3.1 %collective-permute-start.15 = (bf16[32,2560]{1,0:T(8,128)(2,1)S(1)}, bf16[32,2560]{1,0:T(8,128)(2,1)S(1)}, u32[]{:S(2)}, u32[]{:S(2)}) collective-permute-start(bf16[32,2560]{1,0:T(8,128)(2,1)S(1)} %add_convert_fusion.1), channel_id=1, source_target_pairs={{0,3},{1,2},{2,1},{3,0},{4,7},{5,6},{6,5},{7,4},{8,12},{9,13},{10,... | collective-permute-start | bytes 491528 | tf_op jit(solution)/shard_map/ppermute | solution.py:139
  115.9 3.6 %collective-permute-done.15 = bf16[32,2560]{1,0:T(8,128)(2,1)S(1)} collective-permute-done((bf16[32,2560]{1,0:T(8,128)(2,1)S(1)}, bf16[32,2560]{1,0:T(8,128)(2,1)S(1)}, u32[]{:S(2)}, u32[]{:S(2)}) %collective-permute-start.15) | collective-permute-done | bytes 163872 | tf_op jit(solution)/shard_map/ppermute | solution.py:139
  119.7 0.7 dynamic-slice_convert_fusion
  120.4 0.7 multiply_reduce_fusion
  (112 shorter events, 4.9 us)
Async XLA Ops:
  0.6 98.5 %copy-start = (bf16[512,2560]{1,0:T(8,128)(2,1)S(1)}, bf16[512,2560]{1,0:T(8,128)(2,1)}, u32[]{:S(2)}) copy-start(bf16[512,2560]{1,0:T(8,128)(2,1)} %param.30) | copy-start | bytes 7864324
  0.6 9.3 %collective-permute-start = (bf16[1,32,320]{2,1,0:T(8,128)(2,1)}, bf16[1,32,320]{2,1,0:T(8,128)(2,1)S(1)}, u32[]{:S(2)}, u32[]{:S(2)}) collective-permute-start(bf16[1,32,320]{2,1,0:T(8,128)(2,1)} %bitcast.198), channel_id=1, source_target_pairs={{0,128},{8,136},{16,144},{24,152},{32,160},{40,168},{48,176},{56,1... | collective-permute-start | bytes 61448 | tf_op jit(solution)/shard_map/ppermute | solution.py:69
  10.7 5.7 %collective-permute-start.1 = (bf16[2,1,32,320]{3,2,0,1:T(8,128)(2,1)S(1)}, bf16[2,1,32,320]{3,2,0,1:T(8,128)(2,1)S(1)}, u32[]{:S(2)}, u32[]{:S(2)}) collective-permute-start(bf16[2,1,32,320]{3,2,0,1:T(8,128)(2,1)S(1)} %fusion.33), channel_id=1, source_target_pairs={{0,16},{8,24},{16,0},{24,8},{32,48},{40,56},{48,32},{56,40},{64,80... | collective-permute-start | bytes 122888 | tf_op jit(solution)/shard_map/ppermute | solution.py:69
  16.4 14.2 %copy-start.7 = (bf16[32,80]{1,0:T(8,128)(2,1)S(1)}, bf16[32,80]{1,0:T(8,128)(2,1)}, u32[]{:S(2)}) copy-start(bf16[32,80]{1,0:T(8,128)(2,1)} %param.20) | copy-start | bytes 15364
  16.5 6.7 %collective-permute-start.2 = (bf16[2,2,1,32,320]{4,3,1,0,2:T(8,128)(2,1)S(1)}, bf16[2,2,1,32,320]{4,3,1,0,2:T(8,128)(2,1)S(1)}, u32[]{:S(2)}, u32[]{:S(2)}) collective-permute-start(bf16[2,2,1,32,320]{4,3,1,0,2:T(8,128)(2,1)S(1)} %bitcast.191), channel_id=1, source_target_pairs={{0,64},{8,72},{16,80},{24,88},{32,96},{40,104},{48,112},{56,120},{... | collective-permute-start | bytes 245768 | tf_op jit(solution)/shard_map/ppermute | solution.py:69
  23.2 5.8 %collective-permute-start.3 = (bf16[2,2,2,1,32,320]{5,4,2,1,0,3:T(8,128)(2,1)S(1)}, bf16[2,2,2,1,32,320]{5,4,2,1,0,3:T(8,128)(2,1)S(1)}, u32[]{:S(2)}, u32[]{:S(2)}) collective-permute-start(bf16[2,2,2,1,32,320]{5,4,2,1,0,3:T(8,128)(2,1)S(1)} %fusion.11), channel_id=1, source_target_pairs={{0,32},{8,40},{16,48},{24,56},{32,0},{40,8},{48,16},{56,24},{64,96... | collective-permute-start | bytes 491528 | tf_op jit(solution)/shard_map/ppermute | solution.py:69
  29.2 2.3 %collective-permute-start.4 = (bf16[2,2,2,2,1,32,320]{6,5,3,2,1,0,4:T(8,128)(2,1)S(1)}, bf16[2,2,2,2,1,32,320]{6,5,3,2,1,0,4:T(8,128)(2,1)S(1)}, u32[]{:S(2)}, u32[]{:S(2)}) collective-permute-start(bf16[2,2,2,2,1,32,320]{6,5,3,2,1,0,4:T(8,128)(2,1)S(1)} %fusion.8), channel_id=1, source_target_pairs={{0,8},{8,0},{16,24},{24,16},{32,40},{40,32},{48,56},{56,48},{64,72... | collective-permute-start | bytes 983048 | tf_op jit(solution)/shard_map/ppermute | solution.py:69
  39.2 6.1 %collective-permute-start.5 = (f32[16,88,128]{2,1,0:T(8,128)}, f32[16,88,128]{2,1,0:T(8,128)S(1)}, u32[]{:S(2)}, u32[]{:S(2)}) collective-permute-start(f32[16,88,128]{2,1,0:T(8,128)} %shard_map.177), channel_id=1, source_target_pairs={{0,8},{8,0},{16,24},{24,16},{32,40},{40,32},{48,56},{56,48},{64,72... | collective-permute-start | bytes 2162696 | tf_op jit(solution)/shard_map/ppermute | solution.py:69
  48.6 6.6 %collective-permute-start.6 = (bf16[2,2,2,88,128]{4,3,2,1,0:T(8,128)(2,1)S(1)}, bf16[2,2,2,88,128]{4,3,2,1,0:T(8,128)(2,1)S(1)}, u32[]{:S(2)}, u32[]{:S(2)}) collective-permute-start(bf16[2,2,2,88,128]{4,3,2,1,0:T(8,128)(2,1)S(1)} %concatenate.41), channel_id=1, source_target_pairs={{0,32},{8,40},{16,48},{24,56},{32,0},{40,8},{48,16},{56,24},{64,96... | collective-permute-start | bytes 540680 | tf_op jit(solution)/shard_map/ppermute | solution.py:69
  55.3 23.2 %copy-start.3 = (f32[1,16,2,4,80]{4,3,2,1,0:T(4,128)S(1)}, f32[1,16,2,4,80]{4,3,2,1,0:T(4,128)}, u32[]{:S(2)}) copy-start(f32[1,16,2,4,80]{4,3,2,1,0:T(4,128)} %fusion) | copy-start | bytes 122884
  55.5 6.6 %collective-permute-start.7 = (bf16[2,2,88,128]{3,2,0,1:T(8,128)(2,1)S(1)}, bf16[2,2,88,128]{3,2,0,1:T(8,128)(2,1)S(1)}, u32[]{:S(2)}, u32[]{:S(2)}) collective-permute-start(bf16[2,2,88,128]{3,2,0,1:T(8,128)(2,1)S(1)} %concatenate.44), channel_id=1, source_target_pairs={{0,64},{8,72},{16,80},{24,88},{32,96},{40,104},{48,112},{56,120},{... | collective-permute-start | bytes 270344 | tf_op jit(solution)/shard_map/ppermute | solution.py:69
  62.3 36.0 %copy-start.2 = (bf16[32,2560]{1,0:T(8,128)(2,1)S(1)}, bf16[32,2560]{1,0:T(8,128)(2,1)}, u32[]{:S(2)}) copy-start(bf16[32,2560]{1,0:T(8,128)(2,1)} %param.17) | copy-start | bytes 491524
  62.3 36.2 %copy-start.6 = (f32[2560]{0:T(1024)S(1)}, f32[2560]{0:T(1024)}, u32[]{:S(2)}) copy-start(f32[2560]{0:T(1024)} %param.31) | copy-start | bytes 30724
  62.4 5.8 %collective-permute-start.8 = (bf16[2,88,128]{2,1,0:T(8,128)(2,1)S(1)}, bf16[2,88,128]{2,1,0:T(8,128)(2,1)S(1)}, u32[]{:S(2)}, u32[]{:S(2)}) collective-permute-start(bf16[2,88,128]{2,1,0:T(8,128)(2,1)S(1)} %concatenate.47), channel_id=1, source_target_pairs={{0,16},{8,24},{16,0},{24,8},{32,48},{40,56},{48,32},{56,40},{64,80... | collective-permute-start | bytes 135176 | tf_op jit(solution)/shard_map/ppermute | solution.py:69
  68.5 7.9 %collective-permute-start.9 = (bf16[88,128]{1,0:T(8,128)(2,1)S(1)}, bf16[88,128]{1,0:T(8,128)(2,1)S(1)}, u32[]{:S(2)}, u32[]{:S(2)}) collective-permute-start(bf16[88,128]{1,0:T(8,128)(2,1)S(1)} %concatenate.50), channel_id=1, source_target_pairs={{0,128},{8,136},{16,144},{24,152},{32,160},{40,168},{48,176},{56,1... | collective-permute-start | bytes 67592 | tf_op jit(solution)/shard_map/ppermute | solution.py:69
  78.8 19.8 %copy-start.1 = (bf16[2560,512]{1,0:T(8,128)(2,1)S(1)}, bf16[2560,512]{1,0:T(8,128)(2,1)}, u32[]{:S(2)}) copy-start(bf16[2560,512]{1,0:T(8,128)(2,1)} %param.28) | copy-start | bytes 7864324
  80.8 5.4 %collective-permute-start.10 = (bf16[32,2560]{1,0:T(8,128)(2,1)S(1)}, bf16[32,2560]{1,0:T(8,128)(2,1)S(1)}, u32[]{:S(2)}, u32[]{:S(2)}) collective-permute-start(bf16[32,2560]{1,0:T(8,128)(2,1)S(1)} %convolution_convert_fusion.1), channel_id=1, source_target_pairs={{0,4},{1,5},{2,6},{3,7},{4,0},{5,1},{6,2},{7,3},{8,9},{9,8},{10,11... | collective-permute-start | bytes 491528 | tf_op jit(solution)/shard_map/ppermute | solution.py:139
  86.2 5.4 %collective-permute-start.11 = (bf16[32,2560]{1,0:T(8,128)(2,1)S(1)}, bf16[32,2560]{1,0:T(8,128)(2,1)S(1)}, u32[]{:S(2)}, u32[]{:S(2)}) collective-permute-start(bf16[32,2560]{1,0:T(8,128)(2,1)S(1)} %add_convert_fusion.5), channel_id=1, source_target_pairs={{0,1},{1,0},{2,3},{3,2},{4,5},{5,4},{6,7},{7,6},{8,11},{9,10},{10,... | collective-permute-start | bytes 491528 | tf_op jit(solution)/shard_map/ppermute | solution.py:139
  91.7 6.6 %collective-permute-start.12 = (bf16[32,2560]{1,0:T(8,128)(2,1)S(1)}, bf16[32,2560]{1,0:T(8,128)(2,1)S(1)}, u32[]{:S(2)}, u32[]{:S(2)}) collective-permute-start(bf16[32,2560]{1,0:T(8,128)(2,1)S(1)} %add_convert_fusion.4), channel_id=1, source_target_pairs={{0,3},{1,2},{2,1},{3,0},{4,7},{5,6},{6,5},{7,4},{8,12},{9,13},{10,... | collective-permute-start | bytes 491528 | tf_op jit(solution)/shard_map/ppermute | solution.py:139
  99.1 21.3 %copy-start.4 = (f32[2560]{0:T(1024)S(1)}, f32[2560]{0:T(1024)}, u32[]{:S(2)}) copy-start(f32[2560]{0:T(1024)} %param.33) | copy-start | bytes 30724
  99.2 21.3 %copy-start.5 = (f32[2560]{0:T(1024)S(1)}, f32[2560]{0:T(1024)}, u32[]{:S(2)}) copy-start(f32[2560]{0:T(1024)} %param.32) | copy-start | bytes 30724
  102.0 5.4 %collective-permute-start.13 = (bf16[32,2560]{1,0:T(8,128)(2,1)S(1)}, bf16[32,2560]{1,0:T(8,128)(2,1)S(1)}, u32[]{:S(2)}, u32[]{:S(2)}) collective-permute-start(bf16[32,2560]{1,0:T(8,128)(2,1)S(1)} %convolution_convert_fusion), channel_id=1, source_target_pairs={{0,4},{1,5},{2,6},{3,7},{4,0},{5,1},{6,2},{7,3},{8,9},{9,8},{10,11... | collective-permute-start | bytes 491528 | tf_op jit(solution)/shard_map/ppermute | solution.py:139
  107.4 5.4 %collective-permute-start.14 = (bf16[32,2560]{1,0:T(8,128)(2,1)S(1)}, bf16[32,2560]{1,0:T(8,128)(2,1)S(1)}, u32[]{:S(2)}, u32[]{:S(2)}) collective-permute-start(bf16[32,2560]{1,0:T(8,128)(2,1)S(1)} %add_convert_fusion.2), channel_id=1, source_target_pairs={{0,1},{1,0},{2,3},{3,2},{4,5},{5,4},{6,7},{7,6},{8,11},{9,10},{10,... | collective-permute-start | bytes 491528 | tf_op jit(solution)/shard_map/ppermute | solution.py:139
  112.9 6.6 %collective-permute-start.15 = (bf16[32,2560]{1,0:T(8,128)(2,1)S(1)}, bf16[32,2560]{1,0:T(8,128)(2,1)S(1)}, u32[]{:S(2)}, u32[]{:S(2)}) collective-permute-start(bf16[32,2560]{1,0:T(8,128)(2,1)S(1)} %add_convert_fusion.1), channel_id=1, source_target_pairs={{0,3},{1,2},{2,1},{3,0},{4,7},{5,6},{6,5},{7,4},{8,12},{9,13},{10,... | collective-permute-start | bytes 491528 | tf_op jit(solution)/shard_map/ppermute | solution.py:139
